TPU v7x, 128 devices: a whole 4x4x4 slice. The times are simulated.
128 devices in a mesh: lat: 32 (over x, z, core), sub: 4 (over y).
Axes of the slice: x: 4, y: 4, z: 4, core: 2. Of those that a mesh axis runs over, the one named last changes fastest.
Arguments:
- runoff: bfloat16 [262144, 256], P(('lat', 'sub'))
- weight_blocks: bfloat16 [2048, 2, 128, 128], P(('lat', 'sub')), may hold values from -0.1875 to 0.1875
- block_zone: int32 [2048, 2], P(('lat', 'sub')), may hold values from 0 to 511, as said below
- climatology: float32 [65536, 256], P(('lat', 'sub')), may hold values from -6 to 6
- zone_weight: float32 [65536], P(('lat', 'sub')), as said below
Outputs:
- scores: float32 [65536, 256], P(('lat', 'sub'))
- factor: float32 [256, 256], replicated
Inputs may be any that keep to these rules, and one draw needn't show every extreme that they name: block_zone[c, k] names a zone block held by the device that holds cell block c, or by the device just before or just after it in the order lat-major, sub-minor; each device's own zone blocks are all named by its own cell blocks. `zone_weight`: positive.
All inputs are finite; a program needn't handle non-finite values.
Results may differ from a plain program's by a relative error of at most 0.0003.
Values sent between devices are 32-bit elements; how exact they have to be, the bound alone decides.
No kernel may reach another device: no remote copies, remote signals or barrier semaphores. Data moves between devices by JAX's collectives and lax.ppermute only.
A program may use at most 64 MiB of HBM per device.

v0:
```python
import math

import jax
import jax.numpy as jnp
from jax import lax
from jax.sharding import PartitionSpec as P

exact_mode = lax.Precision.HIGHEST


def shifted(value, axis, steps):
    count = lax.axis_size(axis)
    initial, last = (max(0, -steps), min(count, count - steps))
    return lax.ppermute(value, axis, [(source, source + steps) for source in range(initial, last)])


def body(runoff, weight_blocks, block_zone, climatology, zone_weight):
    block_count = weight_blocks.shape[0]
    slot_count = weight_blocks.shape[1]
    block_size = weight_blocks.shape[2]
    day_count = runoff.shape[1]
    owned_blocks = climatology.shape[0] // block_size
    device_index = lax.axis_index(("lat", "sub"))
    cell_rows = runoff.reshape(block_count, block_size, day_count)
    partial_value = jnp.einsum(
        "ckiz,cit->ckzt", weight_blocks, cell_rows, preferred_element_type=jnp.float32
    )
    partial_value = partial_value.reshape(block_count * slot_count, block_size * day_count)
    target_slot = block_zone.reshape(-1) - (device_index - 1) * owned_blocks
    window_slots = jnp.arange(3 * owned_blocks, dtype=jnp.int32)
    one_hot = (window_slots[:, None] == target_slot[None, :]).astype(jnp.float32)
    tables = jnp.dot(
        one_hot, partial_value, precision=exact_mode, preferred_element_type=jnp.float32
    )
    tables = tables.reshape(3 * owned_blocks, block_size, day_count)
    from_before = shifted(tables[2 * owned_blocks :], ("lat", "sub"), 1)
    from_after = shifted(tables[:owned_blocks], ("lat", "sub"), -1)
    summed = tables[owned_blocks : 2 * owned_blocks] + from_before + from_after
    aggregated = summed.reshape(owned_blocks * block_size, day_count)
    anomaly = zone_weight[:, None] * (aggregated - climatology)
    local_gram = jnp.dot(
        anomaly.T, anomaly, precision=exact_mode, preferred_element_type=jnp.float32
    )
    total_gram = lax.psum(local_gram, ("lat", "sub"))
    upper = jnp.linalg.cholesky(total_gram).T
    solved = jax.scipy.linalg.solve_triangular(upper.T, anomaly.T, lower=True)
    root = math.sqrt(anomaly.shape[0] * lax.axis_size(("lat", "sub")))
    return (solved.T * root, upper / root)


def solution(mesh):
    return jax.shard_map(
        body,
        mesh=mesh,
        in_specs=(
            P(("lat", "sub"), None),
            P(("lat", "sub"), None, None, None),
            P(("lat", "sub"), None),
            P(("lat", "sub"), None),
            P(("lat", "sub")),
        ),
        out_specs=(P(("lat", "sub"), None), P()),
        check_vma=False,
    )
```

profile of v0, /device:TPU:1, one launch (start us, length us, event | category | flops | bytes accessed | tf_op | source)
XLA Modules:
  0.0 259.6 jit_solution(4999907190113027815)
XLA Ops:
  7.2 0.0 copy-start
  7.2 0.0 all-reduce.3.cloned.1.call-start
  7.2 1.2 copy-done
  8.4 2.0 fusion.16
  10.4 0.0 copy-start.3
  10.4 4.4 %copy.22 = f32[4,8,128,256]{3,1,2,0:T(8,128)} copy(f32[4,8,128,256]{3,2,1,0:T(8,128)S(1)} %bitcast.68) | data formatting | bytes 8388608
  14.8 0.0 copy-done.3
  14.8 0.1 copy.13
  14.8 0.1 sub.22
  14.9 3.8 %fusion.12 = f32[12,32768]{1,0:T(8,128)S(1)} fusion(f32[32,32768]{1,0:T(8,128)} %bitcast.67, s32[32]{0:T(128)S(1)} %sub.22), kind=kOutput, calls=%fused_computation.33 | convolution fusion | flops 150995328 | bytes 5767296 | tf_op jit(solution)/shard_map/dot_general | solution.py:32
  18.8 0.0 copy-start.1
  18.8 0.0 copy-start.2
  18.8 0.2 fusion.15
  19.0 0.1 copy.29
  19.1 6.0 %collective-permute-start.1 = (f32[4,128,256]{2,1,0:T(8,128)S(1)}, f32[4,128,256]{2,1,0:T(8,128)S(1)}, u32[]{:S(2)}, u32[]{:S(2)}) collective-permute-start(f32[4,128,256]{2,1,0:T(8,128)S(1)} %bitcast.74), channel_id=1, source_target_pairs={{1,0},{2,1},{3,2},{4,3},{5,4},{6,5},{7,6},{8,7},{9,8},{10,9},{11,1... | collective-permute-start | bytes 1572872 | tf_op jit(solution)/shard_map/ppermute | solution.py:14
  25.2 0.1 copy.30
  25.3 2.1 collective-permute-start
  27.4 9.5 %collective-permute-done.1 = f32[4,128,256]{2,1,0:T(8,128)S(1)} collective-permute-done((f32[4,128,256]{2,1,0:T(8,128)S(1)}, f32[4,128,256]{2,1,0:T(8,128)S(1)}, u32[]{:S(2)}, u32[]{:S(2)}) %collective-permute-start.1) | collective-permute-done | bytes 524320 | tf_op jit(solution)/shard_map/ppermute | solution.py:14
  36.9 5.7 %collective-permute-done = f32[4,128,256]{2,1,0:T(8,128)S(1)} collective-permute-done((f32[4,128,256]{2,1,0:T(8,128)S(1)}, f32[4,128,256]{2,1,0:T(8,128)S(1)}, u32[]{:S(2)}, u32[]{:S(2)}) %collective-permute-start) | collective-permute-done | bytes 524320 | tf_op jit(solution)/shard_map/ppermute | solution.py:14
  42.6 0.1 fusion
  42.7 0.0 copy-done.1
  42.7 0.0 copy-done.2
  42.7 0.1 fusion.2
  42.9 1.7 fusion.17
  44.6 0.0 all-reduce.3.cloned.1.call-update
  44.6 143.0 %all-reduce.3.cloned.1.call-done = f32[256,256]{0,1:T(8,128)} async-done(((f32[256,256]{0,1:T(8,128)}), f32[256,256]{0,1:T(8,128)}) %all-reduce.3.cloned.1.call-update) | async-done | bytes 262160 | tf_op jit(solution)/shard_map/psum | solution.py:44
  187.6 1.1 copy.16
  188.7 1.0 fusion.5
  189.7 11.7 %cholesky.50 = f32[128,128]{1,0:T(8,128)S(1)} custom-call(f32[128,128]{1,0:T(8,128)S(1)} %cholesky.118), custom_call_target="Cholesky" | custom-call | tf_op jit(solution)/shard_map/jit(cholesky)/cholesky | solution.py:45
  201.4 9.8 %custom-call.15 = f32[1,128,128]{1,2,0:T(8,128)S(1)} custom-call(f32[1,128,128]{2,1,0:T(8,128)S(1)} %get-tuple-element.32), custom_call_target="InvertDiagBlocksLowerTriangular" | custom-call | tf_op jit(solution)/shard_map/jit(cholesky)/cholesky | solution.py:45
  211.3 0.2 constant_dynamic-update-slice_fusion.1
  211.5 0.3 convolution_subtract_fusion.1
  211.7 11.7 %cholesky.105 = f32[128,128]{1,0:T(8,128)S(1)} custom-call(f32[128,128]{1,0:T(8,128)S(1)} %convolution_subtract_fusion.1), custom_call_target="Cholesky" | custom-call | tf_op jit(solution)/shard_map/jit(cholesky)/cholesky | solution.py:45
  223.5 0.7 compare_reduce_fusion
  225.5 0.1 triangular_solve.57
  225.6 4.1 %while.1 = (s32[]{:T(128)}, f32[256,256]{1,0:T(8,128)S(1)}, s32[2,2]{1,0:T(2,128)S(1)}, f32[2,128,128]{2,1,0:T(8,128)S(1)}, s32[]{:T(128)}) while((s32[]{:T(128)}, f32[256,256]{1,0:T(8,128)S(1)}, s32[2,2]{1,0:T(2,128)S(1)}, f32[2,128,128]{2,1,0:T(8,128)S(1)}, s32[]{:T(128)}) %tuple.32), condition=%wide.while_cond, body=%wide.while_body.sunk | while | flops 2 | bytes 131189 | solution.py:46
  225.8 0.6 fusion.28
  226.4 1.4 bitcast_dynamic-update-slice_fusion.2
  227.8 0.6 fusion.28
  228.4 1.4 bitcast_dynamic-update-slice_fusion.2
  229.7 19.7 %custom-call.16 = f32[2,128,128]{1,2,0:T(8,128)S(1)} custom-call(f32[2,128,128]{2,1,0:T(8,128)S(1)} %get-tuple-element.9), custom_call_target="InvertDiagBlocksLowerTriangular" | custom-call | tf_op jit(solution)/shard_map/jit(_solve_triangular)/triangular_solve | solution.py:46
  249.4 0.4 fusion.3
  249.9 0.6 convolution_subtract_fusion
  250.5 0.4 fusion.8
  250.9 1.0 copy.17
  251.9 0.8 copy.18
  (11 shorter events, 0.2 us)
Async XLA Ops:
  7.2 1.2 copy-start
  7.2 180.4 %all-reduce.3.cloned.1.call-start = ((), (), s32[]{:S(2)}) async-start(), calls=%async_computation | async-start | bytes 524288 | tf_op jit(solution)/shard_map/psum | solution.py:44
  10.4 4.4 %copy-start.3 = (s32[16,2]{0,1:T(2,128)S(1)}, s32[16,2]{0,1:T(2,128)}, u32[]{:S(2)}) copy-start(s32[16,2]{0,1:T(2,128)} %param.7) | copy-start | bytes 388
  18.8 23.9 %copy-start.1 = (f32[512,256]{1,0:T(8,128)S(1)}, f32[512,256]{1,0:T(8,128)}, u32[]{:S(2)}) copy-start(f32[512,256]{1,0:T(8,128)} %param.8) | copy-start | bytes 1572868
  18.8 23.9 %copy-start.2 = (f32[512]{0:T(512)S(1)}, f32[512]{0:T(512)}, u32[]{:S(2)}) copy-start(f32[512]{0:T(512)} %param.9) | copy-start | bytes 6148
  19.1 17.8 %collective-permute-start.1 = (f32[4,128,256]{2,1,0:T(8,128)S(1)}, f32[4,128,256]{2,1,0:T(8,128)S(1)}, u32[]{:S(2)}, u32[]{:S(2)}) collective-permute-start(f32[4,128,256]{2,1,0:T(8,128)S(1)} %bitcast.74), channel_id=1, source_target_pairs={{1,0},{2,1},{3,2},{4,3},{5,4},{6,5},{7,6},{8,7},{9,8},{10,9},{11,1... | collective-permute-start | bytes 1572872 | tf_op jit(solution)/shard_map/ppermute | solution.py:14
  25.3 17.3 %collective-permute-start = (f32[4,128,256]{2,1,0:T(8,128)S(1)}, f32[4,128,256]{2,1,0:T(8,128)S(1)}, u32[]{:S(2)}, u32[]{:S(2)}) collective-permute-start(f32[4,128,256]{2,1,0:T(8,128)S(1)} %bitcast.75), channel_id=1, source_target_pairs={{0,1},{1,2},{2,3},{3,4},{4,5},{5,6},{6,7},{7,8},{8,9},{9,10},{10,1... | collective-permute-start | bytes 1572872 | tf_op jit(solution)/shard_map/ppermute | solution.py:14
Sparse Core Ops, SparseCore 0:
  44.7 142.8 all-reduce.2
where the time goes:
time: 260 us
  waiting for transfers between devices  158 us (61%)
  other arithmetic  55 us (21%)
  between operations  15.5 us (6%)
  local copies, waits for them, and re-layouts  13.1 us (5%)
  matrix products  9.41 us (4%)
  starting transfers between devices  8.16 us (3%)
    psum x1, waiting for transfers between devices, body(): total_gram = lax.psum(local_gram, ('lat', 'sub'))  143 us
    another operation x6, other arithmetic, body(): upper = jnp.linalg.cholesky(total_gram).T  34 us
    another operation x2, other arithmetic, body(): solved = jax.scipy.linalg.solve_triangular(upper.T, anomaly.T, lower=True)  19.7 us
    ppermute x2, waiting for transfers between devices, shifted(): lax.ppermute(value, axis, [(source, source + steps) for source in range(i...  15.2 us
    ppermute x2, starting transfers between devices, shifted(): lax.ppermute(value, axis, [(source, source + steps) for source in range(i...  8.12 us
    unnamed x13, local copies, waits for them, and re-layouts  7.59 us
  transfers between devices with their start and end apart: 3, of which 3 were waited for; matrix products, arithmetic and copies ran while one was open for 0% of the time, Pallas kernels for 0%

commit v1 on v0

v1 whole, which is shorter than its diff:
```python
import itertools
import math

import jax
import jax.numpy as jnp
from jax import lax
from jax.sharding import PartitionSpec as P

exact_mode = lax.Precision.HIGHEST
DEVICE_AXES = ("lat", "sub")


def shifted(value, axis, steps):
    count = lax.axis_size(axis)
    initial, last = (max(0, -steps), min(count, count - steps))
    return lax.ppermute(value, axis, [(source, source + steps) for source in range(initial, last)])


def exchange_stages(count):
    bits = count.bit_length() - 1
    groups, low = [], 0
    for width in (2, 1, 2, 2):
        if low >= bits:
            break
        groups.append(list(range(low, min(bits, low + width))))
        low += width
    if low < bits:
        groups.append(list(range(low, bits)))
    return groups


def all_sum(value, count):
    for group in exchange_stages(count):
        masks = []
        for size in range(1, len(group) + 1):
            for combo in itertools.combinations(group, size):
                masks.append(sum(1 << bit for bit in combo))
        received = [
            lax.ppermute(value, DEVICE_AXES, [(i, i ^ mask) for i in range(count)])
            for mask in masks
        ]
        total = received[0]
        for part in received[1:]:
            total = total + part
        value = value + total
    return value


def pack_gram(gram):
    half = gram.shape[0] // 2
    rows = lax.broadcasted_iota(jnp.int32, (half, half), 0)
    cols = lax.broadcasted_iota(jnp.int32, (half, half), 1)
    g11, g12, g22 = gram[:half, :half], gram[:half, half:], gram[half:, half:]
    tri = jnp.where(rows <= cols, g11, g22)
    diag = jnp.diagonal(g22)
    extra = jnp.zeros((8, 2 * half), gram.dtype).at[0, :half].set(diag)
    return jnp.concatenate([jnp.concatenate([g12, tri], axis=1), extra], axis=0)


def unpack_gram(packed, size):
    half = size // 2
    rows = lax.broadcasted_iota(jnp.int32, (half, half), 0)
    cols = lax.broadcasted_iota(jnp.int32, (half, half), 1)
    g12 = packed[:half, :half]
    tri = packed[:half, half:]
    diag = packed[half, :half]
    g11 = jnp.where(rows <= cols, tri, tri.T)
    g22 = jnp.where(rows > cols, tri, jnp.where(rows < cols, tri.T, jnp.diag(diag)))
    top = jnp.concatenate([g11, g12], axis=1)
    bottom = jnp.concatenate([g12.T, g22], axis=1)
    return jnp.concatenate([top, bottom], axis=0)


def body(runoff, weight_blocks, block_zone, climatology, zone_weight):
    block_count = weight_blocks.shape[0]
    slot_count = weight_blocks.shape[1]
    block_size = weight_blocks.shape[2]
    day_count = runoff.shape[1]
    owned_blocks = climatology.shape[0] // block_size
    device_count = lax.axis_size(DEVICE_AXES)
    device_index = lax.axis_index(DEVICE_AXES)
    cell_rows = runoff.reshape(block_count, block_size, day_count)
    partial_value = jnp.einsum(
        "ckiz,cit->ckzt", weight_blocks, cell_rows, preferred_element_type=jnp.float32
    )
    partial_value = partial_value.reshape(block_count * slot_count, block_size * day_count)
    target_slot = block_zone.reshape(-1) - (device_index - 1) * owned_blocks
    window_slots = jnp.arange(3 * owned_blocks, dtype=jnp.int32)
    one_hot = (window_slots[:, None] == target_slot[None, :]).astype(jnp.float32)
    tables = jnp.dot(
        one_hot, partial_value, precision=exact_mode, preferred_element_type=jnp.float32
    )
    tables = tables.reshape(3 * owned_blocks, block_size, day_count)
    from_before = shifted(tables[2 * owned_blocks :], DEVICE_AXES, 1)
    from_after = shifted(tables[:owned_blocks], DEVICE_AXES, -1)
    summed = tables[owned_blocks : 2 * owned_blocks] + from_before + from_after
    aggregated = summed.reshape(owned_blocks * block_size, day_count)
    anomaly = zone_weight[:, None] * (aggregated - climatology)
    local_gram = jnp.dot(
        anomaly.T, anomaly, precision=exact_mode, preferred_element_type=jnp.float32
    )
    local_gram = 0.5 * (local_gram + local_gram.T)
    total_gram = unpack_gram(all_sum(pack_gram(local_gram), device_count), day_count)
    upper = jnp.linalg.cholesky(total_gram).T
    solved = jax.scipy.linalg.solve_triangular(upper.T, anomaly.T, lower=True)
    root = math.sqrt(anomaly.shape[0] * device_count)
    return (solved.T * root, upper / root)


def solution(mesh):
    return jax.shard_map(
        body,
        mesh=mesh,
        in_specs=(
            P(DEVICE_AXES, None),
            P(DEVICE_AXES, None, None, None),
            P(DEVICE_AXES, None),
            P(DEVICE_AXES, None),
            P(DEVICE_AXES),
        ),
        out_specs=(P(DEVICE_AXES, None), P()),
        check_vma=False,
    )
```

time: 260 us -> 139 us (0.53)
  waiting for transfers between devices: 158 us -> 33.9 us
  starting transfers between devices: 8.16 us -> 23.4 us
  between operations: 15.5 us -> 2.34 us
    psum x1 -> x0, waiting for transfers between devices: 143 us -> none  [body(): total_gram = lax.psum(local_gram, ('lat', 'sub'))]
    ppermute x0 -> x10, waiting for transfers between devices: none -> 18.6 us  [all_sum(): lax.ppermute(value, DEVICE_AXES, [(i, i ^ mask) for i in range(count)])]
    ppermute x0 -> x10, starting transfers between devices: none -> 15.4 us  [all_sum(): lax.ppermute(value, DEVICE_AXES, [(i, i ^ mask) for i in range(count)])]
    unnamed x13 -> x14, local copies, waits for them, and re-layouts: 7.59 us -> 7.74 us
  transfers between devices with their start and end apart: 3 -> 12, of which waited for: 3 -> 11; matrix products, arithmetic and copies ran while one was open for 0% -> 0% of each run, Pallas kernels for 0% -> 0%
where the time goes in v1:
time: 139 us
  other arithmetic  55.7 us (40%)
  waiting for transfers between devices  33.9 us (24%)
  starting transfers between devices  23.4 us (17%)
  local copies, waits for them, and re-layouts  14.3 us (10%)
  matrix products  8.74 us (6%)
  between operations  2.34 us (2%)
    another operation x6, other arithmetic, body(): upper = jnp.linalg.cholesky(total_gram).T  34.1 us
    another operation x2, other arithmetic, body(): solved = jax.scipy.linalg.solve_triangular(upper.T, anomaly.T, lower=True)  19.7 us
    ppermute x10, waiting for transfers between devices, all_sum(): lax.ppermute(value, DEVICE_AXES, [(i, i ^ mask) for i in range(count)])  18.6 us
    ppermute x10, starting transfers between devices, all_sum(): lax.ppermute(value, DEVICE_AXES, [(i, i ^ mask) for i in range(count)])  15.4 us
    ppermute x2, waiting for transfers between devices, shifted(): lax.ppermute(value, axis, [(source, source + steps) for source in range(i...  15.3 us
    ppermute x2, starting transfers between devices, shifted(): lax.ppermute(value, axis, [(source, source + steps) for source in range(i...  7.94 us
    unnamed x14, local copies, waits for them, and re-layouts  7.74 us
    another operation x6, local copies, waits for them, and re-layouts  3.92 us
  transfers between devices with their start and end apart: 12, of which 11 were waited for; matrix products, arithmetic and copies ran while one was open for 0% of the time, Pallas kernels for 0%

profile of v1, /device:TPU:1, one launch (start us, length us, event | category | flops | bytes accessed | tf_op | source)
XLA Modules:
  0.0 138.6 jit_solution(4150130118354598781)
XLA Ops:
  0.6 1.2 copy-done
  1.9 2.0 %fusion.19 = f32[16,2,128,256]{3,2,1,0:T(8,128)S(1)} fusion(bf16[16,2,128,128]{3,2,1,0:T(8,128)(2,1)} %param.8, bf16[16,128,256,1]{2,1,3,0:T(8,128)(2,1)S(1)} %bitcast.80), kind=kOutput, calls=%fused_computation.64 | convolution fusion | flops 268435456 | bytes 6291456 | tf_op jit(solution)/shard_map/ckiz,cit->ckzt/dot_general | solution.py:83
  3.9 4.4 %copy.40 = f32[4,8,128,256]{3,1,2,0:T(8,128)} copy(f32[4,8,128,256]{3,2,1,0:T(8,128)S(1)} %bitcast.82) | data formatting | bytes 8388608
  8.2 0.1 copy.22
  8.3 0.1 sub.22
  8.4 3.8 %fusion.13 = f32[12,32768]{1,0:T(8,128)S(1)} fusion(f32[32,32768]{1,0:T(8,128)} %bitcast.81, s32[32]{0:T(128)S(1)} %sub.22), kind=kOutput, calls=%fused_computation.49 | convolution fusion | flops 150995328 | bytes 5767296 | tf_op jit(solution)/shard_map/dot_general | solution.py:90
  12.3 0.2 fusion.16
  12.5 0.1 copy.47
  12.6 6.0 %collective-permute-start.1 = (f32[4,128,256]{2,1,0:T(8,128)S(1)}, f32[4,128,256]{2,1,0:T(8,128)}, u32[]{:S(2)}, u32[]{:S(2)}) collective-permute-start(f32[4,128,256]{2,1,0:T(8,128)S(1)} %bitcast.88), channel_id=1, source_target_pairs={{1,0},{2,1},{3,2},{4,3},{5,4},{6,5},{7,6},{8,7},{9,8},{10,9},{11,1... | collective-permute-start | bytes 1572872 | tf_op jit(solution)/shard_map/ppermute | solution.py:16
  18.7 0.1 copy.48
  18.8 1.9 %collective-permute-start = (f32[4,128,256]{2,1,0:T(8,128)S(1)}, f32[4,128,256]{2,1,0:T(8,128)}, u32[]{:S(2)}, u32[]{:S(2)}) collective-permute-start(f32[4,128,256]{2,1,0:T(8,128)S(1)} %bitcast.89), channel_id=1, source_target_pairs={{0,1},{1,2},{2,3},{3,4},{4,5},{5,6},{6,7},{7,8},{8,9},{9,10},{10,1... | collective-permute-start | bytes 1572872 | tf_op jit(solution)/shard_map/ppermute | solution.py:16
  20.7 0.1 copy.25
  20.9 9.5 %collective-permute-done.1 = f32[4,128,256]{2,1,0:T(8,128)} collective-permute-done((f32[4,128,256]{2,1,0:T(8,128)S(1)}, f32[4,128,256]{2,1,0:T(8,128)}, u32[]{:S(2)}, u32[]{:S(2)}) %collective-permute-start.1) | collective-permute-done | bytes 524320 | tf_op jit(solution)/shard_map/ppermute | solution.py:16
  30.4 5.8 %collective-permute-done = f32[4,128,256]{2,1,0:T(8,128)} collective-permute-done((f32[4,128,256]{2,1,0:T(8,128)S(1)}, f32[4,128,256]{2,1,0:T(8,128)}, u32[]{:S(2)}, u32[]{:S(2)}) %collective-permute-start) | collective-permute-done | bytes 524320 | tf_op jit(solution)/shard_map/ppermute | solution.py:16
  36.2 1.3 fusion
  37.5 0.1 fusion.2
  37.7 1.0 fusion.20
  38.7 0.1 copy.24
  38.9 1.2 gather_fusion
  40.2 0.1 collective-permute-start.4
  40.3 0.1 collective-permute-start.2
  40.4 3.8 %collective-permute-start.3 = (f32[136,256]{1,0:T(8,128)S(1)}, f32[136,256]{1,0:T(8,128)S(1)}, u32[]{:S(2)}, u32[]{:S(2)}) collective-permute-start(f32[136,256]{1,0:T(8,128)S(1)} %select_maximum_fusion), channel_id=1, source_target_pairs={{0,2},{1,3},{2,0},{3,1},{4,6},{5,7},{6,4},{7,5},{8,10},{9,11},{10,... | collective-permute-start | bytes 417800 | tf_op jit(solution)/shard_map/ppermute | solution.py:39
  44.1 2.5 %collective-permute-done.4 = f32[136,256]{1,0:T(8,128)S(1)} collective-permute-done((f32[136,256]{1,0:T(8,128)S(1)}, f32[136,256]{1,0:T(8,128)S(1)}, u32[]{:S(2)}, u32[]{:S(2)}) %collective-permute-start.4) | collective-permute-done | bytes 139296 | tf_op jit(solution)/shard_map/ppermute | solution.py:39
  46.6 2.7 %collective-permute-done.3 = f32[136,256]{1,0:T(8,128)S(1)} collective-permute-done((f32[136,256]{1,0:T(8,128)S(1)}, f32[136,256]{1,0:T(8,128)S(1)}, u32[]{:S(2)}, u32[]{:S(2)}) %collective-permute-start.3) | collective-permute-done | bytes 139296 | tf_op jit(solution)/shard_map/ppermute | solution.py:39
  49.3 0.1 collective-permute-start.5
  49.4 1.3 collective-permute-done.5
  50.7 4.3 %collective-permute-start.8 = (f32[136,256]{1,0:T(8,128)S(1)}, f32[136,256]{1,0:T(8,128)S(1)}, u32[]{:S(2)}, u32[]{:S(2)}) collective-permute-start(f32[136,256]{1,0:T(8,128)S(1)} %add.81), channel_id=1, source_target_pairs={{0,24},{1,25},{2,26},{3,27},{4,28},{5,29},{6,30},{7,31},{8,16},{9,... | collective-permute-start | bytes 417800 | tf_op jit(solution)/shard_map/ppermute | solution.py:39
  55.0 1.2 collective-permute-start.6
  56.2 0.5 collective-permute-start.7
  56.7 2.0 %collective-permute-done.8 = f32[136,256]{1,0:T(8,128)S(1)} collective-permute-done((f32[136,256]{1,0:T(8,128)S(1)}, f32[136,256]{1,0:T(8,128)S(1)}, u32[]{:S(2)}, u32[]{:S(2)}) %collective-permute-start.8) | collective-permute-done | bytes 139296 | tf_op jit(solution)/shard_map/ppermute | solution.py:39
  58.7 0.9 collective-permute-done.6
  59.6 3.3 %collective-permute-done.7 = f32[136,256]{1,0:T(8,128)S(1)} collective-permute-done((f32[136,256]{1,0:T(8,128)S(1)}, f32[136,256]{1,0:T(8,128)S(1)}, u32[]{:S(2)}, u32[]{:S(2)}) %collective-permute-start.7) | collective-permute-done | bytes 139296 | tf_op jit(solution)/shard_map/ppermute | solution.py:39
  62.9 4.2 %collective-permute-start.11 = (f32[136,256]{1,0:T(8,128)S(1)}, f32[136,256]{1,0:T(8,128)S(1)}, u32[]{:S(2)}, u32[]{:S(2)}) collective-permute-start(f32[136,256]{1,0:T(8,128)S(1)} %add_add_fusion.1), channel_id=1, source_target_pairs={{0,96},{1,97},{2,98},{3,99},{4,100},{5,101},{6,102},{7,103},{8,104... | collective-permute-start | bytes 417800 | tf_op jit(solution)/shard_map/ppermute | solution.py:39
  67.1 1.3 collective-permute-start.10
  68.4 1.5 %collective-permute-done.11 = f32[136,256]{1,0:T(8,128)S(1)} collective-permute-done((f32[136,256]{1,0:T(8,128)S(1)}, f32[136,256]{1,0:T(8,128)S(1)}, u32[]{:S(2)}, u32[]{:S(2)}) %collective-permute-start.11) | collective-permute-done | bytes 139296 | tf_op jit(solution)/shard_map/ppermute | solution.py:39
  70.0 1.4 collective-permute-done.9
  71.3 3.0 %collective-permute-done.10 = f32[136,256]{1,0:T(8,128)S(1)} collective-permute-done((f32[136,256]{1,0:T(8,128)S(1)}, f32[136,256]{1,0:T(8,128)S(1)}, u32[]{:S(2)}, u32[]{:S(2)}) %collective-permute-start.10) | collective-permute-done | bytes 139296 | tf_op jit(solution)/shard_map/ppermute | solution.py:39
  74.4 0.1 copy.39
  74.5 0.1 copy.28
  74.7 0.1 copy.29
  74.8 0.1 copy.30
  75.0 11.7 %cholesky.59 = f32[128,128]{1,0:T(8,128)S(1)} custom-call(f32[128,128]{1,0:T(8,128)S(1)} %cholesky.132), custom_call_target="Cholesky" | custom-call | tf_op jit(solution)/shard_map/jit(cholesky)/cholesky | solution.py:104
  86.7 0.1 copy.31
  86.9 0.1 select_reduce_fusion.1
  87.0 0.1 copy.33
  87.1 9.8 %custom-call.15 = f32[1,128,128]{1,2,0:T(8,128)S(1)} custom-call(f32[1,128,128]{2,1,0:T(8,128)S(1)} %copy.33), custom_call_target="InvertDiagBlocksLowerTriangular" | custom-call | tf_op jit(solution)/shard_map/jit(cholesky)/cholesky | solution.py:104
  96.9 0.2 constant_dynamic-update-slice_fusion.1
  97.1 0.3 convolution_subtract_fusion.1
  97.4 11.7 %cholesky.119 = f32[128,128]{1,0:T(8,128)S(1)} custom-call(f32[128,128]{1,0:T(8,128)S(1)} %convolution_subtract_fusion.1), custom_call_target="Cholesky" | custom-call | tf_op jit(solution)/shard_map/jit(cholesky)/cholesky | solution.py:104
  109.1 0.1 copy.34
  109.2 0.1 select_reduce_fusion
  109.3 0.7 compare_reduce_fusion
  111.3 0.1 triangular_solve.57
  111.4 4.1 %while.2 = (s32[]{:T(128)}, f32[256,256]{1,0:T(8,128)S(1)}, s32[2,2]{1,0:T(2,128)S(1)}, f32[2,128,128]{2,1,0:T(8,128)S(1)}, s32[]{:T(128)}) while((s32[]{:T(128)}, f32[256,256]{1,0:T(8,128)S(1)}, s32[2,2]{1,0:T(2,128)S(1)}, f32[2,128,128]{2,1,0:T(8,128)S(1)}, s32[]{:T(128)}) %tuple.40), condition=%wide.while_cond.1, body=%wide.while_body.1.sunk | while | flops 2 | bytes 131189 | solution.py:105
  111.6 0.6 fusion.31
  112.2 1.4 bitcast_dynamic-update-slice_fusion.2
  113.6 0.6 fusion.31
  114.2 1.4 bitcast_dynamic-update-slice_fusion.2
  115.5 19.7 %custom-call.16 = f32[2,128,128]{1,2,0:T(8,128)S(1)} custom-call(f32[2,128,128]{2,1,0:T(8,128)S(1)} %get-tuple-element.21), custom_call_target="InvertDiagBlocksLowerTriangular" | custom-call | tf_op jit(solution)/shard_map/jit(_solve_triangular)/triangular_solve | solution.py:105
  135.2 0.4 fusion.3
  135.6 0.6 convolution_subtract_fusion
  136.2 0.4 fusion.8
  136.7 1.0 copy.35
  137.7 0.8 copy.36
  (34 shorter events, 0.5 us)
Async XLA Ops:
  0.6 1.2 copy-start
  3.8 4.4 %copy-start.3 = (s32[16,2]{0,1:T(2,128)S(1)}, s32[16,2]{0,1:T(2,128)}, u32[]{:S(2)}) copy-start(s32[16,2]{0,1:T(2,128)} %param.9) | copy-start | bytes 388
  12.3 25.2 %copy-start.1 = (f32[512,256]{1,0:T(8,128)S(1)}, f32[512,256]{1,0:T(8,128)}, u32[]{:S(2)}) copy-start(f32[512,256]{1,0:T(8,128)} %param.10) | copy-start | bytes 1572868
  12.3 25.2 %copy-start.2 = (f32[512]{0:T(512)S(1)}, f32[512]{0:T(512)}, u32[]{:S(2)}) copy-start(f32[512]{0:T(512)} %param.11) | copy-start | bytes 6148
  12.6 17.8 %collective-permute-start.1 = (f32[4,128,256]{2,1,0:T(8,128)S(1)}, f32[4,128,256]{2,1,0:T(8,128)}, u32[]{:S(2)}, u32[]{:S(2)}) collective-permute-start(f32[4,128,256]{2,1,0:T(8,128)S(1)} %bitcast.88), channel_id=1, source_target_pairs={{1,0},{2,1},{3,2},{4,3},{5,4},{6,5},{7,6},{8,7},{9,8},{10,9},{11,1... | collective-permute-start | bytes 1572872 | tf_op jit(solution)/shard_map/ppermute | solution.py:16
  18.8 17.4 %collective-permute-start = (f32[4,128,256]{2,1,0:T(8,128)S(1)}, f32[4,128,256]{2,1,0:T(8,128)}, u32[]{:S(2)}, u32[]{:S(2)}) collective-permute-start(f32[4,128,256]{2,1,0:T(8,128)S(1)} %bitcast.89), channel_id=1, source_target_pairs={{0,1},{1,2},{2,3},{3,4},{4,5},{5,6},{6,7},{7,8},{8,9},{9,10},{10,1... | collective-permute-start | bytes 1572872 | tf_op jit(solution)/shard_map/ppermute | solution.py:16
  40.2 6.4 %collective-permute-start.4 = (f32[136,256]{1,0:T(8,128)S(1)}, f32[136,256]{1,0:T(8,128)S(1)}, u32[]{:S(2)}, u32[]{:S(2)}) collective-permute-start(f32[136,256]{1,0:T(8,128)S(1)} %select_maximum_fusion), channel_id=1, source_target_pairs={{0,3},{1,2},{2,1},{3,0},{4,7},{5,6},{6,5},{7,4},{8,11},{9,10},{10,... | collective-permute-start | bytes 417800 | tf_op jit(solution)/shard_map/ppermute | solution.py:39
  40.3 6.3 %collective-permute-start.2 = (f32[136,256]{1,0:T(8,128)S(1)}, f32[136,256]{1,0:T(8,128)S(1)}, u32[]{:S(2)}, u32[]{:S(2)}) collective-permute-start(f32[136,256]{1,0:T(8,128)S(1)} %select_maximum_fusion), channel_id=1, source_target_pairs={{0,1},{1,0},{2,3},{3,2},{4,5},{5,4},{6,7},{7,6},{8,9},{9,8},{10,11... | collective-permute-start | bytes 417800 | tf_op jit(solution)/shard_map/ppermute | solution.py:39
  40.4 8.9 %collective-permute-start.3 = (f32[136,256]{1,0:T(8,128)S(1)}, f32[136,256]{1,0:T(8,128)S(1)}, u32[]{:S(2)}, u32[]{:S(2)}) collective-permute-start(f32[136,256]{1,0:T(8,128)S(1)} %select_maximum_fusion), channel_id=1, source_target_pairs={{0,2},{1,3},{2,0},{3,1},{4,6},{5,7},{6,4},{7,5},{8,10},{9,11},{10,... | collective-permute-start | bytes 417800 | tf_op jit(solution)/shard_map/ppermute | solution.py:39
  49.3 1.4 %collective-permute-start.5 = (f32[136,256]{1,0:T(8,128)S(1)}, f32[136,256]{1,0:T(8,128)S(1)}, u32[]{:S(2)}, u32[]{:S(2)}) collective-permute-start(f32[136,256]{1,0:T(8,128)S(1)} %add_add_fusion.2), channel_id=1, source_target_pairs={{0,4},{1,5},{2,6},{3,7},{4,0},{5,1},{6,2},{7,3},{8,12},{9,13},{10,... | collective-permute-start | bytes 417800 | tf_op jit(solution)/shard_map/ppermute | solution.py:39
  50.7 8.0 %collective-permute-start.8 = (f32[136,256]{1,0:T(8,128)S(1)}, f32[136,256]{1,0:T(8,128)S(1)}, u32[]{:S(2)}, u32[]{:S(2)}) collective-permute-start(f32[136,256]{1,0:T(8,128)S(1)} %add.81), channel_id=1, source_target_pairs={{0,24},{1,25},{2,26},{3,27},{4,28},{5,29},{6,30},{7,31},{8,16},{9,... | collective-permute-start | bytes 417800 | tf_op jit(solution)/shard_map/ppermute | solution.py:39
  55.0 4.6 %collective-permute-start.6 = (f32[136,256]{1,0:T(8,128)S(1)}, f32[136,256]{1,0:T(8,128)S(1)}, u32[]{:S(2)}, u32[]{:S(2)}) collective-permute-start(f32[136,256]{1,0:T(8,128)S(1)} %add.81), channel_id=1, source_target_pairs={{0,8},{1,9},{2,10},{3,11},{4,12},{5,13},{6,14},{7,15},{8,0},{9,1},... | collective-permute-start | bytes 417800 | tf_op jit(solution)/shard_map/ppermute | solution.py:39
  56.2 6.7 %collective-permute-start.7 = (f32[136,256]{1,0:T(8,128)S(1)}, f32[136,256]{1,0:T(8,128)S(1)}, u32[]{:S(2)}, u32[]{:S(2)}) collective-permute-start(f32[136,256]{1,0:T(8,128)S(1)} %add.81), channel_id=1, source_target_pairs={{0,16},{1,17},{2,18},{3,19},{4,20},{5,21},{6,22},{7,23},{8,24},{9,... | collective-permute-start | bytes 417800 | tf_op jit(solution)/shard_map/ppermute | solution.py:39
  62.9 7.0 %collective-permute-start.11 = (f32[136,256]{1,0:T(8,128)S(1)}, f32[136,256]{1,0:T(8,128)S(1)}, u32[]{:S(2)}, u32[]{:S(2)}) collective-permute-start(f32[136,256]{1,0:T(8,128)S(1)} %add_add_fusion.1), channel_id=1, source_target_pairs={{0,96},{1,97},{2,98},{3,99},{4,100},{5,101},{6,102},{7,103},{8,104... | collective-permute-start | bytes 417800 | tf_op jit(solution)/shard_map/ppermute | solution.py:39
  67.1 4.2 %collective-permute-start.9 = (f32[136,256]{1,0:T(8,128)S(1)}, f32[136,256]{1,0:T(8,128)S(1)}, u32[]{:S(2)}, u32[]{:S(2)}) collective-permute-start(f32[136,256]{1,0:T(8,128)S(1)} %add_add_fusion.1), channel_id=1, source_target_pairs={{0,32},{1,33},{2,34},{3,35},{4,36},{5,37},{6,38},{7,39},{8,40},{9,... | collective-permute-start | bytes 417800 | tf_op jit(solution)/shard_map/ppermute | solution.py:39
  67.1 7.2 %collective-permute-start.10 = (f32[136,256]{1,0:T(8,128)S(1)}, f32[136,256]{1,0:T(8,128)S(1)}, u32[]{:S(2)}, u32[]{:S(2)}) collective-permute-start(f32[136,256]{1,0:T(8,128)S(1)} %add_add_fusion.1), channel_id=1, source_target_pairs={{0,64},{1,65},{2,66},{3,67},{4,68},{5,69},{6,70},{7,71},{8,72},{9,... | collective-permute-start | bytes 417800 | tf_op jit(solution)/shard_map/ppermute | solution.py:39

commit v2 on v1

--- a/solution.py
+++ b/solution.py
@@ -71,6 +71,22 @@
     return jnp.concatenate([top, bottom], axis=0)
 
 
+def blocked_cholesky(gram):
+    half = gram.shape[0] // 2
+    eye = jnp.eye(half, dtype=gram.dtype)
+    zeros = jnp.zeros((half, half), gram.dtype)
+    l11 = jnp.linalg.cholesky(gram[:half, :half], symmetrize_input=False)
+    l11_inv = lax.linalg.triangular_solve(l11, eye, left_side=True, lower=True)
+    l21 = jnp.dot(gram[half:, :half], l11_inv.T, precision=exact_mode)
+    schur = gram[half:, half:] - jnp.dot(l21, l21.T, precision=exact_mode)
+    l22 = jnp.linalg.cholesky(schur, symmetrize_input=False)
+    l22_inv = lax.linalg.triangular_solve(l22, eye, left_side=True, lower=True)
+    l21_inv = -jnp.dot(l22_inv, jnp.dot(l21, l11_inv, precision=exact_mode), precision=exact_mode)
+    lower = jnp.block([[l11, zeros], [l21, l22]])
+    lower_inverse = jnp.block([[l11_inv, zeros], [l21_inv, l22_inv]])
+    return lower, lower_inverse
+
+
 def body(runoff, weight_blocks, block_zone, climatology, zone_weight):
     block_count = weight_blocks.shape[0]
     slot_count = weight_blocks.shape[1]
@@ -101,10 +117,10 @@
     )
     local_gram = 0.5 * (local_gram + local_gram.T)
     total_gram = unpack_gram(all_sum(pack_gram(local_gram), device_count), day_count)
-    upper = jnp.linalg.cholesky(total_gram).T
-    solved = jax.scipy.linalg.solve_triangular(upper.T, anomaly.T, lower=True)
+    lower, lower_inverse = blocked_cholesky(total_gram)
     root = math.sqrt(anomaly.shape[0] * device_count)
-    return (solved.T * root, upper / root)
+    scores = jnp.dot(anomaly, lower_inverse.T * root, precision=exact_mode)
+    return (scores, lower.T / root)
 
 
 def solution(mesh):

time: 139 us -> 124 us (0.89)
  other arithmetic: 55.7 us -> 46.2 us
  local copies, waits for them, and re-layouts: 14.3 us -> 8.69 us
    another operation x8 -> x10, other arithmetic: 53.8 us -> 45.7 us  [the longest x3 12.4 us: blocked_cholesky(): l11 = jnp.linalg.cholesky(gram[:half, :half], symmetrize_input=False)]
    another operation x13 -> x1, local copies, waits for them, and re-layouts: 4.31 us -> 0.09 us  [blocked_cholesky(): l22_inv = lax.linalg.triangular_solve(l22, eye, left_side=True, lower=True)]
    dot_general x0 -> x5, matrix products: none -> 2.49 us  [the longest x1 1.41 us: body(): scores = jnp.dot(anomaly, lower_inverse.T * root, precision=exact_mode)]
    unnamed x14 -> x12, local copies, waits for them, and re-layouts: 7.74 us -> 6.65 us
where the time goes in v2:
time: 124 us; the launch traced here: 123 us
  other arithmetic  46.2 us (37%)
  waiting for transfers between devices  34 us (27%)
  starting transfers between devices  23.3 us (19%)
  matrix products  9.86 us (8%)
  local copies, waits for them, and re-layouts  8.69 us (7%)
    ppermute x10, waiting for transfers between devices, all_sum(): lax.ppermute(value, DEVICE_AXES, [(i, i ^ mask) for i in range(count)])  18.7 us
    ppermute x10, starting transfers between devices, all_sum(): lax.ppermute(value, DEVICE_AXES, [(i, i ^ mask) for i in range(count)])  15.3 us
    ppermute x2, waiting for transfers between devices, shifted(): lax.ppermute(value, axis, [(source, source + steps) for source in range(i...  15.3 us
    another operation x3, other arithmetic, blocked_cholesky(): l11 = jnp.linalg.cholesky(gram[:half, :half], symmetrize_input=False)  12.4 us
    another operation x3, other arithmetic, blocked_cholesky(): l22 = jnp.linalg.cholesky(schur, symmetrize_input=False)  12.4 us
    another operation x2, other arithmetic, blocked_cholesky(): l11_inv = lax.linalg.triangular_solve(l11, eye, left_side=True, lower=True)  10.5 us
    another operation x2, other arithmetic, blocked_cholesky(): l22_inv = lax.linalg.triangular_solve(l22, eye, left_side=True, lower=True)  10.5 us
    ppermute x2, starting transfers between devices, shifted(): lax.ppermute(value, axis, [(source, source + steps) for source in range(i...  7.94 us
  transfers between devices with their start and end apart: 12, of which 11 were waited for; matrix products, arithmetic and copies ran while one was open for 0% of the time, Pallas kernels for 0%

profile of v2, /device:TPU:1, one launch (start us, length us, event | category | flops | bytes accessed | tf_op | source)
XLA Modules:
  0.0 123.1 jit_solution(14001692698538720864)
XLA Ops:
  0.6 0.0 copy-start
  0.6 1.2 copy-done
  1.9 2.0 %fusion.36 = f32[16,2,128,256]{3,2,1,0:T(8,128)S(1)} fusion(bf16[16,2,128,128]{3,2,1,0:T(8,128)(2,1)} %param.11, bf16[16,128,256,1]{2,1,3,0:T(8,128)(2,1)S(1)} %bitcast.66), kind=kOutput, calls=%fused_computation.68 | convolution fusion | flops 268435456 | bytes 6291456 | tf_op jit(solution)/shard_map/ckiz,cit->ckzt/dot_general | solution.py:99
  3.8 0.0 copy-start.3
  3.9 4.4 %copy.23 = f32[4,8,128,256]{3,1,2,0:T(8,128)} copy(f32[4,8,128,256]{3,2,1,0:T(8,128)S(1)} %bitcast.68) | data formatting | bytes 8388608
  8.2 0.0 copy-done.3
  8.2 0.1 copy.14
  8.3 0.1 sub.25
  8.4 3.8 %fusion.27 = f32[12,32768]{1,0:T(8,128)S(1)} fusion(f32[32,32768]{1,0:T(8,128)} %bitcast.67, s32[32]{0:T(128)S(1)} %sub.25), kind=kOutput, calls=%fused_computation.55 | convolution fusion | flops 150995328 | bytes 5767296 | tf_op jit(solution)/shard_map/dot_general | solution.py:106
  12.2 0.0 copy-start.1
  12.3 0.0 copy-start.2
  12.3 0.2 fusion.34
  12.5 0.1 copy.30
  12.6 6.0 %collective-permute-start.1 = (f32[4,128,256]{2,1,0:T(8,128)S(1)}, f32[4,128,256]{2,1,0:T(8,128)S(1)}, u32[]{:S(2)}, u32[]{:S(2)}) collective-permute-start(f32[4,128,256]{2,1,0:T(8,128)S(1)} %bitcast.72), channel_id=1, source_target_pairs={{1,0},{2,1},{3,2},{4,3},{5,4},{6,5},{7,6},{8,7},{9,8},{10,9},{11,1... | collective-permute-start | bytes 1572872 | tf_op jit(solution)/shard_map/ppermute | solution.py:16
  18.6 0.1 copy.31
  18.8 1.9 %collective-permute-start = (f32[4,128,256]{2,1,0:T(8,128)S(1)}, f32[4,128,256]{2,1,0:T(8,128)S(1)}, u32[]{:S(2)}, u32[]{:S(2)}) collective-permute-start(f32[4,128,256]{2,1,0:T(8,128)S(1)} %bitcast.73), channel_id=1, source_target_pairs={{0,1},{1,2},{2,3},{3,4},{4,5},{5,6},{6,7},{7,8},{8,9},{9,10},{10,1... | collective-permute-start | bytes 1572872 | tf_op jit(solution)/shard_map/ppermute | solution.py:16
  20.7 9.7 %collective-permute-done.1 = f32[4,128,256]{2,1,0:T(8,128)S(1)} collective-permute-done((f32[4,128,256]{2,1,0:T(8,128)S(1)}, f32[4,128,256]{2,1,0:T(8,128)S(1)}, u32[]{:S(2)}, u32[]{:S(2)}) %collective-permute-start.1) | collective-permute-done | bytes 524320 | tf_op jit(solution)/shard_map/ppermute | solution.py:16
  30.4 5.7 %collective-permute-done = f32[4,128,256]{2,1,0:T(8,128)S(1)} collective-permute-done((f32[4,128,256]{2,1,0:T(8,128)S(1)}, f32[4,128,256]{2,1,0:T(8,128)S(1)}, u32[]{:S(2)}, u32[]{:S(2)}) %collective-permute-start) | collective-permute-done | bytes 524320 | tf_op jit(solution)/shard_map/ppermute | solution.py:16
  36.0 0.1 fusion
  36.2 0.0 copy-done.1
  36.2 0.0 copy-done.2
  36.2 0.1 fusion.1
  36.3 1.0 fusion.37
  37.4 0.1 copy.16
  37.6 1.2 %gather_fusion = f32[128]{0:T(128)S(1)} fusion(f32[128,128]{1,0:T(8,128)S(1)} %get-tuple-element.28, s32[128]{0:T(128)S(1)} %or_bitcast_fusion), kind=kCustom, calls=%fused_computation | custom fusion | bytes 2048 | tf_op jit(solution)/shard_map/jit(diagonal)/cond/branch_0_fun/gather | solution.py:55
  38.8 0.1 collective-permute-start.4
  38.9 0.1 collective-permute-start.2
  39.0 3.8 %collective-permute-start.3 = (f32[136,256]{1,0:T(8,128)S(1)}, f32[136,256]{1,0:T(8,128)S(1)}, u32[]{:S(2)}, u32[]{:S(2)}) collective-permute-start(f32[136,256]{1,0:T(8,128)S(1)} %select_maximum_fusion.2), channel_id=1, source_target_pairs={{0,2},{1,3},{2,0},{3,1},{4,6},{5,7},{6,4},{7,5},{8,10},{9,11},{10,... | collective-permute-start | bytes 417800 | tf_op jit(solution)/shard_map/ppermute | solution.py:39
  42.8 2.2 %collective-permute-done.4 = f32[136,256]{1,0:T(8,128)S(1)} collective-permute-done((f32[136,256]{1,0:T(8,128)S(1)}, f32[136,256]{1,0:T(8,128)S(1)}, u32[]{:S(2)}, u32[]{:S(2)}) %collective-permute-start.4) | collective-permute-done | bytes 139296 | tf_op jit(solution)/shard_map/ppermute | solution.py:39
  45.0 0.0 collective-permute-done.2
  45.0 3.0 %collective-permute-done.3 = f32[136,256]{1,0:T(8,128)S(1)} collective-permute-done((f32[136,256]{1,0:T(8,128)S(1)}, f32[136,256]{1,0:T(8,128)S(1)}, u32[]{:S(2)}, u32[]{:S(2)}) %collective-permute-start.3) | collective-permute-done | bytes 139296 | tf_op jit(solution)/shard_map/ppermute | solution.py:39
  48.1 0.1 collective-permute-start.5
  48.2 1.3 %collective-permute-done.5 = f32[136,256]{1,0:T(8,128)S(1)} collective-permute-done((f32[136,256]{1,0:T(8,128)S(1)}, f32[136,256]{1,0:T(8,128)S(1)}, u32[]{:S(2)}, u32[]{:S(2)}) %collective-permute-start.5) | collective-permute-done | bytes 139296 | tf_op jit(solution)/shard_map/ppermute | solution.py:39
  49.5 4.2 %collective-permute-start.8 = (f32[136,256]{1,0:T(8,128)S(1)}, f32[136,256]{1,0:T(8,128)S(1)}, u32[]{:S(2)}, u32[]{:S(2)}) collective-permute-start(f32[136,256]{1,0:T(8,128)S(1)} %add.67), channel_id=1, source_target_pairs={{0,24},{1,25},{2,26},{3,27},{4,28},{5,29},{6,30},{7,31},{8,16},{9,... | collective-permute-start | bytes 417800 | tf_op jit(solution)/shard_map/ppermute | solution.py:39
  53.7 1.2 collective-permute-start.6
  54.9 0.5 collective-permute-start.7
  55.4 2.0 %collective-permute-done.8 = f32[136,256]{1,0:T(8,128)S(1)} collective-permute-done((f32[136,256]{1,0:T(8,128)S(1)}, f32[136,256]{1,0:T(8,128)S(1)}, u32[]{:S(2)}, u32[]{:S(2)}) %collective-permute-start.8) | collective-permute-done | bytes 139296 | tf_op jit(solution)/shard_map/ppermute | solution.py:39
  57.4 0.9 collective-permute-done.6
  58.3 3.3 %collective-permute-done.7 = f32[136,256]{1,0:T(8,128)S(1)} collective-permute-done((f32[136,256]{1,0:T(8,128)S(1)}, f32[136,256]{1,0:T(8,128)S(1)}, u32[]{:S(2)}, u32[]{:S(2)}) %collective-permute-start.7) | collective-permute-done | bytes 139296 | tf_op jit(solution)/shard_map/ppermute | solution.py:39
  61.6 4.2 %collective-permute-start.11 = (f32[136,256]{1,0:T(8,128)S(1)}, f32[136,256]{1,0:T(8,128)S(1)}, u32[]{:S(2)}, u32[]{:S(2)}) collective-permute-start(f32[136,256]{1,0:T(8,128)S(1)} %add_add_fusion.1), channel_id=1, source_target_pairs={{0,96},{1,97},{2,98},{3,99},{4,100},{5,101},{6,102},{7,103},{8,104... | collective-permute-start | bytes 417800 | tf_op jit(solution)/shard_map/ppermute | solution.py:39
  65.8 0.0 collective-permute-start.9
  65.8 1.3 %collective-permute-start.10 = (f32[136,256]{1,0:T(8,128)S(1)}, f32[136,256]{1,0:T(8,128)S(1)}, u32[]{:S(2)}, u32[]{:S(2)}) collective-permute-start(f32[136,256]{1,0:T(8,128)S(1)} %add_add_fusion.1), channel_id=1, source_target_pairs={{0,64},{1,65},{2,66},{3,67},{4,68},{5,69},{6,70},{7,71},{8,72},{9,... | collective-permute-start | bytes 417800 | tf_op jit(solution)/shard_map/ppermute | solution.py:39
  67.1 1.6 %collective-permute-done.11 = f32[136,256]{1,0:T(8,128)S(1)} collective-permute-done((f32[136,256]{1,0:T(8,128)S(1)}, f32[136,256]{1,0:T(8,128)S(1)}, u32[]{:S(2)}, u32[]{:S(2)}) %collective-permute-start.11) | collective-permute-done | bytes 139296 | tf_op jit(solution)/shard_map/ppermute | solution.py:39
  68.6 1.4 %collective-permute-done.9 = f32[136,256]{1,0:T(8,128)S(1)} collective-permute-done((f32[136,256]{1,0:T(8,128)S(1)}, f32[136,256]{1,0:T(8,128)S(1)}, u32[]{:S(2)}, u32[]{:S(2)}) %collective-permute-start.9) | collective-permute-done | bytes 139296 | tf_op jit(solution)/shard_map/ppermute | solution.py:39
  70.0 3.0 %collective-permute-done.10 = f32[136,256]{1,0:T(8,128)S(1)} collective-permute-done((f32[136,256]{1,0:T(8,128)S(1)}, f32[136,256]{1,0:T(8,128)S(1)}, u32[]{:S(2)}, u32[]{:S(2)}) %collective-permute-start.10) | collective-permute-done | bytes 139296 | tf_op jit(solution)/shard_map/ppermute | solution.py:39
  73.1 0.1 copy.17
  73.2 11.7 %cholesky.45 = f32[128,128]{1,0:T(8,128)S(1)} custom-call(f32[128,128]{1,0:T(8,128)S(1)} %bitcast_select_fusion.1), custom_call_target="Cholesky" | custom-call | tf_op jit(solution)/shard_map/jit(cholesky)/cholesky | solution.py:78
  84.9 0.6 compare_reduce_fusion.1
  85.6 0.7 select_bitcast_fusion.1
  86.2 9.8 %custom-call.8 = f32[1,128,128]{1,2,0:T(8,128)S(1)} custom-call(f32[1,128,128]{2,1,0:T(8,128)S(1)} %get-tuple-element.22), custom_call_target="InvertDiagBlocksLowerTriangular" | custom-call | tf_op jit(solution)/shard_map/triangular_solve/custom-call.0 | solution.py:79
  96.1 0.3 fusion.17
  96.4 0.2 fusion.19
  96.6 0.3 fusion.38
  96.9 0.1 copy.19
  97.0 0.3 fusion.24
  97.3 11.7 %cholesky.56 = f32[128,128]{1,0:T(8,128)S(1)} custom-call(f32[128,128]{1,0:T(8,128)S(1)} %fusion.24), custom_call_target="Cholesky" | custom-call | tf_op jit(solution)/shard_map/jit(cholesky)/cholesky | solution.py:82
  109.0 0.6 compare_reduce_fusion
  109.6 0.7 select_bitcast_fusion
  110.3 9.8 %custom-call.9 = f32[1,128,128]{1,2,0:T(8,128)S(1)} custom-call(f32[1,128,128]{2,1,0:T(8,128)S(1)} %get-tuple-element.20), custom_call_target="InvertDiagBlocksLowerTriangular" | custom-call | tf_op jit(solution)/shard_map/triangular_solve/custom-call.0 | solution.py:83
  120.1 0.3 fusion.15
  120.4 0.1 copy.18
  120.5 0.3 convolution_negate_fusion
  120.8 0.8 copy.20
  121.7 1.4 %fusion.5 = f32[512,256]{1,0:T(8,128)} fusion(f32[512,256]{1,0:T(8,128)S(1)} %fusion.1, f32[128,128]{1,0:T(8,128)S(1)} %fusion.17, f32[128,128]{1,0:T(8,128)S(1)} %copy.18, f32[128,128]{1,0:T(8,128)S(1)} %convolution_negate_fusion), kind=kOutput, calls=%fused_computation.13 | convolution fusion | flops 402980864 | bytes 1245184 | tf_op jit(solution)/shard_map/dot_general | solution.py:122
  (15 shorter events, 0.3 us)
Async XLA Ops:
  0.6 1.2 %copy-start = (bf16[2048,256]{1,0:T(8,128)(2,1)S(1)}, bf16[2048,256]{1,0:T(8,128)(2,1)}, u32[]{:S(2)}) copy-start(bf16[2048,256]{1,0:T(8,128)(2,1)} %param.10) | copy-start | bytes 3145732
  3.8 4.4 %copy-start.3 = (s32[16,2]{0,1:T(2,128)S(1)}, s32[16,2]{0,1:T(2,128)}, u32[]{:S(2)}) copy-start(s32[16,2]{0,1:T(2,128)} %param.12) | copy-start | bytes 388
  12.2 23.9 %copy-start.1 = (f32[512,256]{1,0:T(8,128)S(1)}, f32[512,256]{1,0:T(8,128)}, u32[]{:S(2)}) copy-start(f32[512,256]{1,0:T(8,128)} %param.13) | copy-start | bytes 1572868
  12.3 23.9 %copy-start.2 = (f32[512]{0:T(512)S(1)}, f32[512]{0:T(512)}, u32[]{:S(2)}) copy-start(f32[512]{0:T(512)} %param.14) | copy-start | bytes 6148
  12.6 17.8 %collective-permute-start.1 = (f32[4,128,256]{2,1,0:T(8,128)S(1)}, f32[4,128,256]{2,1,0:T(8,128)S(1)}, u32[]{:S(2)}, u32[]{:S(2)}) collective-permute-start(f32[4,128,256]{2,1,0:T(8,128)S(1)} %bitcast.72), channel_id=1, source_target_pairs={{1,0},{2,1},{3,2},{4,3},{5,4},{6,5},{7,6},{8,7},{9,8},{10,9},{11,1... | collective-permute-start | bytes 1572872 | tf_op jit(solution)/shard_map/ppermute | solution.py:16
  18.8 17.3 %collective-permute-start = (f32[4,128,256]{2,1,0:T(8,128)S(1)}, f32[4,128,256]{2,1,0:T(8,128)S(1)}, u32[]{:S(2)}, u32[]{:S(2)}) collective-permute-start(f32[4,128,256]{2,1,0:T(8,128)S(1)} %bitcast.73), channel_id=1, source_target_pairs={{0,1},{1,2},{2,3},{3,4},{4,5},{5,6},{6,7},{7,8},{8,9},{9,10},{10,1... | collective-permute-start | bytes 1572872 | tf_op jit(solution)/shard_map/ppermute | solution.py:16
  38.8 6.2 %collective-permute-start.4 = (f32[136,256]{1,0:T(8,128)S(1)}, f32[136,256]{1,0:T(8,128)S(1)}, u32[]{:S(2)}, u32[]{:S(2)}) collective-permute-start(f32[136,256]{1,0:T(8,128)S(1)} %select_maximum_fusion.2), channel_id=1, source_target_pairs={{0,3},{1,2},{2,1},{3,0},{4,7},{5,6},{6,5},{7,4},{8,11},{9,10},{10,... | collective-permute-start | bytes 417800 | tf_op jit(solution)/shard_map/ppermute | solution.py:39
  38.9 6.1 %collective-permute-start.2 = (f32[136,256]{1,0:T(8,128)S(1)}, f32[136,256]{1,0:T(8,128)S(1)}, u32[]{:S(2)}, u32[]{:S(2)}) collective-permute-start(f32[136,256]{1,0:T(8,128)S(1)} %select_maximum_fusion.2), channel_id=1, source_target_pairs={{0,1},{1,0},{2,3},{3,2},{4,5},{5,4},{6,7},{7,6},{8,9},{9,8},{10,11... | collective-permute-start | bytes 417800 | tf_op jit(solution)/shard_map/ppermute | solution.py:39
  39.0 9.0 %collective-permute-start.3 = (f32[136,256]{1,0:T(8,128)S(1)}, f32[136,256]{1,0:T(8,128)S(1)}, u32[]{:S(2)}, u32[]{:S(2)}) collective-permute-start(f32[136,256]{1,0:T(8,128)S(1)} %select_maximum_fusion.2), channel_id=1, source_target_pairs={{0,2},{1,3},{2,0},{3,1},{4,6},{5,7},{6,4},{7,5},{8,10},{9,11},{10,... | collective-permute-start | bytes 417800 | tf_op jit(solution)/shard_map/ppermute | solution.py:39
  48.1 1.4 %collective-permute-start.5 = (f32[136,256]{1,0:T(8,128)S(1)}, f32[136,256]{1,0:T(8,128)S(1)}, u32[]{:S(2)}, u32[]{:S(2)}) collective-permute-start(f32[136,256]{1,0:T(8,128)S(1)} %add_add_fusion.2), channel_id=1, source_target_pairs={{0,4},{1,5},{2,6},{3,7},{4,0},{5,1},{6,2},{7,3},{8,12},{9,13},{10,... | collective-permute-start | bytes 417800 | tf_op jit(solution)/shard_map/ppermute | solution.py:39
  49.5 7.9 %collective-permute-start.8 = (f32[136,256]{1,0:T(8,128)S(1)}, f32[136,256]{1,0:T(8,128)S(1)}, u32[]{:S(2)}, u32[]{:S(2)}) collective-permute-start(f32[136,256]{1,0:T(8,128)S(1)} %add.67), channel_id=1, source_target_pairs={{0,24},{1,25},{2,26},{3,27},{4,28},{5,29},{6,30},{7,31},{8,16},{9,... | collective-permute-start | bytes 417800 | tf_op jit(solution)/shard_map/ppermute | solution.py:39
  53.7 4.6 %collective-permute-start.6 = (f32[136,256]{1,0:T(8,128)S(1)}, f32[136,256]{1,0:T(8,128)S(1)}, u32[]{:S(2)}, u32[]{:S(2)}) collective-permute-start(f32[136,256]{1,0:T(8,128)S(1)} %add.67), channel_id=1, source_target_pairs={{0,8},{1,9},{2,10},{3,11},{4,12},{5,13},{6,14},{7,15},{8,0},{9,1},... | collective-permute-start | bytes 417800 | tf_op jit(solution)/shard_map/ppermute | solution.py:39
  54.9 6.7 %collective-permute-start.7 = (f32[136,256]{1,0:T(8,128)S(1)}, f32[136,256]{1,0:T(8,128)S(1)}, u32[]{:S(2)}, u32[]{:S(2)}) collective-permute-start(f32[136,256]{1,0:T(8,128)S(1)} %add.67), channel_id=1, source_target_pairs={{0,16},{1,17},{2,18},{3,19},{4,20},{5,21},{6,22},{7,23},{8,24},{9,... | collective-permute-start | bytes 417800 | tf_op jit(solution)/shard_map/ppermute | solution.py:39
  61.6 7.0 %collective-permute-start.11 = (f32[136,256]{1,0:T(8,128)S(1)}, f32[136,256]{1,0:T(8,128)S(1)}, u32[]{:S(2)}, u32[]{:S(2)}) collective-permute-start(f32[136,256]{1,0:T(8,128)S(1)} %add_add_fusion.1), channel_id=1, source_target_pairs={{0,96},{1,97},{2,98},{3,99},{4,100},{5,101},{6,102},{7,103},{8,104... | collective-permute-start | bytes 417800 | tf_op jit(solution)/shard_map/ppermute | solution.py:39
  65.8 4.2 %collective-permute-start.9 = (f32[136,256]{1,0:T(8,128)S(1)}, f32[136,256]{1,0:T(8,128)S(1)}, u32[]{:S(2)}, u32[]{:S(2)}) collective-permute-start(f32[136,256]{1,0:T(8,128)S(1)} %add_add_fusion.1), channel_id=1, source_target_pairs={{0,32},{1,33},{2,34},{3,35},{4,36},{5,37},{6,38},{7,39},{8,40},{9,... | collective-permute-start | bytes 417800 | tf_op jit(solution)/shard_map/ppermute | solution.py:39
  65.8 7.2 %collective-permute-start.10 = (f32[136,256]{1,0:T(8,128)S(1)}, f32[136,256]{1,0:T(8,128)S(1)}, u32[]{:S(2)}, u32[]{:S(2)}) collective-permute-start(f32[136,256]{1,0:T(8,128)S(1)} %add_add_fusion.1), channel_id=1, source_target_pairs={{0,64},{1,65},{2,66},{3,67},{4,68},{5,69},{6,70},{7,71},{8,72},{9,... | collective-permute-start | bytes 417800 | tf_op jit(solution)/shard_map/ppermute | solution.py:39

commit v3 on v2

--- a/solution.py
+++ b/solution.py
@@ -4,6 +4,8 @@
 import jax
 import jax.numpy as jnp
 from jax import lax
+from jax.experimental import pallas as pl
+from jax.experimental.pallas import tpu as pltpu
 from jax.sharding import PartitionSpec as P
 
 exact_mode = lax.Precision.HIGHEST
@@ -87,26 +89,48 @@
     return lower, lower_inverse
 
 
+def aggregate_kernel(slot_ref, weight_ref, rows_ref, out_ref):
+    out_ref[...] = jnp.zeros(out_ref.shape, out_ref.dtype)
+    block_count, slot_count = weight_ref.shape[0], weight_ref.shape[1]
+    for block in range(block_count):
+        rows = rows_ref[block]
+        for slot in range(slot_count):
+            part = lax.dot_general(
+                weight_ref[block, slot],
+                rows,
+                (((0,), (0,)), ((), ())),
+                preferred_element_type=jnp.float32,
+            )
+            target = slot_ref[block * slot_count + slot]
+            out_ref[target] = out_ref[target] + part
+
+
+def aggregate(slots, weight_blocks, cell_rows, window_count):
+    block_size = weight_blocks.shape[3]
+    day_count = cell_rows.shape[2]
+    return pl.pallas_call(
+        aggregate_kernel,
+        out_shape=jax.ShapeDtypeStruct((window_count, block_size, day_count), jnp.float32),
+        in_specs=[
+            pl.BlockSpec(memory_space=pltpu.SMEM),
+            pl.BlockSpec(memory_space=pltpu.VMEM),
+            pl.BlockSpec(memory_space=pltpu.VMEM),
+        ],
+        out_specs=pl.BlockSpec(memory_space=pltpu.VMEM),
+    )(slots, weight_blocks, cell_rows)
+
+
 def body(runoff, weight_blocks, block_zone, climatology, zone_weight):
     block_count = weight_blocks.shape[0]
-    slot_count = weight_blocks.shape[1]
     block_size = weight_blocks.shape[2]
     day_count = runoff.shape[1]
     owned_blocks = climatology.shape[0] // block_size
     device_count = lax.axis_size(DEVICE_AXES)
     device_index = lax.axis_index(DEVICE_AXES)
     cell_rows = runoff.reshape(block_count, block_size, day_count)
-    partial_value = jnp.einsum(
-        "ckiz,cit->ckzt", weight_blocks, cell_rows, preferred_element_type=jnp.float32
-    )
-    partial_value = partial_value.reshape(block_count * slot_count, block_size * day_count)
     target_slot = block_zone.reshape(-1) - (device_index - 1) * owned_blocks
-    window_slots = jnp.arange(3 * owned_blocks, dtype=jnp.int32)
-    one_hot = (window_slots[:, None] == target_slot[None, :]).astype(jnp.float32)
-    tables = jnp.dot(
-        one_hot, partial_value, precision=exact_mode, preferred_element_type=jnp.float32
-    )
-    tables = tables.reshape(3 * owned_blocks, block_size, day_count)
+    target_slot = jnp.clip(target_slot, 0, 3 * owned_blocks - 1).astype(jnp.int32)
+    tables = aggregate(target_slot, weight_blocks, cell_rows, 3 * owned_blocks)
     from_before = shifted(tables[2 * owned_blocks :], DEVICE_AXES, 1)
     from_after = shifted(tables[:owned_blocks], DEVICE_AXES, -1)
     summed = tables[owned_blocks : 2 * owned_blocks] + from_before + from_after

time: 124 us -> 118 us (0.952)
  matrix products: 9.86 us -> 4.06 us
  local copies, waits for them, and re-layouts: 8.69 us -> 4.45 us
  Pallas kernels: 0 us -> 3.47 us
  other arithmetic: 46.2 us -> 47.9 us
    dot_general x2 -> x0, matrix products: 5.81 us -> none  [the longest x1 3.83 us: body(): jnp.dot(one_hot, partial_value, precision=exact_mode, preferred_element_t...]
    unnamed x12 -> x5, local copies, waits for them, and re-layouts: 6.65 us -> 0.85 us
    ppermute x10, waiting for transfers between devices: 18.7 us -> 23.3 us  [all_sum(): lax.ppermute(value, DEVICE_AXES, [(i, i ^ mask) for i in range(count)])]
    ppermute x2, waiting for transfers between devices: 15.3 us -> 11.7 us  [shifted(): lax.ppermute(value, axis, [(source, source + steps) for source in range(i...]
    pallas_call x0 -> x1, Pallas kernels: none -> 3.47 us  [aggregate(): pl.pallas_call(aggregate_kernel, out_shape=jax.ShapeDtypeStruct((window_c...]
    ppermute x10, starting transfers between devices: 15.3 us -> 14 us  [all_sum(): lax.ppermute(value, DEVICE_AXES, [(i, i ^ mask) for i in range(count)])]
where the time goes in v3:
time: 118 us
  other arithmetic  47.9 us (41%)
  waiting for transfers between devices  35 us (30%)
  starting transfers between devices  22.1 us (19%)
  local copies, waits for them, and re-layouts  4.45 us (4%)
  matrix products  4.06 us (3%)
  Pallas kernels  3.47 us (3%)
    ppermute x10, waiting for transfers between devices, all_sum(): lax.ppermute(value, DEVICE_AXES, [(i, i ^ mask) for i in range(count)])  23.3 us
    ppermute x10, starting transfers between devices, all_sum(): lax.ppermute(value, DEVICE_AXES, [(i, i ^ mask) for i in range(count)])  14 us
    another operation x3, other arithmetic, blocked_cholesky(): l11 = jnp.linalg.cholesky(gram[:half, :half], symmetrize_input=False)  12.4 us
    another operation x3, other arithmetic, blocked_cholesky(): l22 = jnp.linalg.cholesky(schur, symmetrize_input=False)  12.4 us
    ppermute x2, waiting for transfers between devices, shifted(): lax.ppermute(value, axis, [(source, source + steps) for source in range(i...  11.7 us
    another operation x2, other arithmetic, blocked_cholesky(): l11_inv = lax.linalg.triangular_solve(l11, eye, left_side=True, lower=True)  10.5 us
    another operation x2, other arithmetic, blocked_cholesky(): l22_inv = lax.linalg.triangular_solve(l22, eye, left_side=True, lower=True)  10.5 us
    ppermute x2, starting transfers between devices, shifted(): lax.ppermute(value, axis, [(source, source + steps) for source in range(i...  8.07 us
  transfers between devices with their start and end apart: 12, of which 11 were waited for; matrix products, arithmetic and copies ran while one was open for 0% of the time, Pallas kernels for 0%

profile of v3, /device:TPU:1, one launch (start us, length us, event | category | flops | bytes accessed | tf_op | source)
XLA Modules:
  0.0 118.0 jit_solution(6638645107273003997)
XLA Ops:
  0.6 0.7 subtract_clamp_fusion
  1.3 0.1 copy.13
  1.4 0.6 min.12.slot_ref
  2.0 3.5 %shard_map.68 = f32[12,128,256]{2,1,0:T(8,128)} custom-call(s32[32]{0:T(128)} %min.12.slot_ref, bf16[16,2,128,128]{3,2,1,0:T(8,128)(2,1)} %weight_ref.1, bf16[16,128,256]{2,1,0:T(8,128)(2,1)} %bitcast.43), custom_call_target="tpu_custom_call" | custom-call | tf_op jit(solution)/shard_map/pallas_call | solution.py:111
  5.5 1.3 %fusion.32 = (f32[4,128,256]{2,1,0:T(8,128)S(1)}, f32[4,128,256]{2,1,0:T(8,128)S(1)}) fusion(f32[12,128,256]{2,1,0:T(8,128)} %shard_map.68), kind=kLoop, calls=%fused_computation.61 | loop fusion | bytes 2097152 | tf_op jit(solution)/shard_map/slice | solution.py:134
  6.8 0.0 copy-start
  6.8 0.0 copy-start.1
  6.8 4.2 %collective-permute-start = (f32[4,128,256]{2,1,0:T(8,128)S(1)}, f32[4,128,256]{2,1,0:T(8,128)S(1)}, u32[]{:S(2)}, u32[]{:S(2)}) collective-permute-start(f32[4,128,256]{2,1,0:T(8,128)S(1)} %get-tuple-element.24), channel_id=1, source_target_pairs={{0,1},{1,2},{2,3},{3,4},{4,5},{5,6},{6,7},{7,8},{8,9},{9,10},{10,1... | collective-permute-start | bytes 1572872 | tf_op jit(solution)/shard_map/ppermute | solution.py:18
  10.9 3.9 %collective-permute-start.1 = (f32[4,128,256]{2,1,0:T(8,128)S(1)}, f32[4,128,256]{2,1,0:T(8,128)S(1)}, u32[]{:S(2)}, u32[]{:S(2)}) collective-permute-start(f32[4,128,256]{2,1,0:T(8,128)S(1)} %get-tuple-element.25), channel_id=1, source_target_pairs={{1,0},{2,1},{3,2},{4,3},{5,4},{6,5},{7,6},{8,7},{9,8},{10,9},{11,1... | collective-permute-start | bytes 1572872 | tf_op jit(solution)/shard_map/ppermute | solution.py:18
  14.9 9.5 %collective-permute-done = f32[4,128,256]{2,1,0:T(8,128)S(1)} collective-permute-done((f32[4,128,256]{2,1,0:T(8,128)S(1)}, f32[4,128,256]{2,1,0:T(8,128)S(1)}, u32[]{:S(2)}, u32[]{:S(2)}) %collective-permute-start) | collective-permute-done | bytes 524320 | tf_op jit(solution)/shard_map/ppermute | solution.py:18
  24.4 2.2 %collective-permute-done.1 = f32[4,128,256]{2,1,0:T(8,128)S(1)} collective-permute-done((f32[4,128,256]{2,1,0:T(8,128)S(1)}, f32[4,128,256]{2,1,0:T(8,128)S(1)}, u32[]{:S(2)}, u32[]{:S(2)}) %collective-permute-start.1) | collective-permute-done | bytes 524320 | tf_op jit(solution)/shard_map/ppermute | solution.py:18
  26.6 1.1 fusion
  27.7 0.0 copy-done
  27.8 0.0 copy-done.1
  27.8 0.1 fusion.1
  27.9 1.0 fusion.34
  28.9 0.1 copy.14
  29.1 1.2 %gather_fusion = f32[128]{0:T(128)S(1)} fusion(f32[128,128]{1,0:T(8,128)S(1)} %get-tuple-element.27, s32[128]{0:T(128)S(1)} %or_bitcast_fusion), kind=kCustom, calls=%fused_computation | custom fusion | bytes 2048 | tf_op jit(solution)/shard_map/jit(diagonal)/cond/branch_0_fun/gather | solution.py:57
  30.4 0.2 collective-permute-start.2
  30.6 5.6 %collective-permute-start.3 = (f32[136,256]{1,0:T(8,128)S(1)}, f32[136,256]{1,0:T(8,128)S(1)}, u32[]{:S(2)}, u32[]{:S(2)}) collective-permute-start(f32[136,256]{1,0:T(8,128)S(1)} %select_maximum_fusion.2), channel_id=1, source_target_pairs={{0,2},{1,3},{2,0},{3,1},{4,6},{5,7},{6,4},{7,5},{8,10},{9,11},{10,... | collective-permute-start | bytes 417800 | tf_op jit(solution)/shard_map/ppermute | solution.py:41
  36.1 0.0 collective-permute-start.4
  36.1 0.0 collective-permute-done.2
  36.1 6.8 %collective-permute-done.3 = f32[136,256]{1,0:T(8,128)S(1)} collective-permute-done((f32[136,256]{1,0:T(8,128)S(1)}, f32[136,256]{1,0:T(8,128)S(1)}, u32[]{:S(2)}, u32[]{:S(2)}) %collective-permute-start.3) | collective-permute-done | bytes 139296 | tf_op jit(solution)/shard_map/ppermute | solution.py:41
  43.0 2.8 %collective-permute-done.4 = f32[136,256]{1,0:T(8,128)S(1)} collective-permute-done((f32[136,256]{1,0:T(8,128)S(1)}, f32[136,256]{1,0:T(8,128)S(1)}, u32[]{:S(2)}, u32[]{:S(2)}) %collective-permute-start.4) | collective-permute-done | bytes 139296 | tf_op jit(solution)/shard_map/ppermute | solution.py:41
  45.8 0.7 collective-permute-start.5
  46.5 1.0 collective-permute-done.5
  47.5 0.1 collective-permute-start.6
  47.6 1.6 %collective-permute-start.7 = (f32[136,256]{1,0:T(8,128)S(1)}, f32[136,256]{1,0:T(8,128)S(1)}, u32[]{:S(2)}, u32[]{:S(2)}) collective-permute-start(f32[136,256]{1,0:T(8,128)S(1)} %add.67), channel_id=1, source_target_pairs={{0,16},{1,17},{2,18},{3,19},{4,20},{5,21},{6,22},{7,23},{8,24},{9,... | collective-permute-start | bytes 417800 | tf_op jit(solution)/shard_map/ppermute | solution.py:41
  49.2 2.3 %collective-permute-start.8 = (f32[136,256]{1,0:T(8,128)S(1)}, f32[136,256]{1,0:T(8,128)S(1)}, u32[]{:S(2)}, u32[]{:S(2)}) collective-permute-start(f32[136,256]{1,0:T(8,128)S(1)} %add.67), channel_id=1, source_target_pairs={{0,24},{1,25},{2,26},{3,27},{4,28},{5,29},{6,30},{7,31},{8,16},{9,... | collective-permute-start | bytes 417800 | tf_op jit(solution)/shard_map/ppermute | solution.py:41
  51.5 1.0 collective-permute-done.6
  52.5 3.4 %collective-permute-done.7 = f32[136,256]{1,0:T(8,128)S(1)} collective-permute-done((f32[136,256]{1,0:T(8,128)S(1)}, f32[136,256]{1,0:T(8,128)S(1)}, u32[]{:S(2)}, u32[]{:S(2)}) %collective-permute-start.7) | collective-permute-done | bytes 139296 | tf_op jit(solution)/shard_map/ppermute | solution.py:41
  55.9 2.6 %collective-permute-done.8 = f32[136,256]{1,0:T(8,128)S(1)} collective-permute-done((f32[136,256]{1,0:T(8,128)S(1)}, f32[136,256]{1,0:T(8,128)S(1)}, u32[]{:S(2)}, u32[]{:S(2)}) %collective-permute-start.8) | collective-permute-done | bytes 139296 | tf_op jit(solution)/shard_map/ppermute | solution.py:41
  58.5 2.8 %collective-permute-start.10 = (f32[136,256]{1,0:T(8,128)S(1)}, f32[136,256]{1,0:T(8,128)S(1)}, u32[]{:S(2)}, u32[]{:S(2)}) collective-permute-start(f32[136,256]{1,0:T(8,128)S(1)} %add_add_fusion.1), channel_id=1, source_target_pairs={{0,64},{1,65},{2,66},{3,67},{4,68},{5,69},{6,70},{7,71},{8,72},{9,... | collective-permute-start | bytes 417800 | tf_op jit(solution)/shard_map/ppermute | solution.py:41
  61.3 0.9 collective-permute-start.11
  62.2 0.0 collective-permute-start.9
  62.2 2.3 %collective-permute-done.10 = f32[136,256]{1,0:T(8,128)S(1)} collective-permute-done((f32[136,256]{1,0:T(8,128)S(1)}, f32[136,256]{1,0:T(8,128)S(1)}, u32[]{:S(2)}, u32[]{:S(2)}) %collective-permute-start.10) | collective-permute-done | bytes 139296 | tf_op jit(solution)/shard_map/ppermute | solution.py:41
  64.5 3.3 %collective-permute-done.11 = f32[136,256]{1,0:T(8,128)S(1)} collective-permute-done((f32[136,256]{1,0:T(8,128)S(1)}, f32[136,256]{1,0:T(8,128)S(1)}, u32[]{:S(2)}, u32[]{:S(2)}) %collective-permute-start.11) | collective-permute-done | bytes 139296 | tf_op jit(solution)/shard_map/ppermute | solution.py:41
  67.7 0.1 collective-permute-done.9
  68.0 0.1 copy.15
  68.1 11.7 %cholesky.45 = f32[128,128]{1,0:T(8,128)S(1)} custom-call(f32[128,128]{1,0:T(8,128)S(1)} %bitcast_select_fusion.1), custom_call_target="Cholesky" | custom-call | tf_op jit(solution)/shard_map/jit(cholesky)/cholesky | solution.py:80
  79.8 0.6 compare_reduce_fusion.1
  80.5 0.7 select_bitcast_fusion.1
  81.1 9.8 %custom-call.8 = f32[1,128,128]{1,2,0:T(8,128)S(1)} custom-call(f32[1,128,128]{2,1,0:T(8,128)S(1)} %get-tuple-element.22), custom_call_target="InvertDiagBlocksLowerTriangular" | custom-call | tf_op jit(solution)/shard_map/triangular_solve/custom-call.0 | solution.py:81
  90.9 0.3 fusion.17
  91.2 0.2 fusion.19
  91.4 0.1 copy.17
  91.5 0.3 fusion.35
  91.8 0.3 fusion.24
  92.1 11.7 %cholesky.56 = f32[128,128]{1,0:T(8,128)S(1)} custom-call(f32[128,128]{1,0:T(8,128)S(1)} %fusion.24), custom_call_target="Cholesky" | custom-call | tf_op jit(solution)/shard_map/jit(cholesky)/cholesky | solution.py:84
  103.9 0.6 compare_reduce_fusion
  104.5 0.7 select_bitcast_fusion
  105.2 0.8 copy.18
  106.1 9.8 %custom-call.9 = f32[1,128,128]{1,2,0:T(8,128)S(1)} custom-call(f32[1,128,128]{2,1,0:T(8,128)S(1)} %get-tuple-element.20), custom_call_target="InvertDiagBlocksLowerTriangular" | custom-call | tf_op jit(solution)/shard_map/triangular_solve/custom-call.0 | solution.py:85
  115.9 0.3 fusion.15
  116.1 0.1 copy.16
  116.2 0.3 convolution_negate_fusion
  116.5 1.4 %fusion.5 = f32[512,256]{1,0:T(8,128)} fusion(f32[512,256]{1,0:T(8,128)S(1)} %fusion.1, f32[128,128]{1,0:T(8,128)S(1)} %fusion.17, f32[128,128]{1,0:T(8,128)S(1)} %copy.16, f32[128,128]{1,0:T(8,128)S(1)} %convolution_negate_fusion), kind=kOutput, calls=%fused_computation.11 | convolution fusion | flops 402980864 | bytes 1245184 | tf_op jit(solution)/shard_map/dot_general | solution.py:146
  (14 shorter events, 0.3 us)
Async XLA Ops:
  6.8 21.0 %copy-start = (f32[512,256]{1,0:T(8,128)S(1)}, f32[512,256]{1,0:T(8,128)}, u32[]{:S(2)}) copy-start(f32[512,256]{1,0:T(8,128)} %param.13) | copy-start | bytes 1572868
  6.8 21.0 %copy-start.1 = (f32[512]{0:T(512)S(1)}, f32[512]{0:T(512)}, u32[]{:S(2)}) copy-start(f32[512]{0:T(512)} %param.14) | copy-start | bytes 6148
  6.8 17.6 %collective-permute-start = (f32[4,128,256]{2,1,0:T(8,128)S(1)}, f32[4,128,256]{2,1,0:T(8,128)S(1)}, u32[]{:S(2)}, u32[]{:S(2)}) collective-permute-start(f32[4,128,256]{2,1,0:T(8,128)S(1)} %get-tuple-element.24), channel_id=1, source_target_pairs={{0,1},{1,2},{2,3},{3,4},{4,5},{5,6},{6,7},{7,8},{8,9},{9,10},{10,1... | collective-permute-start | bytes 1572872 | tf_op jit(solution)/shard_map/ppermute | solution.py:18
  10.9 15.7 %collective-permute-start.1 = (f32[4,128,256]{2,1,0:T(8,128)S(1)}, f32[4,128,256]{2,1,0:T(8,128)S(1)}, u32[]{:S(2)}, u32[]{:S(2)}) collective-permute-start(f32[4,128,256]{2,1,0:T(8,128)S(1)} %get-tuple-element.25), channel_id=1, source_target_pairs={{1,0},{2,1},{3,2},{4,3},{5,4},{6,5},{7,6},{8,7},{9,8},{10,9},{11,1... | collective-permute-start | bytes 1572872 | tf_op jit(solution)/shard_map/ppermute | solution.py:18
  30.4 5.7 %collective-permute-start.2 = (f32[136,256]{1,0:T(8,128)S(1)}, f32[136,256]{1,0:T(8,128)S(1)}, u32[]{:S(2)}, u32[]{:S(2)}) collective-permute-start(f32[136,256]{1,0:T(8,128)S(1)} %select_maximum_fusion.2), channel_id=1, source_target_pairs={{0,1},{1,0},{2,3},{3,2},{4,5},{5,4},{6,7},{7,6},{8,9},{9,8},{10,11... | collective-permute-start | bytes 417800 | tf_op jit(solution)/shard_map/ppermute | solution.py:41
  30.6 12.4 %collective-permute-start.3 = (f32[136,256]{1,0:T(8,128)S(1)}, f32[136,256]{1,0:T(8,128)S(1)}, u32[]{:S(2)}, u32[]{:S(2)}) collective-permute-start(f32[136,256]{1,0:T(8,128)S(1)} %select_maximum_fusion.2), channel_id=1, source_target_pairs={{0,2},{1,3},{2,0},{3,1},{4,6},{5,7},{6,4},{7,5},{8,10},{9,11},{10,... | collective-permute-start | bytes 417800 | tf_op jit(solution)/shard_map/ppermute | solution.py:41
  36.1 9.6 %collective-permute-start.4 = (f32[136,256]{1,0:T(8,128)S(1)}, f32[136,256]{1,0:T(8,128)S(1)}, u32[]{:S(2)}, u32[]{:S(2)}) collective-permute-start(f32[136,256]{1,0:T(8,128)S(1)} %select_maximum_fusion.2), channel_id=1, source_target_pairs={{0,3},{1,2},{2,1},{3,0},{4,7},{5,6},{6,5},{7,4},{8,11},{9,10},{10,... | collective-permute-start | bytes 417800 | tf_op jit(solution)/shard_map/ppermute | solution.py:41
  45.8 1.7 %collective-permute-start.5 = (f32[136,256]{1,0:T(8,128)S(1)}, f32[136,256]{1,0:T(8,128)S(1)}, u32[]{:S(2)}, u32[]{:S(2)}) collective-permute-start(f32[136,256]{1,0:T(8,128)S(1)} %add_add_fusion.2), channel_id=1, source_target_pairs={{0,4},{1,5},{2,6},{3,7},{4,0},{5,1},{6,2},{7,3},{8,12},{9,13},{10,... | collective-permute-start | bytes 417800 | tf_op jit(solution)/shard_map/ppermute | solution.py:41
  47.5 4.9 %collective-permute-start.6 = (f32[136,256]{1,0:T(8,128)S(1)}, f32[136,256]{1,0:T(8,128)S(1)}, u32[]{:S(2)}, u32[]{:S(2)}) collective-permute-start(f32[136,256]{1,0:T(8,128)S(1)} %add.67), channel_id=1, source_target_pairs={{0,8},{1,9},{2,10},{3,11},{4,12},{5,13},{6,14},{7,15},{8,0},{9,1},... | collective-permute-start | bytes 417800 | tf_op jit(solution)/shard_map/ppermute | solution.py:41
  47.6 8.2 %collective-permute-start.7 = (f32[136,256]{1,0:T(8,128)S(1)}, f32[136,256]{1,0:T(8,128)S(1)}, u32[]{:S(2)}, u32[]{:S(2)}) collective-permute-start(f32[136,256]{1,0:T(8,128)S(1)} %add.67), channel_id=1, source_target_pairs={{0,16},{1,17},{2,18},{3,19},{4,20},{5,21},{6,22},{7,23},{8,24},{9,... | collective-permute-start | bytes 417800 | tf_op jit(solution)/shard_map/ppermute | solution.py:41
  49.2 9.3 %collective-permute-start.8 = (f32[136,256]{1,0:T(8,128)S(1)}, f32[136,256]{1,0:T(8,128)S(1)}, u32[]{:S(2)}, u32[]{:S(2)}) collective-permute-start(f32[136,256]{1,0:T(8,128)S(1)} %add.67), channel_id=1, source_target_pairs={{0,24},{1,25},{2,26},{3,27},{4,28},{5,29},{6,30},{7,31},{8,16},{9,... | collective-permute-start | bytes 417800 | tf_op jit(solution)/shard_map/ppermute | solution.py:41
  58.5 6.0 %collective-permute-start.10 = (f32[136,256]{1,0:T(8,128)S(1)}, f32[136,256]{1,0:T(8,128)S(1)}, u32[]{:S(2)}, u32[]{:S(2)}) collective-permute-start(f32[136,256]{1,0:T(8,128)S(1)} %add_add_fusion.1), channel_id=1, source_target_pairs={{0,64},{1,65},{2,66},{3,67},{4,68},{5,69},{6,70},{7,71},{8,72},{9,... | collective-permute-start | bytes 417800 | tf_op jit(solution)/shard_map/ppermute | solution.py:41
  61.3 6.4 %collective-permute-start.11 = (f32[136,256]{1,0:T(8,128)S(1)}, f32[136,256]{1,0:T(8,128)S(1)}, u32[]{:S(2)}, u32[]{:S(2)}) collective-permute-start(f32[136,256]{1,0:T(8,128)S(1)} %add_add_fusion.1), channel_id=1, source_target_pairs={{0,96},{1,97},{2,98},{3,99},{4,100},{5,101},{6,102},{7,103},{8,104... | collective-permute-start | bytes 417800 | tf_op jit(solution)/shard_map/ppermute | solution.py:41
  62.2 5.7 %collective-permute-start.9 = (f32[136,256]{1,0:T(8,128)S(1)}, f32[136,256]{1,0:T(8,128)S(1)}, u32[]{:S(2)}, u32[]{:S(2)}) collective-permute-start(f32[136,256]{1,0:T(8,128)S(1)} %add_add_fusion.1), channel_id=1, source_target_pairs={{0,32},{1,33},{2,34},{3,35},{4,36},{5,37},{6,38},{7,39},{8,40},{9,... | collective-permute-start | bytes 417800 | tf_op jit(solution)/shard_map/ppermute | solution.py:41

commit v4 on v3

--- a/solution.py
+++ b/solution.py
@@ -10,6 +10,7 @@
 
 exact_mode = lax.Precision.HIGHEST
 DEVICE_AXES = ("lat", "sub")
+CORE_BIT = 2
 
 
 def shifted(value, axis, steps):
@@ -24,27 +25,45 @@
     for width in (2, 1, 2, 2):
         if low >= bits:
             break
-        groups.append(list(range(low, min(bits, low + width))))
+        if low != CORE_BIT:
+            groups.append(list(range(low, min(bits, low + width))))
         low += width
     if low < bits:
         groups.append(list(range(low, bits)))
     return groups
 
 
+def exchange(value, count, mask):
+    return lax.ppermute(value, DEVICE_AXES, [(i, i ^ mask) for i in range(count)])
+
+
 def all_sum(value, count):
+    device_index = lax.axis_index(DEVICE_AXES)
+    split = count > (1 << CORE_BIT)
+    if split:
+        core = (device_index >> CORE_BIT) & 1
+        half = value.shape[0] // 2
+        low, high = value[:half], value[half:]
+        kept = jnp.where(core == 0, low, high)
+        sent = jnp.where(core == 0, high, low)
+        value = kept + exchange(sent, count, 1 << CORE_BIT)
     for group in exchange_stages(count):
         masks = []
         for size in range(1, len(group) + 1):
             for combo in itertools.combinations(group, size):
                 masks.append(sum(1 << bit for bit in combo))
-        received = [
-            lax.ppermute(value, DEVICE_AXES, [(i, i ^ mask) for i in range(count)])
-            for mask in masks
-        ]
+        received = [exchange(value, count, mask) for mask in masks]
         total = received[0]
         for part in received[1:]:
             total = total + part
         value = value + total
+    if split:
+        other = exchange(value, count, 1 << CORE_BIT)
+        value = jnp.where(
+            core == 0,
+            jnp.concatenate([value, other], axis=0),
+            jnp.concatenate([other, value], axis=0),
+        )
     return value
 
 
@@ -54,9 +73,10 @@
     cols = lax.broadcasted_iota(jnp.int32, (half, half), 1)
     g11, g12, g22 = gram[:half, :half], gram[:half, half:], gram[half:, half:]
     tri = jnp.where(rows <= cols, g11, g22)
-    diag = jnp.diagonal(g22)
-    extra = jnp.zeros((8, 2 * half), gram.dtype).at[0, :half].set(diag)
-    return jnp.concatenate([jnp.concatenate([g12, tri], axis=1), extra], axis=0)
+    diag = jnp.sum(jnp.where(rows == cols, g22, 0.0), axis=0, keepdims=True)
+    extra = jnp.zeros((15, 2 * half), gram.dtype)
+    extra_row = jnp.concatenate([diag, jnp.zeros_like(diag)], axis=1)
+    return jnp.concatenate([jnp.concatenate([g12, tri], axis=1), extra_row, extra], axis=0)
 
 
 def unpack_gram(packed, size):

time: 118 us -> 112 us (0.949)
  waiting for transfers between devices: 35 us -> 27.3 us
  starting transfers between devices: 22.1 us -> 25 us
    ppermute x10 -> x11, waiting for transfers between devices: 23.3 us -> 15.7 us  [exchange(): lax.ppermute(value, DEVICE_AXES, [(i, i ^ mask) for i in range(count)])]
    ppermute x10 -> x11, starting transfers between devices: 14 us -> 16.9 us  [exchange(): lax.ppermute(value, DEVICE_AXES, [(i, i ^ mask) for i in range(count)])]
    gather x1 -> x0, local copies, waits for them, and re-layouts: 1.25 us -> none  [pack_gram(): diag = jnp.diagonal(g22)]
  transfers between devices with their start and end apart: 12 -> 13, of which waited for: 11 -> 10; matrix products, arithmetic and copies ran while one was open for 0% -> 0% of each run, Pallas kernels for 0% -> 0%
where the time goes in v4:
time: 112 us
  other arithmetic  48 us (43%)
  waiting for transfers between devices  27.3 us (24%)
  starting transfers between devices  25 us (22%)
  matrix products  4.05 us (4%)
  Pallas kernels  3.48 us (3%)
  local copies, waits for them, and re-layouts  3.32 us (3%)
    ppermute x11, starting transfers between devices, exchange(): lax.ppermute(value, DEVICE_AXES, [(i, i ^ mask) for i in range(count)])  16.9 us
    ppermute x11, waiting for transfers between devices, exchange(): lax.ppermute(value, DEVICE_AXES, [(i, i ^ mask) for i in range(count)])  15.7 us
    another operation x3, other arithmetic, blocked_cholesky(): l22 = jnp.linalg.cholesky(schur, symmetrize_input=False)  12.4 us
    another operation x3, other arithmetic, blocked_cholesky(): l11 = jnp.linalg.cholesky(gram[:half, :half], symmetrize_input=False)  12.4 us
    ppermute x2, waiting for transfers between devices, shifted(): lax.ppermute(value, axis, [(source, source + steps) for source in range(i...  11.6 us
    another operation x2, other arithmetic, blocked_cholesky(): l11_inv = lax.linalg.triangular_solve(l11, eye, left_side=True, lower=True)  10.5 us
    another operation x2, other arithmetic, blocked_cholesky(): l22_inv = lax.linalg.triangular_solve(l22, eye, left_side=True, lower=True)  10.5 us
    ppermute x2, starting transfers between devices, shifted(): lax.ppermute(value, axis, [(source, source + steps) for source in range(i...  8.07 us
  transfers between devices with their start and end apart: 13, of which 10 were waited for; matrix products, arithmetic and copies ran while one was open for 0% of the time, Pallas kernels for 0%

profile of v4, /device:TPU:1, one launch (start us, length us, event | category | flops | bytes accessed | tf_op | source)
XLA Modules:
  0.0 112.1 jit_solution(1254318593197346477)
XLA Ops:
  0.6 0.7 subtract_clamp_fusion
  1.3 0.1 copy.13
  1.4 0.6 min.12.slot_ref
  2.0 3.5 %shard_map.68 = f32[12,128,256]{2,1,0:T(8,128)} custom-call(s32[32]{0:T(128)} %min.12.slot_ref, bf16[16,2,128,128]{3,2,1,0:T(8,128)(2,1)} %weight_ref.1, bf16[16,128,256]{2,1,0:T(8,128)(2,1)} %bitcast.41), custom_call_target="tpu_custom_call" | custom-call | tf_op jit(solution)/shard_map/pallas_call | solution.py:131
  5.5 1.3 %fusion.39 = (f32[4,128,256]{2,1,0:T(8,128)S(1)}, f32[4,128,256]{2,1,0:T(8,128)S(1)}) fusion(f32[12,128,256]{2,1,0:T(8,128)} %shard_map.68), kind=kLoop, calls=%fused_computation.72 | loop fusion | bytes 2097152 | tf_op jit(solution)/shard_map/slice | solution.py:154
  6.8 0.0 copy-start
  6.8 0.0 copy-start.1
  6.8 4.2 %collective-permute-start = (f32[4,128,256]{2,1,0:T(8,128)S(1)}, f32[4,128,256]{2,1,0:T(8,128)S(1)}, u32[]{:S(2)}, u32[]{:S(2)}) collective-permute-start(f32[4,128,256]{2,1,0:T(8,128)S(1)} %get-tuple-element.12), channel_id=1, source_target_pairs={{0,1},{1,2},{2,3},{3,4},{4,5},{5,6},{6,7},{7,8},{8,9},{9,10},{10,1... | collective-permute-start | bytes 1572872 | tf_op jit(solution)/shard_map/ppermute | solution.py:19
  11.0 3.9 %collective-permute-start.1 = (f32[4,128,256]{2,1,0:T(8,128)S(1)}, f32[4,128,256]{2,1,0:T(8,128)S(1)}, u32[]{:S(2)}, u32[]{:S(2)}) collective-permute-start(f32[4,128,256]{2,1,0:T(8,128)S(1)} %get-tuple-element.13), channel_id=1, source_target_pairs={{1,0},{2,1},{3,2},{4,3},{5,4},{6,5},{7,6},{8,7},{9,8},{10,9},{11,1... | collective-permute-start | bytes 1572872 | tf_op jit(solution)/shard_map/ppermute | solution.py:19
  14.9 0.1 pad_slice_fusion
  15.0 9.4 %collective-permute-done = f32[4,128,256]{2,1,0:T(8,128)S(1)} collective-permute-done((f32[4,128,256]{2,1,0:T(8,128)S(1)}, f32[4,128,256]{2,1,0:T(8,128)S(1)}, u32[]{:S(2)}, u32[]{:S(2)}) %collective-permute-start) | collective-permute-done | bytes 524320 | tf_op jit(solution)/shard_map/ppermute | solution.py:19
  24.5 2.2 %collective-permute-done.1 = f32[4,128,256]{2,1,0:T(8,128)S(1)} collective-permute-done((f32[4,128,256]{2,1,0:T(8,128)S(1)}, f32[4,128,256]{2,1,0:T(8,128)S(1)}, u32[]{:S(2)}, u32[]{:S(2)}) %collective-permute-start.1) | collective-permute-done | bytes 524320 | tf_op jit(solution)/shard_map/ppermute | solution.py:19
  26.6 1.1 %fusion = f32[4,128,256]{2,1,0:T(8,128)S(1)} fusion(f32[4,128,256]{2,1,0:T(8,128)S(1)} %collective-permute-done.1, f32[4,128,256]{2,1,0:T(8,128)S(1)} %collective-permute-done, f32[12,128,256]{2,1,0:T(8,128)} %shard_map.68), kind=kLoop, calls=%fused_computation.2 | loop fusion | flops 262144 | bytes 2097152 | tf_op jit(solution)/shard_map/add | solution.py:156
  27.8 0.0 copy-done
  27.8 0.0 copy-done.1
  27.8 0.1 fusion.1
  27.9 1.0 fusion.40
  29.0 0.1 copy.14
  29.2 0.1 broadcast_select_fusion
  29.3 0.7 collective-permute-start.2
  29.9 0.9 collective-permute-done.2
  30.8 0.1 select_add_fusion
  30.9 1.4 %collective-permute-start.3 = (f32[72,256]{1,0:T(8,128)S(1)}, f32[72,256]{1,0:T(8,128)S(1)}, u32[]{:S(2)}, u32[]{:S(2)}) collective-permute-start(f32[72,256]{1,0:T(8,128)S(1)} %select_add_fusion), channel_id=1, source_target_pairs={{0,1},{1,0},{2,3},{3,2},{4,5},{5,4},{6,7},{7,6},{8,9},{9,8},{10,11... | collective-permute-start | bytes 221192 | tf_op jit(solution)/shard_map/ppermute | solution.py:37
  32.3 4.1 %collective-permute-start.4 = (f32[72,256]{1,0:T(8,128)S(1)}, f32[72,256]{1,0:T(8,128)S(1)}, u32[]{:S(2)}, u32[]{:S(2)}) collective-permute-start(f32[72,256]{1,0:T(8,128)S(1)} %select_add_fusion), channel_id=1, source_target_pairs={{0,2},{1,3},{2,0},{3,1},{4,6},{5,7},{6,4},{7,5},{8,10},{9,11},{10,... | collective-permute-start | bytes 221192 | tf_op jit(solution)/shard_map/ppermute | solution.py:37
  36.4 0.0 collective-permute-start.5
  36.4 0.0 collective-permute-done.3
  36.4 3.8 %collective-permute-done.4 = f32[72,256]{1,0:T(8,128)S(1)} collective-permute-done((f32[72,256]{1,0:T(8,128)S(1)}, f32[72,256]{1,0:T(8,128)S(1)}, u32[]{:S(2)}, u32[]{:S(2)}) %collective-permute-start.4) | collective-permute-done | bytes 73760 | tf_op jit(solution)/shard_map/ppermute | solution.py:37
  40.2 1.5 %collective-permute-done.5 = f32[72,256]{1,0:T(8,128)S(1)} collective-permute-done((f32[72,256]{1,0:T(8,128)S(1)}, f32[72,256]{1,0:T(8,128)S(1)}, u32[]{:S(2)}, u32[]{:S(2)}) %collective-permute-start.5) | collective-permute-done | bytes 73760 | tf_op jit(solution)/shard_map/ppermute | solution.py:37
  41.7 1.7 %collective-permute-start.6 = (f32[72,256]{1,0:T(8,128)S(1)}, f32[72,256]{1,0:T(8,128)S(1)}, u32[]{:S(2)}, u32[]{:S(2)}) collective-permute-start(f32[72,256]{1,0:T(8,128)S(1)} %add_add_fusion.2), channel_id=1, source_target_pairs={{0,8},{1,9},{2,10},{3,11},{4,12},{5,13},{6,14},{7,15},{8,0},{9,1},... | collective-permute-start | bytes 221192 | tf_op jit(solution)/shard_map/ppermute | solution.py:37
  43.5 1.8 %collective-permute-start.7 = (f32[72,256]{1,0:T(8,128)S(1)}, f32[72,256]{1,0:T(8,128)S(1)}, u32[]{:S(2)}, u32[]{:S(2)}) collective-permute-start(f32[72,256]{1,0:T(8,128)S(1)} %add_add_fusion.2), channel_id=1, source_target_pairs={{0,16},{1,17},{2,18},{3,19},{4,20},{5,21},{6,22},{7,23},{8,24},{9,... | collective-permute-start | bytes 221192 | tf_op jit(solution)/shard_map/ppermute | solution.py:37
  45.2 0.7 collective-permute-start.8
  45.9 0.0 collective-permute-done.6
  45.9 3.1 %collective-permute-done.7 = f32[72,256]{1,0:T(8,128)S(1)} collective-permute-done((f32[72,256]{1,0:T(8,128)S(1)}, f32[72,256]{1,0:T(8,128)S(1)}, u32[]{:S(2)}, u32[]{:S(2)}) %collective-permute-start.7) | collective-permute-done | bytes 73760 | tf_op jit(solution)/shard_map/ppermute | solution.py:37
  49.0 1.4 %collective-permute-done.8 = f32[72,256]{1,0:T(8,128)S(1)} collective-permute-done((f32[72,256]{1,0:T(8,128)S(1)}, f32[72,256]{1,0:T(8,128)S(1)}, u32[]{:S(2)}, u32[]{:S(2)}) %collective-permute-start.8) | collective-permute-done | bytes 73760 | tf_op jit(solution)/shard_map/ppermute | solution.py:37
  50.5 2.8 %collective-permute-start.10 = (f32[72,256]{1,0:T(8,128)S(1)}, f32[72,256]{1,0:T(8,128)S(1)}, u32[]{:S(2)}, u32[]{:S(2)}) collective-permute-start(f32[72,256]{1,0:T(8,128)S(1)} %add_add_fusion.1), channel_id=1, source_target_pairs={{0,64},{1,65},{2,66},{3,67},{4,68},{5,69},{6,70},{7,71},{8,72},{9,... | collective-permute-start | bytes 221192 | tf_op jit(solution)/shard_map/ppermute | solution.py:37
  53.3 0.9 collective-permute-start.11
  54.2 0.0 collective-permute-start.9
  54.2 1.1 collective-permute-done.10
  55.3 2.9 %collective-permute-done.11 = f32[72,256]{1,0:T(8,128)S(1)} collective-permute-done((f32[72,256]{1,0:T(8,128)S(1)}, f32[72,256]{1,0:T(8,128)S(1)}, u32[]{:S(2)}, u32[]{:S(2)}) %collective-permute-start.11) | collective-permute-done | bytes 73760 | tf_op jit(solution)/shard_map/ppermute | solution.py:37
  58.2 0.0 collective-permute-done.9
  58.2 2.9 %collective-permute-start.12 = (f32[72,256]{1,0:T(8,128)S(1)}, f32[72,256]{1,0:T(8,128)S(1)}, u32[]{:S(2)}, u32[]{:S(2)}) collective-permute-start(f32[72,256]{1,0:T(8,128)S(1)} %add_add_fusion), channel_id=1, source_target_pairs={{0,4},{1,5},{2,6},{3,7},{4,0},{5,1},{6,2},{7,3},{8,12},{9,13},{10,... | collective-permute-start | bytes 221192 | tf_op jit(solution)/shard_map/ppermute | solution.py:37
  61.1 0.9 collective-permute-done.12
  62.1 0.1 copy.15
  62.2 11.7 %cholesky.45 = f32[128,128]{1,0:T(8,128)S(1)} custom-call(f32[128,128]{1,0:T(8,128)S(1)} %bitcast_select_fusion.1), custom_call_target="Cholesky" | custom-call | tf_op jit(solution)/shard_map/jit(cholesky)/cholesky | solution.py:100
  73.9 0.6 compare_reduce_fusion.1
  74.6 0.7 select_bitcast_fusion.1
  75.2 9.8 %custom-call.6 = f32[1,128,128]{1,2,0:T(8,128)S(1)} custom-call(f32[1,128,128]{2,1,0:T(8,128)S(1)} %get-tuple-element.10), custom_call_target="InvertDiagBlocksLowerTriangular" | custom-call | tf_op jit(solution)/shard_map/triangular_solve/custom-call.0 | solution.py:101
  85.1 0.3 fusion.17
  85.4 0.2 fusion.24
  85.6 0.1 copy.17
  85.7 0.3 fusion.41
  86.0 0.3 fusion.29
  86.3 11.7 %cholesky.56 = f32[128,128]{1,0:T(8,128)S(1)} custom-call(f32[128,128]{1,0:T(8,128)S(1)} %fusion.29), custom_call_target="Cholesky" | custom-call | tf_op jit(solution)/shard_map/jit(cholesky)/cholesky | solution.py:104
  98.0 0.6 compare_reduce_fusion
  98.6 0.7 select_bitcast_fusion
  99.3 0.8 copy.18
  100.2 9.8 %custom-call.7 = f32[1,128,128]{1,2,0:T(8,128)S(1)} custom-call(f32[1,128,128]{2,1,0:T(8,128)S(1)} %get-tuple-element.8), custom_call_target="InvertDiagBlocksLowerTriangular" | custom-call | tf_op jit(solution)/shard_map/triangular_solve/custom-call.0 | solution.py:105
  110.0 0.3 fusion.15
  110.3 0.1 copy.16
  110.4 0.3 convolution_negate_fusion
  110.7 1.4 %fusion.5 = f32[512,256]{1,0:T(8,128)} fusion(f32[512,256]{1,0:T(8,128)S(1)} %fusion.1, f32[128,128]{1,0:T(8,128)S(1)} %fusion.17, f32[128,128]{1,0:T(8,128)S(1)} %copy.16, f32[128,128]{1,0:T(8,128)S(1)} %convolution_negate_fusion), kind=kOutput, calls=%fused_computation.10 | convolution fusion | flops 402980864 | bytes 1245184 | tf_op jit(solution)/shard_map/dot_general | solution.py:166
  (13 shorter events, 0.3 us)
Async XLA Ops:
  6.8 21.0 %copy-start = (f32[512,256]{1,0:T(8,128)S(1)}, f32[512,256]{1,0:T(8,128)}, u32[]{:S(2)}) copy-start(f32[512,256]{1,0:T(8,128)} %param.11) | copy-start | bytes 1572868
  6.8 21.0 %copy-start.1 = (f32[512]{0:T(512)S(1)}, f32[512]{0:T(512)}, u32[]{:S(2)}) copy-start(f32[512]{0:T(512)} %param.12) | copy-start | bytes 6148
  6.8 17.6 %collective-permute-start = (f32[4,128,256]{2,1,0:T(8,128)S(1)}, f32[4,128,256]{2,1,0:T(8,128)S(1)}, u32[]{:S(2)}, u32[]{:S(2)}) collective-permute-start(f32[4,128,256]{2,1,0:T(8,128)S(1)} %get-tuple-element.12), channel_id=1, source_target_pairs={{0,1},{1,2},{2,3},{3,4},{4,5},{5,6},{6,7},{7,8},{8,9},{9,10},{10,1... | collective-permute-start | bytes 1572872 | tf_op jit(solution)/shard_map/ppermute | solution.py:19
  11.0 15.6 %collective-permute-start.1 = (f32[4,128,256]{2,1,0:T(8,128)S(1)}, f32[4,128,256]{2,1,0:T(8,128)S(1)}, u32[]{:S(2)}, u32[]{:S(2)}) collective-permute-start(f32[4,128,256]{2,1,0:T(8,128)S(1)} %get-tuple-element.13), channel_id=1, source_target_pairs={{1,0},{2,1},{3,2},{4,3},{5,4},{6,5},{7,6},{8,7},{9,8},{10,9},{11,1... | collective-permute-start | bytes 1572872 | tf_op jit(solution)/shard_map/ppermute | solution.py:19
  29.3 1.6 %collective-permute-start.2 = (f32[72,256]{1,0:T(8,128)S(1)}, f32[72,256]{1,0:T(8,128)S(1)}, u32[]{:S(2)}, u32[]{:S(2)}) collective-permute-start(f32[72,256]{1,0:T(8,128)S(1)} %broadcast_select_fusion), channel_id=1, source_target_pairs={{0,4},{1,5},{2,6},{3,7},{4,0},{5,1},{6,2},{7,3},{8,12},{9,13},{10,... | collective-permute-start | bytes 221192 | tf_op jit(solution)/shard_map/ppermute | solution.py:37
  30.9 5.5 %collective-permute-start.3 = (f32[72,256]{1,0:T(8,128)S(1)}, f32[72,256]{1,0:T(8,128)S(1)}, u32[]{:S(2)}, u32[]{:S(2)}) collective-permute-start(f32[72,256]{1,0:T(8,128)S(1)} %select_add_fusion), channel_id=1, source_target_pairs={{0,1},{1,0},{2,3},{3,2},{4,5},{5,4},{6,7},{7,6},{8,9},{9,8},{10,11... | collective-permute-start | bytes 221192 | tf_op jit(solution)/shard_map/ppermute | solution.py:37
  32.3 7.9 %collective-permute-start.4 = (f32[72,256]{1,0:T(8,128)S(1)}, f32[72,256]{1,0:T(8,128)S(1)}, u32[]{:S(2)}, u32[]{:S(2)}) collective-permute-start(f32[72,256]{1,0:T(8,128)S(1)} %select_add_fusion), channel_id=1, source_target_pairs={{0,2},{1,3},{2,0},{3,1},{4,6},{5,7},{6,4},{7,5},{8,10},{9,11},{10,... | collective-permute-start | bytes 221192 | tf_op jit(solution)/shard_map/ppermute | solution.py:37
  36.4 5.3 %collective-permute-start.5 = (f32[72,256]{1,0:T(8,128)S(1)}, f32[72,256]{1,0:T(8,128)S(1)}, u32[]{:S(2)}, u32[]{:S(2)}) collective-permute-start(f32[72,256]{1,0:T(8,128)S(1)} %select_add_fusion), channel_id=1, source_target_pairs={{0,3},{1,2},{2,1},{3,0},{4,7},{5,6},{6,5},{7,4},{8,11},{9,10},{10,... | collective-permute-start | bytes 221192 | tf_op jit(solution)/shard_map/ppermute | solution.py:37
  41.7 4.2 %collective-permute-start.6 = (f32[72,256]{1,0:T(8,128)S(1)}, f32[72,256]{1,0:T(8,128)S(1)}, u32[]{:S(2)}, u32[]{:S(2)}) collective-permute-start(f32[72,256]{1,0:T(8,128)S(1)} %add_add_fusion.2), channel_id=1, source_target_pairs={{0,8},{1,9},{2,10},{3,11},{4,12},{5,13},{6,14},{7,15},{8,0},{9,1},... | collective-permute-start | bytes 221192 | tf_op jit(solution)/shard_map/ppermute | solution.py:37
  43.5 5.6 %collective-permute-start.7 = (f32[72,256]{1,0:T(8,128)S(1)}, f32[72,256]{1,0:T(8,128)S(1)}, u32[]{:S(2)}, u32[]{:S(2)}) collective-permute-start(f32[72,256]{1,0:T(8,128)S(1)} %add_add_fusion.2), channel_id=1, source_target_pairs={{0,16},{1,17},{2,18},{3,19},{4,20},{5,21},{6,22},{7,23},{8,24},{9,... | collective-permute-start | bytes 221192 | tf_op jit(solution)/shard_map/ppermute | solution.py:37
  45.2 5.3 %collective-permute-start.8 = (f32[72,256]{1,0:T(8,128)S(1)}, f32[72,256]{1,0:T(8,128)S(1)}, u32[]{:S(2)}, u32[]{:S(2)}) collective-permute-start(f32[72,256]{1,0:T(8,128)S(1)} %add_add_fusion.2), channel_id=1, source_target_pairs={{0,24},{1,25},{2,26},{3,27},{4,28},{5,29},{6,30},{7,31},{8,16},{9,... | collective-permute-start | bytes 221192 | tf_op jit(solution)/shard_map/ppermute | solution.py:37
  50.5 4.8 %collective-permute-start.10 = (f32[72,256]{1,0:T(8,128)S(1)}, f32[72,256]{1,0:T(8,128)S(1)}, u32[]{:S(2)}, u32[]{:S(2)}) collective-permute-start(f32[72,256]{1,0:T(8,128)S(1)} %add_add_fusion.1), channel_id=1, source_target_pairs={{0,64},{1,65},{2,66},{3,67},{4,68},{5,69},{6,70},{7,71},{8,72},{9,... | collective-permute-start | bytes 221192 | tf_op jit(solution)/shard_map/ppermute | solution.py:37
  53.3 4.9 %collective-permute-start.11 = (f32[72,256]{1,0:T(8,128)S(1)}, f32[72,256]{1,0:T(8,128)S(1)}, u32[]{:S(2)}, u32[]{:S(2)}) collective-permute-start(f32[72,256]{1,0:T(8,128)S(1)} %add_add_fusion.1), channel_id=1, source_target_pairs={{0,96},{1,97},{2,98},{3,99},{4,100},{5,101},{6,102},{7,103},{8,104... | collective-permute-start | bytes 221192 | tf_op jit(solution)/shard_map/ppermute | solution.py:37
  54.2 4.0 %collective-permute-start.9 = (f32[72,256]{1,0:T(8,128)S(1)}, f32[72,256]{1,0:T(8,128)S(1)}, u32[]{:S(2)}, u32[]{:S(2)}) collective-permute-start(f32[72,256]{1,0:T(8,128)S(1)} %add_add_fusion.1), channel_id=1, source_target_pairs={{0,32},{1,33},{2,34},{3,35},{4,36},{5,37},{6,38},{7,39},{8,40},{9,... | collective-permute-start | bytes 221192 | tf_op jit(solution)/shard_map/ppermute | solution.py:37
  58.2 3.8 %collective-permute-start.12 = (f32[72,256]{1,0:T(8,128)S(1)}, f32[72,256]{1,0:T(8,128)S(1)}, u32[]{:S(2)}, u32[]{:S(2)}) collective-permute-start(f32[72,256]{1,0:T(8,128)S(1)} %add_add_fusion), channel_id=1, source_target_pairs={{0,4},{1,5},{2,6},{3,7},{4,0},{5,1},{6,2},{7,3},{8,12},{9,13},{10,... | collective-permute-start | bytes 221192 | tf_op jit(solution)/shard_map/ppermute | solution.py:37

commit v5 on v4

--- a/solution.py
+++ b/solution.py
@@ -11,6 +11,7 @@
 exact_mode = lax.Precision.HIGHEST
 DEVICE_AXES = ("lat", "sub")
 CORE_BIT = 2
+PANEL = 8
 
 
 def shifted(value, axis, steps):
@@ -93,20 +94,70 @@
     return jnp.concatenate([top, bottom], axis=0)
 
 
-def blocked_cholesky(gram):
-    half = gram.shape[0] // 2
-    eye = jnp.eye(half, dtype=gram.dtype)
-    zeros = jnp.zeros((half, half), gram.dtype)
-    l11 = jnp.linalg.cholesky(gram[:half, :half], symmetrize_input=False)
-    l11_inv = lax.linalg.triangular_solve(l11, eye, left_side=True, lower=True)
-    l21 = jnp.dot(gram[half:, :half], l11_inv.T, precision=exact_mode)
-    schur = gram[half:, half:] - jnp.dot(l21, l21.T, precision=exact_mode)
-    l22 = jnp.linalg.cholesky(schur, symmetrize_input=False)
-    l22_inv = lax.linalg.triangular_solve(l22, eye, left_side=True, lower=True)
-    l21_inv = -jnp.dot(l22_inv, jnp.dot(l21, l11_inv, precision=exact_mode), precision=exact_mode)
-    lower = jnp.block([[l11, zeros], [l21, l22]])
-    lower_inverse = jnp.block([[l11_inv, zeros], [l21_inv, l22_inv]])
-    return lower, lower_inverse
+def cholesky_kernel(gram_ref, upper_ref, inverse_ref, work_ref):
+    size = gram_ref.shape[0]
+    work_ref[...] = gram_ref[...]
+    rows = lax.broadcasted_iota(jnp.int32, (size, size), 0)
+    cols = lax.broadcasted_iota(jnp.int32, (size, size), 1)
+    inverse_ref[...] = jnp.where(rows == cols, 1.0, 0.0).astype(jnp.float32)
+    lane = lax.broadcasted_iota(jnp.int32, (1, size), 1)
+    sub = lax.broadcasted_iota(jnp.int32, (PANEL, 1), 0)
+    row_ids = lax.broadcasted_iota(jnp.int32, (size, 1), 0)
+
+    def panel(index, carry, row0, col0, col1):
+        first = pl.multiple_of(index * PANEL, PANEL)
+        slab = work_ref[pl.ds(first, PANEL), :]
+        inverse_slab = inverse_ref[pl.ds(first, PANEL), :]
+        upper_slab = jnp.zeros((PANEL, size), jnp.float32)
+        for step in range(PANEL):
+            column = first + step
+            picked = jnp.sum(jnp.where(lane == column, slab, 0.0), axis=1, keepdims=True)
+            scale = lax.rsqrt(picked[step : step + 1, :])
+            upper_row = jnp.where(lane >= column, slab[step : step + 1, :] * scale, 0.0)
+            inverse_row = inverse_slab[step : step + 1, :] * scale
+            coef = jnp.where(sub > step, picked * scale, 0.0)
+            slab = slab - coef * upper_row
+            inverse_slab = jnp.where(sub == step, inverse_row, inverse_slab - coef * inverse_row)
+            upper_slab = jnp.where(sub == step, upper_row, upper_slab)
+        upper_ref[pl.ds(first, PANEL), :] = upper_slab
+        inverse_ref[pl.ds(first, PANEL), :] = inverse_slab
+        lower_cols = jnp.transpose(upper_slab)[row0:]
+        lower_cols = jnp.where(row_ids[row0:] >= first + PANEL, lower_cols, 0.0)
+        work_ref[row0:, col0:] = work_ref[row0:, col0:] - jnp.dot(
+            lower_cols, upper_slab[:, col0:], precision=exact_mode,
+            preferred_element_type=jnp.float32,
+        )
+        inverse_ref[row0:, :col1] = inverse_ref[row0:, :col1] - jnp.dot(
+            lower_cols, inverse_slab[:, :col1], precision=exact_mode,
+            preferred_element_type=jnp.float32,
+        )
+        return carry
+
+    quarter = size // 4
+    for part in range(4):
+        row0 = quarter * part
+        col0 = (size // 2) * (part // 2)
+        col1 = (size // 2) * (part // 2 + 1)
+        lax.fori_loop(
+            row0 // PANEL,
+            (row0 + quarter) // PANEL,
+            lambda index, carry, row0=row0, col0=col0, col1=col1: panel(
+                index, carry, row0, col0, col1
+            ),
+            0,
+        )
+
+
+def cholesky_with_inverse(gram):
+    size = gram.shape[0]
+    return pl.pallas_call(
+        cholesky_kernel,
+        out_shape=(
+            jax.ShapeDtypeStruct((size, size), jnp.float32),
+            jax.ShapeDtypeStruct((size, size), jnp.float32),
+        ),
+        scratch_shapes=[pltpu.VMEM((size, size), jnp.float32)],
+    )(gram)
 
 
 def aggregate_kernel(slot_ref, weight_ref, rows_ref, out_ref):
@@ -161,10 +212,10 @@
     )
     local_gram = 0.5 * (local_gram + local_gram.T)
     total_gram = unpack_gram(all_sum(pack_gram(local_gram), device_count), day_count)
-    lower, lower_inverse = blocked_cholesky(total_gram)
+    upper, lower_inverse = cholesky_with_inverse(total_gram)
     root = math.sqrt(anomaly.shape[0] * device_count)
     scores = jnp.dot(anomaly, lower_inverse.T * root, precision=exact_mode)
-    return (scores, lower.T / root)
+    return (scores, upper / root)
 
 
 def solution(mesh):

time: 112 us -> 105 us (0.938)
  other arithmetic: 48 us -> 4.75 us
  Pallas kernels: 3.48 us -> 40.8 us
    another operation x10 -> x0, other arithmetic: 45.7 us -> none  [the longest x3 12.4 us: blocked_cholesky(): l22 = jnp.linalg.cholesky(schur, symmetrize_input=False)]
    pallas_call x0 -> x1, Pallas kernels: none -> 37.3 us  [cholesky_with_inverse(): pl.pallas_call(cholesky_kernel, out_shape=(jax.ShapeDtypeStruct((size, si...]
    div x1, other arithmetic: 0.02 us -> 1.67 us  [body(): return (scores, upper / root)]
where the time goes in v5:
time: 105 us; the launch traced here: 104 us
  Pallas kernels  40.8 us (39%)
  waiting for transfers between devices  27.3 us (26%)
  starting transfers between devices  24.8 us (24%)
  other arithmetic  4.75 us (5%)
  matrix products  3.38 us (3%)
  local copies, waits for them, and re-layouts  2.39 us (2%)
    pallas_call x1, Pallas kernels, cholesky_with_inverse(): pl.pallas_call(cholesky_kernel, out_shape=(jax.ShapeDtypeStruct((size, si...  37.3 us
    ppermute x11, starting transfers between devices, exchange(): lax.ppermute(value, DEVICE_AXES, [(i, i ^ mask) for i in range(count)])  16.8 us
    ppermute x11, waiting for transfers between devices, exchange(): lax.ppermute(value, DEVICE_AXES, [(i, i ^ mask) for i in range(count)])  15.7 us
    ppermute x2, waiting for transfers between devices, shifted(): lax.ppermute(value, axis, [(source, source + steps) for source in range(i...  11.6 us
    ppermute x2, starting transfers between devices, shifted(): lax.ppermute(value, axis, [(source, source + steps) for source in range(i...  8.08 us
    pallas_call x1, Pallas kernels, aggregate(): pl.pallas_call(aggregate_kernel, out_shape=jax.ShapeDtypeStruct((window_c...  3.5 us
    dot_general x1, matrix products, body(): scores = jnp.dot(anomaly, lower_inverse.T * root, precision=exact_mode)  2.36 us
  transfers between devices with their start and end apart: 13, of which 10 were waited for; matrix products, arithmetic and copies ran while one was open for 0% of the time, Pallas kernels for 0%

profile of v5, /device:TPU:1, one launch (start us, length us, event | category | flops | bytes accessed | tf_op | source)
XLA Modules:
  0.0 104.3 jit_solution(18033485617855569686)
XLA Ops:
  0.6 0.7 subtract_clamp_fusion
  1.3 0.1 copy.13
  1.4 0.6 min.12.slot_ref
  2.0 3.5 %shard_map.68 = f32[12,128,256]{2,1,0:T(8,128)} custom-call(s32[32]{0:T(128)} %min.12.slot_ref, bf16[16,2,128,128]{3,2,1,0:T(8,128)(2,1)} %weight_ref.1, bf16[16,128,256]{2,1,0:T(8,128)(2,1)} %bitcast.22), custom_call_target="tpu_custom_call" | custom-call | tf_op jit(solution)/shard_map/pallas_call | solution.py:182
  5.5 1.3 %fusion.13 = (f32[4,128,256]{2,1,0:T(8,128)S(1)}, f32[4,128,256]{2,1,0:T(8,128)S(1)}) fusion(f32[12,128,256]{2,1,0:T(8,128)} %shard_map.68), kind=kLoop, calls=%fused_computation.40 | loop fusion | bytes 2097152 | tf_op jit(solution)/shard_map/slice | solution.py:205
  6.8 0.0 copy-start
  6.8 0.0 copy-start.1
  6.8 4.2 %collective-permute-start = (f32[4,128,256]{2,1,0:T(8,128)S(1)}, f32[4,128,256]{2,1,0:T(8,128)S(1)}, u32[]{:S(2)}, u32[]{:S(2)}) collective-permute-start(f32[4,128,256]{2,1,0:T(8,128)S(1)} %get-tuple-element.6), channel_id=1, source_target_pairs={{0,1},{1,2},{2,3},{3,4},{4,5},{5,6},{6,7},{7,8},{8,9},{9,10},{10,1... | collective-permute-start | bytes 1572872 | tf_op jit(solution)/shard_map/ppermute | solution.py:20
  11.0 3.9 %collective-permute-start.1 = (f32[4,128,256]{2,1,0:T(8,128)S(1)}, f32[4,128,256]{2,1,0:T(8,128)S(1)}, u32[]{:S(2)}, u32[]{:S(2)}) collective-permute-start(f32[4,128,256]{2,1,0:T(8,128)S(1)} %get-tuple-element.7), channel_id=1, source_target_pairs={{1,0},{2,1},{3,2},{4,3},{5,4},{6,5},{7,6},{8,7},{9,8},{10,9},{11,1... | collective-permute-start | bytes 1572872 | tf_op jit(solution)/shard_map/ppermute | solution.py:20
  15.0 0.1 pad_slice_fusion
  15.0 9.5 %collective-permute-done = f32[4,128,256]{2,1,0:T(8,128)S(1)} collective-permute-done((f32[4,128,256]{2,1,0:T(8,128)S(1)}, f32[4,128,256]{2,1,0:T(8,128)S(1)}, u32[]{:S(2)}, u32[]{:S(2)}) %collective-permute-start) | collective-permute-done | bytes 524320 | tf_op jit(solution)/shard_map/ppermute | solution.py:20
  24.5 2.2 %collective-permute-done.1 = f32[4,128,256]{2,1,0:T(8,128)S(1)} collective-permute-done((f32[4,128,256]{2,1,0:T(8,128)S(1)}, f32[4,128,256]{2,1,0:T(8,128)S(1)}, u32[]{:S(2)}, u32[]{:S(2)}) %collective-permute-start.1) | collective-permute-done | bytes 524320 | tf_op jit(solution)/shard_map/ppermute | solution.py:20
  26.7 1.1 %fusion = f32[4,128,256]{2,1,0:T(8,128)S(1)} fusion(f32[4,128,256]{2,1,0:T(8,128)S(1)} %collective-permute-done.1, f32[4,128,256]{2,1,0:T(8,128)S(1)} %collective-permute-done, f32[12,128,256]{2,1,0:T(8,128)} %shard_map.68), kind=kLoop, calls=%fused_computation.1 | loop fusion | flops 262144 | bytes 2097152 | tf_op jit(solution)/shard_map/add | solution.py:207
  27.8 0.0 copy-done
  27.8 0.0 copy-done.1
  27.8 0.1 fusion.1
  28.0 1.0 fusion.14
  29.0 0.1 copy.14
  29.2 0.1 broadcast_select_fusion
  29.3 0.7 collective-permute-start.2
  29.9 0.9 collective-permute-done.2
  30.9 0.1 select_add_fusion
  30.9 1.4 %collective-permute-start.3 = (f32[72,256]{1,0:T(8,128)S(1)}, f32[72,256]{1,0:T(8,128)S(1)}, u32[]{:S(2)}, u32[]{:S(2)}) collective-permute-start(f32[72,256]{1,0:T(8,128)S(1)} %select_add_fusion), channel_id=1, source_target_pairs={{0,1},{1,0},{2,3},{3,2},{4,5},{5,4},{6,7},{7,6},{8,9},{9,8},{10,11... | collective-permute-start | bytes 221192 | tf_op jit(solution)/shard_map/ppermute | solution.py:38
  32.3 4.1 %collective-permute-start.4 = (f32[72,256]{1,0:T(8,128)S(1)}, f32[72,256]{1,0:T(8,128)S(1)}, u32[]{:S(2)}, u32[]{:S(2)}) collective-permute-start(f32[72,256]{1,0:T(8,128)S(1)} %select_add_fusion), channel_id=1, source_target_pairs={{0,2},{1,3},{2,0},{3,1},{4,6},{5,7},{6,4},{7,5},{8,10},{9,11},{10,... | collective-permute-start | bytes 221192 | tf_op jit(solution)/shard_map/ppermute | solution.py:38
  36.4 0.0 collective-permute-start.5
  36.4 0.0 collective-permute-done.3
  36.4 3.8 %collective-permute-done.4 = f32[72,256]{1,0:T(8,128)S(1)} collective-permute-done((f32[72,256]{1,0:T(8,128)S(1)}, f32[72,256]{1,0:T(8,128)S(1)}, u32[]{:S(2)}, u32[]{:S(2)}) %collective-permute-start.4) | collective-permute-done | bytes 73760 | tf_op jit(solution)/shard_map/ppermute | solution.py:38
  40.2 1.5 %collective-permute-done.5 = f32[72,256]{1,0:T(8,128)S(1)} collective-permute-done((f32[72,256]{1,0:T(8,128)S(1)}, f32[72,256]{1,0:T(8,128)S(1)}, u32[]{:S(2)}, u32[]{:S(2)}) %collective-permute-start.5) | collective-permute-done | bytes 73760 | tf_op jit(solution)/shard_map/ppermute | solution.py:38
  41.7 1.7 %collective-permute-start.6 = (f32[72,256]{1,0:T(8,128)S(1)}, f32[72,256]{1,0:T(8,128)S(1)}, u32[]{:S(2)}, u32[]{:S(2)}) collective-permute-start(f32[72,256]{1,0:T(8,128)S(1)} %add_add_fusion.2), channel_id=1, source_target_pairs={{0,8},{1,9},{2,10},{3,11},{4,12},{5,13},{6,14},{7,15},{8,0},{9,1},... | collective-permute-start | bytes 221192 | tf_op jit(solution)/shard_map/ppermute | solution.py:38
  43.5 1.8 %collective-permute-start.7 = (f32[72,256]{1,0:T(8,128)S(1)}, f32[72,256]{1,0:T(8,128)S(1)}, u32[]{:S(2)}, u32[]{:S(2)}) collective-permute-start(f32[72,256]{1,0:T(8,128)S(1)} %add_add_fusion.2), channel_id=1, source_target_pairs={{0,16},{1,17},{2,18},{3,19},{4,20},{5,21},{6,22},{7,23},{8,24},{9,... | collective-permute-start | bytes 221192 | tf_op jit(solution)/shard_map/ppermute | solution.py:38
  45.2 0.7 collective-permute-start.8
  46.0 0.0 collective-permute-done.6
  46.0 3.1 %collective-permute-done.7 = f32[72,256]{1,0:T(8,128)S(1)} collective-permute-done((f32[72,256]{1,0:T(8,128)S(1)}, f32[72,256]{1,0:T(8,128)S(1)}, u32[]{:S(2)}, u32[]{:S(2)}) %collective-permute-start.7) | collective-permute-done | bytes 73760 | tf_op jit(solution)/shard_map/ppermute | solution.py:38
  49.0 1.5 %collective-permute-done.8 = f32[72,256]{1,0:T(8,128)S(1)} collective-permute-done((f32[72,256]{1,0:T(8,128)S(1)}, f32[72,256]{1,0:T(8,128)S(1)}, u32[]{:S(2)}, u32[]{:S(2)}) %collective-permute-start.8) | collective-permute-done | bytes 73760 | tf_op jit(solution)/shard_map/ppermute | solution.py:38
  50.5 2.8 %collective-permute-start.10 = (f32[72,256]{1,0:T(8,128)S(1)}, f32[72,256]{1,0:T(8,128)S(1)}, u32[]{:S(2)}, u32[]{:S(2)}) collective-permute-start(f32[72,256]{1,0:T(8,128)S(1)} %add_add_fusion.1), channel_id=1, source_target_pairs={{0,64},{1,65},{2,66},{3,67},{4,68},{5,69},{6,70},{7,71},{8,72},{9,... | collective-permute-start | bytes 221192 | tf_op jit(solution)/shard_map/ppermute | solution.py:38
  53.3 0.9 collective-permute-start.11
  54.2 0.0 collective-permute-start.9
  54.2 1.1 %collective-permute-done.10 = f32[72,256]{1,0:T(8,128)S(1)} collective-permute-done((f32[72,256]{1,0:T(8,128)S(1)}, f32[72,256]{1,0:T(8,128)S(1)}, u32[]{:S(2)}, u32[]{:S(2)}) %collective-permute-start.10) | collective-permute-done | bytes 73760 | tf_op jit(solution)/shard_map/ppermute | solution.py:38
  55.3 2.9 %collective-permute-done.11 = f32[72,256]{1,0:T(8,128)S(1)} collective-permute-done((f32[72,256]{1,0:T(8,128)S(1)}, f32[72,256]{1,0:T(8,128)S(1)}, u32[]{:S(2)}, u32[]{:S(2)}) %collective-permute-start.11) | collective-permute-done | bytes 73760 | tf_op jit(solution)/shard_map/ppermute | solution.py:38
  58.2 0.0 collective-permute-done.9
  58.2 2.7 %collective-permute-start.12 = (f32[72,256]{1,0:T(8,128)S(1)}, f32[72,256]{1,0:T(8,128)S(1)}, u32[]{:S(2)}, u32[]{:S(2)}) collective-permute-start(f32[72,256]{1,0:T(8,128)S(1)} %add_add_fusion), channel_id=1, source_target_pairs={{0,4},{1,5},{2,6},{3,7},{4,0},{5,1},{6,2},{7,3},{8,12},{9,13},{10,... | collective-permute-start | bytes 221192 | tf_op jit(solution)/shard_map/ppermute | solution.py:38
  61.0 0.9 collective-permute-done.12
  61.9 0.1 copy.19
  62.0 0.1 bitcast_select_fusion.1
  62.1 0.1 copy.18
  62.2 0.7 maximum_maximum_fusion.gram_ref
  62.9 37.3 %shard_map.69 = (f32[256,256]{1,0:T(8,128)}, f32[256,256]{1,0:T(8,128)}) custom-call(f32[256,256]{1,0:T(8,128)} %maximum_maximum_fusion.gram_ref), custom_call_target="tpu_custom_call" | custom-call | tf_op jit(solution)/shard_map/pallas_call | solution.py:153
  100.2 2.4 %fusion.3 = f32[512,256]{1,0:T(8,128)} fusion(f32[512,256]{1,0:T(8,128)S(1)} %fusion.1, f32[256,256]{1,0:T(8,128)} %get-tuple-element.4), kind=kOutput, calls=%fused_computation.7 | convolution fusion | flops 402718720 | bytes 1310720 | tf_op jit(solution)/shard_map/dot_general | solution.py:217
  102.6 1.7 %broadcast_multiply_fusion = f32[256,256]{1,0:T(8,128)} fusion(f32[256,256]{1,0:T(8,128)} %get-tuple-element.5), kind=kLoop, calls=%fused_computation.10 | loop fusion | flops 65536 | bytes 524288 | tf_op jit(solution)/shard_map/div | solution.py:218
  (9 shorter events, 0.2 us)
Async XLA Ops:
  6.8 21.0 %copy-start = (f32[512,256]{1,0:T(8,128)S(1)}, f32[512,256]{1,0:T(8,128)}, u32[]{:S(2)}) copy-start(f32[512,256]{1,0:T(8,128)} %param.8) | copy-start | bytes 1572868
  6.8 21.0 %copy-start.1 = (f32[512]{0:T(512)S(1)}, f32[512]{0:T(512)}, u32[]{:S(2)}) copy-start(f32[512]{0:T(512)} %param.9) | copy-start | bytes 6148
  6.8 17.6 %collective-permute-start = (f32[4,128,256]{2,1,0:T(8,128)S(1)}, f32[4,128,256]{2,1,0:T(8,128)S(1)}, u32[]{:S(2)}, u32[]{:S(2)}) collective-permute-start(f32[4,128,256]{2,1,0:T(8,128)S(1)} %get-tuple-element.6), channel_id=1, source_target_pairs={{0,1},{1,2},{2,3},{3,4},{4,5},{5,6},{6,7},{7,8},{8,9},{9,10},{10,1... | collective-permute-start | bytes 1572872 | tf_op jit(solution)/shard_map/ppermute | solution.py:20
  11.0 15.6 %collective-permute-start.1 = (f32[4,128,256]{2,1,0:T(8,128)S(1)}, f32[4,128,256]{2,1,0:T(8,128)S(1)}, u32[]{:S(2)}, u32[]{:S(2)}) collective-permute-start(f32[4,128,256]{2,1,0:T(8,128)S(1)} %get-tuple-element.7), channel_id=1, source_target_pairs={{1,0},{2,1},{3,2},{4,3},{5,4},{6,5},{7,6},{8,7},{9,8},{10,9},{11,1... | collective-permute-start | bytes 1572872 | tf_op jit(solution)/shard_map/ppermute | solution.py:20
  29.3 1.6 %collective-permute-start.2 = (f32[72,256]{1,0:T(8,128)S(1)}, f32[72,256]{1,0:T(8,128)S(1)}, u32[]{:S(2)}, u32[]{:S(2)}) collective-permute-start(f32[72,256]{1,0:T(8,128)S(1)} %broadcast_select_fusion), channel_id=1, source_target_pairs={{0,4},{1,5},{2,6},{3,7},{4,0},{5,1},{6,2},{7,3},{8,12},{9,13},{10,... | collective-permute-start | bytes 221192 | tf_op jit(solution)/shard_map/ppermute | solution.py:38
  30.9 5.5 %collective-permute-start.3 = (f32[72,256]{1,0:T(8,128)S(1)}, f32[72,256]{1,0:T(8,128)S(1)}, u32[]{:S(2)}, u32[]{:S(2)}) collective-permute-start(f32[72,256]{1,0:T(8,128)S(1)} %select_add_fusion), channel_id=1, source_target_pairs={{0,1},{1,0},{2,3},{3,2},{4,5},{5,4},{6,7},{7,6},{8,9},{9,8},{10,11... | collective-permute-start | bytes 221192 | tf_op jit(solution)/shard_map/ppermute | solution.py:38
  32.3 7.9 %collective-permute-start.4 = (f32[72,256]{1,0:T(8,128)S(1)}, f32[72,256]{1,0:T(8,128)S(1)}, u32[]{:S(2)}, u32[]{:S(2)}) collective-permute-start(f32[72,256]{1,0:T(8,128)S(1)} %select_add_fusion), channel_id=1, source_target_pairs={{0,2},{1,3},{2,0},{3,1},{4,6},{5,7},{6,4},{7,5},{8,10},{9,11},{10,... | collective-permute-start | bytes 221192 | tf_op jit(solution)/shard_map/ppermute | solution.py:38
  36.4 5.3 %collective-permute-start.5 = (f32[72,256]{1,0:T(8,128)S(1)}, f32[72,256]{1,0:T(8,128)S(1)}, u32[]{:S(2)}, u32[]{:S(2)}) collective-permute-start(f32[72,256]{1,0:T(8,128)S(1)} %select_add_fusion), channel_id=1, source_target_pairs={{0,3},{1,2},{2,1},{3,0},{4,7},{5,6},{6,5},{7,4},{8,11},{9,10},{10,... | collective-permute-start | bytes 221192 | tf_op jit(solution)/shard_map/ppermute | solution.py:38
  41.7 4.2 %collective-permute-start.6 = (f32[72,256]{1,0:T(8,128)S(1)}, f32[72,256]{1,0:T(8,128)S(1)}, u32[]{:S(2)}, u32[]{:S(2)}) collective-permute-start(f32[72,256]{1,0:T(8,128)S(1)} %add_add_fusion.2), channel_id=1, source_target_pairs={{0,8},{1,9},{2,10},{3,11},{4,12},{5,13},{6,14},{7,15},{8,0},{9,1},... | collective-permute-start | bytes 221192 | tf_op jit(solution)/shard_map/ppermute | solution.py:38
  43.5 5.6 %collective-permute-start.7 = (f32[72,256]{1,0:T(8,128)S(1)}, f32[72,256]{1,0:T(8,128)S(1)}, u32[]{:S(2)}, u32[]{:S(2)}) collective-permute-start(f32[72,256]{1,0:T(8,128)S(1)} %add_add_fusion.2), channel_id=1, source_target_pairs={{0,16},{1,17},{2,18},{3,19},{4,20},{5,21},{6,22},{7,23},{8,24},{9,... | collective-permute-start | bytes 221192 | tf_op jit(solution)/shard_map/ppermute | solution.py:38
  45.2 5.3 %collective-permute-start.8 = (f32[72,256]{1,0:T(8,128)S(1)}, f32[72,256]{1,0:T(8,128)S(1)}, u32[]{:S(2)}, u32[]{:S(2)}) collective-permute-start(f32[72,256]{1,0:T(8,128)S(1)} %add_add_fusion.2), channel_id=1, source_target_pairs={{0,24},{1,25},{2,26},{3,27},{4,28},{5,29},{6,30},{7,31},{8,16},{9,... | collective-permute-start | bytes 221192 | tf_op jit(solution)/shard_map/ppermute | solution.py:38
  50.5 4.8 %collective-permute-start.10 = (f32[72,256]{1,0:T(8,128)S(1)}, f32[72,256]{1,0:T(8,128)S(1)}, u32[]{:S(2)}, u32[]{:S(2)}) collective-permute-start(f32[72,256]{1,0:T(8,128)S(1)} %add_add_fusion.1), channel_id=1, source_target_pairs={{0,64},{1,65},{2,66},{3,67},{4,68},{5,69},{6,70},{7,71},{8,72},{9,... | collective-permute-start | bytes 221192 | tf_op jit(solution)/shard_map/ppermute | solution.py:38
  53.3 4.9 %collective-permute-start.11 = (f32[72,256]{1,0:T(8,128)S(1)}, f32[72,256]{1,0:T(8,128)S(1)}, u32[]{:S(2)}, u32[]{:S(2)}) collective-permute-start(f32[72,256]{1,0:T(8,128)S(1)} %add_add_fusion.1), channel_id=1, source_target_pairs={{0,96},{1,97},{2,98},{3,99},{4,100},{5,101},{6,102},{7,103},{8,104... | collective-permute-start | bytes 221192 | tf_op jit(solution)/shard_map/ppermute | solution.py:38
  54.2 4.0 %collective-permute-start.9 = (f32[72,256]{1,0:T(8,128)S(1)}, f32[72,256]{1,0:T(8,128)S(1)}, u32[]{:S(2)}, u32[]{:S(2)}) collective-permute-start(f32[72,256]{1,0:T(8,128)S(1)} %add_add_fusion.1), channel_id=1, source_target_pairs={{0,32},{1,33},{2,34},{3,35},{4,36},{5,37},{6,38},{7,39},{8,40},{9,... | collective-permute-start | bytes 221192 | tf_op jit(solution)/shard_map/ppermute | solution.py:38
  58.2 3.6 %collective-permute-start.12 = (f32[72,256]{1,0:T(8,128)S(1)}, f32[72,256]{1,0:T(8,128)S(1)}, u32[]{:S(2)}, u32[]{:S(2)}) collective-permute-start(f32[72,256]{1,0:T(8,128)S(1)} %add_add_fusion), channel_id=1, source_target_pairs={{0,4},{1,5},{2,6},{3,7},{4,0},{5,1},{6,2},{7,3},{8,12},{9,13},{10,... | collective-permute-start | bytes 221192 | tf_op jit(solution)/shard_map/ppermute | solution.py:38

commit v6 on v5

--- a/solution.py
+++ b/solution.py
@@ -11,7 +11,7 @@
 exact_mode = lax.Precision.HIGHEST
 DEVICE_AXES = ("lat", "sub")
 CORE_BIT = 2
-PANEL = 8
+PANEL = 64
 
 
 def shifted(value, axis, steps):
@@ -100,15 +100,15 @@
     rows = lax.broadcasted_iota(jnp.int32, (size, size), 0)
     cols = lax.broadcasted_iota(jnp.int32, (size, size), 1)
     inverse_ref[...] = jnp.where(rows == cols, 1.0, 0.0).astype(jnp.float32)
-    lane = lax.broadcasted_iota(jnp.int32, (1, size), 1)
+    upper_ref[...] = jnp.zeros((size, size), jnp.float32)
     sub = lax.broadcasted_iota(jnp.int32, (PANEL, 1), 0)
     row_ids = lax.broadcasted_iota(jnp.int32, (size, 1), 0)
-
     def panel(index, carry, row0, col0, col1):
+        lane = lax.broadcasted_iota(jnp.int32, (1, size - col0), 1) + col0
         first = pl.multiple_of(index * PANEL, PANEL)
-        slab = work_ref[pl.ds(first, PANEL), :]
-        inverse_slab = inverse_ref[pl.ds(first, PANEL), :]
-        upper_slab = jnp.zeros((PANEL, size), jnp.float32)
+        slab = work_ref[pl.ds(first, PANEL), col0:]
+        inverse_slab = inverse_ref[pl.ds(first, PANEL), :col1]
+        upper_slab = jnp.zeros((PANEL, size - col0), jnp.float32)
         for step in range(PANEL):
             column = first + step
             picked = jnp.sum(jnp.where(lane == column, slab, 0.0), axis=1, keepdims=True)
@@ -119,34 +119,22 @@
             slab = slab - coef * upper_row
             inverse_slab = jnp.where(sub == step, inverse_row, inverse_slab - coef * inverse_row)
             upper_slab = jnp.where(sub == step, upper_row, upper_slab)
-        upper_ref[pl.ds(first, PANEL), :] = upper_slab
-        inverse_ref[pl.ds(first, PANEL), :] = inverse_slab
-        lower_cols = jnp.transpose(upper_slab)[row0:]
+        upper_ref[pl.ds(first, PANEL), col0:] = upper_slab
+        inverse_ref[pl.ds(first, PANEL), :col1] = inverse_slab
+        lower_cols = jnp.transpose(upper_slab)[row0 - col0:]
         lower_cols = jnp.where(row_ids[row0:] >= first + PANEL, lower_cols, 0.0)
         work_ref[row0:, col0:] = work_ref[row0:, col0:] - jnp.dot(
-            lower_cols, upper_slab[:, col0:], precision=exact_mode,
-            preferred_element_type=jnp.float32,
-        )
+            lower_cols, upper_slab, precision=exact_mode, preferred_element_type=jnp.float32)
         inverse_ref[row0:, :col1] = inverse_ref[row0:, :col1] - jnp.dot(
-            lower_cols, inverse_slab[:, :col1], precision=exact_mode,
-            preferred_element_type=jnp.float32,
-        )
+            lower_cols, inverse_slab, precision=exact_mode, preferred_element_type=jnp.float32)
         return carry
-
     quarter = size // 4
     for part in range(4):
         row0 = quarter * part
         col0 = (size // 2) * (part // 2)
         col1 = (size // 2) * (part // 2 + 1)
-        lax.fori_loop(
-            row0 // PANEL,
-            (row0 + quarter) // PANEL,
-            lambda index, carry, row0=row0, col0=col0, col1=col1: panel(
-                index, carry, row0, col0, col1
-            ),
-            0,
-        )
-
+        lax.fori_loop(row0 // PANEL, (row0 + quarter) // PANEL,
+            lambda index, carry, row0=row0, col0=col0, col1=col1: panel(index, carry, row0, col0, col1), 0)
 
 def cholesky_with_inverse(gram):
     size = gram.shape[0]

time: 105 us -> 93.9 us (0.89)
  Pallas kernels: 40.8 us -> 29.9 us
    pallas_call x1, Pallas kernels: 37.3 us -> 26.4 us  [cholesky_with_inverse(): pl.pallas_call(cholesky_kernel, out_shape=(jax.ShapeDtypeStruct((size, si...]
where the time goes in v6:
time: 93.9 us; the launch traced here: 93.5 us
  Pallas kernels  29.9 us (32%)
  waiting for transfers between devices  27.3 us (29%)
  starting transfers between devices  25 us (27%)
  other arithmetic  4.75 us (5%)
  matrix products  3.38 us (4%)
  local copies, waits for them, and re-layouts  2.39 us (3%)
    pallas_call x1, Pallas kernels, cholesky_with_inverse(): pl.pallas_call(cholesky_kernel, out_shape=(jax.ShapeDtypeStruct((size, si...  26.4 us
    ppermute x11, starting transfers between devices, exchange(): lax.ppermute(value, DEVICE_AXES, [(i, i ^ mask) for i in range(count)])  16.9 us
    ppermute x11, waiting for transfers between devices, exchange(): lax.ppermute(value, DEVICE_AXES, [(i, i ^ mask) for i in range(count)])  15.7 us
    ppermute x2, waiting for transfers between devices, shifted(): lax.ppermute(value, axis, [(source, source + steps) for source in range(i...  11.6 us
    ppermute x2, starting transfers between devices, shifted(): lax.ppermute(value, axis, [(source, source + steps) for source in range(i...  8.07 us
    pallas_call x1, Pallas kernels, aggregate(): pl.pallas_call(aggregate_kernel, out_shape=jax.ShapeDtypeStruct((window_c...  3.5 us
    dot_general x1, matrix products, body(): scores = jnp.dot(anomaly, lower_inverse.T * root, precision=exact_mode)  2.36 us
  transfers between devices with their start and end apart: 13, of which 10 were waited for; matrix products, arithmetic and copies ran while one was open for 0% of the time, Pallas kernels for 0%

profile of v6, /device:TPU:1, one launch (start us, length us, event | category | flops | bytes accessed | tf_op | source)
XLA Modules:
  0.0 93.5 jit_solution(5253775324307971380)
XLA Ops:
  0.6 0.7 subtract_clamp_fusion
  1.3 0.1 copy.13
  1.4 0.6 min.12.slot_ref
  2.0 3.5 %shard_map.68 = f32[12,128,256]{2,1,0:T(8,128)} custom-call(s32[32]{0:T(128)} %min.12.slot_ref, bf16[16,2,128,128]{3,2,1,0:T(8,128)(2,1)} %weight_ref.1, bf16[16,128,256]{2,1,0:T(8,128)(2,1)} %bitcast.22), custom_call_target="tpu_custom_call" | custom-call | tf_op jit(solution)/shard_map/pallas_call | solution.py:170
  5.5 1.3 %fusion.13 = (f32[4,128,256]{2,1,0:T(8,128)S(1)}, f32[4,128,256]{2,1,0:T(8,128)S(1)}) fusion(f32[12,128,256]{2,1,0:T(8,128)} %shard_map.68), kind=kLoop, calls=%fused_computation.40 | loop fusion | bytes 2097152 | tf_op jit(solution)/shard_map/slice | solution.py:193
  6.8 0.0 copy-start
  6.8 0.0 copy-start.1
  6.8 4.2 %collective-permute-start = (f32[4,128,256]{2,1,0:T(8,128)S(1)}, f32[4,128,256]{2,1,0:T(8,128)S(1)}, u32[]{:S(2)}, u32[]{:S(2)}) collective-permute-start(f32[4,128,256]{2,1,0:T(8,128)S(1)} %get-tuple-element.6), channel_id=1, source_target_pairs={{0,1},{1,2},{2,3},{3,4},{4,5},{5,6},{6,7},{7,8},{8,9},{9,10},{10,1... | collective-permute-start | bytes 1572872 | tf_op jit(solution)/shard_map/ppermute | solution.py:20
  11.0 3.9 %collective-permute-start.1 = (f32[4,128,256]{2,1,0:T(8,128)S(1)}, f32[4,128,256]{2,1,0:T(8,128)S(1)}, u32[]{:S(2)}, u32[]{:S(2)}) collective-permute-start(f32[4,128,256]{2,1,0:T(8,128)S(1)} %get-tuple-element.7), channel_id=1, source_target_pairs={{1,0},{2,1},{3,2},{4,3},{5,4},{6,5},{7,6},{8,7},{9,8},{10,9},{11,1... | collective-permute-start | bytes 1572872 | tf_op jit(solution)/shard_map/ppermute | solution.py:20
  14.9 0.1 pad_slice_fusion
  15.0 9.4 %collective-permute-done = f32[4,128,256]{2,1,0:T(8,128)S(1)} collective-permute-done((f32[4,128,256]{2,1,0:T(8,128)S(1)}, f32[4,128,256]{2,1,0:T(8,128)S(1)}, u32[]{:S(2)}, u32[]{:S(2)}) %collective-permute-start) | collective-permute-done | bytes 524320 | tf_op jit(solution)/shard_map/ppermute | solution.py:20
  24.5 2.2 %collective-permute-done.1 = f32[4,128,256]{2,1,0:T(8,128)S(1)} collective-permute-done((f32[4,128,256]{2,1,0:T(8,128)S(1)}, f32[4,128,256]{2,1,0:T(8,128)S(1)}, u32[]{:S(2)}, u32[]{:S(2)}) %collective-permute-start.1) | collective-permute-done | bytes 524320 | tf_op jit(solution)/shard_map/ppermute | solution.py:20
  26.7 1.1 %fusion = f32[4,128,256]{2,1,0:T(8,128)S(1)} fusion(f32[4,128,256]{2,1,0:T(8,128)S(1)} %collective-permute-done.1, f32[4,128,256]{2,1,0:T(8,128)S(1)} %collective-permute-done, f32[12,128,256]{2,1,0:T(8,128)} %shard_map.68), kind=kLoop, calls=%fused_computation.1 | loop fusion | flops 262144 | bytes 2097152 | tf_op jit(solution)/shard_map/add | solution.py:195
  27.8 0.0 copy-done
  27.8 0.0 copy-done.1
  27.8 0.1 fusion.1
  28.0 1.0 %fusion.14 = f32[256,256]{1,0:T(8,128)S(1)} fusion(f32[512,256]{1,0:T(8,128)S(1)} %fusion.1), kind=kOutput, calls=%fused_computation.41 | convolution fusion | flops 402653184 | bytes 786432 | tf_op jit(solution)/shard_map/dot_general | solution.py:198
  29.0 0.1 copy.14
  29.2 0.1 broadcast_select_fusion
  29.3 0.7 collective-permute-start.2
  29.9 0.9 collective-permute-done.2
  30.9 0.1 select_add_fusion
  30.9 1.4 %collective-permute-start.3 = (f32[72,256]{1,0:T(8,128)S(1)}, f32[72,256]{1,0:T(8,128)S(1)}, u32[]{:S(2)}, u32[]{:S(2)}) collective-permute-start(f32[72,256]{1,0:T(8,128)S(1)} %select_add_fusion), channel_id=1, source_target_pairs={{0,1},{1,0},{2,3},{3,2},{4,5},{5,4},{6,7},{7,6},{8,9},{9,8},{10,11... | collective-permute-start | bytes 221192 | tf_op jit(solution)/shard_map/ppermute | solution.py:38
  32.3 4.1 %collective-permute-start.4 = (f32[72,256]{1,0:T(8,128)S(1)}, f32[72,256]{1,0:T(8,128)S(1)}, u32[]{:S(2)}, u32[]{:S(2)}) collective-permute-start(f32[72,256]{1,0:T(8,128)S(1)} %select_add_fusion), channel_id=1, source_target_pairs={{0,2},{1,3},{2,0},{3,1},{4,6},{5,7},{6,4},{7,5},{8,10},{9,11},{10,... | collective-permute-start | bytes 221192 | tf_op jit(solution)/shard_map/ppermute | solution.py:38
  36.4 0.0 collective-permute-start.5
  36.4 0.0 collective-permute-done.3
  36.5 3.8 %collective-permute-done.4 = f32[72,256]{1,0:T(8,128)S(1)} collective-permute-done((f32[72,256]{1,0:T(8,128)S(1)}, f32[72,256]{1,0:T(8,128)S(1)}, u32[]{:S(2)}, u32[]{:S(2)}) %collective-permute-start.4) | collective-permute-done | bytes 73760 | tf_op jit(solution)/shard_map/ppermute | solution.py:38
  40.2 1.5 %collective-permute-done.5 = f32[72,256]{1,0:T(8,128)S(1)} collective-permute-done((f32[72,256]{1,0:T(8,128)S(1)}, f32[72,256]{1,0:T(8,128)S(1)}, u32[]{:S(2)}, u32[]{:S(2)}) %collective-permute-start.5) | collective-permute-done | bytes 73760 | tf_op jit(solution)/shard_map/ppermute | solution.py:38
  41.8 1.7 %collective-permute-start.6 = (f32[72,256]{1,0:T(8,128)S(1)}, f32[72,256]{1,0:T(8,128)S(1)}, u32[]{:S(2)}, u32[]{:S(2)}) collective-permute-start(f32[72,256]{1,0:T(8,128)S(1)} %add_add_fusion.2), channel_id=1, source_target_pairs={{0,8},{1,9},{2,10},{3,11},{4,12},{5,13},{6,14},{7,15},{8,0},{9,1},... | collective-permute-start | bytes 221192 | tf_op jit(solution)/shard_map/ppermute | solution.py:38
  43.5 1.8 %collective-permute-start.7 = (f32[72,256]{1,0:T(8,128)S(1)}, f32[72,256]{1,0:T(8,128)S(1)}, u32[]{:S(2)}, u32[]{:S(2)}) collective-permute-start(f32[72,256]{1,0:T(8,128)S(1)} %add_add_fusion.2), channel_id=1, source_target_pairs={{0,16},{1,17},{2,18},{3,19},{4,20},{5,21},{6,22},{7,23},{8,24},{9,... | collective-permute-start | bytes 221192 | tf_op jit(solution)/shard_map/ppermute | solution.py:38
  45.2 0.7 collective-permute-start.8
  45.9 0.0 collective-permute-done.6
  46.0 3.1 %collective-permute-done.7 = f32[72,256]{1,0:T(8,128)S(1)} collective-permute-done((f32[72,256]{1,0:T(8,128)S(1)}, f32[72,256]{1,0:T(8,128)S(1)}, u32[]{:S(2)}, u32[]{:S(2)}) %collective-permute-start.7) | collective-permute-done | bytes 73760 | tf_op jit(solution)/shard_map/ppermute | solution.py:38
  49.0 1.4 %collective-permute-done.8 = f32[72,256]{1,0:T(8,128)S(1)} collective-permute-done((f32[72,256]{1,0:T(8,128)S(1)}, f32[72,256]{1,0:T(8,128)S(1)}, u32[]{:S(2)}, u32[]{:S(2)}) %collective-permute-start.8) | collective-permute-done | bytes 73760 | tf_op jit(solution)/shard_map/ppermute | solution.py:38
  50.5 2.8 %collective-permute-start.10 = (f32[72,256]{1,0:T(8,128)S(1)}, f32[72,256]{1,0:T(8,128)S(1)}, u32[]{:S(2)}, u32[]{:S(2)}) collective-permute-start(f32[72,256]{1,0:T(8,128)S(1)} %add_add_fusion.1), channel_id=1, source_target_pairs={{0,64},{1,65},{2,66},{3,67},{4,68},{5,69},{6,70},{7,71},{8,72},{9,... | collective-permute-start | bytes 221192 | tf_op jit(solution)/shard_map/ppermute | solution.py:38
  53.3 0.9 collective-permute-start.11
  54.2 0.0 collective-permute-start.9
  54.2 1.1 %collective-permute-done.10 = f32[72,256]{1,0:T(8,128)S(1)} collective-permute-done((f32[72,256]{1,0:T(8,128)S(1)}, f32[72,256]{1,0:T(8,128)S(1)}, u32[]{:S(2)}, u32[]{:S(2)}) %collective-permute-start.10) | collective-permute-done | bytes 73760 | tf_op jit(solution)/shard_map/ppermute | solution.py:38
  55.3 2.9 %collective-permute-done.11 = f32[72,256]{1,0:T(8,128)S(1)} collective-permute-done((f32[72,256]{1,0:T(8,128)S(1)}, f32[72,256]{1,0:T(8,128)S(1)}, u32[]{:S(2)}, u32[]{:S(2)}) %collective-permute-start.11) | collective-permute-done | bytes 73760 | tf_op jit(solution)/shard_map/ppermute | solution.py:38
  58.2 0.0 collective-permute-done.9
  58.2 2.9 %collective-permute-start.12 = (f32[72,256]{1,0:T(8,128)S(1)}, f32[72,256]{1,0:T(8,128)S(1)}, u32[]{:S(2)}, u32[]{:S(2)}) collective-permute-start(f32[72,256]{1,0:T(8,128)S(1)} %add_add_fusion), channel_id=1, source_target_pairs={{0,4},{1,5},{2,6},{3,7},{4,0},{5,1},{6,2},{7,3},{8,12},{9,13},{10,... | collective-permute-start | bytes 221192 | tf_op jit(solution)/shard_map/ppermute | solution.py:38
  61.1 0.9 collective-permute-done.12
  62.1 0.1 copy.19
  62.2 0.1 bitcast_select_fusion.1
  62.3 0.1 copy.18
  62.4 0.7 maximum_maximum_fusion.gram_ref
  63.1 26.4 %shard_map.69 = (f32[256,256]{1,0:T(8,128)}, f32[256,256]{1,0:T(8,128)}) custom-call(f32[256,256]{1,0:T(8,128)} %maximum_maximum_fusion.gram_ref), custom_call_target="tpu_custom_call" | custom-call | tf_op jit(solution)/shard_map/pallas_call | solution.py:141
  89.5 2.4 %fusion.3 = f32[512,256]{1,0:T(8,128)} fusion(f32[512,256]{1,0:T(8,128)S(1)} %fusion.1, f32[256,256]{1,0:T(8,128)} %get-tuple-element.4), kind=kOutput, calls=%fused_computation.7 | convolution fusion | flops 402718720 | bytes 1310720 | tf_op jit(solution)/shard_map/dot_general | solution.py:205
  91.9 1.7 %broadcast_multiply_fusion = f32[256,256]{1,0:T(8,128)} fusion(f32[256,256]{1,0:T(8,128)} %get-tuple-element.5), kind=kLoop, calls=%fused_computation.10 | loop fusion | flops 65536 | bytes 524288 | tf_op jit(solution)/shard_map/div | solution.py:206
  (9 shorter events, 0.2 us)
Async XLA Ops:
  6.8 21.0 %copy-start = (f32[512,256]{1,0:T(8,128)S(1)}, f32[512,256]{1,0:T(8,128)}, u32[]{:S(2)}) copy-start(f32[512,256]{1,0:T(8,128)} %param.8) | copy-start | bytes 1572868
  6.8 21.0 %copy-start.1 = (f32[512]{0:T(512)S(1)}, f32[512]{0:T(512)}, u32[]{:S(2)}) copy-start(f32[512]{0:T(512)} %param.9) | copy-start | bytes 6148
  6.8 17.6 %collective-permute-start = (f32[4,128,256]{2,1,0:T(8,128)S(1)}, f32[4,128,256]{2,1,0:T(8,128)S(1)}, u32[]{:S(2)}, u32[]{:S(2)}) collective-permute-start(f32[4,128,256]{2,1,0:T(8,128)S(1)} %get-tuple-element.6), channel_id=1, source_target_pairs={{0,1},{1,2},{2,3},{3,4},{4,5},{5,6},{6,7},{7,8},{8,9},{9,10},{10,1... | collective-permute-start | bytes 1572872 | tf_op jit(solution)/shard_map/ppermute | solution.py:20
  11.0 15.6 %collective-permute-start.1 = (f32[4,128,256]{2,1,0:T(8,128)S(1)}, f32[4,128,256]{2,1,0:T(8,128)S(1)}, u32[]{:S(2)}, u32[]{:S(2)}) collective-permute-start(f32[4,128,256]{2,1,0:T(8,128)S(1)} %get-tuple-element.7), channel_id=1, source_target_pairs={{1,0},{2,1},{3,2},{4,3},{5,4},{6,5},{7,6},{8,7},{9,8},{10,9},{11,1... | collective-permute-start | bytes 1572872 | tf_op jit(solution)/shard_map/ppermute | solution.py:20
  29.3 1.6 %collective-permute-start.2 = (f32[72,256]{1,0:T(8,128)S(1)}, f32[72,256]{1,0:T(8,128)S(1)}, u32[]{:S(2)}, u32[]{:S(2)}) collective-permute-start(f32[72,256]{1,0:T(8,128)S(1)} %broadcast_select_fusion), channel_id=1, source_target_pairs={{0,4},{1,5},{2,6},{3,7},{4,0},{5,1},{6,2},{7,3},{8,12},{9,13},{10,... | collective-permute-start | bytes 221192 | tf_op jit(solution)/shard_map/ppermute | solution.py:38
  30.9 5.5 %collective-permute-start.3 = (f32[72,256]{1,0:T(8,128)S(1)}, f32[72,256]{1,0:T(8,128)S(1)}, u32[]{:S(2)}, u32[]{:S(2)}) collective-permute-start(f32[72,256]{1,0:T(8,128)S(1)} %select_add_fusion), channel_id=1, source_target_pairs={{0,1},{1,0},{2,3},{3,2},{4,5},{5,4},{6,7},{7,6},{8,9},{9,8},{10,11... | collective-permute-start | bytes 221192 | tf_op jit(solution)/shard_map/ppermute | solution.py:38
  32.3 7.9 %collective-permute-start.4 = (f32[72,256]{1,0:T(8,128)S(1)}, f32[72,256]{1,0:T(8,128)S(1)}, u32[]{:S(2)}, u32[]{:S(2)}) collective-permute-start(f32[72,256]{1,0:T(8,128)S(1)} %select_add_fusion), channel_id=1, source_target_pairs={{0,2},{1,3},{2,0},{3,1},{4,6},{5,7},{6,4},{7,5},{8,10},{9,11},{10,... | collective-permute-start | bytes 221192 | tf_op jit(solution)/shard_map/ppermute | solution.py:38
  36.4 5.3 %collective-permute-start.5 = (f32[72,256]{1,0:T(8,128)S(1)}, f32[72,256]{1,0:T(8,128)S(1)}, u32[]{:S(2)}, u32[]{:S(2)}) collective-permute-start(f32[72,256]{1,0:T(8,128)S(1)} %select_add_fusion), channel_id=1, source_target_pairs={{0,3},{1,2},{2,1},{3,0},{4,7},{5,6},{6,5},{7,4},{8,11},{9,10},{10,... | collective-permute-start | bytes 221192 | tf_op jit(solution)/shard_map/ppermute | solution.py:38
  41.8 4.2 %collective-permute-start.6 = (f32[72,256]{1,0:T(8,128)S(1)}, f32[72,256]{1,0:T(8,128)S(1)}, u32[]{:S(2)}, u32[]{:S(2)}) collective-permute-start(f32[72,256]{1,0:T(8,128)S(1)} %add_add_fusion.2), channel_id=1, source_target_pairs={{0,8},{1,9},{2,10},{3,11},{4,12},{5,13},{6,14},{7,15},{8,0},{9,1},... | collective-permute-start | bytes 221192 | tf_op jit(solution)/shard_map/ppermute | solution.py:38
  43.5 5.6 %collective-permute-start.7 = (f32[72,256]{1,0:T(8,128)S(1)}, f32[72,256]{1,0:T(8,128)S(1)}, u32[]{:S(2)}, u32[]{:S(2)}) collective-permute-start(f32[72,256]{1,0:T(8,128)S(1)} %add_add_fusion.2), channel_id=1, source_target_pairs={{0,16},{1,17},{2,18},{3,19},{4,20},{5,21},{6,22},{7,23},{8,24},{9,... | collective-permute-start | bytes 221192 | tf_op jit(solution)/shard_map/ppermute | solution.py:38
  45.2 5.3 %collective-permute-start.8 = (f32[72,256]{1,0:T(8,128)S(1)}, f32[72,256]{1,0:T(8,128)S(1)}, u32[]{:S(2)}, u32[]{:S(2)}) collective-permute-start(f32[72,256]{1,0:T(8,128)S(1)} %add_add_fusion.2), channel_id=1, source_target_pairs={{0,24},{1,25},{2,26},{3,27},{4,28},{5,29},{6,30},{7,31},{8,16},{9,... | collective-permute-start | bytes 221192 | tf_op jit(solution)/shard_map/ppermute | solution.py:38
  50.5 4.8 %collective-permute-start.10 = (f32[72,256]{1,0:T(8,128)S(1)}, f32[72,256]{1,0:T(8,128)S(1)}, u32[]{:S(2)}, u32[]{:S(2)}) collective-permute-start(f32[72,256]{1,0:T(8,128)S(1)} %add_add_fusion.1), channel_id=1, source_target_pairs={{0,64},{1,65},{2,66},{3,67},{4,68},{5,69},{6,70},{7,71},{8,72},{9,... | collective-permute-start | bytes 221192 | tf_op jit(solution)/shard_map/ppermute | solution.py:38
  53.3 4.9 %collective-permute-start.11 = (f32[72,256]{1,0:T(8,128)S(1)}, f32[72,256]{1,0:T(8,128)S(1)}, u32[]{:S(2)}, u32[]{:S(2)}) collective-permute-start(f32[72,256]{1,0:T(8,128)S(1)} %add_add_fusion.1), channel_id=1, source_target_pairs={{0,96},{1,97},{2,98},{3,99},{4,100},{5,101},{6,102},{7,103},{8,104... | collective-permute-start | bytes 221192 | tf_op jit(solution)/shard_map/ppermute | solution.py:38
  54.2 4.0 %collective-permute-start.9 = (f32[72,256]{1,0:T(8,128)S(1)}, f32[72,256]{1,0:T(8,128)S(1)}, u32[]{:S(2)}, u32[]{:S(2)}) collective-permute-start(f32[72,256]{1,0:T(8,128)S(1)} %add_add_fusion.1), channel_id=1, source_target_pairs={{0,32},{1,33},{2,34},{3,35},{4,36},{5,37},{6,38},{7,39},{8,40},{9,... | collective-permute-start | bytes 221192 | tf_op jit(solution)/shard_map/ppermute | solution.py:38
  58.2 3.8 %collective-permute-start.12 = (f32[72,256]{1,0:T(8,128)S(1)}, f32[72,256]{1,0:T(8,128)S(1)}, u32[]{:S(2)}, u32[]{:S(2)}) collective-permute-start(f32[72,256]{1,0:T(8,128)S(1)} %add_add_fusion), channel_id=1, source_target_pairs={{0,4},{1,5},{2,6},{3,7},{4,0},{5,1},{6,2},{7,3},{8,12},{9,13},{10,... | collective-permute-start | bytes 221192 | tf_op jit(solution)/shard_map/ppermute | solution.py:38

commit v7 on v6

--- a/solution.py
+++ b/solution.py
@@ -103,15 +103,14 @@
     upper_ref[...] = jnp.zeros((size, size), jnp.float32)
     sub = lax.broadcasted_iota(jnp.int32, (PANEL, 1), 0)
     row_ids = lax.broadcasted_iota(jnp.int32, (size, 1), 0)
-    def panel(index, carry, row0, col0, col1):
+    def panel(first, row0, col0, col1):
         lane = lax.broadcasted_iota(jnp.int32, (1, size - col0), 1) + col0
-        first = pl.multiple_of(index * PANEL, PANEL)
-        slab = work_ref[pl.ds(first, PANEL), col0:]
-        inverse_slab = inverse_ref[pl.ds(first, PANEL), :col1]
+        slab = work_ref[first:first + PANEL, col0:]
+        inverse_slab = inverse_ref[first:first + PANEL, :col1]
         upper_slab = jnp.zeros((PANEL, size - col0), jnp.float32)
         for step in range(PANEL):
             column = first + step
-            picked = jnp.sum(jnp.where(lane == column, slab, 0.0), axis=1, keepdims=True)
+            picked = slab[:, column - col0:column - col0 + 1]
             scale = lax.rsqrt(picked[step : step + 1, :])
             upper_row = jnp.where(lane >= column, slab[step : step + 1, :] * scale, 0.0)
             inverse_row = inverse_slab[step : step + 1, :] * scale
@@ -119,22 +118,23 @@
             slab = slab - coef * upper_row
             inverse_slab = jnp.where(sub == step, inverse_row, inverse_slab - coef * inverse_row)
             upper_slab = jnp.where(sub == step, upper_row, upper_slab)
-        upper_ref[pl.ds(first, PANEL), col0:] = upper_slab
-        inverse_ref[pl.ds(first, PANEL), :col1] = inverse_slab
+        upper_ref[first:first + PANEL, col0:] = upper_slab
+        inverse_ref[first:first + PANEL, :col1] = inverse_slab
         lower_cols = jnp.transpose(upper_slab)[row0 - col0:]
         lower_cols = jnp.where(row_ids[row0:] >= first + PANEL, lower_cols, 0.0)
         work_ref[row0:, col0:] = work_ref[row0:, col0:] - jnp.dot(
             lower_cols, upper_slab, precision=exact_mode, preferred_element_type=jnp.float32)
         inverse_ref[row0:, :col1] = inverse_ref[row0:, :col1] - jnp.dot(
             lower_cols, inverse_slab, precision=exact_mode, preferred_element_type=jnp.float32)
-        return carry
+
     quarter = size // 4
     for part in range(4):
         row0 = quarter * part
         col0 = (size // 2) * (part // 2)
         col1 = (size // 2) * (part // 2 + 1)
-        lax.fori_loop(row0 // PANEL, (row0 + quarter) // PANEL,
-            lambda index, carry, row0=row0, col0=col0, col1=col1: panel(index, carry, row0, col0, col1), 0)
+        for first in range(row0, row0 + quarter, PANEL):
+            panel(first, row0, col0, col1)
+
 
 def cholesky_with_inverse(gram):
     size = gram.shape[0]

time: 93.9 us -> 92.1 us (0.981)
  Pallas kernels: 29.9 us -> 28.1 us
    pallas_call x1, Pallas kernels: 26.4 us -> 24.6 us  [cholesky_with_inverse(): pl.pallas_call(cholesky_kernel, out_shape=(jax.ShapeDtypeStruct((size, si...]
where the time goes in v7:
time: 92.1 us; the launch traced here: 91.7 us
  Pallas kernels  28.1 us (31%)
  waiting for transfers between devices  27.3 us (30%)
  starting transfers between devices  25 us (27%)
  other arithmetic  4.75 us (5%)
  matrix products  3.38 us (4%)
  local copies, waits for them, and re-layouts  2.39 us (3%)
    pallas_call x1, Pallas kernels, cholesky_with_inverse(): pl.pallas_call(cholesky_kernel, out_shape=(jax.ShapeDtypeStruct((size, si...  24.6 us
    ppermute x11, starting transfers between devices, exchange(): lax.ppermute(value, DEVICE_AXES, [(i, i ^ mask) for i in range(count)])  16.9 us
    ppermute x11, waiting for transfers between devices, exchange(): lax.ppermute(value, DEVICE_AXES, [(i, i ^ mask) for i in range(count)])  15.7 us
    ppermute x2, waiting for transfers between devices, shifted(): lax.ppermute(value, axis, [(source, source + steps) for source in range(i...  11.6 us
    ppermute x2, starting transfers between devices, shifted(): lax.ppermute(value, axis, [(source, source + steps) for source in range(i...  8.08 us
    pallas_call x1, Pallas kernels, aggregate(): pl.pallas_call(aggregate_kernel, out_shape=jax.ShapeDtypeStruct((window_c...  3.5 us
    dot_general x1, matrix products, body(): scores = jnp.dot(anomaly, lower_inverse.T * root, precision=exact_mode)  2.36 us
  transfers between devices with their start and end apart: 13, of which 10 were waited for; matrix products, arithmetic and copies ran while one was open for 0% of the time, Pallas kernels for 0%

profile of v7, /device:TPU:1, one launch (start us, length us, event | category | flops | bytes accessed | tf_op | source)
XLA Modules:
  0.0 91.7 jit_solution(16512275991559430447)
XLA Ops:
  0.6 0.7 subtract_clamp_fusion
  1.3 0.1 copy.13
  1.4 0.6 min.12.slot_ref
  2.0 3.5 %shard_map.68 = f32[12,128,256]{2,1,0:T(8,128)} custom-call(s32[32]{0:T(128)} %min.12.slot_ref, bf16[16,2,128,128]{3,2,1,0:T(8,128)(2,1)} %weight_ref.1, bf16[16,128,256]{2,1,0:T(8,128)(2,1)} %bitcast.22), custom_call_target="tpu_custom_call" | custom-call | tf_op jit(solution)/shard_map/pallas_call | solution.py:170
  5.5 1.3 %fusion.13 = (f32[4,128,256]{2,1,0:T(8,128)S(1)}, f32[4,128,256]{2,1,0:T(8,128)S(1)}) fusion(f32[12,128,256]{2,1,0:T(8,128)} %shard_map.68), kind=kLoop, calls=%fused_computation.40 | loop fusion | bytes 2097152 | tf_op jit(solution)/shard_map/slice | solution.py:193
  6.8 0.0 copy-start
  6.8 0.0 copy-start.1
  6.8 4.2 %collective-permute-start = (f32[4,128,256]{2,1,0:T(8,128)S(1)}, f32[4,128,256]{2,1,0:T(8,128)S(1)}, u32[]{:S(2)}, u32[]{:S(2)}) collective-permute-start(f32[4,128,256]{2,1,0:T(8,128)S(1)} %get-tuple-element.6), channel_id=1, source_target_pairs={{0,1},{1,2},{2,3},{3,4},{4,5},{5,6},{6,7},{7,8},{8,9},{9,10},{10,1... | collective-permute-start | bytes 1572872 | tf_op jit(solution)/shard_map/ppermute | solution.py:20
  11.0 3.9 %collective-permute-start.1 = (f32[4,128,256]{2,1,0:T(8,128)S(1)}, f32[4,128,256]{2,1,0:T(8,128)S(1)}, u32[]{:S(2)}, u32[]{:S(2)}) collective-permute-start(f32[4,128,256]{2,1,0:T(8,128)S(1)} %get-tuple-element.7), channel_id=1, source_target_pairs={{1,0},{2,1},{3,2},{4,3},{5,4},{6,5},{7,6},{8,7},{9,8},{10,9},{11,1... | collective-permute-start | bytes 1572872 | tf_op jit(solution)/shard_map/ppermute | solution.py:20
  14.9 0.1 pad_slice_fusion
  15.0 9.5 %collective-permute-done = f32[4,128,256]{2,1,0:T(8,128)S(1)} collective-permute-done((f32[4,128,256]{2,1,0:T(8,128)S(1)}, f32[4,128,256]{2,1,0:T(8,128)S(1)}, u32[]{:S(2)}, u32[]{:S(2)}) %collective-permute-start) | collective-permute-done | bytes 524320 | tf_op jit(solution)/shard_map/ppermute | solution.py:20
  24.5 2.2 %collective-permute-done.1 = f32[4,128,256]{2,1,0:T(8,128)S(1)} collective-permute-done((f32[4,128,256]{2,1,0:T(8,128)S(1)}, f32[4,128,256]{2,1,0:T(8,128)S(1)}, u32[]{:S(2)}, u32[]{:S(2)}) %collective-permute-start.1) | collective-permute-done | bytes 524320 | tf_op jit(solution)/shard_map/ppermute | solution.py:20
  26.7 1.1 %fusion = f32[4,128,256]{2,1,0:T(8,128)S(1)} fusion(f32[4,128,256]{2,1,0:T(8,128)S(1)} %collective-permute-done.1, f32[4,128,256]{2,1,0:T(8,128)S(1)} %collective-permute-done, f32[12,128,256]{2,1,0:T(8,128)} %shard_map.68), kind=kLoop, calls=%fused_computation.1 | loop fusion | flops 262144 | bytes 2097152 | tf_op jit(solution)/shard_map/add | solution.py:195
  27.8 0.0 copy-done
  27.8 0.0 copy-done.1
  27.8 0.1 fusion.1
  28.0 1.0 %fusion.14 = f32[256,256]{1,0:T(8,128)S(1)} fusion(f32[512,256]{1,0:T(8,128)S(1)} %fusion.1), kind=kOutput, calls=%fused_computation.41 | convolution fusion | flops 402653184 | bytes 786432 | tf_op jit(solution)/shard_map/dot_general | solution.py:198
  29.0 0.1 copy.14
  29.2 0.1 broadcast_select_fusion
  29.3 0.7 collective-permute-start.2
  29.9 0.9 collective-permute-done.2
  30.9 0.1 select_add_fusion
  30.9 1.4 %collective-permute-start.3 = (f32[72,256]{1,0:T(8,128)S(1)}, f32[72,256]{1,0:T(8,128)S(1)}, u32[]{:S(2)}, u32[]{:S(2)}) collective-permute-start(f32[72,256]{1,0:T(8,128)S(1)} %select_add_fusion), channel_id=1, source_target_pairs={{0,1},{1,0},{2,3},{3,2},{4,5},{5,4},{6,7},{7,6},{8,9},{9,8},{10,11... | collective-permute-start | bytes 221192 | tf_op jit(solution)/shard_map/ppermute | solution.py:38
  32.3 4.1 %collective-permute-start.4 = (f32[72,256]{1,0:T(8,128)S(1)}, f32[72,256]{1,0:T(8,128)S(1)}, u32[]{:S(2)}, u32[]{:S(2)}) collective-permute-start(f32[72,256]{1,0:T(8,128)S(1)} %select_add_fusion), channel_id=1, source_target_pairs={{0,2},{1,3},{2,0},{3,1},{4,6},{5,7},{6,4},{7,5},{8,10},{9,11},{10,... | collective-permute-start | bytes 221192 | tf_op jit(solution)/shard_map/ppermute | solution.py:38
  36.4 0.0 collective-permute-start.5
  36.5 0.0 collective-permute-done.3
  36.5 3.8 %collective-permute-done.4 = f32[72,256]{1,0:T(8,128)S(1)} collective-permute-done((f32[72,256]{1,0:T(8,128)S(1)}, f32[72,256]{1,0:T(8,128)S(1)}, u32[]{:S(2)}, u32[]{:S(2)}) %collective-permute-start.4) | collective-permute-done | bytes 73760 | tf_op jit(solution)/shard_map/ppermute | solution.py:38
  40.2 1.5 %collective-permute-done.5 = f32[72,256]{1,0:T(8,128)S(1)} collective-permute-done((f32[72,256]{1,0:T(8,128)S(1)}, f32[72,256]{1,0:T(8,128)S(1)}, u32[]{:S(2)}, u32[]{:S(2)}) %collective-permute-start.5) | collective-permute-done | bytes 73760 | tf_op jit(solution)/shard_map/ppermute | solution.py:38
  41.8 1.7 %collective-permute-start.6 = (f32[72,256]{1,0:T(8,128)S(1)}, f32[72,256]{1,0:T(8,128)S(1)}, u32[]{:S(2)}, u32[]{:S(2)}) collective-permute-start(f32[72,256]{1,0:T(8,128)S(1)} %add_add_fusion.2), channel_id=1, source_target_pairs={{0,8},{1,9},{2,10},{3,11},{4,12},{5,13},{6,14},{7,15},{8,0},{9,1},... | collective-permute-start | bytes 221192 | tf_op jit(solution)/shard_map/ppermute | solution.py:38
  43.5 1.8 %collective-permute-start.7 = (f32[72,256]{1,0:T(8,128)S(1)}, f32[72,256]{1,0:T(8,128)S(1)}, u32[]{:S(2)}, u32[]{:S(2)}) collective-permute-start(f32[72,256]{1,0:T(8,128)S(1)} %add_add_fusion.2), channel_id=1, source_target_pairs={{0,16},{1,17},{2,18},{3,19},{4,20},{5,21},{6,22},{7,23},{8,24},{9,... | collective-permute-start | bytes 221192 | tf_op jit(solution)/shard_map/ppermute | solution.py:38
  45.2 0.7 collective-permute-start.8
  45.9 0.0 collective-permute-done.6
  46.0 3.1 %collective-permute-done.7 = f32[72,256]{1,0:T(8,128)S(1)} collective-permute-done((f32[72,256]{1,0:T(8,128)S(1)}, f32[72,256]{1,0:T(8,128)S(1)}, u32[]{:S(2)}, u32[]{:S(2)}) %collective-permute-start.7) | collective-permute-done | bytes 73760 | tf_op jit(solution)/shard_map/ppermute | solution.py:38
  49.0 1.4 %collective-permute-done.8 = f32[72,256]{1,0:T(8,128)S(1)} collective-permute-done((f32[72,256]{1,0:T(8,128)S(1)}, f32[72,256]{1,0:T(8,128)S(1)}, u32[]{:S(2)}, u32[]{:S(2)}) %collective-permute-start.8) | collective-permute-done | bytes 73760 | tf_op jit(solution)/shard_map/ppermute | solution.py:38
  50.5 2.8 %collective-permute-start.10 = (f32[72,256]{1,0:T(8,128)S(1)}, f32[72,256]{1,0:T(8,128)S(1)}, u32[]{:S(2)}, u32[]{:S(2)}) collective-permute-start(f32[72,256]{1,0:T(8,128)S(1)} %add_add_fusion.1), channel_id=1, source_target_pairs={{0,64},{1,65},{2,66},{3,67},{4,68},{5,69},{6,70},{7,71},{8,72},{9,... | collective-permute-start | bytes 221192 | tf_op jit(solution)/shard_map/ppermute | solution.py:38
  53.3 0.9 collective-permute-start.11
  54.2 0.0 collective-permute-start.9
  54.2 1.1 %collective-permute-done.10 = f32[72,256]{1,0:T(8,128)S(1)} collective-permute-done((f32[72,256]{1,0:T(8,128)S(1)}, f32[72,256]{1,0:T(8,128)S(1)}, u32[]{:S(2)}, u32[]{:S(2)}) %collective-permute-start.10) | collective-permute-done | bytes 73760 | tf_op jit(solution)/shard_map/ppermute | solution.py:38
  55.3 2.9 %collective-permute-done.11 = f32[72,256]{1,0:T(8,128)S(1)} collective-permute-done((f32[72,256]{1,0:T(8,128)S(1)}, f32[72,256]{1,0:T(8,128)S(1)}, u32[]{:S(2)}, u32[]{:S(2)}) %collective-permute-start.11) | collective-permute-done | bytes 73760 | tf_op jit(solution)/shard_map/ppermute | solution.py:38
  58.2 0.0 collective-permute-done.9
  58.2 2.9 %collective-permute-start.12 = (f32[72,256]{1,0:T(8,128)S(1)}, f32[72,256]{1,0:T(8,128)S(1)}, u32[]{:S(2)}, u32[]{:S(2)}) collective-permute-start(f32[72,256]{1,0:T(8,128)S(1)} %add_add_fusion), channel_id=1, source_target_pairs={{0,4},{1,5},{2,6},{3,7},{4,0},{5,1},{6,2},{7,3},{8,12},{9,13},{10,... | collective-permute-start | bytes 221192 | tf_op jit(solution)/shard_map/ppermute | solution.py:38
  61.1 0.9 collective-permute-done.12
  62.1 0.1 copy.19
  62.2 0.1 bitcast_select_fusion.1
  62.3 0.1 copy.18
  62.4 0.7 maximum_maximum_fusion.gram_ref
  63.1 24.6 %shard_map.69 = (f32[256,256]{1,0:T(8,128)}, f32[256,256]{1,0:T(8,128)}) custom-call(f32[256,256]{1,0:T(8,128)} %maximum_maximum_fusion.gram_ref), custom_call_target="tpu_custom_call" | custom-call | tf_op jit(solution)/shard_map/pallas_call | solution.py:141
  87.7 2.4 %fusion.3 = f32[512,256]{1,0:T(8,128)} fusion(f32[512,256]{1,0:T(8,128)S(1)} %fusion.1, f32[256,256]{1,0:T(8,128)} %get-tuple-element.4), kind=kOutput, calls=%fused_computation.7 | convolution fusion | flops 402718720 | bytes 1310720 | tf_op jit(solution)/shard_map/dot_general | solution.py:205
  90.0 1.7 %broadcast_multiply_fusion = f32[256,256]{1,0:T(8,128)} fusion(f32[256,256]{1,0:T(8,128)} %get-tuple-element.5), kind=kLoop, calls=%fused_computation.10 | loop fusion | flops 65536 | bytes 524288 | tf_op jit(solution)/shard_map/div | solution.py:206
  (9 shorter events, 0.2 us)
Async XLA Ops:
  6.8 21.0 %copy-start = (f32[512,256]{1,0:T(8,128)S(1)}, f32[512,256]{1,0:T(8,128)}, u32[]{:S(2)}) copy-start(f32[512,256]{1,0:T(8,128)} %param.8) | copy-start | bytes 1572868
  6.8 21.0 %copy-start.1 = (f32[512]{0:T(512)S(1)}, f32[512]{0:T(512)}, u32[]{:S(2)}) copy-start(f32[512]{0:T(512)} %param.9) | copy-start | bytes 6148
  6.8 17.6 %collective-permute-start = (f32[4,128,256]{2,1,0:T(8,128)S(1)}, f32[4,128,256]{2,1,0:T(8,128)S(1)}, u32[]{:S(2)}, u32[]{:S(2)}) collective-permute-start(f32[4,128,256]{2,1,0:T(8,128)S(1)} %get-tuple-element.6), channel_id=1, source_target_pairs={{0,1},{1,2},{2,3},{3,4},{4,5},{5,6},{6,7},{7,8},{8,9},{9,10},{10,1... | collective-permute-start | bytes 1572872 | tf_op jit(solution)/shard_map/ppermute | solution.py:20
  11.0 15.7 %collective-permute-start.1 = (f32[4,128,256]{2,1,0:T(8,128)S(1)}, f32[4,128,256]{2,1,0:T(8,128)S(1)}, u32[]{:S(2)}, u32[]{:S(2)}) collective-permute-start(f32[4,128,256]{2,1,0:T(8,128)S(1)} %get-tuple-element.7), channel_id=1, source_target_pairs={{1,0},{2,1},{3,2},{4,3},{5,4},{6,5},{7,6},{8,7},{9,8},{10,9},{11,1... | collective-permute-start | bytes 1572872 | tf_op jit(solution)/shard_map/ppermute | solution.py:20
  29.3 1.6 %collective-permute-start.2 = (f32[72,256]{1,0:T(8,128)S(1)}, f32[72,256]{1,0:T(8,128)S(1)}, u32[]{:S(2)}, u32[]{:S(2)}) collective-permute-start(f32[72,256]{1,0:T(8,128)S(1)} %broadcast_select_fusion), channel_id=1, source_target_pairs={{0,4},{1,5},{2,6},{3,7},{4,0},{5,1},{6,2},{7,3},{8,12},{9,13},{10,... | collective-permute-start | bytes 221192 | tf_op jit(solution)/shard_map/ppermute | solution.py:38
  30.9 5.5 %collective-permute-start.3 = (f32[72,256]{1,0:T(8,128)S(1)}, f32[72,256]{1,0:T(8,128)S(1)}, u32[]{:S(2)}, u32[]{:S(2)}) collective-permute-start(f32[72,256]{1,0:T(8,128)S(1)} %select_add_fusion), channel_id=1, source_target_pairs={{0,1},{1,0},{2,3},{3,2},{4,5},{5,4},{6,7},{7,6},{8,9},{9,8},{10,11... | collective-permute-start | bytes 221192 | tf_op jit(solution)/shard_map/ppermute | solution.py:38
  32.3 7.9 %collective-permute-start.4 = (f32[72,256]{1,0:T(8,128)S(1)}, f32[72,256]{1,0:T(8,128)S(1)}, u32[]{:S(2)}, u32[]{:S(2)}) collective-permute-start(f32[72,256]{1,0:T(8,128)S(1)} %select_add_fusion), channel_id=1, source_target_pairs={{0,2},{1,3},{2,0},{3,1},{4,6},{5,7},{6,4},{7,5},{8,10},{9,11},{10,... | collective-permute-start | bytes 221192 | tf_op jit(solution)/shard_map/ppermute | solution.py:38
  36.4 5.3 %collective-permute-start.5 = (f32[72,256]{1,0:T(8,128)S(1)}, f32[72,256]{1,0:T(8,128)S(1)}, u32[]{:S(2)}, u32[]{:S(2)}) collective-permute-start(f32[72,256]{1,0:T(8,128)S(1)} %select_add_fusion), channel_id=1, source_target_pairs={{0,3},{1,2},{2,1},{3,0},{4,7},{5,6},{6,5},{7,4},{8,11},{9,10},{10,... | collective-permute-start | bytes 221192 | tf_op jit(solution)/shard_map/ppermute | solution.py:38
  41.8 4.2 %collective-permute-start.6 = (f32[72,256]{1,0:T(8,128)S(1)}, f32[72,256]{1,0:T(8,128)S(1)}, u32[]{:S(2)}, u32[]{:S(2)}) collective-permute-start(f32[72,256]{1,0:T(8,128)S(1)} %add_add_fusion.2), channel_id=1, source_target_pairs={{0,8},{1,9},{2,10},{3,11},{4,12},{5,13},{6,14},{7,15},{8,0},{9,1},... | collective-permute-start | bytes 221192 | tf_op jit(solution)/shard_map/ppermute | solution.py:38
  43.5 5.6 %collective-permute-start.7 = (f32[72,256]{1,0:T(8,128)S(1)}, f32[72,256]{1,0:T(8,128)S(1)}, u32[]{:S(2)}, u32[]{:S(2)}) collective-permute-start(f32[72,256]{1,0:T(8,128)S(1)} %add_add_fusion.2), channel_id=1, source_target_pairs={{0,16},{1,17},{2,18},{3,19},{4,20},{5,21},{6,22},{7,23},{8,24},{9,... | collective-permute-start | bytes 221192 | tf_op jit(solution)/shard_map/ppermute | solution.py:38
  45.2 5.3 %collective-permute-start.8 = (f32[72,256]{1,0:T(8,128)S(1)}, f32[72,256]{1,0:T(8,128)S(1)}, u32[]{:S(2)}, u32[]{:S(2)}) collective-permute-start(f32[72,256]{1,0:T(8,128)S(1)} %add_add_fusion.2), channel_id=1, source_target_pairs={{0,24},{1,25},{2,26},{3,27},{4,28},{5,29},{6,30},{7,31},{8,16},{9,... | collective-permute-start | bytes 221192 | tf_op jit(solution)/shard_map/ppermute | solution.py:38
  50.5 4.8 %collective-permute-start.10 = (f32[72,256]{1,0:T(8,128)S(1)}, f32[72,256]{1,0:T(8,128)S(1)}, u32[]{:S(2)}, u32[]{:S(2)}) collective-permute-start(f32[72,256]{1,0:T(8,128)S(1)} %add_add_fusion.1), channel_id=1, source_target_pairs={{0,64},{1,65},{2,66},{3,67},{4,68},{5,69},{6,70},{7,71},{8,72},{9,... | collective-permute-start | bytes 221192 | tf_op jit(solution)/shard_map/ppermute | solution.py:38
  53.3 4.9 %collective-permute-start.11 = (f32[72,256]{1,0:T(8,128)S(1)}, f32[72,256]{1,0:T(8,128)S(1)}, u32[]{:S(2)}, u32[]{:S(2)}) collective-permute-start(f32[72,256]{1,0:T(8,128)S(1)} %add_add_fusion.1), channel_id=1, source_target_pairs={{0,96},{1,97},{2,98},{3,99},{4,100},{5,101},{6,102},{7,103},{8,104... | collective-permute-start | bytes 221192 | tf_op jit(solution)/shard_map/ppermute | solution.py:38
  54.2 4.0 %collective-permute-start.9 = (f32[72,256]{1,0:T(8,128)S(1)}, f32[72,256]{1,0:T(8,128)S(1)}, u32[]{:S(2)}, u32[]{:S(2)}) collective-permute-start(f32[72,256]{1,0:T(8,128)S(1)} %add_add_fusion.1), channel_id=1, source_target_pairs={{0,32},{1,33},{2,34},{3,35},{4,36},{5,37},{6,38},{7,39},{8,40},{9,... | collective-permute-start | bytes 221192 | tf_op jit(solution)/shard_map/ppermute | solution.py:38
  58.2 3.8 %collective-permute-start.12 = (f32[72,256]{1,0:T(8,128)S(1)}, f32[72,256]{1,0:T(8,128)S(1)}, u32[]{:S(2)}, u32[]{:S(2)}) collective-permute-start(f32[72,256]{1,0:T(8,128)S(1)} %add_add_fusion), channel_id=1, source_target_pairs={{0,4},{1,5},{2,6},{3,7},{4,0},{5,1},{6,2},{7,3},{8,12},{9,13},{10,... | collective-permute-start | bytes 221192 | tf_op jit(solution)/shard_map/ppermute | solution.py:38

commit v8 on v7

--- a/solution.py
+++ b/solution.py
@@ -1,3 +1,4 @@
+import functools
 import itertools
 import math
 
@@ -94,7 +95,7 @@
     return jnp.concatenate([top, bottom], axis=0)
 
 
-def cholesky_kernel(gram_ref, upper_ref, inverse_ref, work_ref):
+def cholesky_kernel(gram_ref, upper_ref, inverse_ref, work_ref, *, factor_scale, inverse_scale):
     size = gram_ref.shape[0]
     work_ref[...] = gram_ref[...]
     rows = lax.broadcasted_iota(jnp.int32, (size, size), 0)
@@ -118,8 +119,8 @@
             slab = slab - coef * upper_row
             inverse_slab = jnp.where(sub == step, inverse_row, inverse_slab - coef * inverse_row)
             upper_slab = jnp.where(sub == step, upper_row, upper_slab)
-        upper_ref[first:first + PANEL, col0:] = upper_slab
-        inverse_ref[first:first + PANEL, :col1] = inverse_slab
+        upper_ref[first:first + PANEL, col0:] = upper_slab * factor_scale
+        inverse_ref[first:first + PANEL, :col1] = inverse_slab * inverse_scale
         lower_cols = jnp.transpose(upper_slab)[row0 - col0:]
         lower_cols = jnp.where(row_ids[row0:] >= first + PANEL, lower_cols, 0.0)
         work_ref[row0:, col0:] = work_ref[row0:, col0:] - jnp.dot(
@@ -136,10 +137,10 @@
             panel(first, row0, col0, col1)
 
 
-def cholesky_with_inverse(gram):
+def cholesky_with_inverse(gram, root):
     size = gram.shape[0]
     return pl.pallas_call(
-        cholesky_kernel,
+        functools.partial(cholesky_kernel, factor_scale=1.0 / root, inverse_scale=root),
         out_shape=(
             jax.ShapeDtypeStruct((size, size), jnp.float32),
             jax.ShapeDtypeStruct((size, size), jnp.float32),
@@ -148,8 +149,11 @@
     )(gram)
 
 
-def aggregate_kernel(slot_ref, weight_ref, rows_ref, out_ref):
-    out_ref[...] = jnp.zeros(out_ref.shape, out_ref.dtype)
+def aggregate_kernel(zone_ref, base_ref, weight_ref, rows_ref, before_ref, own_ref, after_ref):
+    owned = own_ref.shape[0]
+    tables = (before_ref, own_ref, after_ref)
+    for table in tables:
+        table[...] = jnp.zeros(table.shape, table.dtype)
     block_count, slot_count = weight_ref.shape[0], weight_ref.shape[1]
     for block in range(block_count):
         rows = rows_ref[block]
@@ -160,23 +164,35 @@
                 (((0,), (0,)), ((), ())),
                 preferred_element_type=jnp.float32,
             )
-            target = slot_ref[block * slot_count + slot]
-            out_ref[target] = out_ref[target] + part
-
-
-def aggregate(slots, weight_blocks, cell_rows, window_count):
+            target = jnp.clip(zone_ref[block, slot] - base_ref[0], 0, 3 * owned - 1)
+            group = target // owned
+            local = target - group * owned
+            for number, table in enumerate(tables):
+
+                @pl.when(group == number)
+                def _(table=table, local=local, part=part):
+                    table[local] = table[local] + part
+
+
+def aggregate(block_zone, base, weight_blocks, cell_rows, owned_blocks):
     block_size = weight_blocks.shape[3]
     day_count = cell_rows.shape[2]
+    table = jax.ShapeDtypeStruct((owned_blocks, block_size, day_count), jnp.float32)
     return pl.pallas_call(
         aggregate_kernel,
-        out_shape=jax.ShapeDtypeStruct((window_count, block_size, day_count), jnp.float32),
+        out_shape=(table, table, table),
         in_specs=[
             pl.BlockSpec(memory_space=pltpu.SMEM),
+            pl.BlockSpec(memory_space=pltpu.SMEM),
             pl.BlockSpec(memory_space=pltpu.VMEM),
             pl.BlockSpec(memory_space=pltpu.VMEM),
         ],
-        out_specs=pl.BlockSpec(memory_space=pltpu.VMEM),
-    )(slots, weight_blocks, cell_rows)
+        out_specs=(
+            pl.BlockSpec(memory_space=pltpu.VMEM),
+            pl.BlockSpec(memory_space=pltpu.VMEM),
+            pl.BlockSpec(memory_space=pltpu.VMEM),
+        ),
+    )(block_zone, base, weight_blocks, cell_rows)
 
 
 def body(runoff, weight_blocks, block_zone, climatology, zone_weight):
@@ -187,12 +203,13 @@
     device_count = lax.axis_size(DEVICE_AXES)
     device_index = lax.axis_index(DEVICE_AXES)
     cell_rows = runoff.reshape(block_count, block_size, day_count)
-    target_slot = block_zone.reshape(-1) - (device_index - 1) * owned_blocks
-    target_slot = jnp.clip(target_slot, 0, 3 * owned_blocks - 1).astype(jnp.int32)
-    tables = aggregate(target_slot, weight_blocks, cell_rows, 3 * owned_blocks)
-    from_before = shifted(tables[2 * owned_blocks :], DEVICE_AXES, 1)
-    from_after = shifted(tables[:owned_blocks], DEVICE_AXES, -1)
-    summed = tables[owned_blocks : 2 * owned_blocks] + from_before + from_after
+    base = jnp.reshape((device_index - 1) * owned_blocks, (1,)).astype(jnp.int32)
+    to_before, own_table, to_after = aggregate(
+        block_zone.astype(jnp.int32), base, weight_blocks, cell_rows, owned_blocks
+    )
+    from_before = shifted(to_after, DEVICE_AXES, 1)
+    from_after = shifted(to_before, DEVICE_AXES, -1)
+    summed = own_table + from_before + from_after
     aggregated = summed.reshape(owned_blocks * block_size, day_count)
     anomaly = zone_weight[:, None] * (aggregated - climatology)
     local_gram = jnp.dot(
@@ -200,10 +217,10 @@
     )
     local_gram = 0.5 * (local_gram + local_gram.T)
     total_gram = unpack_gram(all_sum(pack_gram(local_gram), device_count), day_count)
-    upper, lower_inverse = cholesky_with_inverse(total_gram)
     root = math.sqrt(anomaly.shape[0] * device_count)
-    scores = jnp.dot(anomaly, lower_inverse.T * root, precision=exact_mode)
-    return (scores, upper / root)
+    factor, scaled_inverse = cholesky_with_inverse(total_gram, root)
+    scores = jnp.dot(anomaly, scaled_inverse.T, precision=exact_mode)
+    return (scores, factor)
 
 
 def solution(mesh):

time: 92.1 us -> 95.1 us (1.033)
  Pallas kernels: 28.1 us -> 34 us
  other arithmetic: 4.75 us -> 2.46 us
    pallas_call x2, Pallas kernels: 28.1 us -> 34 us  [the longest x1 24.6 us: cholesky_with_inverse(): pl.pallas_call(functools.partial(cholesky_kernel, factor_scale=1.0 / root...]
    div x1 -> x0, other arithmetic: 1.67 us -> none  [body(): return (scores, upper / root)]
    unnamed x5 -> x8, local copies, waits for them, and re-layouts: 0.1 us -> 1.45 us
    slice x1 -> x0, local copies, waits for them, and re-layouts: 1.3 us -> none  [body(): from_before = shifted(tables[2 * owned_blocks:], DEVICE_AXES, 1)]
where the time goes in v8:
time: 95.1 us; the launch traced here: 94.8 us
  Pallas kernels  34 us (36%)
  waiting for transfers between devices  27.6 us (29%)
  starting transfers between devices  24.8 us (26%)
  matrix products  3.38 us (4%)
  other arithmetic  2.46 us (3%)
  local copies, waits for them, and re-layouts  1.75 us (2%)
    pallas_call x1, Pallas kernels, cholesky_with_inverse(): pl.pallas_call(functools.partial(cholesky_kernel, factor_scale=1.0 / root...  24.6 us
    ppermute x11, starting transfers between devices, exchange(): lax.ppermute(value, DEVICE_AXES, [(i, i ^ mask) for i in range(count)])  16.8 us
    ppermute x11, waiting for transfers between devices, exchange(): lax.ppermute(value, DEVICE_AXES, [(i, i ^ mask) for i in range(count)])  15.6 us
    ppermute x2, waiting for transfers between devices, shifted(): lax.ppermute(value, axis, [(source, source + steps) for source in range(i...  12 us
    pallas_call x1, Pallas kernels, aggregate(): pl.pallas_call(aggregate_kernel, out_shape=(table, table, table), in_spec...  9.44 us
    ppermute x2, starting transfers between devices, shifted(): lax.ppermute(value, axis, [(source, source + steps) for source in range(i...  7.92 us
    dot_general x1, matrix products, body(): scores = jnp.dot(anomaly, scaled_inverse.T, precision=exact_mode)  2.36 us
  transfers between devices with their start and end apart: 13, of which 10 were waited for; matrix products, arithmetic and copies ran while one was open for 0% of the time, Pallas kernels for 0%

profile of v8, /device:TPU:1, one launch (start us, length us, event | category | flops | bytes accessed | tf_op | source)
XLA Modules:
  0.0 94.8 jit_solution(12075594871444106845)
XLA Ops:
  0.6 0.0 copy-start.2
  0.6 0.7 copy-done.2
  1.3 0.7 copy.7.zone_ref
  2.0 9.4 %shard_map.68 = (f32[4,128,256]{2,1,0:T(8,128)}, f32[4,128,256]{2,1,0:T(8,128)}, f32[4,128,256]{2,1,0:T(8,128)}) custom-call(s32[16,2]{1,0:T(8,128)} %copy.7.zone_ref, s32[1]{0:T(128)} %bitcast.base_ref, bf16[16,2,128,128]{3,2,1,0:T(8,128)(2,1)} %weight_ref.1, bf16[16,128,256]{2,1,0:T(8,128)(2,1)} %bitcast.24), custom_call_target="tpu_custom_call" | custom-call | tf_op jit(solution)/shard_map/pallas_call | solution.py:181
  11.4 4.0 %collective-permute-start = (f32[4,128,256]{2,1,0:T(8,128)}, f32[4,128,256]{2,1,0:T(8,128)S(1)}, u32[]{:S(2)}, u32[]{:S(2)}) collective-permute-start(f32[4,128,256]{2,1,0:T(8,128)} %get-tuple-element.8), channel_id=1, source_target_pairs={{0,1},{1,2},{2,3},{3,4},{4,5},{5,6},{6,7},{7,8},{8,9},{9,10},{10,1... | collective-permute-start | bytes 1572872 | tf_op jit(solution)/shard_map/ppermute | solution.py:21
  15.5 3.9 %collective-permute-start.1 = (f32[4,128,256]{2,1,0:T(8,128)}, f32[4,128,256]{2,1,0:T(8,128)S(1)}, u32[]{:S(2)}, u32[]{:S(2)}) collective-permute-start(f32[4,128,256]{2,1,0:T(8,128)} %get-tuple-element.9), channel_id=1, source_target_pairs={{1,0},{2,1},{3,2},{4,3},{5,4},{6,5},{7,6},{8,7},{9,8},{10,9},{11,1... | collective-permute-start | bytes 1572872 | tf_op jit(solution)/shard_map/ppermute | solution.py:21
  19.4 0.1 pad_slice_fusion
  19.5 9.7 %collective-permute-done = f32[4,128,256]{2,1,0:T(8,128)S(1)} collective-permute-done((f32[4,128,256]{2,1,0:T(8,128)}, f32[4,128,256]{2,1,0:T(8,128)S(1)}, u32[]{:S(2)}, u32[]{:S(2)}) %collective-permute-start) | collective-permute-done | bytes 524320 | tf_op jit(solution)/shard_map/ppermute | solution.py:21
  29.1 2.3 %collective-permute-done.1 = f32[4,128,256]{2,1,0:T(8,128)S(1)} collective-permute-done((f32[4,128,256]{2,1,0:T(8,128)}, f32[4,128,256]{2,1,0:T(8,128)S(1)}, u32[]{:S(2)}, u32[]{:S(2)}) %collective-permute-start.1) | collective-permute-done | bytes 524320 | tf_op jit(solution)/shard_map/ppermute | solution.py:21
  31.4 0.0 copy-start
  31.5 0.0 copy-start.1
  31.5 1.2 %add_add_fusion = f32[4,128,256]{2,1,0:T(8,128)S(1)} fusion(f32[4,128,256]{2,1,0:T(8,128)S(1)} %collective-permute-done.1, f32[4,128,256]{2,1,0:T(8,128)} %get-tuple-element.7, f32[4,128,256]{2,1,0:T(8,128)S(1)} %collective-permute-done), kind=kLoop, calls=%fused_computation.2 | loop fusion | flops 262144 | bytes 2097152 | tf_op jit(solution)/shard_map/add | solution.py:212
  32.7 0.0 copy-done
  32.7 0.0 copy-done.1
  32.7 0.1 fusion
  32.8 1.0 %fusion.8 = f32[256,256]{1,0:T(8,128)S(1)} fusion(f32[512,256]{1,0:T(8,128)S(1)} %fusion), kind=kOutput, calls=%fused_computation.33 | convolution fusion | flops 402653184 | bytes 786432 | tf_op jit(solution)/shard_map/dot_general | solution.py:215
  33.8 0.1 copy.8
  34.1 0.1 broadcast_select_fusion
  34.1 0.5 collective-permute-start.2
  34.7 0.9 collective-permute-done.2
  35.6 0.1 select_add_fusion
  35.7 1.4 %collective-permute-start.3 = (f32[72,256]{1,0:T(8,128)S(1)}, f32[72,256]{1,0:T(8,128)S(1)}, u32[]{:S(2)}, u32[]{:S(2)}) collective-permute-start(f32[72,256]{1,0:T(8,128)S(1)} %select_add_fusion), channel_id=1, source_target_pairs={{0,1},{1,0},{2,3},{3,2},{4,5},{5,4},{6,7},{7,6},{8,9},{9,8},{10,11... | collective-permute-start | bytes 221192 | tf_op jit(solution)/shard_map/ppermute | solution.py:39
  37.0 4.1 %collective-permute-start.4 = (f32[72,256]{1,0:T(8,128)S(1)}, f32[72,256]{1,0:T(8,128)S(1)}, u32[]{:S(2)}, u32[]{:S(2)}) collective-permute-start(f32[72,256]{1,0:T(8,128)S(1)} %select_add_fusion), channel_id=1, source_target_pairs={{0,2},{1,3},{2,0},{3,1},{4,6},{5,7},{6,4},{7,5},{8,10},{9,11},{10,... | collective-permute-start | bytes 221192 | tf_op jit(solution)/shard_map/ppermute | solution.py:39
  41.2 0.0 collective-permute-start.5
  41.2 0.0 collective-permute-done.3
  41.2 3.8 %collective-permute-done.4 = f32[72,256]{1,0:T(8,128)S(1)} collective-permute-done((f32[72,256]{1,0:T(8,128)S(1)}, f32[72,256]{1,0:T(8,128)S(1)}, u32[]{:S(2)}, u32[]{:S(2)}) %collective-permute-start.4) | collective-permute-done | bytes 73760 | tf_op jit(solution)/shard_map/ppermute | solution.py:39
  44.9 1.5 %collective-permute-done.5 = f32[72,256]{1,0:T(8,128)S(1)} collective-permute-done((f32[72,256]{1,0:T(8,128)S(1)}, f32[72,256]{1,0:T(8,128)S(1)}, u32[]{:S(2)}, u32[]{:S(2)}) %collective-permute-start.5) | collective-permute-done | bytes 73760 | tf_op jit(solution)/shard_map/ppermute | solution.py:39
  46.5 1.7 %collective-permute-start.6 = (f32[72,256]{1,0:T(8,128)S(1)}, f32[72,256]{1,0:T(8,128)S(1)}, u32[]{:S(2)}, u32[]{:S(2)}) collective-permute-start(f32[72,256]{1,0:T(8,128)S(1)} %add_add_fusion.3), channel_id=1, source_target_pairs={{0,8},{1,9},{2,10},{3,11},{4,12},{5,13},{6,14},{7,15},{8,0},{9,1},... | collective-permute-start | bytes 221192 | tf_op jit(solution)/shard_map/ppermute | solution.py:39
  48.2 1.8 %collective-permute-start.7 = (f32[72,256]{1,0:T(8,128)S(1)}, f32[72,256]{1,0:T(8,128)S(1)}, u32[]{:S(2)}, u32[]{:S(2)}) collective-permute-start(f32[72,256]{1,0:T(8,128)S(1)} %add_add_fusion.3), channel_id=1, source_target_pairs={{0,16},{1,17},{2,18},{3,19},{4,20},{5,21},{6,22},{7,23},{8,24},{9,... | collective-permute-start | bytes 221192 | tf_op jit(solution)/shard_map/ppermute | solution.py:39
  49.9 0.7 collective-permute-start.8
  50.7 0.0 collective-permute-done.6
  50.7 3.1 %collective-permute-done.7 = f32[72,256]{1,0:T(8,128)S(1)} collective-permute-done((f32[72,256]{1,0:T(8,128)S(1)}, f32[72,256]{1,0:T(8,128)S(1)}, u32[]{:S(2)}, u32[]{:S(2)}) %collective-permute-start.7) | collective-permute-done | bytes 73760 | tf_op jit(solution)/shard_map/ppermute | solution.py:39
  53.8 1.5 %collective-permute-done.8 = f32[72,256]{1,0:T(8,128)S(1)} collective-permute-done((f32[72,256]{1,0:T(8,128)S(1)}, f32[72,256]{1,0:T(8,128)S(1)}, u32[]{:S(2)}, u32[]{:S(2)}) %collective-permute-start.8) | collective-permute-done | bytes 73760 | tf_op jit(solution)/shard_map/ppermute | solution.py:39
  55.2 2.8 %collective-permute-start.10 = (f32[72,256]{1,0:T(8,128)S(1)}, f32[72,256]{1,0:T(8,128)S(1)}, u32[]{:S(2)}, u32[]{:S(2)}) collective-permute-start(f32[72,256]{1,0:T(8,128)S(1)} %add_add_fusion.2), channel_id=1, source_target_pairs={{0,64},{1,65},{2,66},{3,67},{4,68},{5,69},{6,70},{7,71},{8,72},{9,... | collective-permute-start | bytes 221192 | tf_op jit(solution)/shard_map/ppermute | solution.py:39
  58.1 0.9 collective-permute-start.11
  58.9 0.0 collective-permute-start.9
  58.9 1.1 %collective-permute-done.10 = f32[72,256]{1,0:T(8,128)S(1)} collective-permute-done((f32[72,256]{1,0:T(8,128)S(1)}, f32[72,256]{1,0:T(8,128)S(1)}, u32[]{:S(2)}, u32[]{:S(2)}) %collective-permute-start.10) | collective-permute-done | bytes 73760 | tf_op jit(solution)/shard_map/ppermute | solution.py:39
  60.0 2.9 %collective-permute-done.11 = f32[72,256]{1,0:T(8,128)S(1)} collective-permute-done((f32[72,256]{1,0:T(8,128)S(1)}, f32[72,256]{1,0:T(8,128)S(1)}, u32[]{:S(2)}, u32[]{:S(2)}) %collective-permute-start.11) | collective-permute-done | bytes 73760 | tf_op jit(solution)/shard_map/ppermute | solution.py:39
  62.9 0.0 collective-permute-done.9
  63.0 2.9 %collective-permute-start.12 = (f32[72,256]{1,0:T(8,128)S(1)}, f32[72,256]{1,0:T(8,128)S(1)}, u32[]{:S(2)}, u32[]{:S(2)}) collective-permute-start(f32[72,256]{1,0:T(8,128)S(1)} %add_add_fusion.1), channel_id=1, source_target_pairs={{0,4},{1,5},{2,6},{3,7},{4,0},{5,1},{6,2},{7,3},{8,12},{9,13},{10,... | collective-permute-start | bytes 221192 | tf_op jit(solution)/shard_map/ppermute | solution.py:39
  65.9 0.9 collective-permute-done.12
  66.8 0.1 copy.13
  66.9 0.1 bitcast_select_fusion.1
  67.0 0.1 copy.12
  67.1 0.7 maximum_maximum_fusion.gram_ref
  67.8 24.6 %shard_map.69 = (f32[256,256]{1,0:T(8,128)}, f32[256,256]{1,0:T(8,128)}) custom-call(f32[256,256]{1,0:T(8,128)} %maximum_maximum_fusion.gram_ref), custom_call_target="tpu_custom_call" | custom-call | tf_op jit(solution)/shard_map/pallas_call | solution.py:142
  92.4 2.4 %fusion.9 = f32[512,256]{1,0:T(8,128)} fusion(f32[512,256]{1,0:T(8,128)S(1)} %fusion, f32[256,256]{1,0:T(8,128)} %get-tuple-element.10), kind=kOutput, calls=%fused_computation.34 | convolution fusion | flops 402653184 | bytes 1310720 | tf_op jit(solution)/shard_map/dot_general | solution.py:222
  (9 shorter events, 0.2 us)
Async XLA Ops:
  0.6 0.7 copy-start.2
  11.4 17.7 %collective-permute-start = (f32[4,128,256]{2,1,0:T(8,128)}, f32[4,128,256]{2,1,0:T(8,128)S(1)}, u32[]{:S(2)}, u32[]{:S(2)}) collective-permute-start(f32[4,128,256]{2,1,0:T(8,128)} %get-tuple-element.8), channel_id=1, source_target_pairs={{0,1},{1,2},{2,3},{3,4},{4,5},{5,6},{6,7},{7,8},{8,9},{9,10},{10,1... | collective-permute-start | bytes 1572872 | tf_op jit(solution)/shard_map/ppermute | solution.py:21
  15.5 16.0 %collective-permute-start.1 = (f32[4,128,256]{2,1,0:T(8,128)}, f32[4,128,256]{2,1,0:T(8,128)S(1)}, u32[]{:S(2)}, u32[]{:S(2)}) collective-permute-start(f32[4,128,256]{2,1,0:T(8,128)} %get-tuple-element.9), channel_id=1, source_target_pairs={{1,0},{2,1},{3,2},{4,3},{5,4},{6,5},{7,6},{8,7},{9,8},{10,9},{11,1... | collective-permute-start | bytes 1572872 | tf_op jit(solution)/shard_map/ppermute | solution.py:21
  31.4 1.2 %copy-start = (f32[512,256]{1,0:T(8,128)S(1)}, f32[512,256]{1,0:T(8,128)}, u32[]{:S(2)}) copy-start(f32[512,256]{1,0:T(8,128)} %param.8) | copy-start | bytes 1572868
  31.5 1.2 %copy-start.1 = (f32[512]{0:T(512)S(1)}, f32[512]{0:T(512)}, u32[]{:S(2)}) copy-start(f32[512]{0:T(512)} %param.9) | copy-start | bytes 6148
  34.1 1.4 %collective-permute-start.2 = (f32[72,256]{1,0:T(8,128)S(1)}, f32[72,256]{1,0:T(8,128)S(1)}, u32[]{:S(2)}, u32[]{:S(2)}) collective-permute-start(f32[72,256]{1,0:T(8,128)S(1)} %broadcast_select_fusion), channel_id=1, source_target_pairs={{0,4},{1,5},{2,6},{3,7},{4,0},{5,1},{6,2},{7,3},{8,12},{9,13},{10,... | collective-permute-start | bytes 221192 | tf_op jit(solution)/shard_map/ppermute | solution.py:39
  35.7 5.5 %collective-permute-start.3 = (f32[72,256]{1,0:T(8,128)S(1)}, f32[72,256]{1,0:T(8,128)S(1)}, u32[]{:S(2)}, u32[]{:S(2)}) collective-permute-start(f32[72,256]{1,0:T(8,128)S(1)} %select_add_fusion), channel_id=1, source_target_pairs={{0,1},{1,0},{2,3},{3,2},{4,5},{5,4},{6,7},{7,6},{8,9},{9,8},{10,11... | collective-permute-start | bytes 221192 | tf_op jit(solution)/shard_map/ppermute | solution.py:39
  37.0 7.9 %collective-permute-start.4 = (f32[72,256]{1,0:T(8,128)S(1)}, f32[72,256]{1,0:T(8,128)S(1)}, u32[]{:S(2)}, u32[]{:S(2)}) collective-permute-start(f32[72,256]{1,0:T(8,128)S(1)} %select_add_fusion), channel_id=1, source_target_pairs={{0,2},{1,3},{2,0},{3,1},{4,6},{5,7},{6,4},{7,5},{8,10},{9,11},{10,... | collective-permute-start | bytes 221192 | tf_op jit(solution)/shard_map/ppermute | solution.py:39
  41.2 5.3 %collective-permute-start.5 = (f32[72,256]{1,0:T(8,128)S(1)}, f32[72,256]{1,0:T(8,128)S(1)}, u32[]{:S(2)}, u32[]{:S(2)}) collective-permute-start(f32[72,256]{1,0:T(8,128)S(1)} %select_add_fusion), channel_id=1, source_target_pairs={{0,3},{1,2},{2,1},{3,0},{4,7},{5,6},{6,5},{7,4},{8,11},{9,10},{10,... | collective-permute-start | bytes 221192 | tf_op jit(solution)/shard_map/ppermute | solution.py:39
  46.5 4.2 %collective-permute-start.6 = (f32[72,256]{1,0:T(8,128)S(1)}, f32[72,256]{1,0:T(8,128)S(1)}, u32[]{:S(2)}, u32[]{:S(2)}) collective-permute-start(f32[72,256]{1,0:T(8,128)S(1)} %add_add_fusion.3), channel_id=1, source_target_pairs={{0,8},{1,9},{2,10},{3,11},{4,12},{5,13},{6,14},{7,15},{8,0},{9,1},... | collective-permute-start | bytes 221192 | tf_op jit(solution)/shard_map/ppermute | solution.py:39
  48.2 5.6 %collective-permute-start.7 = (f32[72,256]{1,0:T(8,128)S(1)}, f32[72,256]{1,0:T(8,128)S(1)}, u32[]{:S(2)}, u32[]{:S(2)}) collective-permute-start(f32[72,256]{1,0:T(8,128)S(1)} %add_add_fusion.3), channel_id=1, source_target_pairs={{0,16},{1,17},{2,18},{3,19},{4,20},{5,21},{6,22},{7,23},{8,24},{9,... | collective-permute-start | bytes 221192 | tf_op jit(solution)/shard_map/ppermute | solution.py:39
  49.9 5.3 %collective-permute-start.8 = (f32[72,256]{1,0:T(8,128)S(1)}, f32[72,256]{1,0:T(8,128)S(1)}, u32[]{:S(2)}, u32[]{:S(2)}) collective-permute-start(f32[72,256]{1,0:T(8,128)S(1)} %add_add_fusion.3), channel_id=1, source_target_pairs={{0,24},{1,25},{2,26},{3,27},{4,28},{5,29},{6,30},{7,31},{8,16},{9,... | collective-permute-start | bytes 221192 | tf_op jit(solution)/shard_map/ppermute | solution.py:39
  55.2 4.8 %collective-permute-start.10 = (f32[72,256]{1,0:T(8,128)S(1)}, f32[72,256]{1,0:T(8,128)S(1)}, u32[]{:S(2)}, u32[]{:S(2)}) collective-permute-start(f32[72,256]{1,0:T(8,128)S(1)} %add_add_fusion.2), channel_id=1, source_target_pairs={{0,64},{1,65},{2,66},{3,67},{4,68},{5,69},{6,70},{7,71},{8,72},{9,... | collective-permute-start | bytes 221192 | tf_op jit(solution)/shard_map/ppermute | solution.py:39
  58.1 4.9 %collective-permute-start.11 = (f32[72,256]{1,0:T(8,128)S(1)}, f32[72,256]{1,0:T(8,128)S(1)}, u32[]{:S(2)}, u32[]{:S(2)}) collective-permute-start(f32[72,256]{1,0:T(8,128)S(1)} %add_add_fusion.2), channel_id=1, source_target_pairs={{0,96},{1,97},{2,98},{3,99},{4,100},{5,101},{6,102},{7,103},{8,104... | collective-permute-start | bytes 221192 | tf_op jit(solution)/shard_map/ppermute | solution.py:39
  58.9 4.0 %collective-permute-start.9 = (f32[72,256]{1,0:T(8,128)S(1)}, f32[72,256]{1,0:T(8,128)S(1)}, u32[]{:S(2)}, u32[]{:S(2)}) collective-permute-start(f32[72,256]{1,0:T(8,128)S(1)} %add_add_fusion.2), channel_id=1, source_target_pairs={{0,32},{1,33},{2,34},{3,35},{4,36},{5,37},{6,38},{7,39},{8,40},{9,... | collective-permute-start | bytes 221192 | tf_op jit(solution)/shard_map/ppermute | solution.py:39
  63.0 3.8 %collective-permute-start.12 = (f32[72,256]{1,0:T(8,128)S(1)}, f32[72,256]{1,0:T(8,128)S(1)}, u32[]{:S(2)}, u32[]{:S(2)}) collective-permute-start(f32[72,256]{1,0:T(8,128)S(1)} %add_add_fusion.1), channel_id=1, source_target_pairs={{0,4},{1,5},{2,6},{3,7},{4,0},{5,1},{6,2},{7,3},{8,12},{9,13},{10,... | collective-permute-start | bytes 221192 | tf_op jit(solution)/shard_map/ppermute | solution.py:39

commit v9 on v8

--- a/solution.py
+++ b/solution.py
@@ -149,11 +149,9 @@
     )(gram)
 
 
-def aggregate_kernel(zone_ref, base_ref, weight_ref, rows_ref, before_ref, own_ref, after_ref):
+def aggregate_kernel(zone_ref, base_ref, weight_ref, rows_ref, before_ref, own_ref, after_ref, work_ref):
     owned = own_ref.shape[0]
-    tables = (before_ref, own_ref, after_ref)
-    for table in tables:
-        table[...] = jnp.zeros(table.shape, table.dtype)
+    work_ref[...] = jnp.zeros(work_ref.shape, work_ref.dtype)
     block_count, slot_count = weight_ref.shape[0], weight_ref.shape[1]
     for block in range(block_count):
         rows = rows_ref[block]
@@ -165,13 +163,10 @@
                 preferred_element_type=jnp.float32,
             )
             target = jnp.clip(zone_ref[block, slot] - base_ref[0], 0, 3 * owned - 1)
-            group = target // owned
-            local = target - group * owned
-            for number, table in enumerate(tables):
-
-                @pl.when(group == number)
-                def _(table=table, local=local, part=part):
-                    table[local] = table[local] + part
+            work_ref[target] = work_ref[target] + part
+    before_ref[...] = work_ref[:owned]
+    own_ref[...] = work_ref[owned : 2 * owned]
+    after_ref[...] = work_ref[2 * owned :]
 
 
 def aggregate(block_zone, base, weight_blocks, cell_rows, owned_blocks):
@@ -192,6 +187,7 @@
             pl.BlockSpec(memory_space=pltpu.VMEM),
             pl.BlockSpec(memory_space=pltpu.VMEM),
         ),
+        scratch_shapes=[pltpu.VMEM((3 * owned_blocks, block_size, day_count), jnp.float32)],
     )(block_zone, base, weight_blocks, cell_rows)
 
 

time: 95.1 us -> 89.1 us (0.937)
  Pallas kernels: 34 us -> 28.1 us
    pallas_call x1, Pallas kernels: 9.44 us -> 3.51 us  [aggregate(): pl.pallas_call(aggregate_kernel, out_shape=(table, table, table), in_spec...]
where the time goes in v9:
time: 89.1 us; the launch traced here: 88.8 us
  Pallas kernels  28.1 us (32%)
  waiting for transfers between devices  27.7 us (31%)
  starting transfers between devices  24.7 us (28%)
  matrix products  3.38 us (4%)
  other arithmetic  2.46 us (3%)
  local copies, waits for them, and re-layouts  1.75 us (2%)
    pallas_call x1, Pallas kernels, cholesky_with_inverse(): pl.pallas_call(functools.partial(cholesky_kernel, factor_scale=1.0 / root...  24.6 us
    ppermute x11, starting transfers between devices, exchange(): lax.ppermute(value, DEVICE_AXES, [(i, i ^ mask) for i in range(count)])  16.8 us
    ppermute x11, waiting for transfers between devices, exchange(): lax.ppermute(value, DEVICE_AXES, [(i, i ^ mask) for i in range(count)])  15.7 us
    ppermute x2, waiting for transfers between devices, shifted(): lax.ppermute(value, axis, [(source, source + steps) for source in range(i...  12 us
    ppermute x2, starting transfers between devices, shifted(): lax.ppermute(value, axis, [(source, source + steps) for source in range(i...  7.92 us
    pallas_call x1, Pallas kernels, aggregate(): pl.pallas_call(aggregate_kernel, out_shape=(table, table, table), in_spec...  3.51 us
    dot_general x1, matrix products, body(): scores = jnp.dot(anomaly, scaled_inverse.T, precision=exact_mode)  2.36 us
  transfers between devices with their start and end apart: 13, of which 10 were waited for; matrix products, arithmetic and copies ran while one was open for 0% of the time, Pallas kernels for 0%

profile of v9, /device:TPU:1, one launch (start us, length us, event | category | flops | bytes accessed | tf_op | source)
XLA Modules:
  0.0 88.8 jit_solution(3393654330399133864)
XLA Ops:
  0.6 0.0 copy-start.2
  0.6 0.7 copy-done.2
  1.3 0.7 copy.7.zone_ref
  2.0 3.5 %shard_map.68 = (f32[4,128,256]{2,1,0:T(8,128)}, f32[4,128,256]{2,1,0:T(8,128)}, f32[4,128,256]{2,1,0:T(8,128)}) custom-call(s32[16,2]{1,0:T(8,128)} %copy.7.zone_ref, s32[1]{0:T(128)} %bitcast.base_ref, bf16[16,2,128,128]{3,2,1,0:T(8,128)(2,1)} %weight_ref.1, bf16[16,128,256]{2,1,0:T(8,128)(2,1)} %bitcast.24), custom_call_target="tpu_custom_call" | custom-call | tf_op jit(solution)/shard_map/pallas_call | solution.py:176
  5.5 4.0 %collective-permute-start = (f32[4,128,256]{2,1,0:T(8,128)}, f32[4,128,256]{2,1,0:T(8,128)S(1)}, u32[]{:S(2)}, u32[]{:S(2)}) collective-permute-start(f32[4,128,256]{2,1,0:T(8,128)} %get-tuple-element.8), channel_id=1, source_target_pairs={{0,1},{1,2},{2,3},{3,4},{4,5},{5,6},{6,7},{7,8},{8,9},{9,10},{10,1... | collective-permute-start | bytes 1572872 | tf_op jit(solution)/shard_map/ppermute | solution.py:21
  9.5 3.9 %collective-permute-start.1 = (f32[4,128,256]{2,1,0:T(8,128)}, f32[4,128,256]{2,1,0:T(8,128)S(1)}, u32[]{:S(2)}, u32[]{:S(2)}) collective-permute-start(f32[4,128,256]{2,1,0:T(8,128)} %get-tuple-element.9), channel_id=1, source_target_pairs={{1,0},{2,1},{3,2},{4,3},{5,4},{6,5},{7,6},{8,7},{9,8},{10,9},{11,1... | collective-permute-start | bytes 1572872 | tf_op jit(solution)/shard_map/ppermute | solution.py:21
  13.5 0.1 pad_slice_fusion
  13.5 9.7 %collective-permute-done = f32[4,128,256]{2,1,0:T(8,128)S(1)} collective-permute-done((f32[4,128,256]{2,1,0:T(8,128)}, f32[4,128,256]{2,1,0:T(8,128)S(1)}, u32[]{:S(2)}, u32[]{:S(2)}) %collective-permute-start) | collective-permute-done | bytes 524320 | tf_op jit(solution)/shard_map/ppermute | solution.py:21
  23.2 2.3 %collective-permute-done.1 = f32[4,128,256]{2,1,0:T(8,128)S(1)} collective-permute-done((f32[4,128,256]{2,1,0:T(8,128)}, f32[4,128,256]{2,1,0:T(8,128)S(1)}, u32[]{:S(2)}, u32[]{:S(2)}) %collective-permute-start.1) | collective-permute-done | bytes 524320 | tf_op jit(solution)/shard_map/ppermute | solution.py:21
  25.5 0.0 copy-start
  25.5 0.0 copy-start.1
  25.5 1.2 %add_add_fusion = f32[4,128,256]{2,1,0:T(8,128)S(1)} fusion(f32[4,128,256]{2,1,0:T(8,128)S(1)} %collective-permute-done.1, f32[4,128,256]{2,1,0:T(8,128)} %get-tuple-element.7, f32[4,128,256]{2,1,0:T(8,128)S(1)} %collective-permute-done), kind=kLoop, calls=%fused_computation.2 | loop fusion | flops 262144 | bytes 2097152 | tf_op jit(solution)/shard_map/add | solution.py:208
  26.7 0.0 copy-done
  26.7 0.0 copy-done.1
  26.7 0.1 fusion
  26.9 1.0 %fusion.8 = f32[256,256]{1,0:T(8,128)S(1)} fusion(f32[512,256]{1,0:T(8,128)S(1)} %fusion), kind=kOutput, calls=%fused_computation.33 | convolution fusion | flops 402653184 | bytes 786432 | tf_op jit(solution)/shard_map/dot_general | solution.py:211
  27.9 0.1 copy.8
  28.1 0.1 broadcast_select_fusion
  28.2 0.5 collective-permute-start.2
  28.7 0.9 %collective-permute-done.2 = f32[72,256]{1,0:T(8,128)S(1)} collective-permute-done((f32[72,256]{1,0:T(8,128)S(1)}, f32[72,256]{1,0:T(8,128)S(1)}, u32[]{:S(2)}, u32[]{:S(2)}) %collective-permute-start.2) | collective-permute-done | bytes 73760 | tf_op jit(solution)/shard_map/ppermute | solution.py:39
  29.6 0.1 select_add_fusion
  29.7 1.4 %collective-permute-start.3 = (f32[72,256]{1,0:T(8,128)S(1)}, f32[72,256]{1,0:T(8,128)S(1)}, u32[]{:S(2)}, u32[]{:S(2)}) collective-permute-start(f32[72,256]{1,0:T(8,128)S(1)} %select_add_fusion), channel_id=1, source_target_pairs={{0,1},{1,0},{2,3},{3,2},{4,5},{5,4},{6,7},{7,6},{8,9},{9,8},{10,11... | collective-permute-start | bytes 221192 | tf_op jit(solution)/shard_map/ppermute | solution.py:39
  31.1 4.1 %collective-permute-start.4 = (f32[72,256]{1,0:T(8,128)S(1)}, f32[72,256]{1,0:T(8,128)S(1)}, u32[]{:S(2)}, u32[]{:S(2)}) collective-permute-start(f32[72,256]{1,0:T(8,128)S(1)} %select_add_fusion), channel_id=1, source_target_pairs={{0,2},{1,3},{2,0},{3,1},{4,6},{5,7},{6,4},{7,5},{8,10},{9,11},{10,... | collective-permute-start | bytes 221192 | tf_op jit(solution)/shard_map/ppermute | solution.py:39
  35.2 0.0 collective-permute-start.5
  35.2 0.0 collective-permute-done.3
  35.2 3.8 %collective-permute-done.4 = f32[72,256]{1,0:T(8,128)S(1)} collective-permute-done((f32[72,256]{1,0:T(8,128)S(1)}, f32[72,256]{1,0:T(8,128)S(1)}, u32[]{:S(2)}, u32[]{:S(2)}) %collective-permute-start.4) | collective-permute-done | bytes 73760 | tf_op jit(solution)/shard_map/ppermute | solution.py:39
  39.0 1.5 %collective-permute-done.5 = f32[72,256]{1,0:T(8,128)S(1)} collective-permute-done((f32[72,256]{1,0:T(8,128)S(1)}, f32[72,256]{1,0:T(8,128)S(1)}, u32[]{:S(2)}, u32[]{:S(2)}) %collective-permute-start.5) | collective-permute-done | bytes 73760 | tf_op jit(solution)/shard_map/ppermute | solution.py:39
  40.5 1.7 %collective-permute-start.6 = (f32[72,256]{1,0:T(8,128)S(1)}, f32[72,256]{1,0:T(8,128)S(1)}, u32[]{:S(2)}, u32[]{:S(2)}) collective-permute-start(f32[72,256]{1,0:T(8,128)S(1)} %add_add_fusion.3), channel_id=1, source_target_pairs={{0,8},{1,9},{2,10},{3,11},{4,12},{5,13},{6,14},{7,15},{8,0},{9,1},... | collective-permute-start | bytes 221192 | tf_op jit(solution)/shard_map/ppermute | solution.py:39
  42.3 1.8 %collective-permute-start.7 = (f32[72,256]{1,0:T(8,128)S(1)}, f32[72,256]{1,0:T(8,128)S(1)}, u32[]{:S(2)}, u32[]{:S(2)}) collective-permute-start(f32[72,256]{1,0:T(8,128)S(1)} %add_add_fusion.3), channel_id=1, source_target_pairs={{0,16},{1,17},{2,18},{3,19},{4,20},{5,21},{6,22},{7,23},{8,24},{9,... | collective-permute-start | bytes 221192 | tf_op jit(solution)/shard_map/ppermute | solution.py:39
  44.0 0.7 collective-permute-start.8
  44.7 0.0 collective-permute-done.6
  44.7 3.1 %collective-permute-done.7 = f32[72,256]{1,0:T(8,128)S(1)} collective-permute-done((f32[72,256]{1,0:T(8,128)S(1)}, f32[72,256]{1,0:T(8,128)S(1)}, u32[]{:S(2)}, u32[]{:S(2)}) %collective-permute-start.7) | collective-permute-done | bytes 73760 | tf_op jit(solution)/shard_map/ppermute | solution.py:39
  47.8 1.4 %collective-permute-done.8 = f32[72,256]{1,0:T(8,128)S(1)} collective-permute-done((f32[72,256]{1,0:T(8,128)S(1)}, f32[72,256]{1,0:T(8,128)S(1)}, u32[]{:S(2)}, u32[]{:S(2)}) %collective-permute-start.8) | collective-permute-done | bytes 73760 | tf_op jit(solution)/shard_map/ppermute | solution.py:39
  49.3 2.8 %collective-permute-start.10 = (f32[72,256]{1,0:T(8,128)S(1)}, f32[72,256]{1,0:T(8,128)S(1)}, u32[]{:S(2)}, u32[]{:S(2)}) collective-permute-start(f32[72,256]{1,0:T(8,128)S(1)} %add_add_fusion.2), channel_id=1, source_target_pairs={{0,64},{1,65},{2,66},{3,67},{4,68},{5,69},{6,70},{7,71},{8,72},{9,... | collective-permute-start | bytes 221192 | tf_op jit(solution)/shard_map/ppermute | solution.py:39
  52.1 0.9 collective-permute-start.11
  53.0 0.0 collective-permute-start.9
  53.0 1.1 %collective-permute-done.10 = f32[72,256]{1,0:T(8,128)S(1)} collective-permute-done((f32[72,256]{1,0:T(8,128)S(1)}, f32[72,256]{1,0:T(8,128)S(1)}, u32[]{:S(2)}, u32[]{:S(2)}) %collective-permute-start.10) | collective-permute-done | bytes 73760 | tf_op jit(solution)/shard_map/ppermute | solution.py:39
  54.1 2.9 %collective-permute-done.11 = f32[72,256]{1,0:T(8,128)S(1)} collective-permute-done((f32[72,256]{1,0:T(8,128)S(1)}, f32[72,256]{1,0:T(8,128)S(1)}, u32[]{:S(2)}, u32[]{:S(2)}) %collective-permute-start.11) | collective-permute-done | bytes 73760 | tf_op jit(solution)/shard_map/ppermute | solution.py:39
  57.0 0.0 collective-permute-done.9
  57.0 2.9 %collective-permute-start.12 = (f32[72,256]{1,0:T(8,128)S(1)}, f32[72,256]{1,0:T(8,128)S(1)}, u32[]{:S(2)}, u32[]{:S(2)}) collective-permute-start(f32[72,256]{1,0:T(8,128)S(1)} %add_add_fusion.1), channel_id=1, source_target_pairs={{0,4},{1,5},{2,6},{3,7},{4,0},{5,1},{6,2},{7,3},{8,12},{9,13},{10,... | collective-permute-start | bytes 221192 | tf_op jit(solution)/shard_map/ppermute | solution.py:39
  59.9 0.9 %collective-permute-done.12 = f32[72,256]{1,0:T(8,128)S(1)} collective-permute-done((f32[72,256]{1,0:T(8,128)S(1)}, f32[72,256]{1,0:T(8,128)S(1)}, u32[]{:S(2)}, u32[]{:S(2)}) %collective-permute-start.12) | collective-permute-done | bytes 73760 | tf_op jit(solution)/shard_map/ppermute | solution.py:39
  60.9 0.1 copy.13
  61.0 0.1 bitcast_select_fusion.1
  61.1 0.1 copy.12
  61.2 0.7 maximum_maximum_fusion.gram_ref
  61.9 24.6 %shard_map.69 = (f32[256,256]{1,0:T(8,128)}, f32[256,256]{1,0:T(8,128)}) custom-call(f32[256,256]{1,0:T(8,128)} %maximum_maximum_fusion.gram_ref), custom_call_target="tpu_custom_call" | custom-call | tf_op jit(solution)/shard_map/pallas_call | solution.py:142
  86.5 2.4 %fusion.9 = f32[512,256]{1,0:T(8,128)} fusion(f32[512,256]{1,0:T(8,128)S(1)} %fusion, f32[256,256]{1,0:T(8,128)} %get-tuple-element.10), kind=kOutput, calls=%fused_computation.34 | convolution fusion | flops 402653184 | bytes 1310720 | tf_op jit(solution)/shard_map/dot_general | solution.py:218
  (9 shorter events, 0.2 us)
Async XLA Ops:
  0.6 0.7 copy-start.2
  5.5 17.7 %collective-permute-start = (f32[4,128,256]{2,1,0:T(8,128)}, f32[4,128,256]{2,1,0:T(8,128)S(1)}, u32[]{:S(2)}, u32[]{:S(2)}) collective-permute-start(f32[4,128,256]{2,1,0:T(8,128)} %get-tuple-element.8), channel_id=1, source_target_pairs={{0,1},{1,2},{2,3},{3,4},{4,5},{5,6},{6,7},{7,8},{8,9},{9,10},{10,1... | collective-permute-start | bytes 1572872 | tf_op jit(solution)/shard_map/ppermute | solution.py:21
  9.5 16.0 %collective-permute-start.1 = (f32[4,128,256]{2,1,0:T(8,128)}, f32[4,128,256]{2,1,0:T(8,128)S(1)}, u32[]{:S(2)}, u32[]{:S(2)}) collective-permute-start(f32[4,128,256]{2,1,0:T(8,128)} %get-tuple-element.9), channel_id=1, source_target_pairs={{1,0},{2,1},{3,2},{4,3},{5,4},{6,5},{7,6},{8,7},{9,8},{10,9},{11,1... | collective-permute-start | bytes 1572872 | tf_op jit(solution)/shard_map/ppermute | solution.py:21
  25.5 1.2 %copy-start = (f32[512,256]{1,0:T(8,128)S(1)}, f32[512,256]{1,0:T(8,128)}, u32[]{:S(2)}) copy-start(f32[512,256]{1,0:T(8,128)} %param.8) | copy-start | bytes 1572868
  25.5 1.2 %copy-start.1 = (f32[512]{0:T(512)S(1)}, f32[512]{0:T(512)}, u32[]{:S(2)}) copy-start(f32[512]{0:T(512)} %param.9) | copy-start | bytes 6148
  28.2 1.4 %collective-permute-start.2 = (f32[72,256]{1,0:T(8,128)S(1)}, f32[72,256]{1,0:T(8,128)S(1)}, u32[]{:S(2)}, u32[]{:S(2)}) collective-permute-start(f32[72,256]{1,0:T(8,128)S(1)} %broadcast_select_fusion), channel_id=1, source_target_pairs={{0,4},{1,5},{2,6},{3,7},{4,0},{5,1},{6,2},{7,3},{8,12},{9,13},{10,... | collective-permute-start | bytes 221192 | tf_op jit(solution)/shard_map/ppermute | solution.py:39
  29.7 5.5 %collective-permute-start.3 = (f32[72,256]{1,0:T(8,128)S(1)}, f32[72,256]{1,0:T(8,128)S(1)}, u32[]{:S(2)}, u32[]{:S(2)}) collective-permute-start(f32[72,256]{1,0:T(8,128)S(1)} %select_add_fusion), channel_id=1, source_target_pairs={{0,1},{1,0},{2,3},{3,2},{4,5},{5,4},{6,7},{7,6},{8,9},{9,8},{10,11... | collective-permute-start | bytes 221192 | tf_op jit(solution)/shard_map/ppermute | solution.py:39
  31.1 7.9 %collective-permute-start.4 = (f32[72,256]{1,0:T(8,128)S(1)}, f32[72,256]{1,0:T(8,128)S(1)}, u32[]{:S(2)}, u32[]{:S(2)}) collective-permute-start(f32[72,256]{1,0:T(8,128)S(1)} %select_add_fusion), channel_id=1, source_target_pairs={{0,2},{1,3},{2,0},{3,1},{4,6},{5,7},{6,4},{7,5},{8,10},{9,11},{10,... | collective-permute-start | bytes 221192 | tf_op jit(solution)/shard_map/ppermute | solution.py:39
  35.2 5.3 %collective-permute-start.5 = (f32[72,256]{1,0:T(8,128)S(1)}, f32[72,256]{1,0:T(8,128)S(1)}, u32[]{:S(2)}, u32[]{:S(2)}) collective-permute-start(f32[72,256]{1,0:T(8,128)S(1)} %select_add_fusion), channel_id=1, source_target_pairs={{0,3},{1,2},{2,1},{3,0},{4,7},{5,6},{6,5},{7,4},{8,11},{9,10},{10,... | collective-permute-start | bytes 221192 | tf_op jit(solution)/shard_map/ppermute | solution.py:39
  40.5 4.2 %collective-permute-start.6 = (f32[72,256]{1,0:T(8,128)S(1)}, f32[72,256]{1,0:T(8,128)S(1)}, u32[]{:S(2)}, u32[]{:S(2)}) collective-permute-start(f32[72,256]{1,0:T(8,128)S(1)} %add_add_fusion.3), channel_id=1, source_target_pairs={{0,8},{1,9},{2,10},{3,11},{4,12},{5,13},{6,14},{7,15},{8,0},{9,1},... | collective-permute-start | bytes 221192 | tf_op jit(solution)/shard_map/ppermute | solution.py:39
  42.3 5.6 %collective-permute-start.7 = (f32[72,256]{1,0:T(8,128)S(1)}, f32[72,256]{1,0:T(8,128)S(1)}, u32[]{:S(2)}, u32[]{:S(2)}) collective-permute-start(f32[72,256]{1,0:T(8,128)S(1)} %add_add_fusion.3), channel_id=1, source_target_pairs={{0,16},{1,17},{2,18},{3,19},{4,20},{5,21},{6,22},{7,23},{8,24},{9,... | collective-permute-start | bytes 221192 | tf_op jit(solution)/shard_map/ppermute | solution.py:39
  44.0 5.3 %collective-permute-start.8 = (f32[72,256]{1,0:T(8,128)S(1)}, f32[72,256]{1,0:T(8,128)S(1)}, u32[]{:S(2)}, u32[]{:S(2)}) collective-permute-start(f32[72,256]{1,0:T(8,128)S(1)} %add_add_fusion.3), channel_id=1, source_target_pairs={{0,24},{1,25},{2,26},{3,27},{4,28},{5,29},{6,30},{7,31},{8,16},{9,... | collective-permute-start | bytes 221192 | tf_op jit(solution)/shard_map/ppermute | solution.py:39
  49.3 4.8 %collective-permute-start.10 = (f32[72,256]{1,0:T(8,128)S(1)}, f32[72,256]{1,0:T(8,128)S(1)}, u32[]{:S(2)}, u32[]{:S(2)}) collective-permute-start(f32[72,256]{1,0:T(8,128)S(1)} %add_add_fusion.2), channel_id=1, source_target_pairs={{0,64},{1,65},{2,66},{3,67},{4,68},{5,69},{6,70},{7,71},{8,72},{9,... | collective-permute-start | bytes 221192 | tf_op jit(solution)/shard_map/ppermute | solution.py:39
  52.1 4.9 %collective-permute-start.11 = (f32[72,256]{1,0:T(8,128)S(1)}, f32[72,256]{1,0:T(8,128)S(1)}, u32[]{:S(2)}, u32[]{:S(2)}) collective-permute-start(f32[72,256]{1,0:T(8,128)S(1)} %add_add_fusion.2), channel_id=1, source_target_pairs={{0,96},{1,97},{2,98},{3,99},{4,100},{5,101},{6,102},{7,103},{8,104... | collective-permute-start | bytes 221192 | tf_op jit(solution)/shard_map/ppermute | solution.py:39
  53.0 4.0 %collective-permute-start.9 = (f32[72,256]{1,0:T(8,128)S(1)}, f32[72,256]{1,0:T(8,128)S(1)}, u32[]{:S(2)}, u32[]{:S(2)}) collective-permute-start(f32[72,256]{1,0:T(8,128)S(1)} %add_add_fusion.2), channel_id=1, source_target_pairs={{0,32},{1,33},{2,34},{3,35},{4,36},{5,37},{6,38},{7,39},{8,40},{9,... | collective-permute-start | bytes 221192 | tf_op jit(solution)/shard_map/ppermute | solution.py:39
  57.0 3.8 %collective-permute-start.12 = (f32[72,256]{1,0:T(8,128)S(1)}, f32[72,256]{1,0:T(8,128)S(1)}, u32[]{:S(2)}, u32[]{:S(2)}) collective-permute-start(f32[72,256]{1,0:T(8,128)S(1)} %add_add_fusion.1), channel_id=1, source_target_pairs={{0,4},{1,5},{2,6},{3,7},{4,0},{5,1},{6,2},{7,3},{8,12},{9,13},{10,... | collective-permute-start | bytes 221192 | tf_op jit(solution)/shard_map/ppermute | solution.py:39

commit v10 on v9

--- a/solution.py
+++ b/solution.py
@@ -215,7 +215,7 @@
     total_gram = unpack_gram(all_sum(pack_gram(local_gram), device_count), day_count)
     root = math.sqrt(anomaly.shape[0] * device_count)
     factor, scaled_inverse = cholesky_with_inverse(total_gram, root)
-    scores = jnp.dot(anomaly, scaled_inverse.T, precision=exact_mode)
+    scores = jnp.dot(anomaly, scaled_inverse.T, precision=lax.Precision.HIGH)
     return (scores, factor)
 
 

time: 89.1 us -> 88.9 us (level)
  no operation moved by 1% of the time
where the time goes in v10:
time: 88.9 us; the launch traced here: 88.6 us
  Pallas kernels  28.1 us (32%)
  waiting for transfers between devices  27.7 us (31%)
  starting transfers between devices  24.7 us (28%)
  matrix products  3.18 us (4%)
  other arithmetic  2.46 us (3%)
  local copies, waits for them, and re-layouts  1.75 us (2%)
    pallas_call x1, Pallas kernels, cholesky_with_inverse(): pl.pallas_call(functools.partial(cholesky_kernel, factor_scale=1.0 / root...  24.6 us
    ppermute x11, starting transfers between devices, exchange(): lax.ppermute(value, DEVICE_AXES, [(i, i ^ mask) for i in range(count)])  16.8 us
    ppermute x11, waiting for transfers between devices, exchange(): lax.ppermute(value, DEVICE_AXES, [(i, i ^ mask) for i in range(count)])  15.7 us
    ppermute x2, waiting for transfers between devices, shifted(): lax.ppermute(value, axis, [(source, source + steps) for source in range(i...  12 us
    ppermute x2, starting transfers between devices, shifted(): lax.ppermute(value, axis, [(source, source + steps) for source in range(i...  7.92 us
    pallas_call x1, Pallas kernels, aggregate(): pl.pallas_call(aggregate_kernel, out_shape=(table, table, table), in_spec...  3.51 us
    dot_general x1, matrix products, body(): scores = jnp.dot(anomaly, scaled_inverse.T, precision=lax.Precision.HIGH)  2.16 us
  transfers between devices with their start and end apart: 13, of which 10 were waited for; matrix products, arithmetic and copies ran while one was open for 0% of the time, Pallas kernels for 0%

profile of v10, /device:TPU:1, one launch (start us, length us, event | category | flops | bytes accessed | tf_op | source)
XLA Modules:
  0.0 88.6 jit_solution(8818673329690499214)
XLA Ops:
  0.6 0.0 copy-start.2
  0.6 0.7 copy-done.2
  1.3 0.7 copy.7.zone_ref
  2.0 3.5 %shard_map.68 = (f32[4,128,256]{2,1,0:T(8,128)}, f32[4,128,256]{2,1,0:T(8,128)}, f32[4,128,256]{2,1,0:T(8,128)}) custom-call(s32[16,2]{1,0:T(8,128)} %copy.7.zone_ref, s32[1]{0:T(128)} %bitcast.base_ref, bf16[16,2,128,128]{3,2,1,0:T(8,128)(2,1)} %weight_ref.1, bf16[16,128,256]{2,1,0:T(8,128)(2,1)} %bitcast.24), custom_call_target="tpu_custom_call" | custom-call | tf_op jit(solution)/shard_map/pallas_call | solution.py:176
  5.5 4.0 %collective-permute-start = (f32[4,128,256]{2,1,0:T(8,128)}, f32[4,128,256]{2,1,0:T(8,128)S(1)}, u32[]{:S(2)}, u32[]{:S(2)}) collective-permute-start(f32[4,128,256]{2,1,0:T(8,128)} %get-tuple-element.8), channel_id=1, source_target_pairs={{0,1},{1,2},{2,3},{3,4},{4,5},{5,6},{6,7},{7,8},{8,9},{9,10},{10,1... | collective-permute-start | bytes 1572872 | tf_op jit(solution)/shard_map/ppermute | solution.py:21
  9.5 3.9 %collective-permute-start.1 = (f32[4,128,256]{2,1,0:T(8,128)}, f32[4,128,256]{2,1,0:T(8,128)S(1)}, u32[]{:S(2)}, u32[]{:S(2)}) collective-permute-start(f32[4,128,256]{2,1,0:T(8,128)} %get-tuple-element.9), channel_id=1, source_target_pairs={{1,0},{2,1},{3,2},{4,3},{5,4},{6,5},{7,6},{8,7},{9,8},{10,9},{11,1... | collective-permute-start | bytes 1572872 | tf_op jit(solution)/shard_map/ppermute | solution.py:21
  13.5 0.1 pad_slice_fusion
  13.5 9.7 %collective-permute-done = f32[4,128,256]{2,1,0:T(8,128)S(1)} collective-permute-done((f32[4,128,256]{2,1,0:T(8,128)}, f32[4,128,256]{2,1,0:T(8,128)S(1)}, u32[]{:S(2)}, u32[]{:S(2)}) %collective-permute-start) | collective-permute-done | bytes 524320 | tf_op jit(solution)/shard_map/ppermute | solution.py:21
  23.2 2.3 %collective-permute-done.1 = f32[4,128,256]{2,1,0:T(8,128)S(1)} collective-permute-done((f32[4,128,256]{2,1,0:T(8,128)}, f32[4,128,256]{2,1,0:T(8,128)S(1)}, u32[]{:S(2)}, u32[]{:S(2)}) %collective-permute-start.1) | collective-permute-done | bytes 524320 | tf_op jit(solution)/shard_map/ppermute | solution.py:21
  25.5 0.0 copy-start
  25.5 0.0 copy-start.1
  25.5 1.2 %add_add_fusion = f32[4,128,256]{2,1,0:T(8,128)S(1)} fusion(f32[4,128,256]{2,1,0:T(8,128)S(1)} %collective-permute-done.1, f32[4,128,256]{2,1,0:T(8,128)} %get-tuple-element.7, f32[4,128,256]{2,1,0:T(8,128)S(1)} %collective-permute-done), kind=kLoop, calls=%fused_computation.2 | loop fusion | flops 262144 | bytes 2097152 | tf_op jit(solution)/shard_map/add | solution.py:208
  26.7 0.0 copy-done
  26.7 0.0 copy-done.1
  26.7 0.1 fusion
  26.9 1.0 %fusion.8 = f32[256,256]{1,0:T(8,128)S(1)} fusion(f32[512,256]{1,0:T(8,128)S(1)} %fusion), kind=kOutput, calls=%fused_computation.33 | convolution fusion | flops 402653184 | bytes 786432 | tf_op jit(solution)/shard_map/dot_general | solution.py:211
  27.9 0.1 copy.8
  28.1 0.1 broadcast_select_fusion
  28.2 0.5 collective-permute-start.2
  28.7 0.9 %collective-permute-done.2 = f32[72,256]{1,0:T(8,128)S(1)} collective-permute-done((f32[72,256]{1,0:T(8,128)S(1)}, f32[72,256]{1,0:T(8,128)S(1)}, u32[]{:S(2)}, u32[]{:S(2)}) %collective-permute-start.2) | collective-permute-done | bytes 73760 | tf_op jit(solution)/shard_map/ppermute | solution.py:39
  29.6 0.1 select_add_fusion
  29.7 1.4 %collective-permute-start.3 = (f32[72,256]{1,0:T(8,128)S(1)}, f32[72,256]{1,0:T(8,128)S(1)}, u32[]{:S(2)}, u32[]{:S(2)}) collective-permute-start(f32[72,256]{1,0:T(8,128)S(1)} %select_add_fusion), channel_id=1, source_target_pairs={{0,1},{1,0},{2,3},{3,2},{4,5},{5,4},{6,7},{7,6},{8,9},{9,8},{10,11... | collective-permute-start | bytes 221192 | tf_op jit(solution)/shard_map/ppermute | solution.py:39
  31.1 4.1 %collective-permute-start.4 = (f32[72,256]{1,0:T(8,128)S(1)}, f32[72,256]{1,0:T(8,128)S(1)}, u32[]{:S(2)}, u32[]{:S(2)}) collective-permute-start(f32[72,256]{1,0:T(8,128)S(1)} %select_add_fusion), channel_id=1, source_target_pairs={{0,2},{1,3},{2,0},{3,1},{4,6},{5,7},{6,4},{7,5},{8,10},{9,11},{10,... | collective-permute-start | bytes 221192 | tf_op jit(solution)/shard_map/ppermute | solution.py:39
  35.2 0.0 collective-permute-start.5
  35.2 0.0 collective-permute-done.3
  35.2 3.8 %collective-permute-done.4 = f32[72,256]{1,0:T(8,128)S(1)} collective-permute-done((f32[72,256]{1,0:T(8,128)S(1)}, f32[72,256]{1,0:T(8,128)S(1)}, u32[]{:S(2)}, u32[]{:S(2)}) %collective-permute-start.4) | collective-permute-done | bytes 73760 | tf_op jit(solution)/shard_map/ppermute | solution.py:39
  39.0 1.5 %collective-permute-done.5 = f32[72,256]{1,0:T(8,128)S(1)} collective-permute-done((f32[72,256]{1,0:T(8,128)S(1)}, f32[72,256]{1,0:T(8,128)S(1)}, u32[]{:S(2)}, u32[]{:S(2)}) %collective-permute-start.5) | collective-permute-done | bytes 73760 | tf_op jit(solution)/shard_map/ppermute | solution.py:39
  40.5 1.7 %collective-permute-start.6 = (f32[72,256]{1,0:T(8,128)S(1)}, f32[72,256]{1,0:T(8,128)S(1)}, u32[]{:S(2)}, u32[]{:S(2)}) collective-permute-start(f32[72,256]{1,0:T(8,128)S(1)} %add_add_fusion.3), channel_id=1, source_target_pairs={{0,8},{1,9},{2,10},{3,11},{4,12},{5,13},{6,14},{7,15},{8,0},{9,1},... | collective-permute-start | bytes 221192 | tf_op jit(solution)/shard_map/ppermute | solution.py:39
  42.3 1.8 %collective-permute-start.7 = (f32[72,256]{1,0:T(8,128)S(1)}, f32[72,256]{1,0:T(8,128)S(1)}, u32[]{:S(2)}, u32[]{:S(2)}) collective-permute-start(f32[72,256]{1,0:T(8,128)S(1)} %add_add_fusion.3), channel_id=1, source_target_pairs={{0,16},{1,17},{2,18},{3,19},{4,20},{5,21},{6,22},{7,23},{8,24},{9,... | collective-permute-start | bytes 221192 | tf_op jit(solution)/shard_map/ppermute | solution.py:39
  44.0 0.7 collective-permute-start.8
  44.7 0.0 collective-permute-done.6
  44.7 3.1 %collective-permute-done.7 = f32[72,256]{1,0:T(8,128)S(1)} collective-permute-done((f32[72,256]{1,0:T(8,128)S(1)}, f32[72,256]{1,0:T(8,128)S(1)}, u32[]{:S(2)}, u32[]{:S(2)}) %collective-permute-start.7) | collective-permute-done | bytes 73760 | tf_op jit(solution)/shard_map/ppermute | solution.py:39
  47.8 1.4 %collective-permute-done.8 = f32[72,256]{1,0:T(8,128)S(1)} collective-permute-done((f32[72,256]{1,0:T(8,128)S(1)}, f32[72,256]{1,0:T(8,128)S(1)}, u32[]{:S(2)}, u32[]{:S(2)}) %collective-permute-start.8) | collective-permute-done | bytes 73760 | tf_op jit(solution)/shard_map/ppermute | solution.py:39
  49.3 2.8 %collective-permute-start.10 = (f32[72,256]{1,0:T(8,128)S(1)}, f32[72,256]{1,0:T(8,128)S(1)}, u32[]{:S(2)}, u32[]{:S(2)}) collective-permute-start(f32[72,256]{1,0:T(8,128)S(1)} %add_add_fusion.2), channel_id=1, source_target_pairs={{0,64},{1,65},{2,66},{3,67},{4,68},{5,69},{6,70},{7,71},{8,72},{9,... | collective-permute-start | bytes 221192 | tf_op jit(solution)/shard_map/ppermute | solution.py:39
  52.1 0.9 collective-permute-start.11
  53.0 0.0 collective-permute-start.9
  53.0 1.1 %collective-permute-done.10 = f32[72,256]{1,0:T(8,128)S(1)} collective-permute-done((f32[72,256]{1,0:T(8,128)S(1)}, f32[72,256]{1,0:T(8,128)S(1)}, u32[]{:S(2)}, u32[]{:S(2)}) %collective-permute-start.10) | collective-permute-done | bytes 73760 | tf_op jit(solution)/shard_map/ppermute | solution.py:39
  54.1 2.9 %collective-permute-done.11 = f32[72,256]{1,0:T(8,128)S(1)} collective-permute-done((f32[72,256]{1,0:T(8,128)S(1)}, f32[72,256]{1,0:T(8,128)S(1)}, u32[]{:S(2)}, u32[]{:S(2)}) %collective-permute-start.11) | collective-permute-done | bytes 73760 | tf_op jit(solution)/shard_map/ppermute | solution.py:39
  57.0 0.0 collective-permute-done.9
  57.0 2.9 %collective-permute-start.12 = (f32[72,256]{1,0:T(8,128)S(1)}, f32[72,256]{1,0:T(8,128)S(1)}, u32[]{:S(2)}, u32[]{:S(2)}) collective-permute-start(f32[72,256]{1,0:T(8,128)S(1)} %add_add_fusion.1), channel_id=1, source_target_pairs={{0,4},{1,5},{2,6},{3,7},{4,0},{5,1},{6,2},{7,3},{8,12},{9,13},{10,... | collective-permute-start | bytes 221192 | tf_op jit(solution)/shard_map/ppermute | solution.py:39
  59.9 0.9 %collective-permute-done.12 = f32[72,256]{1,0:T(8,128)S(1)} collective-permute-done((f32[72,256]{1,0:T(8,128)S(1)}, f32[72,256]{1,0:T(8,128)S(1)}, u32[]{:S(2)}, u32[]{:S(2)}) %collective-permute-start.12) | collective-permute-done | bytes 73760 | tf_op jit(solution)/shard_map/ppermute | solution.py:39
  60.9 0.1 copy.13
  61.0 0.1 bitcast_select_fusion.1
  61.1 0.1 copy.12
  61.2 0.7 maximum_maximum_fusion.gram_ref
  61.9 24.6 %shard_map.69 = (f32[256,256]{1,0:T(8,128)}, f32[256,256]{1,0:T(8,128)}) custom-call(f32[256,256]{1,0:T(8,128)} %maximum_maximum_fusion.gram_ref), custom_call_target="tpu_custom_call" | custom-call | tf_op jit(solution)/shard_map/pallas_call | solution.py:142
  86.5 2.2 %fusion.9 = f32[512,256]{1,0:T(8,128)} fusion(f32[512,256]{1,0:T(8,128)S(1)} %fusion, f32[256,256]{1,0:T(8,128)} %get-tuple-element.10), kind=kOutput, calls=%fused_computation.34 | convolution fusion | flops 201326592 | bytes 1310720 | tf_op jit(solution)/shard_map/dot_general | solution.py:218
  (9 shorter events, 0.2 us)
Async XLA Ops:
  0.6 0.7 copy-start.2
  5.5 17.7 %collective-permute-start = (f32[4,128,256]{2,1,0:T(8,128)}, f32[4,128,256]{2,1,0:T(8,128)S(1)}, u32[]{:S(2)}, u32[]{:S(2)}) collective-permute-start(f32[4,128,256]{2,1,0:T(8,128)} %get-tuple-element.8), channel_id=1, source_target_pairs={{0,1},{1,2},{2,3},{3,4},{4,5},{5,6},{6,7},{7,8},{8,9},{9,10},{10,1... | collective-permute-start | bytes 1572872 | tf_op jit(solution)/shard_map/ppermute | solution.py:21
  9.5 16.0 %collective-permute-start.1 = (f32[4,128,256]{2,1,0:T(8,128)}, f32[4,128,256]{2,1,0:T(8,128)S(1)}, u32[]{:S(2)}, u32[]{:S(2)}) collective-permute-start(f32[4,128,256]{2,1,0:T(8,128)} %get-tuple-element.9), channel_id=1, source_target_pairs={{1,0},{2,1},{3,2},{4,3},{5,4},{6,5},{7,6},{8,7},{9,8},{10,9},{11,1... | collective-permute-start | bytes 1572872 | tf_op jit(solution)/shard_map/ppermute | solution.py:21
  25.5 1.2 %copy-start = (f32[512,256]{1,0:T(8,128)S(1)}, f32[512,256]{1,0:T(8,128)}, u32[]{:S(2)}) copy-start(f32[512,256]{1,0:T(8,128)} %param.8) | copy-start | bytes 1572868
  25.5 1.2 %copy-start.1 = (f32[512]{0:T(512)S(1)}, f32[512]{0:T(512)}, u32[]{:S(2)}) copy-start(f32[512]{0:T(512)} %param.9) | copy-start | bytes 6148
  28.2 1.4 %collective-permute-start.2 = (f32[72,256]{1,0:T(8,128)S(1)}, f32[72,256]{1,0:T(8,128)S(1)}, u32[]{:S(2)}, u32[]{:S(2)}) collective-permute-start(f32[72,256]{1,0:T(8,128)S(1)} %broadcast_select_fusion), channel_id=1, source_target_pairs={{0,4},{1,5},{2,6},{3,7},{4,0},{5,1},{6,2},{7,3},{8,12},{9,13},{10,... | collective-permute-start | bytes 221192 | tf_op jit(solution)/shard_map/ppermute | solution.py:39
  29.7 5.5 %collective-permute-start.3 = (f32[72,256]{1,0:T(8,128)S(1)}, f32[72,256]{1,0:T(8,128)S(1)}, u32[]{:S(2)}, u32[]{:S(2)}) collective-permute-start(f32[72,256]{1,0:T(8,128)S(1)} %select_add_fusion), channel_id=1, source_target_pairs={{0,1},{1,0},{2,3},{3,2},{4,5},{5,4},{6,7},{7,6},{8,9},{9,8},{10,11... | collective-permute-start | bytes 221192 | tf_op jit(solution)/shard_map/ppermute | solution.py:39
  31.1 7.9 %collective-permute-start.4 = (f32[72,256]{1,0:T(8,128)S(1)}, f32[72,256]{1,0:T(8,128)S(1)}, u32[]{:S(2)}, u32[]{:S(2)}) collective-permute-start(f32[72,256]{1,0:T(8,128)S(1)} %select_add_fusion), channel_id=1, source_target_pairs={{0,2},{1,3},{2,0},{3,1},{4,6},{5,7},{6,4},{7,5},{8,10},{9,11},{10,... | collective-permute-start | bytes 221192 | tf_op jit(solution)/shard_map/ppermute | solution.py:39
  35.2 5.3 %collective-permute-start.5 = (f32[72,256]{1,0:T(8,128)S(1)}, f32[72,256]{1,0:T(8,128)S(1)}, u32[]{:S(2)}, u32[]{:S(2)}) collective-permute-start(f32[72,256]{1,0:T(8,128)S(1)} %select_add_fusion), channel_id=1, source_target_pairs={{0,3},{1,2},{2,1},{3,0},{4,7},{5,6},{6,5},{7,4},{8,11},{9,10},{10,... | collective-permute-start | bytes 221192 | tf_op jit(solution)/shard_map/ppermute | solution.py:39
  40.5 4.2 %collective-permute-start.6 = (f32[72,256]{1,0:T(8,128)S(1)}, f32[72,256]{1,0:T(8,128)S(1)}, u32[]{:S(2)}, u32[]{:S(2)}) collective-permute-start(f32[72,256]{1,0:T(8,128)S(1)} %add_add_fusion.3), channel_id=1, source_target_pairs={{0,8},{1,9},{2,10},{3,11},{4,12},{5,13},{6,14},{7,15},{8,0},{9,1},... | collective-permute-start | bytes 221192 | tf_op jit(solution)/shard_map/ppermute | solution.py:39
  42.3 5.6 %collective-permute-start.7 = (f32[72,256]{1,0:T(8,128)S(1)}, f32[72,256]{1,0:T(8,128)S(1)}, u32[]{:S(2)}, u32[]{:S(2)}) collective-permute-start(f32[72,256]{1,0:T(8,128)S(1)} %add_add_fusion.3), channel_id=1, source_target_pairs={{0,16},{1,17},{2,18},{3,19},{4,20},{5,21},{6,22},{7,23},{8,24},{9,... | collective-permute-start | bytes 221192 | tf_op jit(solution)/shard_map/ppermute | solution.py:39
  44.0 5.3 %collective-permute-start.8 = (f32[72,256]{1,0:T(8,128)S(1)}, f32[72,256]{1,0:T(8,128)S(1)}, u32[]{:S(2)}, u32[]{:S(2)}) collective-permute-start(f32[72,256]{1,0:T(8,128)S(1)} %add_add_fusion.3), channel_id=1, source_target_pairs={{0,24},{1,25},{2,26},{3,27},{4,28},{5,29},{6,30},{7,31},{8,16},{9,... | collective-permute-start | bytes 221192 | tf_op jit(solution)/shard_map/ppermute | solution.py:39
  49.3 4.8 %collective-permute-start.10 = (f32[72,256]{1,0:T(8,128)S(1)}, f32[72,256]{1,0:T(8,128)S(1)}, u32[]{:S(2)}, u32[]{:S(2)}) collective-permute-start(f32[72,256]{1,0:T(8,128)S(1)} %add_add_fusion.2), channel_id=1, source_target_pairs={{0,64},{1,65},{2,66},{3,67},{4,68},{5,69},{6,70},{7,71},{8,72},{9,... | collective-permute-start | bytes 221192 | tf_op jit(solution)/shard_map/ppermute | solution.py:39
  52.1 4.9 %collective-permute-start.11 = (f32[72,256]{1,0:T(8,128)S(1)}, f32[72,256]{1,0:T(8,128)S(1)}, u32[]{:S(2)}, u32[]{:S(2)}) collective-permute-start(f32[72,256]{1,0:T(8,128)S(1)} %add_add_fusion.2), channel_id=1, source_target_pairs={{0,96},{1,97},{2,98},{3,99},{4,100},{5,101},{6,102},{7,103},{8,104... | collective-permute-start | bytes 221192 | tf_op jit(solution)/shard_map/ppermute | solution.py:39
  53.0 4.0 %collective-permute-start.9 = (f32[72,256]{1,0:T(8,128)S(1)}, f32[72,256]{1,0:T(8,128)S(1)}, u32[]{:S(2)}, u32[]{:S(2)}) collective-permute-start(f32[72,256]{1,0:T(8,128)S(1)} %add_add_fusion.2), channel_id=1, source_target_pairs={{0,32},{1,33},{2,34},{3,35},{4,36},{5,37},{6,38},{7,39},{8,40},{9,... | collective-permute-start | bytes 221192 | tf_op jit(solution)/shard_map/ppermute | solution.py:39
  57.0 3.8 %collective-permute-start.12 = (f32[72,256]{1,0:T(8,128)S(1)}, f32[72,256]{1,0:T(8,128)S(1)}, u32[]{:S(2)}, u32[]{:S(2)}) collective-permute-start(f32[72,256]{1,0:T(8,128)S(1)} %add_add_fusion.1), channel_id=1, source_target_pairs={{0,4},{1,5},{2,6},{3,7},{4,0},{5,1},{6,2},{7,3},{8,12},{9,13},{10,... | collective-permute-start | bytes 221192 | tf_op jit(solution)/shard_map/ppermute | solution.py:39

commit v11 on v10

--- a/solution.py
+++ b/solution.py
@@ -95,7 +95,7 @@
     return jnp.concatenate([top, bottom], axis=0)
 
 
-def cholesky_kernel(gram_ref, upper_ref, inverse_ref, work_ref, *, factor_scale, inverse_scale):
+def cholesky_kernel(gram_ref, anomaly_ref, upper_ref, scores_ref, inverse_ref, work_ref, *, factor_scale, inverse_scale):
     size = gram_ref.shape[0]
     work_ref[...] = gram_ref[...]
     rows = lax.broadcasted_iota(jnp.int32, (size, size), 0)
@@ -135,18 +135,20 @@
         col1 = (size // 2) * (part // 2 + 1)
         for first in range(row0, row0 + quarter, PANEL):
             panel(first, row0, col0, col1)
-
-
-def cholesky_with_inverse(gram, root):
+    scores_ref[...] = lax.dot_general(
+        anomaly_ref[...], inverse_ref[...], (((1,), (1,)), ((), ())),
+        precision=exact_mode, preferred_element_type=jnp.float32,
+    )
+
+
+def cholesky_with_inverse(gram, anomaly, root):
     size = gram.shape[0]
+    square = jax.ShapeDtypeStruct((size, size), jnp.float32)
     return pl.pallas_call(
         functools.partial(cholesky_kernel, factor_scale=1.0 / root, inverse_scale=root),
-        out_shape=(
-            jax.ShapeDtypeStruct((size, size), jnp.float32),
-            jax.ShapeDtypeStruct((size, size), jnp.float32),
-        ),
-        scratch_shapes=[pltpu.VMEM((size, size), jnp.float32)],
-    )(gram)
+        out_shape=(square, jax.ShapeDtypeStruct(anomaly.shape, jnp.float32)),
+        scratch_shapes=[pltpu.VMEM((size, size), jnp.float32), pltpu.VMEM((size, size), jnp.float32)],
+    )(gram, anomaly)
 
 
 def aggregate_kernel(zone_ref, base_ref, weight_ref, rows_ref, before_ref, own_ref, after_ref, work_ref):
@@ -214,8 +216,7 @@
     local_gram = 0.5 * (local_gram + local_gram.T)
     total_gram = unpack_gram(all_sum(pack_gram(local_gram), device_count), day_count)
     root = math.sqrt(anomaly.shape[0] * device_count)
-    factor, scaled_inverse = cholesky_with_inverse(total_gram, root)
-    scores = jnp.dot(anomaly, scaled_inverse.T, precision=lax.Precision.HIGH)
+    factor, scores = cholesky_with_inverse(total_gram, anomaly, root)
     return (scores, factor)
 
 

time: 88.9 us -> 87.7 us (0.987)
  matrix products: 3.18 us -> 1.02 us
  Pallas kernels: 28.1 us -> 29 us
    dot_general x1 -> x0, matrix products: 2.16 us -> none  [body(): scores = jnp.dot(anomaly, scaled_inverse.T, precision=lax.Precision.HIGH)]
    pallas_call x1, Pallas kernels: 24.6 us -> 25.5 us  [cholesky_with_inverse(): pl.pallas_call(functools.partial(cholesky_kernel, factor_scale=1.0 / root...]
where the time goes in v11:
time: 87.7 us; the launch traced here: 87.4 us
  Pallas kernels  29 us (33%)
  waiting for transfers between devices  27.7 us (32%)
  starting transfers between devices  24.7 us (28%)
  other arithmetic  2.46 us (3%)
  local copies, waits for them, and re-layouts  1.75 us (2%)
  matrix products  1.02 us (1%)
    pallas_call x1, Pallas kernels, cholesky_with_inverse(): pl.pallas_call(functools.partial(cholesky_kernel, factor_scale=1.0 / root...  25.5 us
    ppermute x11, starting transfers between devices, exchange(): lax.ppermute(value, DEVICE_AXES, [(i, i ^ mask) for i in range(count)])  16.8 us
    ppermute x11, waiting for transfers between devices, exchange(): lax.ppermute(value, DEVICE_AXES, [(i, i ^ mask) for i in range(count)])  15.7 us
    ppermute x2, waiting for transfers between devices, shifted(): lax.ppermute(value, axis, [(source, source + steps) for source in range(i...  12 us
    ppermute x2, starting transfers between devices, shifted(): lax.ppermute(value, axis, [(source, source + steps) for source in range(i...  7.93 us
    pallas_call x1, Pallas kernels, aggregate(): pl.pallas_call(aggregate_kernel, out_shape=(table, table, table), in_spec...  3.5 us
  transfers between devices with their start and end apart: 13, of which 10 were waited for; matrix products, arithmetic and copies ran while one was open for 0% of the time, Pallas kernels for 0%

profile of v11, /device:TPU:1, one launch (start us, length us, event | category | flops | bytes accessed | tf_op | source)
XLA Modules:
  0.0 87.4 jit_solution(8718268132409124474)
XLA Ops:
  0.6 0.0 copy-start.3
  0.6 0.7 copy-done.3
  1.3 0.7 copy.7.zone_ref
  2.0 3.5 %shard_map.68 = (f32[4,128,256]{2,1,0:T(8,128)}, f32[4,128,256]{2,1,0:T(8,128)}, f32[4,128,256]{2,1,0:T(8,128)}) custom-call(s32[16,2]{1,0:T(8,128)} %copy.7.zone_ref, s32[1]{0:T(128)} %bitcast.base_ref, bf16[16,2,128,128]{3,2,1,0:T(8,128)(2,1)} %weight_ref.1, bf16[16,128,256]{2,1,0:T(8,128)(2,1)} %bitcast.22), custom_call_target="tpu_custom_call" | custom-call | tf_op jit(solution)/shard_map/pallas_call | solution.py:178
  5.5 4.0 %collective-permute-start = (f32[4,128,256]{2,1,0:T(8,128)}, f32[4,128,256]{2,1,0:T(8,128)S(1)}, u32[]{:S(2)}, u32[]{:S(2)}) collective-permute-start(f32[4,128,256]{2,1,0:T(8,128)} %get-tuple-element.8), channel_id=1, source_target_pairs={{0,1},{1,2},{2,3},{3,4},{4,5},{5,6},{6,7},{7,8},{8,9},{9,10},{10,1... | collective-permute-start | bytes 1572872 | tf_op jit(solution)/shard_map/ppermute | solution.py:21
  9.5 3.9 %collective-permute-start.1 = (f32[4,128,256]{2,1,0:T(8,128)}, f32[4,128,256]{2,1,0:T(8,128)S(1)}, u32[]{:S(2)}, u32[]{:S(2)}) collective-permute-start(f32[4,128,256]{2,1,0:T(8,128)} %get-tuple-element.9), channel_id=1, source_target_pairs={{1,0},{2,1},{3,2},{4,3},{5,4},{6,5},{7,6},{8,7},{9,8},{10,9},{11,1... | collective-permute-start | bytes 1572872 | tf_op jit(solution)/shard_map/ppermute | solution.py:21
  13.5 0.1 pad_slice_fusion
  13.5 9.7 %collective-permute-done = f32[4,128,256]{2,1,0:T(8,128)S(1)} collective-permute-done((f32[4,128,256]{2,1,0:T(8,128)}, f32[4,128,256]{2,1,0:T(8,128)S(1)}, u32[]{:S(2)}, u32[]{:S(2)}) %collective-permute-start) | collective-permute-done | bytes 524320 | tf_op jit(solution)/shard_map/ppermute | solution.py:21
  23.2 2.3 %collective-permute-done.1 = f32[4,128,256]{2,1,0:T(8,128)S(1)} collective-permute-done((f32[4,128,256]{2,1,0:T(8,128)}, f32[4,128,256]{2,1,0:T(8,128)S(1)}, u32[]{:S(2)}, u32[]{:S(2)}) %collective-permute-start.1) | collective-permute-done | bytes 524320 | tf_op jit(solution)/shard_map/ppermute | solution.py:21
  25.5 0.0 copy-start.1
  25.5 0.0 copy-start.2
  25.5 1.2 %add_add_fusion = f32[4,128,256]{2,1,0:T(8,128)S(1)} fusion(f32[4,128,256]{2,1,0:T(8,128)S(1)} %collective-permute-done.1, f32[4,128,256]{2,1,0:T(8,128)} %get-tuple-element.7, f32[4,128,256]{2,1,0:T(8,128)S(1)} %collective-permute-done), kind=kLoop, calls=%fused_computation.2 | loop fusion | flops 262144 | bytes 2097152 | tf_op jit(solution)/shard_map/add | solution.py:210
  26.7 0.0 copy-done.1
  26.7 0.0 copy-done.2
  26.7 0.1 fusion.anomaly_ref
  26.9 0.0 copy-start
  26.9 1.0 %fusion.8 = f32[256,256]{1,0:T(8,128)S(1)} fusion(f32[512,256]{1,0:T(8,128)S(1)} %fusion.anomaly_ref), kind=kOutput, calls=%fused_computation.33 | convolution fusion | flops 402653184 | bytes 786432 | tf_op jit(solution)/shard_map/dot_general | solution.py:213
  27.9 0.0 copy-done
  27.9 0.1 copy.8
  28.1 0.1 broadcast_select_fusion
  28.2 0.5 collective-permute-start.2
  28.8 0.9 %collective-permute-done.2 = f32[72,256]{1,0:T(8,128)S(1)} collective-permute-done((f32[72,256]{1,0:T(8,128)S(1)}, f32[72,256]{1,0:T(8,128)S(1)}, u32[]{:S(2)}, u32[]{:S(2)}) %collective-permute-start.2) | collective-permute-done | bytes 73760 | tf_op jit(solution)/shard_map/ppermute | solution.py:39
  29.7 0.1 select_add_fusion
  29.7 1.4 %collective-permute-start.3 = (f32[72,256]{1,0:T(8,128)S(1)}, f32[72,256]{1,0:T(8,128)S(1)}, u32[]{:S(2)}, u32[]{:S(2)}) collective-permute-start(f32[72,256]{1,0:T(8,128)S(1)} %select_add_fusion), channel_id=1, source_target_pairs={{0,1},{1,0},{2,3},{3,2},{4,5},{5,4},{6,7},{7,6},{8,9},{9,8},{10,11... | collective-permute-start | bytes 221192 | tf_op jit(solution)/shard_map/ppermute | solution.py:39
  31.1 4.1 %collective-permute-start.4 = (f32[72,256]{1,0:T(8,128)S(1)}, f32[72,256]{1,0:T(8,128)S(1)}, u32[]{:S(2)}, u32[]{:S(2)}) collective-permute-start(f32[72,256]{1,0:T(8,128)S(1)} %select_add_fusion), channel_id=1, source_target_pairs={{0,2},{1,3},{2,0},{3,1},{4,6},{5,7},{6,4},{7,5},{8,10},{9,11},{10,... | collective-permute-start | bytes 221192 | tf_op jit(solution)/shard_map/ppermute | solution.py:39
  35.2 0.0 collective-permute-start.5
  35.3 0.0 collective-permute-done.3
  35.3 3.8 %collective-permute-done.4 = f32[72,256]{1,0:T(8,128)S(1)} collective-permute-done((f32[72,256]{1,0:T(8,128)S(1)}, f32[72,256]{1,0:T(8,128)S(1)}, u32[]{:S(2)}, u32[]{:S(2)}) %collective-permute-start.4) | collective-permute-done | bytes 73760 | tf_op jit(solution)/shard_map/ppermute | solution.py:39
  39.0 1.5 %collective-permute-done.5 = f32[72,256]{1,0:T(8,128)S(1)} collective-permute-done((f32[72,256]{1,0:T(8,128)S(1)}, f32[72,256]{1,0:T(8,128)S(1)}, u32[]{:S(2)}, u32[]{:S(2)}) %collective-permute-start.5) | collective-permute-done | bytes 73760 | tf_op jit(solution)/shard_map/ppermute | solution.py:39
  40.6 1.7 %collective-permute-start.6 = (f32[72,256]{1,0:T(8,128)S(1)}, f32[72,256]{1,0:T(8,128)S(1)}, u32[]{:S(2)}, u32[]{:S(2)}) collective-permute-start(f32[72,256]{1,0:T(8,128)S(1)} %add_add_fusion.3), channel_id=1, source_target_pairs={{0,8},{1,9},{2,10},{3,11},{4,12},{5,13},{6,14},{7,15},{8,0},{9,1},... | collective-permute-start | bytes 221192 | tf_op jit(solution)/shard_map/ppermute | solution.py:39
  42.3 1.8 %collective-permute-start.7 = (f32[72,256]{1,0:T(8,128)S(1)}, f32[72,256]{1,0:T(8,128)S(1)}, u32[]{:S(2)}, u32[]{:S(2)}) collective-permute-start(f32[72,256]{1,0:T(8,128)S(1)} %add_add_fusion.3), channel_id=1, source_target_pairs={{0,16},{1,17},{2,18},{3,19},{4,20},{5,21},{6,22},{7,23},{8,24},{9,... | collective-permute-start | bytes 221192 | tf_op jit(solution)/shard_map/ppermute | solution.py:39
  44.0 0.7 collective-permute-start.8
  44.8 0.0 collective-permute-done.6
  44.8 3.1 %collective-permute-done.7 = f32[72,256]{1,0:T(8,128)S(1)} collective-permute-done((f32[72,256]{1,0:T(8,128)S(1)}, f32[72,256]{1,0:T(8,128)S(1)}, u32[]{:S(2)}, u32[]{:S(2)}) %collective-permute-start.7) | collective-permute-done | bytes 73760 | tf_op jit(solution)/shard_map/ppermute | solution.py:39
  47.8 1.4 %collective-permute-done.8 = f32[72,256]{1,0:T(8,128)S(1)} collective-permute-done((f32[72,256]{1,0:T(8,128)S(1)}, f32[72,256]{1,0:T(8,128)S(1)}, u32[]{:S(2)}, u32[]{:S(2)}) %collective-permute-start.8) | collective-permute-done | bytes 73760 | tf_op jit(solution)/shard_map/ppermute | solution.py:39
  49.3 2.8 %collective-permute-start.10 = (f32[72,256]{1,0:T(8,128)S(1)}, f32[72,256]{1,0:T(8,128)S(1)}, u32[]{:S(2)}, u32[]{:S(2)}) collective-permute-start(f32[72,256]{1,0:T(8,128)S(1)} %add_add_fusion.2), channel_id=1, source_target_pairs={{0,64},{1,65},{2,66},{3,67},{4,68},{5,69},{6,70},{7,71},{8,72},{9,... | collective-permute-start | bytes 221192 | tf_op jit(solution)/shard_map/ppermute | solution.py:39
  52.1 0.9 collective-permute-start.11
  53.0 0.0 collective-permute-start.9
  53.0 1.1 %collective-permute-done.10 = f32[72,256]{1,0:T(8,128)S(1)} collective-permute-done((f32[72,256]{1,0:T(8,128)S(1)}, f32[72,256]{1,0:T(8,128)S(1)}, u32[]{:S(2)}, u32[]{:S(2)}) %collective-permute-start.10) | collective-permute-done | bytes 73760 | tf_op jit(solution)/shard_map/ppermute | solution.py:39
  54.1 2.9 %collective-permute-done.11 = f32[72,256]{1,0:T(8,128)S(1)} collective-permute-done((f32[72,256]{1,0:T(8,128)S(1)}, f32[72,256]{1,0:T(8,128)S(1)}, u32[]{:S(2)}, u32[]{:S(2)}) %collective-permute-start.11) | collective-permute-done | bytes 73760 | tf_op jit(solution)/shard_map/ppermute | solution.py:39
  57.0 0.0 collective-permute-done.9
  57.1 2.9 %collective-permute-start.12 = (f32[72,256]{1,0:T(8,128)S(1)}, f32[72,256]{1,0:T(8,128)S(1)}, u32[]{:S(2)}, u32[]{:S(2)}) collective-permute-start(f32[72,256]{1,0:T(8,128)S(1)} %add_add_fusion.1), channel_id=1, source_target_pairs={{0,4},{1,5},{2,6},{3,7},{4,0},{5,1},{6,2},{7,3},{8,12},{9,13},{10,... | collective-permute-start | bytes 221192 | tf_op jit(solution)/shard_map/ppermute | solution.py:39
  59.9 0.9 %collective-permute-done.12 = f32[72,256]{1,0:T(8,128)S(1)} collective-permute-done((f32[72,256]{1,0:T(8,128)S(1)}, f32[72,256]{1,0:T(8,128)S(1)}, u32[]{:S(2)}, u32[]{:S(2)}) %collective-permute-start.12) | collective-permute-done | bytes 73760 | tf_op jit(solution)/shard_map/ppermute | solution.py:39
  60.9 0.1 copy.13
  61.0 0.1 bitcast_select_fusion.1
  61.1 0.1 copy.12
  61.2 0.7 maximum_maximum_fusion.gram_ref
  61.9 25.5 %shard_map.69 = (f32[256,256]{1,0:T(8,128)}, f32[512,256]{1,0:T(8,128)}) custom-call(f32[256,256]{1,0:T(8,128)} %maximum_maximum_fusion.gram_ref, f32[512,256]{1,0:T(8,128)} %copy-done), custom_call_target="tpu_custom_call" | custom-call | tf_op jit(solution)/shard_map/pallas_call | solution.py:147
  (9 shorter events, 0.2 us)
Async XLA Ops:
  0.6 0.7 copy-start.3
  5.5 17.7 %collective-permute-start = (f32[4,128,256]{2,1,0:T(8,128)}, f32[4,128,256]{2,1,0:T(8,128)S(1)}, u32[]{:S(2)}, u32[]{:S(2)}) collective-permute-start(f32[4,128,256]{2,1,0:T(8,128)} %get-tuple-element.8), channel_id=1, source_target_pairs={{0,1},{1,2},{2,3},{3,4},{4,5},{5,6},{6,7},{7,8},{8,9},{9,10},{10,1... | collective-permute-start | bytes 1572872 | tf_op jit(solution)/shard_map/ppermute | solution.py:21
  9.5 16.0 %collective-permute-start.1 = (f32[4,128,256]{2,1,0:T(8,128)}, f32[4,128,256]{2,1,0:T(8,128)S(1)}, u32[]{:S(2)}, u32[]{:S(2)}) collective-permute-start(f32[4,128,256]{2,1,0:T(8,128)} %get-tuple-element.9), channel_id=1, source_target_pairs={{1,0},{2,1},{3,2},{4,3},{5,4},{6,5},{7,6},{8,7},{9,8},{10,9},{11,1... | collective-permute-start | bytes 1572872 | tf_op jit(solution)/shard_map/ppermute | solution.py:21
  25.5 1.2 %copy-start.1 = (f32[512,256]{1,0:T(8,128)S(1)}, f32[512,256]{1,0:T(8,128)}, u32[]{:S(2)}) copy-start(f32[512,256]{1,0:T(8,128)} %param.8) | copy-start | bytes 1572868
  25.5 1.2 %copy-start.2 = (f32[512]{0:T(512)S(1)}, f32[512]{0:T(512)}, u32[]{:S(2)}) copy-start(f32[512]{0:T(512)} %param.9) | copy-start | bytes 6148
  26.9 1.0 %copy-start = (f32[512,256]{1,0:T(8,128)}, f32[512,256]{1,0:T(8,128)S(1)}, u32[]{:S(2)}) copy-start(f32[512,256]{1,0:T(8,128)S(1)} %fusion.anomaly_ref) | copy-start | bytes 1572868
  28.2 1.4 %collective-permute-start.2 = (f32[72,256]{1,0:T(8,128)S(1)}, f32[72,256]{1,0:T(8,128)S(1)}, u32[]{:S(2)}, u32[]{:S(2)}) collective-permute-start(f32[72,256]{1,0:T(8,128)S(1)} %broadcast_select_fusion), channel_id=1, source_target_pairs={{0,4},{1,5},{2,6},{3,7},{4,0},{5,1},{6,2},{7,3},{8,12},{9,13},{10,... | collective-permute-start | bytes 221192 | tf_op jit(solution)/shard_map/ppermute | solution.py:39
  29.7 5.5 %collective-permute-start.3 = (f32[72,256]{1,0:T(8,128)S(1)}, f32[72,256]{1,0:T(8,128)S(1)}, u32[]{:S(2)}, u32[]{:S(2)}) collective-permute-start(f32[72,256]{1,0:T(8,128)S(1)} %select_add_fusion), channel_id=1, source_target_pairs={{0,1},{1,0},{2,3},{3,2},{4,5},{5,4},{6,7},{7,6},{8,9},{9,8},{10,11... | collective-permute-start | bytes 221192 | tf_op jit(solution)/shard_map/ppermute | solution.py:39
  31.1 7.9 %collective-permute-start.4 = (f32[72,256]{1,0:T(8,128)S(1)}, f32[72,256]{1,0:T(8,128)S(1)}, u32[]{:S(2)}, u32[]{:S(2)}) collective-permute-start(f32[72,256]{1,0:T(8,128)S(1)} %select_add_fusion), channel_id=1, source_target_pairs={{0,2},{1,3},{2,0},{3,1},{4,6},{5,7},{6,4},{7,5},{8,10},{9,11},{10,... | collective-permute-start | bytes 221192 | tf_op jit(solution)/shard_map/ppermute | solution.py:39
  35.2 5.3 %collective-permute-start.5 = (f32[72,256]{1,0:T(8,128)S(1)}, f32[72,256]{1,0:T(8,128)S(1)}, u32[]{:S(2)}, u32[]{:S(2)}) collective-permute-start(f32[72,256]{1,0:T(8,128)S(1)} %select_add_fusion), channel_id=1, source_target_pairs={{0,3},{1,2},{2,1},{3,0},{4,7},{5,6},{6,5},{7,4},{8,11},{9,10},{10,... | collective-permute-start | bytes 221192 | tf_op jit(solution)/shard_map/ppermute | solution.py:39
  40.6 4.2 %collective-permute-start.6 = (f32[72,256]{1,0:T(8,128)S(1)}, f32[72,256]{1,0:T(8,128)S(1)}, u32[]{:S(2)}, u32[]{:S(2)}) collective-permute-start(f32[72,256]{1,0:T(8,128)S(1)} %add_add_fusion.3), channel_id=1, source_target_pairs={{0,8},{1,9},{2,10},{3,11},{4,12},{5,13},{6,14},{7,15},{8,0},{9,1},... | collective-permute-start | bytes 221192 | tf_op jit(solution)/shard_map/ppermute | solution.py:39
  42.3 5.6 %collective-permute-start.7 = (f32[72,256]{1,0:T(8,128)S(1)}, f32[72,256]{1,0:T(8,128)S(1)}, u32[]{:S(2)}, u32[]{:S(2)}) collective-permute-start(f32[72,256]{1,0:T(8,128)S(1)} %add_add_fusion.3), channel_id=1, source_target_pairs={{0,16},{1,17},{2,18},{3,19},{4,20},{5,21},{6,22},{7,23},{8,24},{9,... | collective-permute-start | bytes 221192 | tf_op jit(solution)/shard_map/ppermute | solution.py:39
  44.0 5.3 %collective-permute-start.8 = (f32[72,256]{1,0:T(8,128)S(1)}, f32[72,256]{1,0:T(8,128)S(1)}, u32[]{:S(2)}, u32[]{:S(2)}) collective-permute-start(f32[72,256]{1,0:T(8,128)S(1)} %add_add_fusion.3), channel_id=1, source_target_pairs={{0,24},{1,25},{2,26},{3,27},{4,28},{5,29},{6,30},{7,31},{8,16},{9,... | collective-permute-start | bytes 221192 | tf_op jit(solution)/shard_map/ppermute | solution.py:39
  49.3 4.8 %collective-permute-start.10 = (f32[72,256]{1,0:T(8,128)S(1)}, f32[72,256]{1,0:T(8,128)S(1)}, u32[]{:S(2)}, u32[]{:S(2)}) collective-permute-start(f32[72,256]{1,0:T(8,128)S(1)} %add_add_fusion.2), channel_id=1, source_target_pairs={{0,64},{1,65},{2,66},{3,67},{4,68},{5,69},{6,70},{7,71},{8,72},{9,... | collective-permute-start | bytes 221192 | tf_op jit(solution)/shard_map/ppermute | solution.py:39
  52.1 4.9 %collective-permute-start.11 = (f32[72,256]{1,0:T(8,128)S(1)}, f32[72,256]{1,0:T(8,128)S(1)}, u32[]{:S(2)}, u32[]{:S(2)}) collective-permute-start(f32[72,256]{1,0:T(8,128)S(1)} %add_add_fusion.2), channel_id=1, source_target_pairs={{0,96},{1,97},{2,98},{3,99},{4,100},{5,101},{6,102},{7,103},{8,104... | collective-permute-start | bytes 221192 | tf_op jit(solution)/shard_map/ppermute | solution.py:39
  53.0 4.0 %collective-permute-start.9 = (f32[72,256]{1,0:T(8,128)S(1)}, f32[72,256]{1,0:T(8,128)S(1)}, u32[]{:S(2)}, u32[]{:S(2)}) collective-permute-start(f32[72,256]{1,0:T(8,128)S(1)} %add_add_fusion.2), channel_id=1, source_target_pairs={{0,32},{1,33},{2,34},{3,35},{4,36},{5,37},{6,38},{7,39},{8,40},{9,... | collective-permute-start | bytes 221192 | tf_op jit(solution)/shard_map/ppermute | solution.py:39
  57.1 3.8 %collective-permute-start.12 = (f32[72,256]{1,0:T(8,128)S(1)}, f32[72,256]{1,0:T(8,128)S(1)}, u32[]{:S(2)}, u32[]{:S(2)}) collective-permute-start(f32[72,256]{1,0:T(8,128)S(1)} %add_add_fusion.1), channel_id=1, source_target_pairs={{0,4},{1,5},{2,6},{3,7},{4,0},{5,1},{6,2},{7,3},{8,12},{9,13},{10,... | collective-permute-start | bytes 221192 | tf_op jit(solution)/shard_map/ppermute | solution.py:39

commit v12 on v11

--- a/solution.py
+++ b/solution.py
@@ -164,14 +164,14 @@
                 (((0,), (0,)), ((), ())),
                 preferred_element_type=jnp.float32,
             )
-            target = jnp.clip(zone_ref[block, slot] - base_ref[0], 0, 3 * owned - 1)
+            target = jnp.clip(zone_ref[slot, block] - base_ref[0], 0, 3 * owned - 1)
             work_ref[target] = work_ref[target] + part
     before_ref[...] = work_ref[:owned]
     own_ref[...] = work_ref[owned : 2 * owned]
     after_ref[...] = work_ref[2 * owned :]
 
 
-def aggregate(block_zone, base, weight_blocks, cell_rows, owned_blocks):
+def aggregate(zone_by_slot, base, weight_blocks, cell_rows, owned_blocks):
     block_size = weight_blocks.shape[3]
     day_count = cell_rows.shape[2]
     table = jax.ShapeDtypeStruct((owned_blocks, block_size, day_count), jnp.float32)
@@ -190,7 +190,7 @@
             pl.BlockSpec(memory_space=pltpu.VMEM),
         ),
         scratch_shapes=[pltpu.VMEM((3 * owned_blocks, block_size, day_count), jnp.float32)],
-    )(block_zone, base, weight_blocks, cell_rows)
+    )(zone_by_slot, base, weight_blocks, cell_rows)
 
 
 def body(runoff, weight_blocks, block_zone, climatology, zone_weight):
@@ -203,7 +203,7 @@
     cell_rows = runoff.reshape(block_count, block_size, day_count)
     base = jnp.reshape((device_index - 1) * owned_blocks, (1,)).astype(jnp.int32)
     to_before, own_table, to_after = aggregate(
-        block_zone.astype(jnp.int32), base, weight_blocks, cell_rows, owned_blocks
+        block_zone.astype(jnp.int32).T, base, weight_blocks, cell_rows, owned_blocks
     )
     from_before = shifted(to_after, DEVICE_AXES, 1)
     from_after = shifted(to_before, DEVICE_AXES, -1)

time: 87.7 us -> 86.3 us (0.984)
  local copies, waits for them, and re-layouts: 1.75 us -> 0.4 us
    unnamed x10 -> x7, local copies, waits for them, and re-layouts: 1.45 us -> 0.1 us
where the time goes in v12:
time: 86.3 us; the launch traced here: 86.1 us
  Pallas kernels  29 us (34%)
  waiting for transfers between devices  27.7 us (32%)
  starting transfers between devices  24.7 us (29%)
  other arithmetic  2.46 us (3%)
  matrix products  1.02 us (1%)
    pallas_call x1, Pallas kernels, cholesky_with_inverse(): pl.pallas_call(functools.partial(cholesky_kernel, factor_scale=1.0 / root...  25.5 us
    ppermute x11, starting transfers between devices, exchange(): lax.ppermute(value, DEVICE_AXES, [(i, i ^ mask) for i in range(count)])  16.8 us
    ppermute x11, waiting for transfers between devices, exchange(): lax.ppermute(value, DEVICE_AXES, [(i, i ^ mask) for i in range(count)])  15.7 us
    ppermute x2, waiting for transfers between devices, shifted(): lax.ppermute(value, axis, [(source, source + steps) for source in range(i...  12 us
    ppermute x2, starting transfers between devices, shifted(): lax.ppermute(value, axis, [(source, source + steps) for source in range(i...  7.93 us
    pallas_call x1, Pallas kernels, aggregate(): pl.pallas_call(aggregate_kernel, out_shape=(table, table, table), in_spec...  3.5 us
  transfers between devices with their start and end apart: 13, of which 10 were waited for; matrix products, arithmetic and copies ran while one was open for 0% of the time, Pallas kernels for 0%

profile of v12, /device:TPU:1, one launch (start us, length us, event | category | flops | bytes accessed | tf_op | source)
XLA Modules:
  0.0 86.1 jit_solution(16997102054753932563)
XLA Ops:
  0.6 3.5 %shard_map.68 = (f32[4,128,256]{2,1,0:T(8,128)}, f32[4,128,256]{2,1,0:T(8,128)}, f32[4,128,256]{2,1,0:T(8,128)}) custom-call(s32[2,16]{1,0:T(2,128)} %bitcast.26, s32[1]{0:T(128)} %bitcast.1.base_ref, bf16[16,2,128,128]{3,2,1,0:T(8,128)(2,1)} %weight_ref.1, bf16[16,128,256]{2,1,0:T(8,128)(2,1)} %bitcast.23), custom_call_target="tpu_custom_call" | custom-call | tf_op jit(solution)/shard_map/pallas_call | solution.py:178
  4.1 4.0 %collective-permute-start = (f32[4,128,256]{2,1,0:T(8,128)}, f32[4,128,256]{2,1,0:T(8,128)S(1)}, u32[]{:S(2)}, u32[]{:S(2)}) collective-permute-start(f32[4,128,256]{2,1,0:T(8,128)} %get-tuple-element.8), channel_id=1, source_target_pairs={{0,1},{1,2},{2,3},{3,4},{4,5},{5,6},{6,7},{7,8},{8,9},{9,10},{10,1... | collective-permute-start | bytes 1572872 | tf_op jit(solution)/shard_map/ppermute | solution.py:21
  8.2 3.9 %collective-permute-start.1 = (f32[4,128,256]{2,1,0:T(8,128)}, f32[4,128,256]{2,1,0:T(8,128)S(1)}, u32[]{:S(2)}, u32[]{:S(2)}) collective-permute-start(f32[4,128,256]{2,1,0:T(8,128)} %get-tuple-element.9), channel_id=1, source_target_pairs={{1,0},{2,1},{3,2},{4,3},{5,4},{6,5},{7,6},{8,7},{9,8},{10,9},{11,1... | collective-permute-start | bytes 1572872 | tf_op jit(solution)/shard_map/ppermute | solution.py:21
  12.1 0.1 pad_slice_fusion
  12.2 9.7 %collective-permute-done = f32[4,128,256]{2,1,0:T(8,128)S(1)} collective-permute-done((f32[4,128,256]{2,1,0:T(8,128)}, f32[4,128,256]{2,1,0:T(8,128)S(1)}, u32[]{:S(2)}, u32[]{:S(2)}) %collective-permute-start) | collective-permute-done | bytes 524320 | tf_op jit(solution)/shard_map/ppermute | solution.py:21
  21.8 2.3 %collective-permute-done.1 = f32[4,128,256]{2,1,0:T(8,128)S(1)} collective-permute-done((f32[4,128,256]{2,1,0:T(8,128)}, f32[4,128,256]{2,1,0:T(8,128)S(1)}, u32[]{:S(2)}, u32[]{:S(2)}) %collective-permute-start.1) | collective-permute-done | bytes 524320 | tf_op jit(solution)/shard_map/ppermute | solution.py:21
  24.2 0.0 copy-start.1
  24.2 0.0 copy-start.2
  24.2 1.2 %add_add_fusion = f32[4,128,256]{2,1,0:T(8,128)S(1)} fusion(f32[4,128,256]{2,1,0:T(8,128)S(1)} %collective-permute-done.1, f32[4,128,256]{2,1,0:T(8,128)} %get-tuple-element.7, f32[4,128,256]{2,1,0:T(8,128)S(1)} %collective-permute-done), kind=kLoop, calls=%fused_computation.2 | loop fusion | flops 262144 | bytes 2097152 | tf_op jit(solution)/shard_map/add | solution.py:210
  25.4 0.0 copy-done.1
  25.4 0.0 copy-done.2
  25.4 0.1 fusion.anomaly_ref
  25.5 0.0 copy-start
  25.5 1.0 %fusion.8 = f32[256,256]{1,0:T(8,128)S(1)} fusion(f32[512,256]{1,0:T(8,128)S(1)} %fusion.anomaly_ref), kind=kOutput, calls=%fused_computation.33 | convolution fusion | flops 402653184 | bytes 786432 | tf_op jit(solution)/shard_map/dot_general | solution.py:213
  26.6 0.0 copy-done
  26.6 0.1 copy.7
  26.8 0.1 broadcast_select_fusion
  26.9 0.5 collective-permute-start.2
  27.4 0.9 %collective-permute-done.2 = f32[72,256]{1,0:T(8,128)S(1)} collective-permute-done((f32[72,256]{1,0:T(8,128)S(1)}, f32[72,256]{1,0:T(8,128)S(1)}, u32[]{:S(2)}, u32[]{:S(2)}) %collective-permute-start.2) | collective-permute-done | bytes 73760 | tf_op jit(solution)/shard_map/ppermute | solution.py:39
  28.3 0.1 select_add_fusion
  28.4 1.4 %collective-permute-start.3 = (f32[72,256]{1,0:T(8,128)S(1)}, f32[72,256]{1,0:T(8,128)S(1)}, u32[]{:S(2)}, u32[]{:S(2)}) collective-permute-start(f32[72,256]{1,0:T(8,128)S(1)} %select_add_fusion), channel_id=1, source_target_pairs={{0,1},{1,0},{2,3},{3,2},{4,5},{5,4},{6,7},{7,6},{8,9},{9,8},{10,11... | collective-permute-start | bytes 221192 | tf_op jit(solution)/shard_map/ppermute | solution.py:39
  29.8 4.1 %collective-permute-start.4 = (f32[72,256]{1,0:T(8,128)S(1)}, f32[72,256]{1,0:T(8,128)S(1)}, u32[]{:S(2)}, u32[]{:S(2)}) collective-permute-start(f32[72,256]{1,0:T(8,128)S(1)} %select_add_fusion), channel_id=1, source_target_pairs={{0,2},{1,3},{2,0},{3,1},{4,6},{5,7},{6,4},{7,5},{8,10},{9,11},{10,... | collective-permute-start | bytes 221192 | tf_op jit(solution)/shard_map/ppermute | solution.py:39
  33.9 0.0 collective-permute-start.5
  33.9 0.0 collective-permute-done.3
  33.9 3.8 %collective-permute-done.4 = f32[72,256]{1,0:T(8,128)S(1)} collective-permute-done((f32[72,256]{1,0:T(8,128)S(1)}, f32[72,256]{1,0:T(8,128)S(1)}, u32[]{:S(2)}, u32[]{:S(2)}) %collective-permute-start.4) | collective-permute-done | bytes 73760 | tf_op jit(solution)/shard_map/ppermute | solution.py:39
  37.7 1.5 %collective-permute-done.5 = f32[72,256]{1,0:T(8,128)S(1)} collective-permute-done((f32[72,256]{1,0:T(8,128)S(1)}, f32[72,256]{1,0:T(8,128)S(1)}, u32[]{:S(2)}, u32[]{:S(2)}) %collective-permute-start.5) | collective-permute-done | bytes 73760 | tf_op jit(solution)/shard_map/ppermute | solution.py:39
  39.2 1.7 %collective-permute-start.6 = (f32[72,256]{1,0:T(8,128)S(1)}, f32[72,256]{1,0:T(8,128)S(1)}, u32[]{:S(2)}, u32[]{:S(2)}) collective-permute-start(f32[72,256]{1,0:T(8,128)S(1)} %add_add_fusion.3), channel_id=1, source_target_pairs={{0,8},{1,9},{2,10},{3,11},{4,12},{5,13},{6,14},{7,15},{8,0},{9,1},... | collective-permute-start | bytes 221192 | tf_op jit(solution)/shard_map/ppermute | solution.py:39
  40.9 1.8 %collective-permute-start.7 = (f32[72,256]{1,0:T(8,128)S(1)}, f32[72,256]{1,0:T(8,128)S(1)}, u32[]{:S(2)}, u32[]{:S(2)}) collective-permute-start(f32[72,256]{1,0:T(8,128)S(1)} %add_add_fusion.3), channel_id=1, source_target_pairs={{0,16},{1,17},{2,18},{3,19},{4,20},{5,21},{6,22},{7,23},{8,24},{9,... | collective-permute-start | bytes 221192 | tf_op jit(solution)/shard_map/ppermute | solution.py:39
  42.7 0.7 collective-permute-start.8
  43.4 0.0 collective-permute-done.6
  43.4 3.1 %collective-permute-done.7 = f32[72,256]{1,0:T(8,128)S(1)} collective-permute-done((f32[72,256]{1,0:T(8,128)S(1)}, f32[72,256]{1,0:T(8,128)S(1)}, u32[]{:S(2)}, u32[]{:S(2)}) %collective-permute-start.7) | collective-permute-done | bytes 73760 | tf_op jit(solution)/shard_map/ppermute | solution.py:39
  46.5 1.4 %collective-permute-done.8 = f32[72,256]{1,0:T(8,128)S(1)} collective-permute-done((f32[72,256]{1,0:T(8,128)S(1)}, f32[72,256]{1,0:T(8,128)S(1)}, u32[]{:S(2)}, u32[]{:S(2)}) %collective-permute-start.8) | collective-permute-done | bytes 73760 | tf_op jit(solution)/shard_map/ppermute | solution.py:39
  48.0 2.8 %collective-permute-start.10 = (f32[72,256]{1,0:T(8,128)S(1)}, f32[72,256]{1,0:T(8,128)S(1)}, u32[]{:S(2)}, u32[]{:S(2)}) collective-permute-start(f32[72,256]{1,0:T(8,128)S(1)} %add_add_fusion.2), channel_id=1, source_target_pairs={{0,64},{1,65},{2,66},{3,67},{4,68},{5,69},{6,70},{7,71},{8,72},{9,... | collective-permute-start | bytes 221192 | tf_op jit(solution)/shard_map/ppermute | solution.py:39
  50.8 0.9 collective-permute-start.11
  51.6 0.0 collective-permute-start.9
  51.6 1.1 %collective-permute-done.10 = f32[72,256]{1,0:T(8,128)S(1)} collective-permute-done((f32[72,256]{1,0:T(8,128)S(1)}, f32[72,256]{1,0:T(8,128)S(1)}, u32[]{:S(2)}, u32[]{:S(2)}) %collective-permute-start.10) | collective-permute-done | bytes 73760 | tf_op jit(solution)/shard_map/ppermute | solution.py:39
  52.8 2.9 %collective-permute-done.11 = f32[72,256]{1,0:T(8,128)S(1)} collective-permute-done((f32[72,256]{1,0:T(8,128)S(1)}, f32[72,256]{1,0:T(8,128)S(1)}, u32[]{:S(2)}, u32[]{:S(2)}) %collective-permute-start.11) | collective-permute-done | bytes 73760 | tf_op jit(solution)/shard_map/ppermute | solution.py:39
  55.7 0.0 collective-permute-done.9
  55.7 2.9 %collective-permute-start.12 = (f32[72,256]{1,0:T(8,128)S(1)}, f32[72,256]{1,0:T(8,128)S(1)}, u32[]{:S(2)}, u32[]{:S(2)}) collective-permute-start(f32[72,256]{1,0:T(8,128)S(1)} %add_add_fusion.1), channel_id=1, source_target_pairs={{0,4},{1,5},{2,6},{3,7},{4,0},{5,1},{6,2},{7,3},{8,12},{9,13},{10,... | collective-permute-start | bytes 221192 | tf_op jit(solution)/shard_map/ppermute | solution.py:39
  58.6 0.9 %collective-permute-done.12 = f32[72,256]{1,0:T(8,128)S(1)} collective-permute-done((f32[72,256]{1,0:T(8,128)S(1)}, f32[72,256]{1,0:T(8,128)S(1)}, u32[]{:S(2)}, u32[]{:S(2)}) %collective-permute-start.12) | collective-permute-done | bytes 73760 | tf_op jit(solution)/shard_map/ppermute | solution.py:39
  59.5 0.1 copy.12
  59.6 0.1 bitcast_select_fusion.1
  59.7 0.1 copy.11
  59.8 0.7 maximum_maximum_fusion.gram_ref
  60.6 25.5 %shard_map.69 = (f32[256,256]{1,0:T(8,128)}, f32[512,256]{1,0:T(8,128)}) custom-call(f32[256,256]{1,0:T(8,128)} %maximum_maximum_fusion.gram_ref, f32[512,256]{1,0:T(8,128)} %copy-done), custom_call_target="tpu_custom_call" | custom-call | tf_op jit(solution)/shard_map/pallas_call | solution.py:147
  (9 shorter events, 0.2 us)
Async XLA Ops:
  4.1 17.7 %collective-permute-start = (f32[4,128,256]{2,1,0:T(8,128)}, f32[4,128,256]{2,1,0:T(8,128)S(1)}, u32[]{:S(2)}, u32[]{:S(2)}) collective-permute-start(f32[4,128,256]{2,1,0:T(8,128)} %get-tuple-element.8), channel_id=1, source_target_pairs={{0,1},{1,2},{2,3},{3,4},{4,5},{5,6},{6,7},{7,8},{8,9},{9,10},{10,1... | collective-permute-start | bytes 1572872 | tf_op jit(solution)/shard_map/ppermute | solution.py:21
  8.2 16.0 %collective-permute-start.1 = (f32[4,128,256]{2,1,0:T(8,128)}, f32[4,128,256]{2,1,0:T(8,128)S(1)}, u32[]{:S(2)}, u32[]{:S(2)}) collective-permute-start(f32[4,128,256]{2,1,0:T(8,128)} %get-tuple-element.9), channel_id=1, source_target_pairs={{1,0},{2,1},{3,2},{4,3},{5,4},{6,5},{7,6},{8,7},{9,8},{10,9},{11,1... | collective-permute-start | bytes 1572872 | tf_op jit(solution)/shard_map/ppermute | solution.py:21
  24.2 1.2 %copy-start.1 = (f32[512,256]{1,0:T(8,128)S(1)}, f32[512,256]{1,0:T(8,128)}, u32[]{:S(2)}) copy-start(f32[512,256]{1,0:T(8,128)} %param.8) | copy-start | bytes 1572868
  24.2 1.2 %copy-start.2 = (f32[512]{0:T(512)S(1)}, f32[512]{0:T(512)}, u32[]{:S(2)}) copy-start(f32[512]{0:T(512)} %param.9) | copy-start | bytes 6148
  25.5 1.0 %copy-start = (f32[512,256]{1,0:T(8,128)}, f32[512,256]{1,0:T(8,128)S(1)}, u32[]{:S(2)}) copy-start(f32[512,256]{1,0:T(8,128)S(1)} %fusion.anomaly_ref) | copy-start | bytes 1572868
  26.9 1.4 %collective-permute-start.2 = (f32[72,256]{1,0:T(8,128)S(1)}, f32[72,256]{1,0:T(8,128)S(1)}, u32[]{:S(2)}, u32[]{:S(2)}) collective-permute-start(f32[72,256]{1,0:T(8,128)S(1)} %broadcast_select_fusion), channel_id=1, source_target_pairs={{0,4},{1,5},{2,6},{3,7},{4,0},{5,1},{6,2},{7,3},{8,12},{9,13},{10,... | collective-permute-start | bytes 221192 | tf_op jit(solution)/shard_map/ppermute | solution.py:39
  28.4 5.5 %collective-permute-start.3 = (f32[72,256]{1,0:T(8,128)S(1)}, f32[72,256]{1,0:T(8,128)S(1)}, u32[]{:S(2)}, u32[]{:S(2)}) collective-permute-start(f32[72,256]{1,0:T(8,128)S(1)} %select_add_fusion), channel_id=1, source_target_pairs={{0,1},{1,0},{2,3},{3,2},{4,5},{5,4},{6,7},{7,6},{8,9},{9,8},{10,11... | collective-permute-start | bytes 221192 | tf_op jit(solution)/shard_map/ppermute | solution.py:39
  29.8 7.9 %collective-permute-start.4 = (f32[72,256]{1,0:T(8,128)S(1)}, f32[72,256]{1,0:T(8,128)S(1)}, u32[]{:S(2)}, u32[]{:S(2)}) collective-permute-start(f32[72,256]{1,0:T(8,128)S(1)} %select_add_fusion), channel_id=1, source_target_pairs={{0,2},{1,3},{2,0},{3,1},{4,6},{5,7},{6,4},{7,5},{8,10},{9,11},{10,... | collective-permute-start | bytes 221192 | tf_op jit(solution)/shard_map/ppermute | solution.py:39
  33.9 5.3 %collective-permute-start.5 = (f32[72,256]{1,0:T(8,128)S(1)}, f32[72,256]{1,0:T(8,128)S(1)}, u32[]{:S(2)}, u32[]{:S(2)}) collective-permute-start(f32[72,256]{1,0:T(8,128)S(1)} %select_add_fusion), channel_id=1, source_target_pairs={{0,3},{1,2},{2,1},{3,0},{4,7},{5,6},{6,5},{7,4},{8,11},{9,10},{10,... | collective-permute-start | bytes 221192 | tf_op jit(solution)/shard_map/ppermute | solution.py:39
  39.2 4.2 %collective-permute-start.6 = (f32[72,256]{1,0:T(8,128)S(1)}, f32[72,256]{1,0:T(8,128)S(1)}, u32[]{:S(2)}, u32[]{:S(2)}) collective-permute-start(f32[72,256]{1,0:T(8,128)S(1)} %add_add_fusion.3), channel_id=1, source_target_pairs={{0,8},{1,9},{2,10},{3,11},{4,12},{5,13},{6,14},{7,15},{8,0},{9,1},... | collective-permute-start | bytes 221192 | tf_op jit(solution)/shard_map/ppermute | solution.py:39
  40.9 5.6 %collective-permute-start.7 = (f32[72,256]{1,0:T(8,128)S(1)}, f32[72,256]{1,0:T(8,128)S(1)}, u32[]{:S(2)}, u32[]{:S(2)}) collective-permute-start(f32[72,256]{1,0:T(8,128)S(1)} %add_add_fusion.3), channel_id=1, source_target_pairs={{0,16},{1,17},{2,18},{3,19},{4,20},{5,21},{6,22},{7,23},{8,24},{9,... | collective-permute-start | bytes 221192 | tf_op jit(solution)/shard_map/ppermute | solution.py:39
  42.7 5.3 %collective-permute-start.8 = (f32[72,256]{1,0:T(8,128)S(1)}, f32[72,256]{1,0:T(8,128)S(1)}, u32[]{:S(2)}, u32[]{:S(2)}) collective-permute-start(f32[72,256]{1,0:T(8,128)S(1)} %add_add_fusion.3), channel_id=1, source_target_pairs={{0,24},{1,25},{2,26},{3,27},{4,28},{5,29},{6,30},{7,31},{8,16},{9,... | collective-permute-start | bytes 221192 | tf_op jit(solution)/shard_map/ppermute | solution.py:39
  48.0 4.8 %collective-permute-start.10 = (f32[72,256]{1,0:T(8,128)S(1)}, f32[72,256]{1,0:T(8,128)S(1)}, u32[]{:S(2)}, u32[]{:S(2)}) collective-permute-start(f32[72,256]{1,0:T(8,128)S(1)} %add_add_fusion.2), channel_id=1, source_target_pairs={{0,64},{1,65},{2,66},{3,67},{4,68},{5,69},{6,70},{7,71},{8,72},{9,... | collective-permute-start | bytes 221192 | tf_op jit(solution)/shard_map/ppermute | solution.py:39
  50.8 4.9 %collective-permute-start.11 = (f32[72,256]{1,0:T(8,128)S(1)}, f32[72,256]{1,0:T(8,128)S(1)}, u32[]{:S(2)}, u32[]{:S(2)}) collective-permute-start(f32[72,256]{1,0:T(8,128)S(1)} %add_add_fusion.2), channel_id=1, source_target_pairs={{0,96},{1,97},{2,98},{3,99},{4,100},{5,101},{6,102},{7,103},{8,104... | collective-permute-start | bytes 221192 | tf_op jit(solution)/shard_map/ppermute | solution.py:39
  51.6 4.0 %collective-permute-start.9 = (f32[72,256]{1,0:T(8,128)S(1)}, f32[72,256]{1,0:T(8,128)S(1)}, u32[]{:S(2)}, u32[]{:S(2)}) collective-permute-start(f32[72,256]{1,0:T(8,128)S(1)} %add_add_fusion.2), channel_id=1, source_target_pairs={{0,32},{1,33},{2,34},{3,35},{4,36},{5,37},{6,38},{7,39},{8,40},{9,... | collective-permute-start | bytes 221192 | tf_op jit(solution)/shard_map/ppermute | solution.py:39
  55.7 3.8 %collective-permute-start.12 = (f32[72,256]{1,0:T(8,128)S(1)}, f32[72,256]{1,0:T(8,128)S(1)}, u32[]{:S(2)}, u32[]{:S(2)}) collective-permute-start(f32[72,256]{1,0:T(8,128)S(1)} %add_add_fusion.1), channel_id=1, source_target_pairs={{0,4},{1,5},{2,6},{3,7},{4,0},{5,1},{6,2},{7,3},{8,12},{9,13},{10,... | collective-permute-start | bytes 221192 | tf_op jit(solution)/shard_map/ppermute | solution.py:39

commit v13 on v12

--- a/solution.py
+++ b/solution.py
@@ -95,9 +95,21 @@
     return jnp.concatenate([top, bottom], axis=0)
 
 
-def cholesky_kernel(gram_ref, anomaly_ref, upper_ref, scores_ref, inverse_ref, work_ref, *, factor_scale, inverse_scale):
-    size = gram_ref.shape[0]
-    work_ref[...] = gram_ref[...]
+def cholesky_kernel(packed_ref, anomaly_ref, upper_ref, scores_ref, inverse_ref, work_ref, *, factor_scale, inverse_scale):
+    size = packed_ref.shape[1]
+    half = size // 2
+    tri = packed_ref[:half, half:]
+    g12 = packed_ref[:half, :half]
+    diag = jnp.broadcast_to(packed_ref[half : half + 1, :half], (half, half))
+    tri_t = jnp.transpose(tri)
+    rows_h = lax.broadcasted_iota(jnp.int32, (half, half), 0)
+    cols_h = lax.broadcasted_iota(jnp.int32, (half, half), 1)
+    work_ref[:half, :half] = jnp.where(rows_h <= cols_h, tri, tri_t)
+    work_ref[:half, half:] = g12
+    work_ref[half:, :half] = jnp.transpose(g12)
+    work_ref[half:, half:] = jnp.where(
+        rows_h > cols_h, tri, jnp.where(rows_h < cols_h, tri_t, diag)
+    )
     rows = lax.broadcasted_iota(jnp.int32, (size, size), 0)
     cols = lax.broadcasted_iota(jnp.int32, (size, size), 1)
     inverse_ref[...] = jnp.where(rows == cols, 1.0, 0.0).astype(jnp.float32)
@@ -141,14 +153,14 @@
     )
 
 
-def cholesky_with_inverse(gram, anomaly, root):
-    size = gram.shape[0]
+def cholesky_with_inverse(packed, anomaly, root):
+    size = packed.shape[1]
     square = jax.ShapeDtypeStruct((size, size), jnp.float32)
     return pl.pallas_call(
         functools.partial(cholesky_kernel, factor_scale=1.0 / root, inverse_scale=root),
         out_shape=(square, jax.ShapeDtypeStruct(anomaly.shape, jnp.float32)),
         scratch_shapes=[pltpu.VMEM((size, size), jnp.float32), pltpu.VMEM((size, size), jnp.float32)],
-    )(gram, anomaly)
+    )(packed, anomaly)
 
 
 def aggregate_kernel(zone_ref, base_ref, weight_ref, rows_ref, before_ref, own_ref, after_ref, work_ref):
@@ -214,9 +226,9 @@
         anomaly.T, anomaly, precision=exact_mode, preferred_element_type=jnp.float32
     )
     local_gram = 0.5 * (local_gram + local_gram.T)
-    total_gram = unpack_gram(all_sum(pack_gram(local_gram), device_count), day_count)
+    total_packed = all_sum(pack_gram(local_gram), device_count)
     root = math.sqrt(anomaly.shape[0] * device_count)
-    factor, scores = cholesky_with_inverse(total_gram, anomaly, root)
+    factor, scores = cholesky_with_inverse(total_packed, anomaly, root)
     return (scores, factor)
 
 

time: 86.3 us -> 86 us (level)
  no operation moved by 1% of the time
where the time goes in v13:
time: 86 us; the launch traced here: 85.8 us
  Pallas kernels  29.1 us (34%)
  waiting for transfers between devices  27.6 us (32%)
  starting transfers between devices  24.7 us (29%)
  other arithmetic  2.31 us (3%)
  matrix products  1.02 us (1%)
    pallas_call x1, Pallas kernels, cholesky_with_inverse(): pl.pallas_call(functools.partial(cholesky_kernel, factor_scale=1.0 / root...  25.6 us
    ppermute x11, starting transfers between devices, exchange(): lax.ppermute(value, DEVICE_AXES, [(i, i ^ mask) for i in range(count)])  16.8 us
    ppermute x11, waiting for transfers between devices, exchange(): lax.ppermute(value, DEVICE_AXES, [(i, i ^ mask) for i in range(count)])  15.7 us
    ppermute x2, waiting for transfers between devices, shifted(): lax.ppermute(value, axis, [(source, source + steps) for source in range(i...  12 us
    ppermute x2, starting transfers between devices, shifted(): lax.ppermute(value, axis, [(source, source + steps) for source in range(i...  7.93 us
    pallas_call x1, Pallas kernels, aggregate(): pl.pallas_call(aggregate_kernel, out_shape=(table, table, table), in_spec...  3.5 us
  transfers between devices with their start and end apart: 13, of which 10 were waited for; matrix products, arithmetic and copies ran while one was open for 0% of the time, Pallas kernels for 0%

profile of v13, /device:TPU:1, one launch (start us, length us, event | category | flops | bytes accessed | tf_op | source)
XLA Modules:
  0.0 85.8 jit_solution(970045600731206898)
XLA Ops:
  0.6 3.5 %shard_map.68 = (f32[4,128,256]{2,1,0:T(8,128)}, f32[4,128,256]{2,1,0:T(8,128)}, f32[4,128,256]{2,1,0:T(8,128)}) custom-call(s32[2,16]{1,0:T(2,128)} %bitcast.17, s32[1]{0:T(128)} %bitcast.1.base_ref, bf16[16,2,128,128]{3,2,1,0:T(8,128)(2,1)} %weight_ref.1, bf16[16,128,256]{2,1,0:T(8,128)(2,1)} %bitcast.14), custom_call_target="tpu_custom_call" | custom-call | tf_op jit(solution)/shard_map/pallas_call | solution.py:190
  4.1 4.0 %collective-permute-start = (f32[4,128,256]{2,1,0:T(8,128)}, f32[4,128,256]{2,1,0:T(8,128)S(1)}, u32[]{:S(2)}, u32[]{:S(2)}) collective-permute-start(f32[4,128,256]{2,1,0:T(8,128)} %get-tuple-element.8), channel_id=1, source_target_pairs={{0,1},{1,2},{2,3},{3,4},{4,5},{5,6},{6,7},{7,8},{8,9},{9,10},{10,1... | collective-permute-start | bytes 1572872 | tf_op jit(solution)/shard_map/ppermute | solution.py:21
  8.2 3.9 %collective-permute-start.1 = (f32[4,128,256]{2,1,0:T(8,128)}, f32[4,128,256]{2,1,0:T(8,128)S(1)}, u32[]{:S(2)}, u32[]{:S(2)}) collective-permute-start(f32[4,128,256]{2,1,0:T(8,128)} %get-tuple-element.9), channel_id=1, source_target_pairs={{1,0},{2,1},{3,2},{4,3},{5,4},{6,5},{7,6},{8,7},{9,8},{10,9},{11,1... | collective-permute-start | bytes 1572872 | tf_op jit(solution)/shard_map/ppermute | solution.py:21
  12.1 0.1 pad_slice_fusion
  12.2 9.7 %collective-permute-done = f32[4,128,256]{2,1,0:T(8,128)S(1)} collective-permute-done((f32[4,128,256]{2,1,0:T(8,128)}, f32[4,128,256]{2,1,0:T(8,128)S(1)}, u32[]{:S(2)}, u32[]{:S(2)}) %collective-permute-start) | collective-permute-done | bytes 524320 | tf_op jit(solution)/shard_map/ppermute | solution.py:21
  21.8 2.3 %collective-permute-done.1 = f32[4,128,256]{2,1,0:T(8,128)S(1)} collective-permute-done((f32[4,128,256]{2,1,0:T(8,128)}, f32[4,128,256]{2,1,0:T(8,128)S(1)}, u32[]{:S(2)}, u32[]{:S(2)}) %collective-permute-start.1) | collective-permute-done | bytes 524320 | tf_op jit(solution)/shard_map/ppermute | solution.py:21
  24.2 0.0 copy-start.1
  24.2 0.0 copy-start.2
  24.2 1.2 %add_add_fusion = f32[4,128,256]{2,1,0:T(8,128)S(1)} fusion(f32[4,128,256]{2,1,0:T(8,128)S(1)} %collective-permute-done.1, f32[4,128,256]{2,1,0:T(8,128)} %get-tuple-element.7, f32[4,128,256]{2,1,0:T(8,128)S(1)} %collective-permute-done), kind=kLoop, calls=%fused_computation.2 | loop fusion | flops 262144 | bytes 2097152 | tf_op jit(solution)/shard_map/add | solution.py:222
  25.4 0.0 copy-done.1
  25.4 0.0 copy-done.2
  25.4 0.1 fusion.anomaly_ref
  25.5 0.0 copy-start
  25.5 1.0 %fusion.7 = f32[256,256]{1,0:T(8,128)S(1)} fusion(f32[512,256]{1,0:T(8,128)S(1)} %fusion.anomaly_ref), kind=kOutput, calls=%fused_computation.25 | convolution fusion | flops 402653184 | bytes 786432 | tf_op jit(solution)/shard_map/dot_general | solution.py:225
  26.6 0.0 copy-done
  26.6 0.1 copy.7
  26.8 0.1 broadcast_select_fusion
  26.9 0.5 collective-permute-start.2
  27.4 0.9 %collective-permute-done.2 = f32[72,256]{1,0:T(8,128)S(1)} collective-permute-done((f32[72,256]{1,0:T(8,128)S(1)}, f32[72,256]{1,0:T(8,128)S(1)}, u32[]{:S(2)}, u32[]{:S(2)}) %collective-permute-start.2) | collective-permute-done | bytes 73760 | tf_op jit(solution)/shard_map/ppermute | solution.py:39
  28.3 0.1 select_add_fusion
  28.4 1.4 %collective-permute-start.3 = (f32[72,256]{1,0:T(8,128)S(1)}, f32[72,256]{1,0:T(8,128)S(1)}, u32[]{:S(2)}, u32[]{:S(2)}) collective-permute-start(f32[72,256]{1,0:T(8,128)S(1)} %select_add_fusion), channel_id=1, source_target_pairs={{0,1},{1,0},{2,3},{3,2},{4,5},{5,4},{6,7},{7,6},{8,9},{9,8},{10,11... | collective-permute-start | bytes 221192 | tf_op jit(solution)/shard_map/ppermute | solution.py:39
  29.8 4.1 %collective-permute-start.4 = (f32[72,256]{1,0:T(8,128)S(1)}, f32[72,256]{1,0:T(8,128)S(1)}, u32[]{:S(2)}, u32[]{:S(2)}) collective-permute-start(f32[72,256]{1,0:T(8,128)S(1)} %select_add_fusion), channel_id=1, source_target_pairs={{0,2},{1,3},{2,0},{3,1},{4,6},{5,7},{6,4},{7,5},{8,10},{9,11},{10,... | collective-permute-start | bytes 221192 | tf_op jit(solution)/shard_map/ppermute | solution.py:39
  33.9 0.0 collective-permute-start.5
  33.9 0.0 collective-permute-done.3
  33.9 3.8 %collective-permute-done.4 = f32[72,256]{1,0:T(8,128)S(1)} collective-permute-done((f32[72,256]{1,0:T(8,128)S(1)}, f32[72,256]{1,0:T(8,128)S(1)}, u32[]{:S(2)}, u32[]{:S(2)}) %collective-permute-start.4) | collective-permute-done | bytes 73760 | tf_op jit(solution)/shard_map/ppermute | solution.py:39
  37.7 1.5 %collective-permute-done.5 = f32[72,256]{1,0:T(8,128)S(1)} collective-permute-done((f32[72,256]{1,0:T(8,128)S(1)}, f32[72,256]{1,0:T(8,128)S(1)}, u32[]{:S(2)}, u32[]{:S(2)}) %collective-permute-start.5) | collective-permute-done | bytes 73760 | tf_op jit(solution)/shard_map/ppermute | solution.py:39
  39.2 1.7 %collective-permute-start.6 = (f32[72,256]{1,0:T(8,128)S(1)}, f32[72,256]{1,0:T(8,128)S(1)}, u32[]{:S(2)}, u32[]{:S(2)}) collective-permute-start(f32[72,256]{1,0:T(8,128)S(1)} %add_add_fusion.3), channel_id=1, source_target_pairs={{0,8},{1,9},{2,10},{3,11},{4,12},{5,13},{6,14},{7,15},{8,0},{9,1},... | collective-permute-start | bytes 221192 | tf_op jit(solution)/shard_map/ppermute | solution.py:39
  40.9 1.8 %collective-permute-start.7 = (f32[72,256]{1,0:T(8,128)S(1)}, f32[72,256]{1,0:T(8,128)S(1)}, u32[]{:S(2)}, u32[]{:S(2)}) collective-permute-start(f32[72,256]{1,0:T(8,128)S(1)} %add_add_fusion.3), channel_id=1, source_target_pairs={{0,16},{1,17},{2,18},{3,19},{4,20},{5,21},{6,22},{7,23},{8,24},{9,... | collective-permute-start | bytes 221192 | tf_op jit(solution)/shard_map/ppermute | solution.py:39
  42.7 0.7 collective-permute-start.8
  43.4 0.0 collective-permute-done.6
  43.4 3.1 %collective-permute-done.7 = f32[72,256]{1,0:T(8,128)S(1)} collective-permute-done((f32[72,256]{1,0:T(8,128)S(1)}, f32[72,256]{1,0:T(8,128)S(1)}, u32[]{:S(2)}, u32[]{:S(2)}) %collective-permute-start.7) | collective-permute-done | bytes 73760 | tf_op jit(solution)/shard_map/ppermute | solution.py:39
  46.5 1.4 %collective-permute-done.8 = f32[72,256]{1,0:T(8,128)S(1)} collective-permute-done((f32[72,256]{1,0:T(8,128)S(1)}, f32[72,256]{1,0:T(8,128)S(1)}, u32[]{:S(2)}, u32[]{:S(2)}) %collective-permute-start.8) | collective-permute-done | bytes 73760 | tf_op jit(solution)/shard_map/ppermute | solution.py:39
  48.0 2.8 %collective-permute-start.10 = (f32[72,256]{1,0:T(8,128)S(1)}, f32[72,256]{1,0:T(8,128)S(1)}, u32[]{:S(2)}, u32[]{:S(2)}) collective-permute-start(f32[72,256]{1,0:T(8,128)S(1)} %add_add_fusion.2), channel_id=1, source_target_pairs={{0,64},{1,65},{2,66},{3,67},{4,68},{5,69},{6,70},{7,71},{8,72},{9,... | collective-permute-start | bytes 221192 | tf_op jit(solution)/shard_map/ppermute | solution.py:39
  50.8 0.9 %collective-permute-start.11 = (f32[72,256]{1,0:T(8,128)S(1)}, f32[72,256]{1,0:T(8,128)S(1)}, u32[]{:S(2)}, u32[]{:S(2)}) collective-permute-start(f32[72,256]{1,0:T(8,128)S(1)} %add_add_fusion.2), channel_id=1, source_target_pairs={{0,96},{1,97},{2,98},{3,99},{4,100},{5,101},{6,102},{7,103},{8,104... | collective-permute-start | bytes 221192 | tf_op jit(solution)/shard_map/ppermute | solution.py:39
  51.6 0.0 collective-permute-start.9
  51.6 1.1 %collective-permute-done.10 = f32[72,256]{1,0:T(8,128)S(1)} collective-permute-done((f32[72,256]{1,0:T(8,128)S(1)}, f32[72,256]{1,0:T(8,128)S(1)}, u32[]{:S(2)}, u32[]{:S(2)}) %collective-permute-start.10) | collective-permute-done | bytes 73760 | tf_op jit(solution)/shard_map/ppermute | solution.py:39
  52.7 2.9 %collective-permute-done.11 = f32[72,256]{1,0:T(8,128)S(1)} collective-permute-done((f32[72,256]{1,0:T(8,128)S(1)}, f32[72,256]{1,0:T(8,128)S(1)}, u32[]{:S(2)}, u32[]{:S(2)}) %collective-permute-start.11) | collective-permute-done | bytes 73760 | tf_op jit(solution)/shard_map/ppermute | solution.py:39
  55.7 0.0 collective-permute-done.9
  55.7 2.9 %collective-permute-start.12 = (f32[72,256]{1,0:T(8,128)S(1)}, f32[72,256]{1,0:T(8,128)S(1)}, u32[]{:S(2)}, u32[]{:S(2)}) collective-permute-start(f32[72,256]{1,0:T(8,128)S(1)} %add_add_fusion.1), channel_id=1, source_target_pairs={{0,4},{1,5},{2,6},{3,7},{4,0},{5,1},{6,2},{7,3},{8,12},{9,13},{10,... | collective-permute-start | bytes 221192 | tf_op jit(solution)/shard_map/ppermute | solution.py:39
  58.6 0.9 %collective-permute-done.12 = f32[72,256]{1,0:T(8,128)S(1)} collective-permute-done((f32[72,256]{1,0:T(8,128)S(1)}, f32[72,256]{1,0:T(8,128)S(1)}, u32[]{:S(2)}, u32[]{:S(2)}) %collective-permute-start.12) | collective-permute-done | bytes 73760 | tf_op jit(solution)/shard_map/ppermute | solution.py:39
  59.5 0.7 maximum_select_fusion.packed_ref
  60.2 25.6 %shard_map.69 = (f32[256,256]{1,0:T(8,128)}, f32[512,256]{1,0:T(8,128)}) custom-call(f32[144,256]{1,0:T(8,128)} %maximum_select_fusion.packed_ref, f32[512,256]{1,0:T(8,128)} %copy-done), custom_call_target="tpu_custom_call" | custom-call | tf_op jit(solution)/shard_map/pallas_call | solution.py:159
  (6 shorter events, 0.1 us)
Async XLA Ops:
  4.1 17.7 %collective-permute-start = (f32[4,128,256]{2,1,0:T(8,128)}, f32[4,128,256]{2,1,0:T(8,128)S(1)}, u32[]{:S(2)}, u32[]{:S(2)}) collective-permute-start(f32[4,128,256]{2,1,0:T(8,128)} %get-tuple-element.8), channel_id=1, source_target_pairs={{0,1},{1,2},{2,3},{3,4},{4,5},{5,6},{6,7},{7,8},{8,9},{9,10},{10,1... | collective-permute-start | bytes 1572872 | tf_op jit(solution)/shard_map/ppermute | solution.py:21
  8.2 16.0 %collective-permute-start.1 = (f32[4,128,256]{2,1,0:T(8,128)}, f32[4,128,256]{2,1,0:T(8,128)S(1)}, u32[]{:S(2)}, u32[]{:S(2)}) collective-permute-start(f32[4,128,256]{2,1,0:T(8,128)} %get-tuple-element.9), channel_id=1, source_target_pairs={{1,0},{2,1},{3,2},{4,3},{5,4},{6,5},{7,6},{8,7},{9,8},{10,9},{11,1... | collective-permute-start | bytes 1572872 | tf_op jit(solution)/shard_map/ppermute | solution.py:21
  24.2 1.2 %copy-start.1 = (f32[512,256]{1,0:T(8,128)S(1)}, f32[512,256]{1,0:T(8,128)}, u32[]{:S(2)}) copy-start(f32[512,256]{1,0:T(8,128)} %param.8) | copy-start | bytes 1572868
  24.2 1.2 %copy-start.2 = (f32[512]{0:T(512)S(1)}, f32[512]{0:T(512)}, u32[]{:S(2)}) copy-start(f32[512]{0:T(512)} %param.9) | copy-start | bytes 6148
  25.5 1.0 %copy-start = (f32[512,256]{1,0:T(8,128)}, f32[512,256]{1,0:T(8,128)S(1)}, u32[]{:S(2)}) copy-start(f32[512,256]{1,0:T(8,128)S(1)} %fusion.anomaly_ref) | copy-start | bytes 1572868
  26.9 1.4 %collective-permute-start.2 = (f32[72,256]{1,0:T(8,128)S(1)}, f32[72,256]{1,0:T(8,128)S(1)}, u32[]{:S(2)}, u32[]{:S(2)}) collective-permute-start(f32[72,256]{1,0:T(8,128)S(1)} %broadcast_select_fusion), channel_id=1, source_target_pairs={{0,4},{1,5},{2,6},{3,7},{4,0},{5,1},{6,2},{7,3},{8,12},{9,13},{10,... | collective-permute-start | bytes 221192 | tf_op jit(solution)/shard_map/ppermute | solution.py:39
  28.4 5.5 %collective-permute-start.3 = (f32[72,256]{1,0:T(8,128)S(1)}, f32[72,256]{1,0:T(8,128)S(1)}, u32[]{:S(2)}, u32[]{:S(2)}) collective-permute-start(f32[72,256]{1,0:T(8,128)S(1)} %select_add_fusion), channel_id=1, source_target_pairs={{0,1},{1,0},{2,3},{3,2},{4,5},{5,4},{6,7},{7,6},{8,9},{9,8},{10,11... | collective-permute-start | bytes 221192 | tf_op jit(solution)/shard_map/ppermute | solution.py:39
  29.8 7.9 %collective-permute-start.4 = (f32[72,256]{1,0:T(8,128)S(1)}, f32[72,256]{1,0:T(8,128)S(1)}, u32[]{:S(2)}, u32[]{:S(2)}) collective-permute-start(f32[72,256]{1,0:T(8,128)S(1)} %select_add_fusion), channel_id=1, source_target_pairs={{0,2},{1,3},{2,0},{3,1},{4,6},{5,7},{6,4},{7,5},{8,10},{9,11},{10,... | collective-permute-start | bytes 221192 | tf_op jit(solution)/shard_map/ppermute | solution.py:39
  33.9 5.3 %collective-permute-start.5 = (f32[72,256]{1,0:T(8,128)S(1)}, f32[72,256]{1,0:T(8,128)S(1)}, u32[]{:S(2)}, u32[]{:S(2)}) collective-permute-start(f32[72,256]{1,0:T(8,128)S(1)} %select_add_fusion), channel_id=1, source_target_pairs={{0,3},{1,2},{2,1},{3,0},{4,7},{5,6},{6,5},{7,4},{8,11},{9,10},{10,... | collective-permute-start | bytes 221192 | tf_op jit(solution)/shard_map/ppermute | solution.py:39
  39.2 4.2 %collective-permute-start.6 = (f32[72,256]{1,0:T(8,128)S(1)}, f32[72,256]{1,0:T(8,128)S(1)}, u32[]{:S(2)}, u32[]{:S(2)}) collective-permute-start(f32[72,256]{1,0:T(8,128)S(1)} %add_add_fusion.3), channel_id=1, source_target_pairs={{0,8},{1,9},{2,10},{3,11},{4,12},{5,13},{6,14},{7,15},{8,0},{9,1},... | collective-permute-start | bytes 221192 | tf_op jit(solution)/shard_map/ppermute | solution.py:39
  40.9 5.6 %collective-permute-start.7 = (f32[72,256]{1,0:T(8,128)S(1)}, f32[72,256]{1,0:T(8,128)S(1)}, u32[]{:S(2)}, u32[]{:S(2)}) collective-permute-start(f32[72,256]{1,0:T(8,128)S(1)} %add_add_fusion.3), channel_id=1, source_target_pairs={{0,16},{1,17},{2,18},{3,19},{4,20},{5,21},{6,22},{7,23},{8,24},{9,... | collective-permute-start | bytes 221192 | tf_op jit(solution)/shard_map/ppermute | solution.py:39
  42.7 5.3 %collective-permute-start.8 = (f32[72,256]{1,0:T(8,128)S(1)}, f32[72,256]{1,0:T(8,128)S(1)}, u32[]{:S(2)}, u32[]{:S(2)}) collective-permute-start(f32[72,256]{1,0:T(8,128)S(1)} %add_add_fusion.3), channel_id=1, source_target_pairs={{0,24},{1,25},{2,26},{3,27},{4,28},{5,29},{6,30},{7,31},{8,16},{9,... | collective-permute-start | bytes 221192 | tf_op jit(solution)/shard_map/ppermute | solution.py:39
  48.0 4.8 %collective-permute-start.10 = (f32[72,256]{1,0:T(8,128)S(1)}, f32[72,256]{1,0:T(8,128)S(1)}, u32[]{:S(2)}, u32[]{:S(2)}) collective-permute-start(f32[72,256]{1,0:T(8,128)S(1)} %add_add_fusion.2), channel_id=1, source_target_pairs={{0,64},{1,65},{2,66},{3,67},{4,68},{5,69},{6,70},{7,71},{8,72},{9,... | collective-permute-start | bytes 221192 | tf_op jit(solution)/shard_map/ppermute | solution.py:39
  50.8 4.9 %collective-permute-start.11 = (f32[72,256]{1,0:T(8,128)S(1)}, f32[72,256]{1,0:T(8,128)S(1)}, u32[]{:S(2)}, u32[]{:S(2)}) collective-permute-start(f32[72,256]{1,0:T(8,128)S(1)} %add_add_fusion.2), channel_id=1, source_target_pairs={{0,96},{1,97},{2,98},{3,99},{4,100},{5,101},{6,102},{7,103},{8,104... | collective-permute-start | bytes 221192 | tf_op jit(solution)/shard_map/ppermute | solution.py:39
  51.6 4.0 %collective-permute-start.9 = (f32[72,256]{1,0:T(8,128)S(1)}, f32[72,256]{1,0:T(8,128)S(1)}, u32[]{:S(2)}, u32[]{:S(2)}) collective-permute-start(f32[72,256]{1,0:T(8,128)S(1)} %add_add_fusion.2), channel_id=1, source_target_pairs={{0,32},{1,33},{2,34},{3,35},{4,36},{5,37},{6,38},{7,39},{8,40},{9,... | collective-permute-start | bytes 221192 | tf_op jit(solution)/shard_map/ppermute | solution.py:39
  55.7 3.8 %collective-permute-start.12 = (f32[72,256]{1,0:T(8,128)S(1)}, f32[72,256]{1,0:T(8,128)S(1)}, u32[]{:S(2)}, u32[]{:S(2)}) collective-permute-start(f32[72,256]{1,0:T(8,128)S(1)} %add_add_fusion.1), channel_id=1, source_target_pairs={{0,4},{1,5},{2,6},{3,7},{4,0},{5,1},{6,2},{7,3},{8,12},{9,13},{10,... | collective-permute-start | bytes 221192 | tf_op jit(solution)/shard_map/ppermute | solution.py:39

commit v14 on v13

--- a/solution.py
+++ b/solution.py
@@ -49,7 +49,7 @@
         kept = jnp.where(core == 0, low, high)
         sent = jnp.where(core == 0, high, low)
         value = kept + exchange(sent, count, 1 << CORE_BIT)
-    for group in exchange_stages(count):
+    for group in reversed(exchange_stages(count)):
         masks = []
         for size in range(1, len(group) + 1):
             for combo in itertools.combinations(group, size):

time: 86 us -> 86.2 us (level)
  no operation moved by 1% of the time
where the time goes in v14:
time: 86.2 us; the launch traced here: 86 us
  Pallas kernels  29.1 us (34%)
  waiting for transfers between devices  28 us (32%)
  starting transfers between devices  24.6 us (29%)
  other arithmetic  2.31 us (3%)
  matrix products  1.02 us (1%)
    pallas_call x1, Pallas kernels, cholesky_with_inverse(): pl.pallas_call(functools.partial(cholesky_kernel, factor_scale=1.0 / root...  25.6 us
    ppermute x11, starting transfers between devices, exchange(): lax.ppermute(value, DEVICE_AXES, [(i, i ^ mask) for i in range(count)])  16.6 us
    ppermute x11, waiting for transfers between devices, exchange(): lax.ppermute(value, DEVICE_AXES, [(i, i ^ mask) for i in range(count)])  16 us
    ppermute x2, waiting for transfers between devices, shifted(): lax.ppermute(value, axis, [(source, source + steps) for source in range(i...  12 us
    ppermute x2, starting transfers between devices, shifted(): lax.ppermute(value, axis, [(source, source + steps) for source in range(i...  7.93 us
    pallas_call x1, Pallas kernels, aggregate(): pl.pallas_call(aggregate_kernel, out_shape=(table, table, table), in_spec...  3.5 us
  transfers between devices with their start and end apart: 13, of which 10 were waited for; matrix products, arithmetic and copies ran while one was open for 0% of the time, Pallas kernels for 0%

profile of v14, /device:TPU:1, one launch (start us, length us, event | category | flops | bytes accessed | tf_op | source)
XLA Modules:
  0.0 86.0 jit_solution(7383223780535700788)
XLA Ops:
  0.6 3.5 %shard_map.68 = (f32[4,128,256]{2,1,0:T(8,128)}, f32[4,128,256]{2,1,0:T(8,128)}, f32[4,128,256]{2,1,0:T(8,128)}) custom-call(s32[2,16]{1,0:T(2,128)} %bitcast.17, s32[1]{0:T(128)} %bitcast.1.base_ref, bf16[16,2,128,128]{3,2,1,0:T(8,128)(2,1)} %weight_ref.1, bf16[16,128,256]{2,1,0:T(8,128)(2,1)} %bitcast.14), custom_call_target="tpu_custom_call" | custom-call | tf_op jit(solution)/shard_map/pallas_call | solution.py:190
  4.1 4.0 %collective-permute-start = (f32[4,128,256]{2,1,0:T(8,128)}, f32[4,128,256]{2,1,0:T(8,128)S(1)}, u32[]{:S(2)}, u32[]{:S(2)}) collective-permute-start(f32[4,128,256]{2,1,0:T(8,128)} %get-tuple-element.8), channel_id=1, source_target_pairs={{0,1},{1,2},{2,3},{3,4},{4,5},{5,6},{6,7},{7,8},{8,9},{9,10},{10,1... | collective-permute-start | bytes 1572872 | tf_op jit(solution)/shard_map/ppermute | solution.py:21
  8.2 3.9 %collective-permute-start.1 = (f32[4,128,256]{2,1,0:T(8,128)}, f32[4,128,256]{2,1,0:T(8,128)S(1)}, u32[]{:S(2)}, u32[]{:S(2)}) collective-permute-start(f32[4,128,256]{2,1,0:T(8,128)} %get-tuple-element.9), channel_id=1, source_target_pairs={{1,0},{2,1},{3,2},{4,3},{5,4},{6,5},{7,6},{8,7},{9,8},{10,9},{11,1... | collective-permute-start | bytes 1572872 | tf_op jit(solution)/shard_map/ppermute | solution.py:21
  12.1 0.1 pad_slice_fusion
  12.2 9.7 %collective-permute-done = f32[4,128,256]{2,1,0:T(8,128)S(1)} collective-permute-done((f32[4,128,256]{2,1,0:T(8,128)}, f32[4,128,256]{2,1,0:T(8,128)S(1)}, u32[]{:S(2)}, u32[]{:S(2)}) %collective-permute-start) | collective-permute-done | bytes 524320 | tf_op jit(solution)/shard_map/ppermute | solution.py:21
  21.8 2.3 %collective-permute-done.1 = f32[4,128,256]{2,1,0:T(8,128)S(1)} collective-permute-done((f32[4,128,256]{2,1,0:T(8,128)}, f32[4,128,256]{2,1,0:T(8,128)S(1)}, u32[]{:S(2)}, u32[]{:S(2)}) %collective-permute-start.1) | collective-permute-done | bytes 524320 | tf_op jit(solution)/shard_map/ppermute | solution.py:21
  24.2 0.0 copy-start.1
  24.2 0.0 copy-start.2
  24.2 1.2 %add_add_fusion = f32[4,128,256]{2,1,0:T(8,128)S(1)} fusion(f32[4,128,256]{2,1,0:T(8,128)S(1)} %collective-permute-done.1, f32[4,128,256]{2,1,0:T(8,128)} %get-tuple-element.7, f32[4,128,256]{2,1,0:T(8,128)S(1)} %collective-permute-done), kind=kLoop, calls=%fused_computation.2 | loop fusion | flops 262144 | bytes 2097152 | tf_op jit(solution)/shard_map/add | solution.py:222
  25.4 0.0 copy-done.1
  25.4 0.0 copy-done.2
  25.4 0.1 fusion.anomaly_ref
  25.5 0.0 copy-start
  25.5 1.0 %fusion.7 = f32[256,256]{1,0:T(8,128)S(1)} fusion(f32[512,256]{1,0:T(8,128)S(1)} %fusion.anomaly_ref), kind=kOutput, calls=%fused_computation.25 | convolution fusion | flops 402653184 | bytes 786432 | tf_op jit(solution)/shard_map/dot_general | solution.py:225
  26.6 0.0 copy-done
  26.6 0.1 copy.7
  26.8 0.1 broadcast_select_fusion
  26.9 0.5 collective-permute-start.2
  27.4 0.9 %collective-permute-done.2 = f32[72,256]{1,0:T(8,128)S(1)} collective-permute-done((f32[72,256]{1,0:T(8,128)S(1)}, f32[72,256]{1,0:T(8,128)S(1)}, u32[]{:S(2)}, u32[]{:S(2)}) %collective-permute-start.2) | collective-permute-done | bytes 73760 | tf_op jit(solution)/shard_map/ppermute | solution.py:39
  28.3 0.1 select_add_fusion
  28.4 1.3 %collective-permute-start.3 = (f32[72,256]{1,0:T(8,128)S(1)}, f32[72,256]{1,0:T(8,128)S(1)}, u32[]{:S(2)}, u32[]{:S(2)}) collective-permute-start(f32[72,256]{1,0:T(8,128)S(1)} %select_add_fusion), channel_id=1, source_target_pairs={{0,32},{1,33},{2,34},{3,35},{4,36},{5,37},{6,38},{7,39},{8,40},{9,... | collective-permute-start | bytes 221192 | tf_op jit(solution)/shard_map/ppermute | solution.py:39
  29.7 2.4 %collective-permute-start.4 = (f32[72,256]{1,0:T(8,128)S(1)}, f32[72,256]{1,0:T(8,128)S(1)}, u32[]{:S(2)}, u32[]{:S(2)}) collective-permute-start(f32[72,256]{1,0:T(8,128)S(1)} %select_add_fusion), channel_id=1, source_target_pairs={{0,64},{1,65},{2,66},{3,67},{4,68},{5,69},{6,70},{7,71},{8,72},{9,... | collective-permute-start | bytes 221192 | tf_op jit(solution)/shard_map/ppermute | solution.py:39
  32.1 0.2 collective-permute-start.5
  32.3 0.0 collective-permute-done.3
  32.3 3.1 %collective-permute-done.4 = f32[72,256]{1,0:T(8,128)S(1)} collective-permute-done((f32[72,256]{1,0:T(8,128)S(1)}, f32[72,256]{1,0:T(8,128)S(1)}, u32[]{:S(2)}, u32[]{:S(2)}) %collective-permute-start.4) | collective-permute-done | bytes 73760 | tf_op jit(solution)/shard_map/ppermute | solution.py:39
  35.4 1.6 %collective-permute-done.5 = f32[72,256]{1,0:T(8,128)S(1)} collective-permute-done((f32[72,256]{1,0:T(8,128)S(1)}, f32[72,256]{1,0:T(8,128)S(1)}, u32[]{:S(2)}, u32[]{:S(2)}) %collective-permute-start.5) | collective-permute-done | bytes 73760 | tf_op jit(solution)/shard_map/ppermute | solution.py:39
  37.0 1.7 %collective-permute-start.6 = (f32[72,256]{1,0:T(8,128)S(1)}, f32[72,256]{1,0:T(8,128)S(1)}, u32[]{:S(2)}, u32[]{:S(2)}) collective-permute-start(f32[72,256]{1,0:T(8,128)S(1)} %add_add_fusion.3), channel_id=1, source_target_pairs={{0,8},{1,9},{2,10},{3,11},{4,12},{5,13},{6,14},{7,15},{8,0},{9,1},... | collective-permute-start | bytes 221192 | tf_op jit(solution)/shard_map/ppermute | solution.py:39
  38.8 3.3 %collective-permute-start.7 = (f32[72,256]{1,0:T(8,128)S(1)}, f32[72,256]{1,0:T(8,128)S(1)}, u32[]{:S(2)}, u32[]{:S(2)}) collective-permute-start(f32[72,256]{1,0:T(8,128)S(1)} %add_add_fusion.3), channel_id=1, source_target_pairs={{0,16},{1,17},{2,18},{3,19},{4,20},{5,21},{6,22},{7,23},{8,24},{9,... | collective-permute-start | bytes 221192 | tf_op jit(solution)/shard_map/ppermute | solution.py:39
  42.1 0.0 collective-permute-start.8
  42.1 0.0 collective-permute-done.6
  42.1 2.5 %collective-permute-done.7 = f32[72,256]{1,0:T(8,128)S(1)} collective-permute-done((f32[72,256]{1,0:T(8,128)S(1)}, f32[72,256]{1,0:T(8,128)S(1)}, u32[]{:S(2)}, u32[]{:S(2)}) %collective-permute-start.7) | collective-permute-done | bytes 73760 | tf_op jit(solution)/shard_map/ppermute | solution.py:39
  44.6 2.7 %collective-permute-done.8 = f32[72,256]{1,0:T(8,128)S(1)} collective-permute-done((f32[72,256]{1,0:T(8,128)S(1)}, f32[72,256]{1,0:T(8,128)S(1)}, u32[]{:S(2)}, u32[]{:S(2)}) %collective-permute-start.8) | collective-permute-done | bytes 73760 | tf_op jit(solution)/shard_map/ppermute | solution.py:39
  47.3 2.7 %collective-permute-start.10 = (f32[72,256]{1,0:T(8,128)S(1)}, f32[72,256]{1,0:T(8,128)S(1)}, u32[]{:S(2)}, u32[]{:S(2)}) collective-permute-start(f32[72,256]{1,0:T(8,128)S(1)} %add_add_fusion.2), channel_id=1, source_target_pairs={{0,2},{1,3},{2,0},{3,1},{4,6},{5,7},{6,4},{7,5},{8,10},{9,11},{10,... | collective-permute-start | bytes 221192 | tf_op jit(solution)/shard_map/ppermute | solution.py:39
  50.0 1.1 %collective-permute-start.11 = (f32[72,256]{1,0:T(8,128)S(1)}, f32[72,256]{1,0:T(8,128)S(1)}, u32[]{:S(2)}, u32[]{:S(2)}) collective-permute-start(f32[72,256]{1,0:T(8,128)S(1)} %add_add_fusion.2), channel_id=1, source_target_pairs={{0,3},{1,2},{2,1},{3,0},{4,7},{5,6},{6,5},{7,4},{8,11},{9,10},{10,... | collective-permute-start | bytes 221192 | tf_op jit(solution)/shard_map/ppermute | solution.py:39
  51.1 0.0 collective-permute-start.9
  51.1 1.0 %collective-permute-done.10 = f32[72,256]{1,0:T(8,128)S(1)} collective-permute-done((f32[72,256]{1,0:T(8,128)S(1)}, f32[72,256]{1,0:T(8,128)S(1)}, u32[]{:S(2)}, u32[]{:S(2)}) %collective-permute-start.10) | collective-permute-done | bytes 73760 | tf_op jit(solution)/shard_map/ppermute | solution.py:39
  52.1 3.3 %collective-permute-done.11 = f32[72,256]{1,0:T(8,128)S(1)} collective-permute-done((f32[72,256]{1,0:T(8,128)S(1)}, f32[72,256]{1,0:T(8,128)S(1)}, u32[]{:S(2)}, u32[]{:S(2)}) %collective-permute-start.11) | collective-permute-done | bytes 73760 | tf_op jit(solution)/shard_map/ppermute | solution.py:39
  55.4 0.0 collective-permute-done.9
  55.4 3.3 %collective-permute-start.12 = (f32[72,256]{1,0:T(8,128)S(1)}, f32[72,256]{1,0:T(8,128)S(1)}, u32[]{:S(2)}, u32[]{:S(2)}) collective-permute-start(f32[72,256]{1,0:T(8,128)S(1)} %add_add_fusion.1), channel_id=1, source_target_pairs={{0,4},{1,5},{2,6},{3,7},{4,0},{5,1},{6,2},{7,3},{8,12},{9,13},{10,... | collective-permute-start | bytes 221192 | tf_op jit(solution)/shard_map/ppermute | solution.py:39
  58.8 0.9 %collective-permute-done.12 = f32[72,256]{1,0:T(8,128)S(1)} collective-permute-done((f32[72,256]{1,0:T(8,128)S(1)}, f32[72,256]{1,0:T(8,128)S(1)}, u32[]{:S(2)}, u32[]{:S(2)}) %collective-permute-start.12) | collective-permute-done | bytes 73760 | tf_op jit(solution)/shard_map/ppermute | solution.py:39
  59.7 0.7 maximum_select_fusion.packed_ref
  60.3 25.6 %shard_map.69 = (f32[256,256]{1,0:T(8,128)}, f32[512,256]{1,0:T(8,128)}) custom-call(f32[144,256]{1,0:T(8,128)} %maximum_select_fusion.packed_ref, f32[512,256]{1,0:T(8,128)} %copy-done), custom_call_target="tpu_custom_call" | custom-call | tf_op jit(solution)/shard_map/pallas_call | solution.py:159
  (6 shorter events, 0.1 us)
Async XLA Ops:
  4.1 17.7 %collective-permute-start = (f32[4,128,256]{2,1,0:T(8,128)}, f32[4,128,256]{2,1,0:T(8,128)S(1)}, u32[]{:S(2)}, u32[]{:S(2)}) collective-permute-start(f32[4,128,256]{2,1,0:T(8,128)} %get-tuple-element.8), channel_id=1, source_target_pairs={{0,1},{1,2},{2,3},{3,4},{4,5},{5,6},{6,7},{7,8},{8,9},{9,10},{10,1... | collective-permute-start | bytes 1572872 | tf_op jit(solution)/shard_map/ppermute | solution.py:21
  8.2 16.0 %collective-permute-start.1 = (f32[4,128,256]{2,1,0:T(8,128)}, f32[4,128,256]{2,1,0:T(8,128)S(1)}, u32[]{:S(2)}, u32[]{:S(2)}) collective-permute-start(f32[4,128,256]{2,1,0:T(8,128)} %get-tuple-element.9), channel_id=1, source_target_pairs={{1,0},{2,1},{3,2},{4,3},{5,4},{6,5},{7,6},{8,7},{9,8},{10,9},{11,1... | collective-permute-start | bytes 1572872 | tf_op jit(solution)/shard_map/ppermute | solution.py:21
  24.2 1.2 %copy-start.1 = (f32[512,256]{1,0:T(8,128)S(1)}, f32[512,256]{1,0:T(8,128)}, u32[]{:S(2)}) copy-start(f32[512,256]{1,0:T(8,128)} %param.8) | copy-start | bytes 1572868
  24.2 1.2 %copy-start.2 = (f32[512]{0:T(512)S(1)}, f32[512]{0:T(512)}, u32[]{:S(2)}) copy-start(f32[512]{0:T(512)} %param.9) | copy-start | bytes 6148
  25.5 1.0 %copy-start = (f32[512,256]{1,0:T(8,128)}, f32[512,256]{1,0:T(8,128)S(1)}, u32[]{:S(2)}) copy-start(f32[512,256]{1,0:T(8,128)S(1)} %fusion.anomaly_ref) | copy-start | bytes 1572868
  26.9 1.4 %collective-permute-start.2 = (f32[72,256]{1,0:T(8,128)S(1)}, f32[72,256]{1,0:T(8,128)S(1)}, u32[]{:S(2)}, u32[]{:S(2)}) collective-permute-start(f32[72,256]{1,0:T(8,128)S(1)} %broadcast_select_fusion), channel_id=1, source_target_pairs={{0,4},{1,5},{2,6},{3,7},{4,0},{5,1},{6,2},{7,3},{8,12},{9,13},{10,... | collective-permute-start | bytes 221192 | tf_op jit(solution)/shard_map/ppermute | solution.py:39
  28.4 3.9 %collective-permute-start.3 = (f32[72,256]{1,0:T(8,128)S(1)}, f32[72,256]{1,0:T(8,128)S(1)}, u32[]{:S(2)}, u32[]{:S(2)}) collective-permute-start(f32[72,256]{1,0:T(8,128)S(1)} %select_add_fusion), channel_id=1, source_target_pairs={{0,32},{1,33},{2,34},{3,35},{4,36},{5,37},{6,38},{7,39},{8,40},{9,... | collective-permute-start | bytes 221192 | tf_op jit(solution)/shard_map/ppermute | solution.py:39
  29.7 5.7 %collective-permute-start.4 = (f32[72,256]{1,0:T(8,128)S(1)}, f32[72,256]{1,0:T(8,128)S(1)}, u32[]{:S(2)}, u32[]{:S(2)}) collective-permute-start(f32[72,256]{1,0:T(8,128)S(1)} %select_add_fusion), channel_id=1, source_target_pairs={{0,64},{1,65},{2,66},{3,67},{4,68},{5,69},{6,70},{7,71},{8,72},{9,... | collective-permute-start | bytes 221192 | tf_op jit(solution)/shard_map/ppermute | solution.py:39
  32.1 4.9 %collective-permute-start.5 = (f32[72,256]{1,0:T(8,128)S(1)}, f32[72,256]{1,0:T(8,128)S(1)}, u32[]{:S(2)}, u32[]{:S(2)}) collective-permute-start(f32[72,256]{1,0:T(8,128)S(1)} %select_add_fusion), channel_id=1, source_target_pairs={{0,96},{1,97},{2,98},{3,99},{4,100},{5,101},{6,102},{7,103},{8,104... | collective-permute-start | bytes 221192 | tf_op jit(solution)/shard_map/ppermute | solution.py:39
  37.0 5.0 %collective-permute-start.6 = (f32[72,256]{1,0:T(8,128)S(1)}, f32[72,256]{1,0:T(8,128)S(1)}, u32[]{:S(2)}, u32[]{:S(2)}) collective-permute-start(f32[72,256]{1,0:T(8,128)S(1)} %add_add_fusion.3), channel_id=1, source_target_pairs={{0,8},{1,9},{2,10},{3,11},{4,12},{5,13},{6,14},{7,15},{8,0},{9,1},... | collective-permute-start | bytes 221192 | tf_op jit(solution)/shard_map/ppermute | solution.py:39
  38.8 5.8 %collective-permute-start.7 = (f32[72,256]{1,0:T(8,128)S(1)}, f32[72,256]{1,0:T(8,128)S(1)}, u32[]{:S(2)}, u32[]{:S(2)}) collective-permute-start(f32[72,256]{1,0:T(8,128)S(1)} %add_add_fusion.3), channel_id=1, source_target_pairs={{0,16},{1,17},{2,18},{3,19},{4,20},{5,21},{6,22},{7,23},{8,24},{9,... | collective-permute-start | bytes 221192 | tf_op jit(solution)/shard_map/ppermute | solution.py:39
  42.1 5.2 %collective-permute-start.8 = (f32[72,256]{1,0:T(8,128)S(1)}, f32[72,256]{1,0:T(8,128)S(1)}, u32[]{:S(2)}, u32[]{:S(2)}) collective-permute-start(f32[72,256]{1,0:T(8,128)S(1)} %add_add_fusion.3), channel_id=1, source_target_pairs={{0,24},{1,25},{2,26},{3,27},{4,28},{5,29},{6,30},{7,31},{8,16},{9,... | collective-permute-start | bytes 221192 | tf_op jit(solution)/shard_map/ppermute | solution.py:39
  47.3 4.8 %collective-permute-start.10 = (f32[72,256]{1,0:T(8,128)S(1)}, f32[72,256]{1,0:T(8,128)S(1)}, u32[]{:S(2)}, u32[]{:S(2)}) collective-permute-start(f32[72,256]{1,0:T(8,128)S(1)} %add_add_fusion.2), channel_id=1, source_target_pairs={{0,2},{1,3},{2,0},{3,1},{4,6},{5,7},{6,4},{7,5},{8,10},{9,11},{10,... | collective-permute-start | bytes 221192 | tf_op jit(solution)/shard_map/ppermute | solution.py:39
  50.0 5.4 %collective-permute-start.11 = (f32[72,256]{1,0:T(8,128)S(1)}, f32[72,256]{1,0:T(8,128)S(1)}, u32[]{:S(2)}, u32[]{:S(2)}) collective-permute-start(f32[72,256]{1,0:T(8,128)S(1)} %add_add_fusion.2), channel_id=1, source_target_pairs={{0,3},{1,2},{2,1},{3,0},{4,7},{5,6},{6,5},{7,4},{8,11},{9,10},{10,... | collective-permute-start | bytes 221192 | tf_op jit(solution)/shard_map/ppermute | solution.py:39
  51.1 4.3 %collective-permute-start.9 = (f32[72,256]{1,0:T(8,128)S(1)}, f32[72,256]{1,0:T(8,128)S(1)}, u32[]{:S(2)}, u32[]{:S(2)}) collective-permute-start(f32[72,256]{1,0:T(8,128)S(1)} %add_add_fusion.2), channel_id=1, source_target_pairs={{0,1},{1,0},{2,3},{3,2},{4,5},{5,4},{6,7},{7,6},{8,9},{9,8},{10,11... | collective-permute-start | bytes 221192 | tf_op jit(solution)/shard_map/ppermute | solution.py:39
  55.4 4.3 %collective-permute-start.12 = (f32[72,256]{1,0:T(8,128)S(1)}, f32[72,256]{1,0:T(8,128)S(1)}, u32[]{:S(2)}, u32[]{:S(2)}) collective-permute-start(f32[72,256]{1,0:T(8,128)S(1)} %add_add_fusion.1), channel_id=1, source_target_pairs={{0,4},{1,5},{2,6},{3,7},{4,0},{5,1},{6,2},{7,3},{8,12},{9,13},{10,... | collective-permute-start | bytes 221192 | tf_op jit(solution)/shard_map/ppermute | solution.py:39

commit v15 on v13

--- a/solution.py
+++ b/solution.py
@@ -12,7 +12,7 @@
 exact_mode = lax.Precision.HIGHEST
 DEVICE_AXES = ("lat", "sub")
 CORE_BIT = 2
-PANEL = 64
+PANEL = 32
 
 
 def shifted(value, axis, steps):

time: 86 us -> 87 us (1.012)
  Pallas kernels: 29.1 us -> 30.1 us
    pallas_call x1, Pallas kernels: 25.6 us -> 26.6 us  [cholesky_with_inverse(): pl.pallas_call(functools.partial(cholesky_kernel, factor_scale=1.0 / root...]
where the time goes in v15:
time: 87 us; the launch traced here: 86.8 us
  Pallas kernels  30.1 us (35%)
  waiting for transfers between devices  27.6 us (32%)
  starting transfers between devices  24.7 us (28%)
  other arithmetic  2.31 us (3%)
  matrix products  1.02 us (1%)
    pallas_call x1, Pallas kernels, cholesky_with_inverse(): pl.pallas_call(functools.partial(cholesky_kernel, factor_scale=1.0 / root...  26.6 us
    ppermute x11, starting transfers between devices, exchange(): lax.ppermute(value, DEVICE_AXES, [(i, i ^ mask) for i in range(count)])  16.8 us
    ppermute x11, waiting for transfers between devices, exchange(): lax.ppermute(value, DEVICE_AXES, [(i, i ^ mask) for i in range(count)])  15.7 us
    ppermute x2, waiting for transfers between devices, shifted(): lax.ppermute(value, axis, [(source, source + steps) for source in range(i...  12 us
    ppermute x2, starting transfers between devices, shifted(): lax.ppermute(value, axis, [(source, source + steps) for source in range(i...  7.93 us
    pallas_call x1, Pallas kernels, aggregate(): pl.pallas_call(aggregate_kernel, out_shape=(table, table, table), in_spec...  3.5 us
  transfers between devices with their start and end apart: 13, of which 10 were waited for; matrix products, arithmetic and copies ran while one was open for 0% of the time, Pallas kernels for 0%

profile of v15, /device:TPU:1, one launch (start us, length us, event | category | flops | bytes accessed | tf_op | source)
XLA Modules:
  0.0 86.8 jit_solution(11775982369711203930)
XLA Ops:
  0.6 3.5 %shard_map.68 = (f32[4,128,256]{2,1,0:T(8,128)}, f32[4,128,256]{2,1,0:T(8,128)}, f32[4,128,256]{2,1,0:T(8,128)}) custom-call(s32[2,16]{1,0:T(2,128)} %bitcast.17, s32[1]{0:T(128)} %bitcast.1.base_ref, bf16[16,2,128,128]{3,2,1,0:T(8,128)(2,1)} %weight_ref.1, bf16[16,128,256]{2,1,0:T(8,128)(2,1)} %bitcast.14), custom_call_target="tpu_custom_call" | custom-call | tf_op jit(solution)/shard_map/pallas_call | solution.py:190
  4.1 4.0 %collective-permute-start = (f32[4,128,256]{2,1,0:T(8,128)}, f32[4,128,256]{2,1,0:T(8,128)S(1)}, u32[]{:S(2)}, u32[]{:S(2)}) collective-permute-start(f32[4,128,256]{2,1,0:T(8,128)} %get-tuple-element.8), channel_id=1, source_target_pairs={{0,1},{1,2},{2,3},{3,4},{4,5},{5,6},{6,7},{7,8},{8,9},{9,10},{10,1... | collective-permute-start | bytes 1572872 | tf_op jit(solution)/shard_map/ppermute | solution.py:21
  8.2 3.9 %collective-permute-start.1 = (f32[4,128,256]{2,1,0:T(8,128)}, f32[4,128,256]{2,1,0:T(8,128)S(1)}, u32[]{:S(2)}, u32[]{:S(2)}) collective-permute-start(f32[4,128,256]{2,1,0:T(8,128)} %get-tuple-element.9), channel_id=1, source_target_pairs={{1,0},{2,1},{3,2},{4,3},{5,4},{6,5},{7,6},{8,7},{9,8},{10,9},{11,1... | collective-permute-start | bytes 1572872 | tf_op jit(solution)/shard_map/ppermute | solution.py:21
  12.1 0.1 pad_slice_fusion
  12.2 9.7 %collective-permute-done = f32[4,128,256]{2,1,0:T(8,128)S(1)} collective-permute-done((f32[4,128,256]{2,1,0:T(8,128)}, f32[4,128,256]{2,1,0:T(8,128)S(1)}, u32[]{:S(2)}, u32[]{:S(2)}) %collective-permute-start) | collective-permute-done | bytes 524320 | tf_op jit(solution)/shard_map/ppermute | solution.py:21
  21.8 2.3 %collective-permute-done.1 = f32[4,128,256]{2,1,0:T(8,128)S(1)} collective-permute-done((f32[4,128,256]{2,1,0:T(8,128)}, f32[4,128,256]{2,1,0:T(8,128)S(1)}, u32[]{:S(2)}, u32[]{:S(2)}) %collective-permute-start.1) | collective-permute-done | bytes 524320 | tf_op jit(solution)/shard_map/ppermute | solution.py:21
  24.1 0.0 copy-start.1
  24.1 0.0 copy-start.2
  24.2 1.2 %add_add_fusion = f32[4,128,256]{2,1,0:T(8,128)S(1)} fusion(f32[4,128,256]{2,1,0:T(8,128)S(1)} %collective-permute-done.1, f32[4,128,256]{2,1,0:T(8,128)} %get-tuple-element.7, f32[4,128,256]{2,1,0:T(8,128)S(1)} %collective-permute-done), kind=kLoop, calls=%fused_computation.2 | loop fusion | flops 262144 | bytes 2097152 | tf_op jit(solution)/shard_map/add | solution.py:222
  25.4 0.0 copy-done.1
  25.4 0.0 copy-done.2
  25.4 0.1 fusion.anomaly_ref
  25.5 0.0 copy-start
  25.5 1.0 %fusion.7 = f32[256,256]{1,0:T(8,128)S(1)} fusion(f32[512,256]{1,0:T(8,128)S(1)} %fusion.anomaly_ref), kind=kOutput, calls=%fused_computation.25 | convolution fusion | flops 402653184 | bytes 786432 | tf_op jit(solution)/shard_map/dot_general | solution.py:225
  26.6 0.0 copy-done
  26.6 0.1 copy.7
  26.8 0.1 broadcast_select_fusion
  26.9 0.5 collective-permute-start.2
  27.4 0.9 %collective-permute-done.2 = f32[72,256]{1,0:T(8,128)S(1)} collective-permute-done((f32[72,256]{1,0:T(8,128)S(1)}, f32[72,256]{1,0:T(8,128)S(1)}, u32[]{:S(2)}, u32[]{:S(2)}) %collective-permute-start.2) | collective-permute-done | bytes 73760 | tf_op jit(solution)/shard_map/ppermute | solution.py:39
  28.3 0.1 select_add_fusion
  28.4 1.4 %collective-permute-start.3 = (f32[72,256]{1,0:T(8,128)S(1)}, f32[72,256]{1,0:T(8,128)S(1)}, u32[]{:S(2)}, u32[]{:S(2)}) collective-permute-start(f32[72,256]{1,0:T(8,128)S(1)} %select_add_fusion), channel_id=1, source_target_pairs={{0,1},{1,0},{2,3},{3,2},{4,5},{5,4},{6,7},{7,6},{8,9},{9,8},{10,11... | collective-permute-start | bytes 221192 | tf_op jit(solution)/shard_map/ppermute | solution.py:39
  29.8 4.1 %collective-permute-start.4 = (f32[72,256]{1,0:T(8,128)S(1)}, f32[72,256]{1,0:T(8,128)S(1)}, u32[]{:S(2)}, u32[]{:S(2)}) collective-permute-start(f32[72,256]{1,0:T(8,128)S(1)} %select_add_fusion), channel_id=1, source_target_pairs={{0,2},{1,3},{2,0},{3,1},{4,6},{5,7},{6,4},{7,5},{8,10},{9,11},{10,... | collective-permute-start | bytes 221192 | tf_op jit(solution)/shard_map/ppermute | solution.py:39
  33.9 0.0 collective-permute-start.5
  33.9 0.0 collective-permute-done.3
  33.9 3.8 %collective-permute-done.4 = f32[72,256]{1,0:T(8,128)S(1)} collective-permute-done((f32[72,256]{1,0:T(8,128)S(1)}, f32[72,256]{1,0:T(8,128)S(1)}, u32[]{:S(2)}, u32[]{:S(2)}) %collective-permute-start.4) | collective-permute-done | bytes 73760 | tf_op jit(solution)/shard_map/ppermute | solution.py:39
  37.7 1.5 %collective-permute-done.5 = f32[72,256]{1,0:T(8,128)S(1)} collective-permute-done((f32[72,256]{1,0:T(8,128)S(1)}, f32[72,256]{1,0:T(8,128)S(1)}, u32[]{:S(2)}, u32[]{:S(2)}) %collective-permute-start.5) | collective-permute-done | bytes 73760 | tf_op jit(solution)/shard_map/ppermute | solution.py:39
  39.2 1.7 %collective-permute-start.6 = (f32[72,256]{1,0:T(8,128)S(1)}, f32[72,256]{1,0:T(8,128)S(1)}, u32[]{:S(2)}, u32[]{:S(2)}) collective-permute-start(f32[72,256]{1,0:T(8,128)S(1)} %add_add_fusion.3), channel_id=1, source_target_pairs={{0,8},{1,9},{2,10},{3,11},{4,12},{5,13},{6,14},{7,15},{8,0},{9,1},... | collective-permute-start | bytes 221192 | tf_op jit(solution)/shard_map/ppermute | solution.py:39
  40.9 1.8 %collective-permute-start.7 = (f32[72,256]{1,0:T(8,128)S(1)}, f32[72,256]{1,0:T(8,128)S(1)}, u32[]{:S(2)}, u32[]{:S(2)}) collective-permute-start(f32[72,256]{1,0:T(8,128)S(1)} %add_add_fusion.3), channel_id=1, source_target_pairs={{0,16},{1,17},{2,18},{3,19},{4,20},{5,21},{6,22},{7,23},{8,24},{9,... | collective-permute-start | bytes 221192 | tf_op jit(solution)/shard_map/ppermute | solution.py:39
  42.7 0.7 collective-permute-start.8
  43.4 0.0 collective-permute-done.6
  43.4 3.1 %collective-permute-done.7 = f32[72,256]{1,0:T(8,128)S(1)} collective-permute-done((f32[72,256]{1,0:T(8,128)S(1)}, f32[72,256]{1,0:T(8,128)S(1)}, u32[]{:S(2)}, u32[]{:S(2)}) %collective-permute-start.7) | collective-permute-done | bytes 73760 | tf_op jit(solution)/shard_map/ppermute | solution.py:39
  46.5 1.4 %collective-permute-done.8 = f32[72,256]{1,0:T(8,128)S(1)} collective-permute-done((f32[72,256]{1,0:T(8,128)S(1)}, f32[72,256]{1,0:T(8,128)S(1)}, u32[]{:S(2)}, u32[]{:S(2)}) %collective-permute-start.8) | collective-permute-done | bytes 73760 | tf_op jit(solution)/shard_map/ppermute | solution.py:39
  48.0 2.8 %collective-permute-start.10 = (f32[72,256]{1,0:T(8,128)S(1)}, f32[72,256]{1,0:T(8,128)S(1)}, u32[]{:S(2)}, u32[]{:S(2)}) collective-permute-start(f32[72,256]{1,0:T(8,128)S(1)} %add_add_fusion.2), channel_id=1, source_target_pairs={{0,64},{1,65},{2,66},{3,67},{4,68},{5,69},{6,70},{7,71},{8,72},{9,... | collective-permute-start | bytes 221192 | tf_op jit(solution)/shard_map/ppermute | solution.py:39
  50.8 0.9 collective-permute-start.11
  51.6 0.0 collective-permute-start.9
  51.6 1.1 %collective-permute-done.10 = f32[72,256]{1,0:T(8,128)S(1)} collective-permute-done((f32[72,256]{1,0:T(8,128)S(1)}, f32[72,256]{1,0:T(8,128)S(1)}, u32[]{:S(2)}, u32[]{:S(2)}) %collective-permute-start.10) | collective-permute-done | bytes 73760 | tf_op jit(solution)/shard_map/ppermute | solution.py:39
  52.7 2.9 %collective-permute-done.11 = f32[72,256]{1,0:T(8,128)S(1)} collective-permute-done((f32[72,256]{1,0:T(8,128)S(1)}, f32[72,256]{1,0:T(8,128)S(1)}, u32[]{:S(2)}, u32[]{:S(2)}) %collective-permute-start.11) | collective-permute-done | bytes 73760 | tf_op jit(solution)/shard_map/ppermute | solution.py:39
  55.7 0.0 collective-permute-done.9
  55.7 2.9 %collective-permute-start.12 = (f32[72,256]{1,0:T(8,128)S(1)}, f32[72,256]{1,0:T(8,128)S(1)}, u32[]{:S(2)}, u32[]{:S(2)}) collective-permute-start(f32[72,256]{1,0:T(8,128)S(1)} %add_add_fusion.1), channel_id=1, source_target_pairs={{0,4},{1,5},{2,6},{3,7},{4,0},{5,1},{6,2},{7,3},{8,12},{9,13},{10,... | collective-permute-start | bytes 221192 | tf_op jit(solution)/shard_map/ppermute | solution.py:39
  58.6 0.9 %collective-permute-done.12 = f32[72,256]{1,0:T(8,128)S(1)} collective-permute-done((f32[72,256]{1,0:T(8,128)S(1)}, f32[72,256]{1,0:T(8,128)S(1)}, u32[]{:S(2)}, u32[]{:S(2)}) %collective-permute-start.12) | collective-permute-done | bytes 73760 | tf_op jit(solution)/shard_map/ppermute | solution.py:39
  59.5 0.7 maximum_select_fusion.packed_ref
  60.2 26.6 %shard_map.69 = (f32[256,256]{1,0:T(8,128)}, f32[512,256]{1,0:T(8,128)}) custom-call(f32[144,256]{1,0:T(8,128)} %maximum_select_fusion.packed_ref, f32[512,256]{1,0:T(8,128)} %copy-done), custom_call_target="tpu_custom_call" | custom-call | tf_op jit(solution)/shard_map/pallas_call | solution.py:159
  (6 shorter events, 0.1 us)
Async XLA Ops:
  4.1 17.7 %collective-permute-start = (f32[4,128,256]{2,1,0:T(8,128)}, f32[4,128,256]{2,1,0:T(8,128)S(1)}, u32[]{:S(2)}, u32[]{:S(2)}) collective-permute-start(f32[4,128,256]{2,1,0:T(8,128)} %get-tuple-element.8), channel_id=1, source_target_pairs={{0,1},{1,2},{2,3},{3,4},{4,5},{5,6},{6,7},{7,8},{8,9},{9,10},{10,1... | collective-permute-start | bytes 1572872 | tf_op jit(solution)/shard_map/ppermute | solution.py:21
  8.2 16.0 %collective-permute-start.1 = (f32[4,128,256]{2,1,0:T(8,128)}, f32[4,128,256]{2,1,0:T(8,128)S(1)}, u32[]{:S(2)}, u32[]{:S(2)}) collective-permute-start(f32[4,128,256]{2,1,0:T(8,128)} %get-tuple-element.9), channel_id=1, source_target_pairs={{1,0},{2,1},{3,2},{4,3},{5,4},{6,5},{7,6},{8,7},{9,8},{10,9},{11,1... | collective-permute-start | bytes 1572872 | tf_op jit(solution)/shard_map/ppermute | solution.py:21
  24.1 1.2 %copy-start.1 = (f32[512,256]{1,0:T(8,128)S(1)}, f32[512,256]{1,0:T(8,128)}, u32[]{:S(2)}) copy-start(f32[512,256]{1,0:T(8,128)} %param.8) | copy-start | bytes 1572868
  24.1 1.2 %copy-start.2 = (f32[512]{0:T(512)S(1)}, f32[512]{0:T(512)}, u32[]{:S(2)}) copy-start(f32[512]{0:T(512)} %param.9) | copy-start | bytes 6148
  25.5 1.0 %copy-start = (f32[512,256]{1,0:T(8,128)}, f32[512,256]{1,0:T(8,128)S(1)}, u32[]{:S(2)}) copy-start(f32[512,256]{1,0:T(8,128)S(1)} %fusion.anomaly_ref) | copy-start | bytes 1572868
  26.9 1.4 %collective-permute-start.2 = (f32[72,256]{1,0:T(8,128)S(1)}, f32[72,256]{1,0:T(8,128)S(1)}, u32[]{:S(2)}, u32[]{:S(2)}) collective-permute-start(f32[72,256]{1,0:T(8,128)S(1)} %broadcast_select_fusion), channel_id=1, source_target_pairs={{0,4},{1,5},{2,6},{3,7},{4,0},{5,1},{6,2},{7,3},{8,12},{9,13},{10,... | collective-permute-start | bytes 221192 | tf_op jit(solution)/shard_map/ppermute | solution.py:39
  28.4 5.5 %collective-permute-start.3 = (f32[72,256]{1,0:T(8,128)S(1)}, f32[72,256]{1,0:T(8,128)S(1)}, u32[]{:S(2)}, u32[]{:S(2)}) collective-permute-start(f32[72,256]{1,0:T(8,128)S(1)} %select_add_fusion), channel_id=1, source_target_pairs={{0,1},{1,0},{2,3},{3,2},{4,5},{5,4},{6,7},{7,6},{8,9},{9,8},{10,11... | collective-permute-start | bytes 221192 | tf_op jit(solution)/shard_map/ppermute | solution.py:39
  29.8 7.9 %collective-permute-start.4 = (f32[72,256]{1,0:T(8,128)S(1)}, f32[72,256]{1,0:T(8,128)S(1)}, u32[]{:S(2)}, u32[]{:S(2)}) collective-permute-start(f32[72,256]{1,0:T(8,128)S(1)} %select_add_fusion), channel_id=1, source_target_pairs={{0,2},{1,3},{2,0},{3,1},{4,6},{5,7},{6,4},{7,5},{8,10},{9,11},{10,... | collective-permute-start | bytes 221192 | tf_op jit(solution)/shard_map/ppermute | solution.py:39
  33.9 5.3 %collective-permute-start.5 = (f32[72,256]{1,0:T(8,128)S(1)}, f32[72,256]{1,0:T(8,128)S(1)}, u32[]{:S(2)}, u32[]{:S(2)}) collective-permute-start(f32[72,256]{1,0:T(8,128)S(1)} %select_add_fusion), channel_id=1, source_target_pairs={{0,3},{1,2},{2,1},{3,0},{4,7},{5,6},{6,5},{7,4},{8,11},{9,10},{10,... | collective-permute-start | bytes 221192 | tf_op jit(solution)/shard_map/ppermute | solution.py:39
  39.2 4.2 %collective-permute-start.6 = (f32[72,256]{1,0:T(8,128)S(1)}, f32[72,256]{1,0:T(8,128)S(1)}, u32[]{:S(2)}, u32[]{:S(2)}) collective-permute-start(f32[72,256]{1,0:T(8,128)S(1)} %add_add_fusion.3), channel_id=1, source_target_pairs={{0,8},{1,9},{2,10},{3,11},{4,12},{5,13},{6,14},{7,15},{8,0},{9,1},... | collective-permute-start | bytes 221192 | tf_op jit(solution)/shard_map/ppermute | solution.py:39
  40.9 5.6 %collective-permute-start.7 = (f32[72,256]{1,0:T(8,128)S(1)}, f32[72,256]{1,0:T(8,128)S(1)}, u32[]{:S(2)}, u32[]{:S(2)}) collective-permute-start(f32[72,256]{1,0:T(8,128)S(1)} %add_add_fusion.3), channel_id=1, source_target_pairs={{0,16},{1,17},{2,18},{3,19},{4,20},{5,21},{6,22},{7,23},{8,24},{9,... | collective-permute-start | bytes 221192 | tf_op jit(solution)/shard_map/ppermute | solution.py:39
  42.7 5.3 %collective-permute-start.8 = (f32[72,256]{1,0:T(8,128)S(1)}, f32[72,256]{1,0:T(8,128)S(1)}, u32[]{:S(2)}, u32[]{:S(2)}) collective-permute-start(f32[72,256]{1,0:T(8,128)S(1)} %add_add_fusion.3), channel_id=1, source_target_pairs={{0,24},{1,25},{2,26},{3,27},{4,28},{5,29},{6,30},{7,31},{8,16},{9,... | collective-permute-start | bytes 221192 | tf_op jit(solution)/shard_map/ppermute | solution.py:39
  48.0 4.8 %collective-permute-start.10 = (f32[72,256]{1,0:T(8,128)S(1)}, f32[72,256]{1,0:T(8,128)S(1)}, u32[]{:S(2)}, u32[]{:S(2)}) collective-permute-start(f32[72,256]{1,0:T(8,128)S(1)} %add_add_fusion.2), channel_id=1, source_target_pairs={{0,64},{1,65},{2,66},{3,67},{4,68},{5,69},{6,70},{7,71},{8,72},{9,... | collective-permute-start | bytes 221192 | tf_op jit(solution)/shard_map/ppermute | solution.py:39
  50.8 4.9 %collective-permute-start.11 = (f32[72,256]{1,0:T(8,128)S(1)}, f32[72,256]{1,0:T(8,128)S(1)}, u32[]{:S(2)}, u32[]{:S(2)}) collective-permute-start(f32[72,256]{1,0:T(8,128)S(1)} %add_add_fusion.2), channel_id=1, source_target_pairs={{0,96},{1,97},{2,98},{3,99},{4,100},{5,101},{6,102},{7,103},{8,104... | collective-permute-start | bytes 221192 | tf_op jit(solution)/shard_map/ppermute | solution.py:39
  51.6 4.0 %collective-permute-start.9 = (f32[72,256]{1,0:T(8,128)S(1)}, f32[72,256]{1,0:T(8,128)S(1)}, u32[]{:S(2)}, u32[]{:S(2)}) collective-permute-start(f32[72,256]{1,0:T(8,128)S(1)} %add_add_fusion.2), channel_id=1, source_target_pairs={{0,32},{1,33},{2,34},{3,35},{4,36},{5,37},{6,38},{7,39},{8,40},{9,... | collective-permute-start | bytes 221192 | tf_op jit(solution)/shard_map/ppermute | solution.py:39
  55.7 3.8 %collective-permute-start.12 = (f32[72,256]{1,0:T(8,128)S(1)}, f32[72,256]{1,0:T(8,128)S(1)}, u32[]{:S(2)}, u32[]{:S(2)}) collective-permute-start(f32[72,256]{1,0:T(8,128)S(1)} %add_add_fusion.1), channel_id=1, source_target_pairs={{0,4},{1,5},{2,6},{3,7},{4,0},{5,1},{6,2},{7,3},{8,12},{9,13},{10,... | collective-permute-start | bytes 221192 | tf_op jit(solution)/shard_map/ppermute | solution.py:39

commit v16 on v15

--- a/solution.py
+++ b/solution.py
@@ -12,7 +12,7 @@
 exact_mode = lax.Precision.HIGHEST
 DEVICE_AXES = ("lat", "sub")
 CORE_BIT = 2
-PANEL = 32
+PANEL = 128
 
 
 def shifted(value, axis, steps):
@@ -140,12 +140,11 @@
         inverse_ref[row0:, :col1] = inverse_ref[row0:, :col1] - jnp.dot(
             lower_cols, inverse_slab, precision=exact_mode, preferred_element_type=jnp.float32)
 
-    quarter = size // 4
-    for part in range(4):
-        row0 = quarter * part
-        col0 = (size // 2) * (part // 2)
-        col1 = (size // 2) * (part // 2 + 1)
-        for first in range(row0, row0 + quarter, PANEL):
+    part_rows = max(PANEL, size // 4)
+    for row0 in range(0, size, part_rows):
+        col0 = (size // 2) * (row0 // (size // 2))
+        col1 = col0 + size // 2
+        for first in range(row0, row0 + part_rows, PANEL):
             panel(first, row0, col0, col1)
     scores_ref[...] = lax.dot_general(
         anomaly_ref[...], inverse_ref[...], (((1,), (1,)), ((), ())),

time: 87 us -> 85.6 us (0.984)
  Pallas kernels: 30.1 us -> 28.8 us
    pallas_call x1, Pallas kernels: 26.6 us -> 25.3 us  [cholesky_with_inverse(): pl.pallas_call(functools.partial(cholesky_kernel, factor_scale=1.0 / root...]
where the time goes in v16:
time: 85.6 us; the launch traced here: 85.4 us
  Pallas kernels  28.8 us (34%)
  waiting for transfers between devices  27.6 us (32%)
  starting transfers between devices  24.7 us (29%)
  other arithmetic  2.31 us (3%)
  matrix products  1.02 us (1%)
    pallas_call x1, Pallas kernels, cholesky_with_inverse(): pl.pallas_call(functools.partial(cholesky_kernel, factor_scale=1.0 / root...  25.3 us
    ppermute x11, starting transfers between devices, exchange(): lax.ppermute(value, DEVICE_AXES, [(i, i ^ mask) for i in range(count)])  16.8 us
    ppermute x11, waiting for transfers between devices, exchange(): lax.ppermute(value, DEVICE_AXES, [(i, i ^ mask) for i in range(count)])  15.7 us
    ppermute x2, waiting for transfers between devices, shifted(): lax.ppermute(value, axis, [(source, source + steps) for source in range(i...  12 us
    ppermute x2, starting transfers between devices, shifted(): lax.ppermute(value, axis, [(source, source + steps) for source in range(i...  7.93 us
    pallas_call x1, Pallas kernels, aggregate(): pl.pallas_call(aggregate_kernel, out_shape=(table, table, table), in_spec...  3.5 us
  transfers between devices with their start and end apart: 13, of which 10 were waited for; matrix products, arithmetic and copies ran while one was open for 0% of the time, Pallas kernels for 0%

profile of v16, /device:TPU:1, one launch (start us, length us, event | category | flops | bytes accessed | tf_op | source)
XLA Modules:
  0.0 85.4 jit_solution(15310471030377810352)
XLA Ops:
  0.6 3.5 %shard_map.68 = (f32[4,128,256]{2,1,0:T(8,128)}, f32[4,128,256]{2,1,0:T(8,128)}, f32[4,128,256]{2,1,0:T(8,128)}) custom-call(s32[2,16]{1,0:T(2,128)} %bitcast.17, s32[1]{0:T(128)} %bitcast.1.base_ref, bf16[16,2,128,128]{3,2,1,0:T(8,128)(2,1)} %weight_ref.1, bf16[16,128,256]{2,1,0:T(8,128)(2,1)} %bitcast.14), custom_call_target="tpu_custom_call" | custom-call | tf_op jit(solution)/shard_map/pallas_call | solution.py:189
  4.1 4.0 %collective-permute-start = (f32[4,128,256]{2,1,0:T(8,128)}, f32[4,128,256]{2,1,0:T(8,128)S(1)}, u32[]{:S(2)}, u32[]{:S(2)}) collective-permute-start(f32[4,128,256]{2,1,0:T(8,128)} %get-tuple-element.8), channel_id=1, source_target_pairs={{0,1},{1,2},{2,3},{3,4},{4,5},{5,6},{6,7},{7,8},{8,9},{9,10},{10,1... | collective-permute-start | bytes 1572872 | tf_op jit(solution)/shard_map/ppermute | solution.py:21
  8.2 3.9 %collective-permute-start.1 = (f32[4,128,256]{2,1,0:T(8,128)}, f32[4,128,256]{2,1,0:T(8,128)S(1)}, u32[]{:S(2)}, u32[]{:S(2)}) collective-permute-start(f32[4,128,256]{2,1,0:T(8,128)} %get-tuple-element.9), channel_id=1, source_target_pairs={{1,0},{2,1},{3,2},{4,3},{5,4},{6,5},{7,6},{8,7},{9,8},{10,9},{11,1... | collective-permute-start | bytes 1572872 | tf_op jit(solution)/shard_map/ppermute | solution.py:21
  12.1 0.1 pad_slice_fusion
  12.2 9.7 %collective-permute-done = f32[4,128,256]{2,1,0:T(8,128)S(1)} collective-permute-done((f32[4,128,256]{2,1,0:T(8,128)}, f32[4,128,256]{2,1,0:T(8,128)S(1)}, u32[]{:S(2)}, u32[]{:S(2)}) %collective-permute-start) | collective-permute-done | bytes 524320 | tf_op jit(solution)/shard_map/ppermute | solution.py:21
  21.8 2.3 %collective-permute-done.1 = f32[4,128,256]{2,1,0:T(8,128)S(1)} collective-permute-done((f32[4,128,256]{2,1,0:T(8,128)}, f32[4,128,256]{2,1,0:T(8,128)S(1)}, u32[]{:S(2)}, u32[]{:S(2)}) %collective-permute-start.1) | collective-permute-done | bytes 524320 | tf_op jit(solution)/shard_map/ppermute | solution.py:21
  24.1 0.0 copy-start.1
  24.1 0.0 copy-start.2
  24.2 1.2 %add_add_fusion = f32[4,128,256]{2,1,0:T(8,128)S(1)} fusion(f32[4,128,256]{2,1,0:T(8,128)S(1)} %collective-permute-done.1, f32[4,128,256]{2,1,0:T(8,128)} %get-tuple-element.7, f32[4,128,256]{2,1,0:T(8,128)S(1)} %collective-permute-done), kind=kLoop, calls=%fused_computation.2 | loop fusion | flops 262144 | bytes 2097152 | tf_op jit(solution)/shard_map/add | solution.py:221
  25.4 0.0 copy-done.1
  25.4 0.0 copy-done.2
  25.4 0.1 fusion.anomaly_ref
  25.5 0.0 copy-start
  25.5 1.0 %fusion.7 = f32[256,256]{1,0:T(8,128)S(1)} fusion(f32[512,256]{1,0:T(8,128)S(1)} %fusion.anomaly_ref), kind=kOutput, calls=%fused_computation.25 | convolution fusion | flops 402653184 | bytes 786432 | tf_op jit(solution)/shard_map/dot_general | solution.py:224
  26.6 0.0 copy-done
  26.6 0.1 copy.7
  26.8 0.1 broadcast_select_fusion
  26.9 0.5 collective-permute-start.2
  27.4 0.9 %collective-permute-done.2 = f32[72,256]{1,0:T(8,128)S(1)} collective-permute-done((f32[72,256]{1,0:T(8,128)S(1)}, f32[72,256]{1,0:T(8,128)S(1)}, u32[]{:S(2)}, u32[]{:S(2)}) %collective-permute-start.2) | collective-permute-done | bytes 73760 | tf_op jit(solution)/shard_map/ppermute | solution.py:39
  28.3 0.1 select_add_fusion
  28.4 1.4 %collective-permute-start.3 = (f32[72,256]{1,0:T(8,128)S(1)}, f32[72,256]{1,0:T(8,128)S(1)}, u32[]{:S(2)}, u32[]{:S(2)}) collective-permute-start(f32[72,256]{1,0:T(8,128)S(1)} %select_add_fusion), channel_id=1, source_target_pairs={{0,1},{1,0},{2,3},{3,2},{4,5},{5,4},{6,7},{7,6},{8,9},{9,8},{10,11... | collective-permute-start | bytes 221192 | tf_op jit(solution)/shard_map/ppermute | solution.py:39
  29.8 4.1 %collective-permute-start.4 = (f32[72,256]{1,0:T(8,128)S(1)}, f32[72,256]{1,0:T(8,128)S(1)}, u32[]{:S(2)}, u32[]{:S(2)}) collective-permute-start(f32[72,256]{1,0:T(8,128)S(1)} %select_add_fusion), channel_id=1, source_target_pairs={{0,2},{1,3},{2,0},{3,1},{4,6},{5,7},{6,4},{7,5},{8,10},{9,11},{10,... | collective-permute-start | bytes 221192 | tf_op jit(solution)/shard_map/ppermute | solution.py:39
  33.9 0.0 collective-permute-start.5
  33.9 0.0 collective-permute-done.3
  33.9 3.8 %collective-permute-done.4 = f32[72,256]{1,0:T(8,128)S(1)} collective-permute-done((f32[72,256]{1,0:T(8,128)S(1)}, f32[72,256]{1,0:T(8,128)S(1)}, u32[]{:S(2)}, u32[]{:S(2)}) %collective-permute-start.4) | collective-permute-done | bytes 73760 | tf_op jit(solution)/shard_map/ppermute | solution.py:39
  37.7 1.5 %collective-permute-done.5 = f32[72,256]{1,0:T(8,128)S(1)} collective-permute-done((f32[72,256]{1,0:T(8,128)S(1)}, f32[72,256]{1,0:T(8,128)S(1)}, u32[]{:S(2)}, u32[]{:S(2)}) %collective-permute-start.5) | collective-permute-done | bytes 73760 | tf_op jit(solution)/shard_map/ppermute | solution.py:39
  39.2 1.7 %collective-permute-start.6 = (f32[72,256]{1,0:T(8,128)S(1)}, f32[72,256]{1,0:T(8,128)S(1)}, u32[]{:S(2)}, u32[]{:S(2)}) collective-permute-start(f32[72,256]{1,0:T(8,128)S(1)} %add_add_fusion.3), channel_id=1, source_target_pairs={{0,8},{1,9},{2,10},{3,11},{4,12},{5,13},{6,14},{7,15},{8,0},{9,1},... | collective-permute-start | bytes 221192 | tf_op jit(solution)/shard_map/ppermute | solution.py:39
  40.9 1.8 %collective-permute-start.7 = (f32[72,256]{1,0:T(8,128)S(1)}, f32[72,256]{1,0:T(8,128)S(1)}, u32[]{:S(2)}, u32[]{:S(2)}) collective-permute-start(f32[72,256]{1,0:T(8,128)S(1)} %add_add_fusion.3), channel_id=1, source_target_pairs={{0,16},{1,17},{2,18},{3,19},{4,20},{5,21},{6,22},{7,23},{8,24},{9,... | collective-permute-start | bytes 221192 | tf_op jit(solution)/shard_map/ppermute | solution.py:39
  42.7 0.7 collective-permute-start.8
  43.4 0.0 collective-permute-done.6
  43.4 3.1 %collective-permute-done.7 = f32[72,256]{1,0:T(8,128)S(1)} collective-permute-done((f32[72,256]{1,0:T(8,128)S(1)}, f32[72,256]{1,0:T(8,128)S(1)}, u32[]{:S(2)}, u32[]{:S(2)}) %collective-permute-start.7) | collective-permute-done | bytes 73760 | tf_op jit(solution)/shard_map/ppermute | solution.py:39
  46.5 1.4 %collective-permute-done.8 = f32[72,256]{1,0:T(8,128)S(1)} collective-permute-done((f32[72,256]{1,0:T(8,128)S(1)}, f32[72,256]{1,0:T(8,128)S(1)}, u32[]{:S(2)}, u32[]{:S(2)}) %collective-permute-start.8) | collective-permute-done | bytes 73760 | tf_op jit(solution)/shard_map/ppermute | solution.py:39
  48.0 2.8 %collective-permute-start.10 = (f32[72,256]{1,0:T(8,128)S(1)}, f32[72,256]{1,0:T(8,128)S(1)}, u32[]{:S(2)}, u32[]{:S(2)}) collective-permute-start(f32[72,256]{1,0:T(8,128)S(1)} %add_add_fusion.2), channel_id=1, source_target_pairs={{0,64},{1,65},{2,66},{3,67},{4,68},{5,69},{6,70},{7,71},{8,72},{9,... | collective-permute-start | bytes 221192 | tf_op jit(solution)/shard_map/ppermute | solution.py:39
  50.8 0.9 %collective-permute-start.11 = (f32[72,256]{1,0:T(8,128)S(1)}, f32[72,256]{1,0:T(8,128)S(1)}, u32[]{:S(2)}, u32[]{:S(2)}) collective-permute-start(f32[72,256]{1,0:T(8,128)S(1)} %add_add_fusion.2), channel_id=1, source_target_pairs={{0,96},{1,97},{2,98},{3,99},{4,100},{5,101},{6,102},{7,103},{8,104... | collective-permute-start | bytes 221192 | tf_op jit(solution)/shard_map/ppermute | solution.py:39
  51.6 0.0 collective-permute-start.9
  51.6 1.1 %collective-permute-done.10 = f32[72,256]{1,0:T(8,128)S(1)} collective-permute-done((f32[72,256]{1,0:T(8,128)S(1)}, f32[72,256]{1,0:T(8,128)S(1)}, u32[]{:S(2)}, u32[]{:S(2)}) %collective-permute-start.10) | collective-permute-done | bytes 73760 | tf_op jit(solution)/shard_map/ppermute | solution.py:39
  52.7 2.9 %collective-permute-done.11 = f32[72,256]{1,0:T(8,128)S(1)} collective-permute-done((f32[72,256]{1,0:T(8,128)S(1)}, f32[72,256]{1,0:T(8,128)S(1)}, u32[]{:S(2)}, u32[]{:S(2)}) %collective-permute-start.11) | collective-permute-done | bytes 73760 | tf_op jit(solution)/shard_map/ppermute | solution.py:39
  55.7 0.0 collective-permute-done.9
  55.7 2.9 %collective-permute-start.12 = (f32[72,256]{1,0:T(8,128)S(1)}, f32[72,256]{1,0:T(8,128)S(1)}, u32[]{:S(2)}, u32[]{:S(2)}) collective-permute-start(f32[72,256]{1,0:T(8,128)S(1)} %add_add_fusion.1), channel_id=1, source_target_pairs={{0,4},{1,5},{2,6},{3,7},{4,0},{5,1},{6,2},{7,3},{8,12},{9,13},{10,... | collective-permute-start | bytes 221192 | tf_op jit(solution)/shard_map/ppermute | solution.py:39
  58.6 0.9 %collective-permute-done.12 = f32[72,256]{1,0:T(8,128)S(1)} collective-permute-done((f32[72,256]{1,0:T(8,128)S(1)}, f32[72,256]{1,0:T(8,128)S(1)}, u32[]{:S(2)}, u32[]{:S(2)}) %collective-permute-start.12) | collective-permute-done | bytes 73760 | tf_op jit(solution)/shard_map/ppermute | solution.py:39
  59.5 0.7 maximum_select_fusion.packed_ref
  60.2 25.3 %shard_map.69 = (f32[256,256]{1,0:T(8,128)}, f32[512,256]{1,0:T(8,128)}) custom-call(f32[144,256]{1,0:T(8,128)} %maximum_select_fusion.packed_ref, f32[512,256]{1,0:T(8,128)} %copy-done), custom_call_target="tpu_custom_call" | custom-call | tf_op jit(solution)/shard_map/pallas_call | solution.py:158
  (6 shorter events, 0.1 us)
Async XLA Ops:
  4.1 17.7 %collective-permute-start = (f32[4,128,256]{2,1,0:T(8,128)}, f32[4,128,256]{2,1,0:T(8,128)S(1)}, u32[]{:S(2)}, u32[]{:S(2)}) collective-permute-start(f32[4,128,256]{2,1,0:T(8,128)} %get-tuple-element.8), channel_id=1, source_target_pairs={{0,1},{1,2},{2,3},{3,4},{4,5},{5,6},{6,7},{7,8},{8,9},{9,10},{10,1... | collective-permute-start | bytes 1572872 | tf_op jit(solution)/shard_map/ppermute | solution.py:21
  8.2 16.0 %collective-permute-start.1 = (f32[4,128,256]{2,1,0:T(8,128)}, f32[4,128,256]{2,1,0:T(8,128)S(1)}, u32[]{:S(2)}, u32[]{:S(2)}) collective-permute-start(f32[4,128,256]{2,1,0:T(8,128)} %get-tuple-element.9), channel_id=1, source_target_pairs={{1,0},{2,1},{3,2},{4,3},{5,4},{6,5},{7,6},{8,7},{9,8},{10,9},{11,1... | collective-permute-start | bytes 1572872 | tf_op jit(solution)/shard_map/ppermute | solution.py:21
  24.1 1.2 %copy-start.1 = (f32[512,256]{1,0:T(8,128)S(1)}, f32[512,256]{1,0:T(8,128)}, u32[]{:S(2)}) copy-start(f32[512,256]{1,0:T(8,128)} %param.8) | copy-start | bytes 1572868
  24.1 1.2 %copy-start.2 = (f32[512]{0:T(512)S(1)}, f32[512]{0:T(512)}, u32[]{:S(2)}) copy-start(f32[512]{0:T(512)} %param.9) | copy-start | bytes 6148
  25.5 1.0 %copy-start = (f32[512,256]{1,0:T(8,128)}, f32[512,256]{1,0:T(8,128)S(1)}, u32[]{:S(2)}) copy-start(f32[512,256]{1,0:T(8,128)S(1)} %fusion.anomaly_ref) | copy-start | bytes 1572868
  26.9 1.4 %collective-permute-start.2 = (f32[72,256]{1,0:T(8,128)S(1)}, f32[72,256]{1,0:T(8,128)S(1)}, u32[]{:S(2)}, u32[]{:S(2)}) collective-permute-start(f32[72,256]{1,0:T(8,128)S(1)} %broadcast_select_fusion), channel_id=1, source_target_pairs={{0,4},{1,5},{2,6},{3,7},{4,0},{5,1},{6,2},{7,3},{8,12},{9,13},{10,... | collective-permute-start | bytes 221192 | tf_op jit(solution)/shard_map/ppermute | solution.py:39
  28.4 5.5 %collective-permute-start.3 = (f32[72,256]{1,0:T(8,128)S(1)}, f32[72,256]{1,0:T(8,128)S(1)}, u32[]{:S(2)}, u32[]{:S(2)}) collective-permute-start(f32[72,256]{1,0:T(8,128)S(1)} %select_add_fusion), channel_id=1, source_target_pairs={{0,1},{1,0},{2,3},{3,2},{4,5},{5,4},{6,7},{7,6},{8,9},{9,8},{10,11... | collective-permute-start | bytes 221192 | tf_op jit(solution)/shard_map/ppermute | solution.py:39
  29.8 7.9 %collective-permute-start.4 = (f32[72,256]{1,0:T(8,128)S(1)}, f32[72,256]{1,0:T(8,128)S(1)}, u32[]{:S(2)}, u32[]{:S(2)}) collective-permute-start(f32[72,256]{1,0:T(8,128)S(1)} %select_add_fusion), channel_id=1, source_target_pairs={{0,2},{1,3},{2,0},{3,1},{4,6},{5,7},{6,4},{7,5},{8,10},{9,11},{10,... | collective-permute-start | bytes 221192 | tf_op jit(solution)/shard_map/ppermute | solution.py:39
  33.9 5.3 %collective-permute-start.5 = (f32[72,256]{1,0:T(8,128)S(1)}, f32[72,256]{1,0:T(8,128)S(1)}, u32[]{:S(2)}, u32[]{:S(2)}) collective-permute-start(f32[72,256]{1,0:T(8,128)S(1)} %select_add_fusion), channel_id=1, source_target_pairs={{0,3},{1,2},{2,1},{3,0},{4,7},{5,6},{6,5},{7,4},{8,11},{9,10},{10,... | collective-permute-start | bytes 221192 | tf_op jit(solution)/shard_map/ppermute | solution.py:39
  39.2 4.2 %collective-permute-start.6 = (f32[72,256]{1,0:T(8,128)S(1)}, f32[72,256]{1,0:T(8,128)S(1)}, u32[]{:S(2)}, u32[]{:S(2)}) collective-permute-start(f32[72,256]{1,0:T(8,128)S(1)} %add_add_fusion.3), channel_id=1, source_target_pairs={{0,8},{1,9},{2,10},{3,11},{4,12},{5,13},{6,14},{7,15},{8,0},{9,1},... | collective-permute-start | bytes 221192 | tf_op jit(solution)/shard_map/ppermute | solution.py:39
  40.9 5.6 %collective-permute-start.7 = (f32[72,256]{1,0:T(8,128)S(1)}, f32[72,256]{1,0:T(8,128)S(1)}, u32[]{:S(2)}, u32[]{:S(2)}) collective-permute-start(f32[72,256]{1,0:T(8,128)S(1)} %add_add_fusion.3), channel_id=1, source_target_pairs={{0,16},{1,17},{2,18},{3,19},{4,20},{5,21},{6,22},{7,23},{8,24},{9,... | collective-permute-start | bytes 221192 | tf_op jit(solution)/shard_map/ppermute | solution.py:39
  42.7 5.3 %collective-permute-start.8 = (f32[72,256]{1,0:T(8,128)S(1)}, f32[72,256]{1,0:T(8,128)S(1)}, u32[]{:S(2)}, u32[]{:S(2)}) collective-permute-start(f32[72,256]{1,0:T(8,128)S(1)} %add_add_fusion.3), channel_id=1, source_target_pairs={{0,24},{1,25},{2,26},{3,27},{4,28},{5,29},{6,30},{7,31},{8,16},{9,... | collective-permute-start | bytes 221192 | tf_op jit(solution)/shard_map/ppermute | solution.py:39
  48.0 4.8 %collective-permute-start.10 = (f32[72,256]{1,0:T(8,128)S(1)}, f32[72,256]{1,0:T(8,128)S(1)}, u32[]{:S(2)}, u32[]{:S(2)}) collective-permute-start(f32[72,256]{1,0:T(8,128)S(1)} %add_add_fusion.2), channel_id=1, source_target_pairs={{0,64},{1,65},{2,66},{3,67},{4,68},{5,69},{6,70},{7,71},{8,72},{9,... | collective-permute-start | bytes 221192 | tf_op jit(solution)/shard_map/ppermute | solution.py:39
  50.8 4.9 %collective-permute-start.11 = (f32[72,256]{1,0:T(8,128)S(1)}, f32[72,256]{1,0:T(8,128)S(1)}, u32[]{:S(2)}, u32[]{:S(2)}) collective-permute-start(f32[72,256]{1,0:T(8,128)S(1)} %add_add_fusion.2), channel_id=1, source_target_pairs={{0,96},{1,97},{2,98},{3,99},{4,100},{5,101},{6,102},{7,103},{8,104... | collective-permute-start | bytes 221192 | tf_op jit(solution)/shard_map/ppermute | solution.py:39
  51.6 4.0 %collective-permute-start.9 = (f32[72,256]{1,0:T(8,128)S(1)}, f32[72,256]{1,0:T(8,128)S(1)}, u32[]{:S(2)}, u32[]{:S(2)}) collective-permute-start(f32[72,256]{1,0:T(8,128)S(1)} %add_add_fusion.2), channel_id=1, source_target_pairs={{0,32},{1,33},{2,34},{3,35},{4,36},{5,37},{6,38},{7,39},{8,40},{9,... | collective-permute-start | bytes 221192 | tf_op jit(solution)/shard_map/ppermute | solution.py:39
  55.7 3.8 %collective-permute-start.12 = (f32[72,256]{1,0:T(8,128)S(1)}, f32[72,256]{1,0:T(8,128)S(1)}, u32[]{:S(2)}, u32[]{:S(2)}) collective-permute-start(f32[72,256]{1,0:T(8,128)S(1)} %add_add_fusion.1), channel_id=1, source_target_pairs={{0,4},{1,5},{2,6},{3,7},{4,0},{5,1},{6,2},{7,3},{8,12},{9,13},{10,... | collective-permute-start | bytes 221192 | tf_op jit(solution)/shard_map/ppermute | solution.py:39

commit v17 on v16

--- a/solution.py
+++ b/solution.py
@@ -12,7 +12,7 @@
 exact_mode = lax.Precision.HIGHEST
 DEVICE_AXES = ("lat", "sub")
 CORE_BIT = 2
-PANEL = 128
+PANEL = 256
 
 
 def shifted(value, axis, steps):
@@ -143,7 +143,7 @@
     part_rows = max(PANEL, size // 4)
     for row0 in range(0, size, part_rows):
         col0 = (size // 2) * (row0 // (size // 2))
-        col1 = col0 + size // 2
+        col1 = -(-(row0 + part_rows) // (size // 2)) * (size // 2)
         for first in range(row0, row0 + part_rows, PANEL):
             panel(first, row0, col0, col1)
     scores_ref[...] = lax.dot_general(

time: 85.6 us -> 86.6 us (1.012)
  Pallas kernels: 28.8 us -> 29.7 us
    pallas_call x1, Pallas kernels: 25.3 us -> 26.2 us  [cholesky_with_inverse(): pl.pallas_call(functools.partial(cholesky_kernel, factor_scale=1.0 / root...]
where the time goes in v17:
time: 86.6 us; the launch traced here: 86.4 us
  Pallas kernels  29.7 us (34%)
  waiting for transfers between devices  27.6 us (32%)
  starting transfers between devices  24.7 us (29%)
  other arithmetic  2.31 us (3%)
  matrix products  1.02 us (1%)
    pallas_call x1, Pallas kernels, cholesky_with_inverse(): pl.pallas_call(functools.partial(cholesky_kernel, factor_scale=1.0 / root...  26.2 us
    ppermute x11, starting transfers between devices, exchange(): lax.ppermute(value, DEVICE_AXES, [(i, i ^ mask) for i in range(count)])  16.8 us
    ppermute x11, waiting for transfers between devices, exchange(): lax.ppermute(value, DEVICE_AXES, [(i, i ^ mask) for i in range(count)])  15.7 us
    ppermute x2, waiting for transfers between devices, shifted(): lax.ppermute(value, axis, [(source, source + steps) for source in range(i...  12 us
    ppermute x2, starting transfers between devices, shifted(): lax.ppermute(value, axis, [(source, source + steps) for source in range(i...  7.93 us
    pallas_call x1, Pallas kernels, aggregate(): pl.pallas_call(aggregate_kernel, out_shape=(table, table, table), in_spec...  3.5 us
  transfers between devices with their start and end apart: 13, of which 10 were waited for; matrix products, arithmetic and copies ran while one was open for 0% of the time, Pallas kernels for 0%

profile of v17, /device:TPU:1, one launch (start us, length us, event | category | flops | bytes accessed | tf_op | source)
XLA Modules:
  0.0 86.4 jit_solution(13725259098949956128)
XLA Ops:
  0.6 3.5 %shard_map.68 = (f32[4,128,256]{2,1,0:T(8,128)}, f32[4,128,256]{2,1,0:T(8,128)}, f32[4,128,256]{2,1,0:T(8,128)}) custom-call(s32[2,16]{1,0:T(2,128)} %bitcast.17, s32[1]{0:T(128)} %bitcast.1.base_ref, bf16[16,2,128,128]{3,2,1,0:T(8,128)(2,1)} %weight_ref.1, bf16[16,128,256]{2,1,0:T(8,128)(2,1)} %bitcast.14), custom_call_target="tpu_custom_call" | custom-call | tf_op jit(solution)/shard_map/pallas_call | solution.py:189
  4.1 4.0 %collective-permute-start = (f32[4,128,256]{2,1,0:T(8,128)}, f32[4,128,256]{2,1,0:T(8,128)S(1)}, u32[]{:S(2)}, u32[]{:S(2)}) collective-permute-start(f32[4,128,256]{2,1,0:T(8,128)} %get-tuple-element.8), channel_id=1, source_target_pairs={{0,1},{1,2},{2,3},{3,4},{4,5},{5,6},{6,7},{7,8},{8,9},{9,10},{10,1... | collective-permute-start | bytes 1572872 | tf_op jit(solution)/shard_map/ppermute | solution.py:21
  8.2 3.9 %collective-permute-start.1 = (f32[4,128,256]{2,1,0:T(8,128)}, f32[4,128,256]{2,1,0:T(8,128)S(1)}, u32[]{:S(2)}, u32[]{:S(2)}) collective-permute-start(f32[4,128,256]{2,1,0:T(8,128)} %get-tuple-element.9), channel_id=1, source_target_pairs={{1,0},{2,1},{3,2},{4,3},{5,4},{6,5},{7,6},{8,7},{9,8},{10,9},{11,1... | collective-permute-start | bytes 1572872 | tf_op jit(solution)/shard_map/ppermute | solution.py:21
  12.1 0.1 pad_slice_fusion
  12.2 9.7 %collective-permute-done = f32[4,128,256]{2,1,0:T(8,128)S(1)} collective-permute-done((f32[4,128,256]{2,1,0:T(8,128)}, f32[4,128,256]{2,1,0:T(8,128)S(1)}, u32[]{:S(2)}, u32[]{:S(2)}) %collective-permute-start) | collective-permute-done | bytes 524320 | tf_op jit(solution)/shard_map/ppermute | solution.py:21
  21.8 2.3 %collective-permute-done.1 = f32[4,128,256]{2,1,0:T(8,128)S(1)} collective-permute-done((f32[4,128,256]{2,1,0:T(8,128)}, f32[4,128,256]{2,1,0:T(8,128)S(1)}, u32[]{:S(2)}, u32[]{:S(2)}) %collective-permute-start.1) | collective-permute-done | bytes 524320 | tf_op jit(solution)/shard_map/ppermute | solution.py:21
  24.1 0.0 copy-start.1
  24.1 0.0 copy-start.2
  24.2 1.2 %add_add_fusion = f32[4,128,256]{2,1,0:T(8,128)S(1)} fusion(f32[4,128,256]{2,1,0:T(8,128)S(1)} %collective-permute-done.1, f32[4,128,256]{2,1,0:T(8,128)} %get-tuple-element.7, f32[4,128,256]{2,1,0:T(8,128)S(1)} %collective-permute-done), kind=kLoop, calls=%fused_computation.2 | loop fusion | flops 262144 | bytes 2097152 | tf_op jit(solution)/shard_map/add | solution.py:221
  25.4 0.0 copy-done.1
  25.4 0.0 copy-done.2
  25.4 0.1 fusion.anomaly_ref
  25.5 0.0 copy-start
  25.5 1.0 %fusion.7 = f32[256,256]{1,0:T(8,128)S(1)} fusion(f32[512,256]{1,0:T(8,128)S(1)} %fusion.anomaly_ref), kind=kOutput, calls=%fused_computation.25 | convolution fusion | flops 402653184 | bytes 786432 | tf_op jit(solution)/shard_map/dot_general | solution.py:224
  26.6 0.0 copy-done
  26.6 0.1 copy.7
  26.8 0.1 broadcast_select_fusion
  26.9 0.5 collective-permute-start.2
  27.4 0.9 %collective-permute-done.2 = f32[72,256]{1,0:T(8,128)S(1)} collective-permute-done((f32[72,256]{1,0:T(8,128)S(1)}, f32[72,256]{1,0:T(8,128)S(1)}, u32[]{:S(2)}, u32[]{:S(2)}) %collective-permute-start.2) | collective-permute-done | bytes 73760 | tf_op jit(solution)/shard_map/ppermute | solution.py:39
  28.3 0.1 select_add_fusion
  28.4 1.4 %collective-permute-start.3 = (f32[72,256]{1,0:T(8,128)S(1)}, f32[72,256]{1,0:T(8,128)S(1)}, u32[]{:S(2)}, u32[]{:S(2)}) collective-permute-start(f32[72,256]{1,0:T(8,128)S(1)} %select_add_fusion), channel_id=1, source_target_pairs={{0,1},{1,0},{2,3},{3,2},{4,5},{5,4},{6,7},{7,6},{8,9},{9,8},{10,11... | collective-permute-start | bytes 221192 | tf_op jit(solution)/shard_map/ppermute | solution.py:39
  29.8 4.1 %collective-permute-start.4 = (f32[72,256]{1,0:T(8,128)S(1)}, f32[72,256]{1,0:T(8,128)S(1)}, u32[]{:S(2)}, u32[]{:S(2)}) collective-permute-start(f32[72,256]{1,0:T(8,128)S(1)} %select_add_fusion), channel_id=1, source_target_pairs={{0,2},{1,3},{2,0},{3,1},{4,6},{5,7},{6,4},{7,5},{8,10},{9,11},{10,... | collective-permute-start | bytes 221192 | tf_op jit(solution)/shard_map/ppermute | solution.py:39
  33.9 0.0 collective-permute-start.5
  33.9 0.0 collective-permute-done.3
  33.9 3.8 %collective-permute-done.4 = f32[72,256]{1,0:T(8,128)S(1)} collective-permute-done((f32[72,256]{1,0:T(8,128)S(1)}, f32[72,256]{1,0:T(8,128)S(1)}, u32[]{:S(2)}, u32[]{:S(2)}) %collective-permute-start.4) | collective-permute-done | bytes 73760 | tf_op jit(solution)/shard_map/ppermute | solution.py:39
  37.7 1.5 %collective-permute-done.5 = f32[72,256]{1,0:T(8,128)S(1)} collective-permute-done((f32[72,256]{1,0:T(8,128)S(1)}, f32[72,256]{1,0:T(8,128)S(1)}, u32[]{:S(2)}, u32[]{:S(2)}) %collective-permute-start.5) | collective-permute-done | bytes 73760 | tf_op jit(solution)/shard_map/ppermute | solution.py:39
  39.2 1.7 %collective-permute-start.6 = (f32[72,256]{1,0:T(8,128)S(1)}, f32[72,256]{1,0:T(8,128)S(1)}, u32[]{:S(2)}, u32[]{:S(2)}) collective-permute-start(f32[72,256]{1,0:T(8,128)S(1)} %add_add_fusion.3), channel_id=1, source_target_pairs={{0,8},{1,9},{2,10},{3,11},{4,12},{5,13},{6,14},{7,15},{8,0},{9,1},... | collective-permute-start | bytes 221192 | tf_op jit(solution)/shard_map/ppermute | solution.py:39
  40.9 1.8 %collective-permute-start.7 = (f32[72,256]{1,0:T(8,128)S(1)}, f32[72,256]{1,0:T(8,128)S(1)}, u32[]{:S(2)}, u32[]{:S(2)}) collective-permute-start(f32[72,256]{1,0:T(8,128)S(1)} %add_add_fusion.3), channel_id=1, source_target_pairs={{0,16},{1,17},{2,18},{3,19},{4,20},{5,21},{6,22},{7,23},{8,24},{9,... | collective-permute-start | bytes 221192 | tf_op jit(solution)/shard_map/ppermute | solution.py:39
  42.7 0.7 collective-permute-start.8
  43.4 0.0 collective-permute-done.6
  43.4 3.1 %collective-permute-done.7 = f32[72,256]{1,0:T(8,128)S(1)} collective-permute-done((f32[72,256]{1,0:T(8,128)S(1)}, f32[72,256]{1,0:T(8,128)S(1)}, u32[]{:S(2)}, u32[]{:S(2)}) %collective-permute-start.7) | collective-permute-done | bytes 73760 | tf_op jit(solution)/shard_map/ppermute | solution.py:39
  46.5 1.4 %collective-permute-done.8 = f32[72,256]{1,0:T(8,128)S(1)} collective-permute-done((f32[72,256]{1,0:T(8,128)S(1)}, f32[72,256]{1,0:T(8,128)S(1)}, u32[]{:S(2)}, u32[]{:S(2)}) %collective-permute-start.8) | collective-permute-done | bytes 73760 | tf_op jit(solution)/shard_map/ppermute | solution.py:39
  48.0 2.8 %collective-permute-start.10 = (f32[72,256]{1,0:T(8,128)S(1)}, f32[72,256]{1,0:T(8,128)S(1)}, u32[]{:S(2)}, u32[]{:S(2)}) collective-permute-start(f32[72,256]{1,0:T(8,128)S(1)} %add_add_fusion.2), channel_id=1, source_target_pairs={{0,64},{1,65},{2,66},{3,67},{4,68},{5,69},{6,70},{7,71},{8,72},{9,... | collective-permute-start | bytes 221192 | tf_op jit(solution)/shard_map/ppermute | solution.py:39
  50.8 0.9 collective-permute-start.11
  51.6 0.0 collective-permute-start.9
  51.6 1.1 %collective-permute-done.10 = f32[72,256]{1,0:T(8,128)S(1)} collective-permute-done((f32[72,256]{1,0:T(8,128)S(1)}, f32[72,256]{1,0:T(8,128)S(1)}, u32[]{:S(2)}, u32[]{:S(2)}) %collective-permute-start.10) | collective-permute-done | bytes 73760 | tf_op jit(solution)/shard_map/ppermute | solution.py:39
  52.7 2.9 %collective-permute-done.11 = f32[72,256]{1,0:T(8,128)S(1)} collective-permute-done((f32[72,256]{1,0:T(8,128)S(1)}, f32[72,256]{1,0:T(8,128)S(1)}, u32[]{:S(2)}, u32[]{:S(2)}) %collective-permute-start.11) | collective-permute-done | bytes 73760 | tf_op jit(solution)/shard_map/ppermute | solution.py:39
  55.7 0.0 collective-permute-done.9
  55.7 2.9 %collective-permute-start.12 = (f32[72,256]{1,0:T(8,128)S(1)}, f32[72,256]{1,0:T(8,128)S(1)}, u32[]{:S(2)}, u32[]{:S(2)}) collective-permute-start(f32[72,256]{1,0:T(8,128)S(1)} %add_add_fusion.1), channel_id=1, source_target_pairs={{0,4},{1,5},{2,6},{3,7},{4,0},{5,1},{6,2},{7,3},{8,12},{9,13},{10,... | collective-permute-start | bytes 221192 | tf_op jit(solution)/shard_map/ppermute | solution.py:39
  58.6 0.9 %collective-permute-done.12 = f32[72,256]{1,0:T(8,128)S(1)} collective-permute-done((f32[72,256]{1,0:T(8,128)S(1)}, f32[72,256]{1,0:T(8,128)S(1)}, u32[]{:S(2)}, u32[]{:S(2)}) %collective-permute-start.12) | collective-permute-done | bytes 73760 | tf_op jit(solution)/shard_map/ppermute | solution.py:39
  59.5 0.7 maximum_select_fusion.packed_ref
  60.2 26.2 %shard_map.69 = (f32[256,256]{1,0:T(8,128)}, f32[512,256]{1,0:T(8,128)}) custom-call(f32[144,256]{1,0:T(8,128)} %maximum_select_fusion.packed_ref, f32[512,256]{1,0:T(8,128)} %copy-done), custom_call_target="tpu_custom_call" | custom-call | tf_op jit(solution)/shard_map/pallas_call | solution.py:158
  (6 shorter events, 0.1 us)
Async XLA Ops:
  4.1 17.7 %collective-permute-start = (f32[4,128,256]{2,1,0:T(8,128)}, f32[4,128,256]{2,1,0:T(8,128)S(1)}, u32[]{:S(2)}, u32[]{:S(2)}) collective-permute-start(f32[4,128,256]{2,1,0:T(8,128)} %get-tuple-element.8), channel_id=1, source_target_pairs={{0,1},{1,2},{2,3},{3,4},{4,5},{5,6},{6,7},{7,8},{8,9},{9,10},{10,1... | collective-permute-start | bytes 1572872 | tf_op jit(solution)/shard_map/ppermute | solution.py:21
  8.2 16.0 %collective-permute-start.1 = (f32[4,128,256]{2,1,0:T(8,128)}, f32[4,128,256]{2,1,0:T(8,128)S(1)}, u32[]{:S(2)}, u32[]{:S(2)}) collective-permute-start(f32[4,128,256]{2,1,0:T(8,128)} %get-tuple-element.9), channel_id=1, source_target_pairs={{1,0},{2,1},{3,2},{4,3},{5,4},{6,5},{7,6},{8,7},{9,8},{10,9},{11,1... | collective-permute-start | bytes 1572872 | tf_op jit(solution)/shard_map/ppermute | solution.py:21
  24.1 1.2 %copy-start.1 = (f32[512,256]{1,0:T(8,128)S(1)}, f32[512,256]{1,0:T(8,128)}, u32[]{:S(2)}) copy-start(f32[512,256]{1,0:T(8,128)} %param.8) | copy-start | bytes 1572868
  24.1 1.2 %copy-start.2 = (f32[512]{0:T(512)S(1)}, f32[512]{0:T(512)}, u32[]{:S(2)}) copy-start(f32[512]{0:T(512)} %param.9) | copy-start | bytes 6148
  25.5 1.0 %copy-start = (f32[512,256]{1,0:T(8,128)}, f32[512,256]{1,0:T(8,128)S(1)}, u32[]{:S(2)}) copy-start(f32[512,256]{1,0:T(8,128)S(1)} %fusion.anomaly_ref) | copy-start | bytes 1572868
  26.9 1.4 %collective-permute-start.2 = (f32[72,256]{1,0:T(8,128)S(1)}, f32[72,256]{1,0:T(8,128)S(1)}, u32[]{:S(2)}, u32[]{:S(2)}) collective-permute-start(f32[72,256]{1,0:T(8,128)S(1)} %broadcast_select_fusion), channel_id=1, source_target_pairs={{0,4},{1,5},{2,6},{3,7},{4,0},{5,1},{6,2},{7,3},{8,12},{9,13},{10,... | collective-permute-start | bytes 221192 | tf_op jit(solution)/shard_map/ppermute | solution.py:39
  28.4 5.5 %collective-permute-start.3 = (f32[72,256]{1,0:T(8,128)S(1)}, f32[72,256]{1,0:T(8,128)S(1)}, u32[]{:S(2)}, u32[]{:S(2)}) collective-permute-start(f32[72,256]{1,0:T(8,128)S(1)} %select_add_fusion), channel_id=1, source_target_pairs={{0,1},{1,0},{2,3},{3,2},{4,5},{5,4},{6,7},{7,6},{8,9},{9,8},{10,11... | collective-permute-start | bytes 221192 | tf_op jit(solution)/shard_map/ppermute | solution.py:39
  29.8 7.9 %collective-permute-start.4 = (f32[72,256]{1,0:T(8,128)S(1)}, f32[72,256]{1,0:T(8,128)S(1)}, u32[]{:S(2)}, u32[]{:S(2)}) collective-permute-start(f32[72,256]{1,0:T(8,128)S(1)} %select_add_fusion), channel_id=1, source_target_pairs={{0,2},{1,3},{2,0},{3,1},{4,6},{5,7},{6,4},{7,5},{8,10},{9,11},{10,... | collective-permute-start | bytes 221192 | tf_op jit(solution)/shard_map/ppermute | solution.py:39
  33.9 5.3 %collective-permute-start.5 = (f32[72,256]{1,0:T(8,128)S(1)}, f32[72,256]{1,0:T(8,128)S(1)}, u32[]{:S(2)}, u32[]{:S(2)}) collective-permute-start(f32[72,256]{1,0:T(8,128)S(1)} %select_add_fusion), channel_id=1, source_target_pairs={{0,3},{1,2},{2,1},{3,0},{4,7},{5,6},{6,5},{7,4},{8,11},{9,10},{10,... | collective-permute-start | bytes 221192 | tf_op jit(solution)/shard_map/ppermute | solution.py:39
  39.2 4.2 %collective-permute-start.6 = (f32[72,256]{1,0:T(8,128)S(1)}, f32[72,256]{1,0:T(8,128)S(1)}, u32[]{:S(2)}, u32[]{:S(2)}) collective-permute-start(f32[72,256]{1,0:T(8,128)S(1)} %add_add_fusion.3), channel_id=1, source_target_pairs={{0,8},{1,9},{2,10},{3,11},{4,12},{5,13},{6,14},{7,15},{8,0},{9,1},... | collective-permute-start | bytes 221192 | tf_op jit(solution)/shard_map/ppermute | solution.py:39
  40.9 5.6 %collective-permute-start.7 = (f32[72,256]{1,0:T(8,128)S(1)}, f32[72,256]{1,0:T(8,128)S(1)}, u32[]{:S(2)}, u32[]{:S(2)}) collective-permute-start(f32[72,256]{1,0:T(8,128)S(1)} %add_add_fusion.3), channel_id=1, source_target_pairs={{0,16},{1,17},{2,18},{3,19},{4,20},{5,21},{6,22},{7,23},{8,24},{9,... | collective-permute-start | bytes 221192 | tf_op jit(solution)/shard_map/ppermute | solution.py:39
  42.7 5.3 %collective-permute-start.8 = (f32[72,256]{1,0:T(8,128)S(1)}, f32[72,256]{1,0:T(8,128)S(1)}, u32[]{:S(2)}, u32[]{:S(2)}) collective-permute-start(f32[72,256]{1,0:T(8,128)S(1)} %add_add_fusion.3), channel_id=1, source_target_pairs={{0,24},{1,25},{2,26},{3,27},{4,28},{5,29},{6,30},{7,31},{8,16},{9,... | collective-permute-start | bytes 221192 | tf_op jit(solution)/shard_map/ppermute | solution.py:39
  48.0 4.8 %collective-permute-start.10 = (f32[72,256]{1,0:T(8,128)S(1)}, f32[72,256]{1,0:T(8,128)S(1)}, u32[]{:S(2)}, u32[]{:S(2)}) collective-permute-start(f32[72,256]{1,0:T(8,128)S(1)} %add_add_fusion.2), channel_id=1, source_target_pairs={{0,64},{1,65},{2,66},{3,67},{4,68},{5,69},{6,70},{7,71},{8,72},{9,... | collective-permute-start | bytes 221192 | tf_op jit(solution)/shard_map/ppermute | solution.py:39
  50.8 4.9 %collective-permute-start.11 = (f32[72,256]{1,0:T(8,128)S(1)}, f32[72,256]{1,0:T(8,128)S(1)}, u32[]{:S(2)}, u32[]{:S(2)}) collective-permute-start(f32[72,256]{1,0:T(8,128)S(1)} %add_add_fusion.2), channel_id=1, source_target_pairs={{0,96},{1,97},{2,98},{3,99},{4,100},{5,101},{6,102},{7,103},{8,104... | collective-permute-start | bytes 221192 | tf_op jit(solution)/shard_map/ppermute | solution.py:39
  51.6 4.0 %collective-permute-start.9 = (f32[72,256]{1,0:T(8,128)S(1)}, f32[72,256]{1,0:T(8,128)S(1)}, u32[]{:S(2)}, u32[]{:S(2)}) collective-permute-start(f32[72,256]{1,0:T(8,128)S(1)} %add_add_fusion.2), channel_id=1, source_target_pairs={{0,32},{1,33},{2,34},{3,35},{4,36},{5,37},{6,38},{7,39},{8,40},{9,... | collective-permute-start | bytes 221192 | tf_op jit(solution)/shard_map/ppermute | solution.py:39
  55.7 3.8 %collective-permute-start.12 = (f32[72,256]{1,0:T(8,128)S(1)}, f32[72,256]{1,0:T(8,128)S(1)}, u32[]{:S(2)}, u32[]{:S(2)}) collective-permute-start(f32[72,256]{1,0:T(8,128)S(1)} %add_add_fusion.1), channel_id=1, source_target_pairs={{0,4},{1,5},{2,6},{3,7},{4,0},{5,1},{6,2},{7,3},{8,12},{9,13},{10,... | collective-permute-start | bytes 221192 | tf_op jit(solution)/shard_map/ppermute | solution.py:39
